TPU v7x, 32 devices: a whole 2x2x4 slice. The times are simulated.
32 devices in a mesh: dp: 1, tensor: 32 (over z, y, x, core).
Axes of the slice: x: 2, y: 2, z: 4, core: 2. Of those that a mesh axis runs over, the one named last changes fastest.
Arguments:
- hidden: bfloat16 [1024, 2048], P(('dp', 'tensor')), may hold values from -6 to 6
- norm_gain: bfloat16 [2048], replicated, may hold values from 0.099609375 to 1.8984375
- router_weight: bfloat16 [2048, 8], replicated, may hold values from -0.125 to 0.125
- kv_weight: bfloat16 [2048, 4096], P(None, 'tensor'), may hold values from -0.125 to 0.125
- query_weight: bfloat16 [2048, 16384], P(None, 'tensor'), may hold values from -0.125 to 0.125
- out_weight: bfloat16 [16384, 2048], P('tensor'), may hold values from -0.5 to 0.5
- routes: int32 [1024, 2], P('dp'), may hold values from 0 to 7, all different within a row; in each aligned block of 1024 rows (0 to 1023, 1024 to 2047, ...) at most 384 rows name the same one
- segment_ids: int32 [1024], P('dp'), may hold values from 0 to 3, never falling along the last dimension, each value on 1 to 512 neighbouring positions
- page_table: int32 [8], P('dp'), may hold values from 0 to 15, as said below
- kv_cache: bfloat16 [16, 128, 4096], P('dp', None, 'tensor'), may hold values from -6 to 6
Outputs:
- attended_out: bfloat16 [1024, 2048], P(('dp', 'tensor'))
- new_cache: bfloat16 [16, 128, 4096], P('dp', None, 'tensor')
Inputs may be any that keep to these rules, and one draw needn't show every extreme that they name: `routes`: no expert is named by more than 384 tokens of a batch, and one is named by exactly 384; a token names two different experts. `segment_ids`: ids never fall along the pack; each prompt has 1 to 512 tokens and one has exactly 512. `page_table`: distinct pages.
All inputs are finite; a program needn't handle non-finite values.
Results may differ from a plain program's by a relative error of at most 0.025.
Values may be sent and summed in bfloat16 or wider, within the bound.
No kernel may reach another device: no remote copies, remote signals or barrier semaphores. Data moves between devices by JAX's collectives and lax.ppermute only.
A program may use at most 128 MiB of HBM per device.

v0:
```python
import jax
import jax.numpy as jnp
from jax import lax
from jax.sharding import PartitionSpec as P

D = 2048
HD = 128
EA = 8
PAGE = 128


def swapped(array, axis, bit):
    return lax.ppermute(array, axis, [(i, i ^ 1 << bit) for i in range(lax.axis_size(axis))])


def normalize(hidden, norm_gain):
    values = hidden.astype(jnp.float32)
    factor = lax.rsqrt(jnp.mean(values * values, axis=-1, keepdims=True) + 1e-05)
    return (values * factor * norm_gain.astype(jnp.float32)).astype(jnp.bfloat16)


def gate_table(normed, router_weight, routes):
    logits = jnp.dot(normed, router_weight, preferred_element_type=jnp.float32)
    chosen = jnp.take_along_axis(logits, routes, axis=1)
    weights = jax.nn.softmax(chosen, axis=-1)
    expert_ids = jnp.arange(router_weight.shape[1], dtype=jnp.int32)
    onehot = (routes[:, :, None] == expert_ids[None, None, :]).astype(jnp.float32)
    return jnp.sum(weights[:, :, None] * onehot, axis=1)


def positions_of(segment_ids):
    index_row = jnp.arange(segment_ids.shape[0], dtype=jnp.int32)
    starts_here = jnp.concatenate([jnp.ones((1,), dtype=bool), segment_ids[1:] != segment_ids[:-1]])
    segment_start = lax.cummax(jnp.where(starts_here, index_row, 0), axis=0)
    return index_row - segment_start


def rotate(values, positions):
    half_width = values.shape[-1] // 2
    frequency = 10000.0 ** (-jnp.arange(half_width, dtype=jnp.float32) / half_width)
    angles = positions.astype(jnp.float32)[:, None] * frequency[None, :]
    angles = angles.reshape((values.shape[0],) + (1,) * (values.ndim - 2) + (half_width,))
    cosine = jnp.cos(angles)
    sine_part = jnp.sin(angles)
    leading = values[..., :half_width]
    trailing = values[..., half_width:]
    return jnp.concatenate(
        [leading * cosine - trailing * sine_part, trailing * cosine + leading * sine_part], axis=-1
    )


def expert_slots(routes, expert, capacity):
    is_hit = jnp.any(routes == expert, axis=1)
    running = jnp.cumsum(is_hit.astype(jnp.int32))
    placed = jnp.where(is_hit, running - 1, capacity)
    index_row = jnp.arange(routes.shape[0], dtype=jnp.int32)
    slot_tok = jnp.zeros((capacity + 1,), jnp.int32).at[placed].set(index_row)[:capacity]
    is_valid = jnp.arange(capacity, dtype=jnp.int32) < running[-1]
    return (slot_tok, is_valid)


def attend(queries, key_rows, value_rows, allowed):
    scores = jnp.dot(queries, key_rows.T, preferred_element_type=jnp.float32)
    scores = jnp.where(allowed, scores, -1e30)
    probabilities = jax.nn.softmax(scores, axis=-1).astype(jnp.bfloat16)
    return jnp.dot(probabilities, value_rows, preferred_element_type=jnp.float32)


def project_kv(normed, weight, positions, first_block):
    projected = jnp.dot(normed, weight, preferred_element_type=jnp.float32)
    block_total = weight.shape[1] // HD
    blocks = projected.reshape(normed.shape[0], block_total, HD)
    block_index = first_block + jnp.arange(block_total, dtype=jnp.int32)
    turned = rotate(blocks, positions)
    chosen = jnp.where((block_index % 2 == 0)[None, :, None], turned, blocks)
    return chosen.astype(jnp.bfloat16).reshape(normed.shape[0], weight.shape[1])


def local(
    hidden,
    norm_gain,
    router_weight,
    kv_weight,
    query_weight,
    out_weight,
    routes,
    segment_ids,
    page_table,
    kv_cache,
):
    device_index = lax.axis_index("tensor")
    token_count = routes.shape[0]
    capacity = 3 * token_count // 8
    normed = lax.all_gather(normalize(hidden, norm_gain), "tensor", axis=0, tiled=True)
    gates = gate_table(normed, router_weight, routes)
    positions = positions_of(segment_ids)
    kv_width = kv_weight.shape[1]
    block_count = kv_width // HD
    own_rows = project_kv(normed, kv_weight, positions, device_index * block_count)
    new_cache = kv_cache.at[page_table].set(own_rows.reshape(page_table.shape[0], PAGE, kv_width))
    partner_rows = swapped(own_rows, "tensor", 0)
    leading_first = device_index % 2 == 0
    head_rows = jnp.where(
        leading_first,
        jnp.concatenate([own_rows, partner_rows], axis=1),
        jnp.concatenate([partner_rows, own_rows], axis=1),
    )
    local_heads = head_rows.shape[1] // (2 * HD)
    head_rows = head_rows.reshape(token_count, local_heads, 2, HD)
    pair_count = query_weight.shape[1] // HD
    local_experts = pair_count // local_heads
    query_cols = query_weight.reshape(D, local_heads, local_experts, HD)
    index_row = jnp.arange(token_count, dtype=jnp.int32)
    scale_factor = HD ** (-0.5)
    spread = jnp.zeros((token_count, local_heads, local_experts, HD), jnp.bfloat16)
    for expert_slot in range(local_experts):
        expert = (device_index * pair_count + expert_slot) % EA
        slot_tok, is_valid = expert_slots(routes, expert, capacity)
        queries = jnp.einsum(
            "cd,dhk->chk",
            normed[slot_tok],
            query_cols[:, :, expert_slot],
            preferred_element_type=jnp.float32,
        )
        queries = (rotate(queries, positions[slot_tok]) * scale_factor).astype(jnp.bfloat16)
        allowed = (segment_ids[slot_tok][:, None] == segment_ids[None, :]) & (
            index_row[None, :] <= slot_tok[:, None]
        )
        attended = jnp.stack(
            [attend(queries[:, 0], head_rows[:, 0, 0], head_rows[:, 0, 1], allowed)], axis=1
        )
        gate_here = gates[slot_tok, expert] * is_valid.astype(jnp.float32)
        gated = (attended * gate_here[:, None, None]).astype(jnp.bfloat16)
        target = jnp.where(is_valid, slot_tok, token_count)
        spread = spread.at[target, :, expert_slot].set(gated, mode="drop")
    flat_spread = spread.reshape(token_count, pair_count * HD)
    reduced = lax.psum_scatter(
        jnp.dot(flat_spread, out_weight, preferred_element_type=jnp.float32).astype(jnp.bfloat16),
        "tensor",
        scatter_dimension=0,
        tiled=True,
    ).astype(jnp.float32)
    attended_out = (hidden.astype(jnp.float32) + reduced).astype(jnp.bfloat16)
    return (attended_out, new_cache)


def solution(mesh):
    placed = (
        P(("dp", "tensor"), None),
        P(),
        P(),
        P(None, "tensor"),
        P(None, "tensor"),
        P("tensor", None),
        P("dp", None),
        P("dp"),
        P("dp"),
        P("dp", None, "tensor"),
    )
    return jax.shard_map(
        local,
        mesh=mesh,
        in_specs=placed,
        out_specs=(P(("dp", "tensor"), None), P("dp", None, "tensor")),
        check_vma=False,
    )
```

profile of v0, /device:TPU:0, one launch (start us, length us, event | category | flops | bytes accessed | tf_op | source)
XLA Modules:
  0.0 394.6 jit_solution(3704315912084242757)
XLA Ops:
  14.0 4.3 %scatter_custom_fusion.6 = s32[385]{0:T(512)S(1)} fusion(s32[1024]{0:T(1024)S(1)} %bitcast.143, s32[1024]{0:T(1024)S(1)} %iota.89, s32[]{:T(128)} %constant.112.clone.1), kind=kCustom, calls=%fused_computation.224 | custom fusion | bytes 1544 | tf_op jit(solution)/shard_map/scatter | solution.py:57
  19.4 3.0 gather_fusion.12
  24.5 4.3 %scatter_custom_fusion.4 = s32[385]{0:T(512)S(1)} fusion(s32[1024]{0:T(1024)S(1)} %bitcast.142, s32[1024]{0:T(1024)S(1)} %iota.87, s32[]{:T(128)} %constant.112.clone.1), kind=kCustom, calls=%fused_computation.226 | custom fusion | bytes 1544 | tf_op jit(solution)/shard_map/scatter | solution.py:57
  32.0 3.0 gather_fusion.8
  36.9 4.3 %scatter_custom_fusion.2 = s32[385]{0:T(512)S(1)} fusion(s32[1024]{0:T(1024)S(1)} %bitcast.144, s32[1024]{0:T(1024)S(1)} %iota.85, s32[]{:T(128)} %constant.112.clone.1), kind=kCustom, calls=%fused_computation.228 | custom fusion | bytes 1544 | tf_op jit(solution)/shard_map/scatter | solution.py:57
  44.3 3.0 gather_fusion.4
  48.0 4.5 %scatter_custom_fusion = s32[385]{0:T(512)S(1)} fusion(s32[1024]{0:T(1024)S(1)} %bitcast.141, s32[1024]{0:T(1024)S(1)} %iota.76, s32[]{:T(128)} %constant.112.clone.1), kind=kCustom, calls=%fused_computation.230 | custom fusion | bytes 1544 | tf_op jit(solution)/shard_map/scatter | solution.py:57
  55.6 3.0 gather_fusion
  58.6 3.9 copy.62
  67.8 8.0 %all-gather.2.cloned.1.call-done = bf16[1024,2048]{1,0:T(8,128)(2,1)} async-done(((bf16[32,2048]{1,0:T(8,128)(2,1)}), bf16[1024,2048]{1,0:T(8,128)(2,1)}) %all-gather.2.cloned.1.call-update) | async-done | bytes 4194320 | tf_op jit(solution)/shard_map/all_gather | solution.py:94
  75.8 7.8 %gather_fusion.13 = bf16[384,2048]{1,0:T(8,128)(2,1)} fusion(bf16[1024,2048]{1,0:T(8,128)(2,1)} %all-gather.2.cloned.1.call-done, s32[1024]{0:T(1024)S(1)} %pad_clamp_fusion), kind=kCustom, calls=%fused_computation.13 | custom fusion | bytes 3147264 | tf_op jit(solution)/shard_map/gather | solution.py:121
  86.4 7.8 %gather_fusion.9 = bf16[384,2048]{1,0:T(8,128)(2,1)} fusion(bf16[1024,2048]{1,0:T(8,128)(2,1)} %all-gather.2.cloned.1.call-done, s32[1024]{0:T(1024)S(1)} %pad_clamp_fusion.1), kind=kCustom, calls=%fused_computation.9 | custom fusion | bytes 3147264 | tf_op jit(solution)/shard_map/gather | solution.py:121
  94.1 2.9 convolution_bitcast_fusion.1
  97.0 3.9 fusion.110
  104.3 12.5 %gather_fusion.16 = f32[2048]{0:T(1024)S(1)} fusion(f32[1024,8]{0,1:T(8,128)S(1)} %fusion.111, s32[2048]{0:T(1024)S(1)} %reshape.1033), kind=kCustom, calls=%fused_computation.16 | custom fusion | bytes 32768 | tf_op jit(solution)/shard_map/jit(take_along_axis)/gather | solution.py:24
  124.3 2.9 gather_fusion.7
  127.8 7.8 %gather_fusion.1 = bf16[384,2048]{1,0:T(8,128)(2,1)} fusion(bf16[1024,2048]{1,0:T(8,128)(2,1)} %all-gather.2.cloned.1.call-done, s32[1024]{0:T(1024)S(1)} %copy-done.24), kind=kCustom, calls=%fused_computation.1 | custom fusion | bytes 3147264 | tf_op jit(solution)/shard_map/gather | solution.py:121
  141.6 7.8 %gather_fusion.5 = bf16[384,2048]{1,0:T(8,128)(2,1)} fusion(bf16[1024,2048]{1,0:T(8,128)(2,1)} %all-gather.2.cloned.1.call-done, s32[1024]{0:T(1024)S(1)} %copy-done.22), kind=kCustom, calls=%fused_computation.5 | custom fusion | bytes 3147264 | tf_op jit(solution)/shard_map/gather | solution.py:121
  161.5 19.2 %scatter_fusion = bf16[1024,4,128]{2,1,0:T(4,128)(2,1)S(1)} fusion(bf16[1024,4,128]{2,1,0:T(4,128)(2,1)S(1)} %broadcast.766, s32[384]{0:T(512)S(1)} %copy-done.7, bf16[384,128]{1,0:T(8,128)(2,1)S(1)} %fusion.12), kind=kCustom, calls=%fused_computation.18 | custom fusion | bytes 297984 | tf_op jit(solution)/shard_map/scatter | solution.py:135
  180.7 19.4 %scatter_fusion.1 = bf16[1024,4,128]{2,1,0:T(4,128)(2,1)S(1)} fusion(bf16[1024,4,128]{2,1,0:T(4,128)(2,1)S(1)} %scatter_fusion, s32[384]{0:T(512)S(1)} %copy-done.6, bf16[384,128]{1,0:T(8,128)(2,1)S(1)} %fusion.13), kind=kCustom, calls=%fused_computation.20 | custom fusion | bytes 297984 | tf_op jit(solution)/shard_map/scatter | solution.py:135
  200.1 19.6 %scatter_fusion.2 = bf16[1024,4,128]{2,1,0:T(4,128)(2,1)S(1)} fusion(bf16[1024,4,128]{2,1,0:T(4,128)(2,1)S(1)} %scatter_fusion.1, s32[384]{0:T(512)S(1)} %copy-done.5, bf16[384,128]{1,0:T(8,128)(2,1)S(1)} %fusion.14), kind=kCustom, calls=%fused_computation.22 | custom fusion | bytes 297984 | tf_op jit(solution)/shard_map/scatter | solution.py:135
  219.7 19.6 %scatter_fusion.3 = bf16[1024,4,128]{2,1,0:T(4,128)(2,1)S(1)} fusion(bf16[1024,4,128]{2,1,0:T(4,128)(2,1)S(1)} %scatter_fusion.2, s32[384]{0:T(512)S(1)} %copy-done.4, bf16[384,128]{1,0:T(8,128)(2,1)S(1)} %fusion.15), kind=kCustom, calls=%fused_computation.24 | custom fusion | bytes 297984 | tf_op jit(solution)/shard_map/scatter | solution.py:135
  239.4 4.3 %convolution_convert_fusion = bf16[1024,2048]{1,0:T(8,128)(2,1)} fusion(bf16[512,2048]{1,0:T(8,128)(2,1)S(1)} %copy-done, bf16[128,8,4,128]{3,2,1,0:T(4,128)(2,1)S(1)} %bitcast.122), kind=kOutput, calls=%fused_computation.26 | convolution fusion | flops 2149580800 | bytes 7340032 | tf_op jit(solution)/shard_map/dot_general | solution.py:138
  246.3 139.4 %reduce-scatter.2.cloned.1.call-done = bf16[32,2048]{1,0:T(8,128)(2,1)} async-done(((bf16[1024,2048]{1,0:T(8,128)(2,1)}), bf16[32,2048]{1,0:T(8,128)(2,1)}) %reduce-scatter.2.cloned.1.call-update) | async-done | bytes 131088 | tf_op jit(solution)/shard_map/reduce_scatter | solution.py:137
  (195 shorter events, 63.1 us)
Async XLA Ops:
  7.2 232.2 %copy-start = (bf16[512,2048]{1,0:T(8,128)(2,1)S(1)}, bf16[512,2048]{1,0:T(8,128)(2,1)}, u32[]{:S(2)}) copy-start(bf16[512,2048]{1,0:T(8,128)(2,1)} %param.15) | copy-start | bytes 6291460
  7.2 3.7 copy-start.18
  7.2 6.2 %copy-start.1 = (s32[1024]{0:T(1024)S(1)}, s32[1024]{0:T(1024)}, u32[]{:S(2)}) copy-start(s32[1024]{0:T(1024)} %param.17) | copy-start | bytes 12292
  7.2 68.6 %all-gather.2.cloned.1.call-start = ((), (), s32[]{:S(2)}) async-start(), calls=%async_computation.1 | async-start | bytes 4325376 | tf_op jit(solution)/shard_map/all_gather | solution.py:94
  10.8 374.9 %reduce-scatter.2.cloned.1.call-start = ((), (), s32[]{:S(2)}) async-start(), calls=%async_computation.2 | async-start | bytes 4325376 | tf_op jit(solution)/shard_map/reduce_scatter | solution.py:137
  42.4 4.9 %copy-start.21 = (s32[1024]{0:T(1024)}, s32[1024]{0:T(1024)S(1)}, u32[]{:S(2)}) copy-start(s32[1024]{0:T(1024)S(1)} %pad_clamp_fusion.2) | copy-start | bytes 12292
  53.7 4.9 %copy-start.23 = (s32[1024]{0:T(1024)}, s32[1024]{0:T(1024)S(1)}, u32[]{:S(2)}) copy-start(s32[1024]{0:T(1024)S(1)} %pad_clamp_fusion.3) | copy-start | bytes 12292
  67.8 33.1 %copy-start.29 = (f32[64]{0:T(128)}, f32[64]{0:T(128)S(1)}, u32[]{:S(2)}) copy-start(f32[64]{0:T(128)S(1)} %multiply_power_fusion) | copy-start | bytes 772
  97.0 6.1 %copy-start.3 = (bf16[1024,2048]{1,0:T(8,128)(2,1)S(1)}, bf16[1024,2048]{1,0:T(8,128)(2,1)}, u32[]{:S(2)}) copy-start(bf16[1024,2048]{1,0:T(8,128)(2,1)} %all-gather.2.cloned.1.call-done) | copy-start | bytes 12582916
  102.8 50.3 %collective-permute-start = (bf16[1024,128]{0,1:T(8,128)(2,1)}, bf16[1024,128]{0,1:T(8,128)(2,1)}, u32[]{:S(2)}, u32[]{:S(2)}) collective-permute-start(bf16[1024,128]{0,1:T(8,128)(2,1)} %fusion.18), channel_id=1, source_target_pairs={{0,1},{1,0},{2,3},{3,2},{4,5},{5,4},{6,7},{7,6},{8,9},{9,8},{10,11... | collective-permute-start | bytes 786440 | tf_op jit(solution)/shard_map/ppermute | solution.py:13
  104.3 13.2 %copy-start.19 = (s32[1024,2]{0,1:T(2,128)S(1)}, s32[1024,2]{0,1:T(2,128)}, u32[]{:S(2)}) copy-start(s32[1024,2]{0,1:T(2,128)} %param.16) | copy-start | bytes 24580
  104.3 13.3 %copy-start.8 = (s32[384]{0:T(512)S(1)}, s32[384]{0:T(512)}, u32[]{:S(2)}) copy-start(s32[384]{0:T(512)} %get-tuple-element.28) | copy-start | bytes 4612
  117.3 3.6 copy-start.9
  120.3 4.0 %copy-start.10 = (s32[384]{0:T(512)S(1)}, s32[384]{0:T(512)}, u32[]{:S(2)}) copy-start(s32[384]{0:T(512)} %get-tuple-element.36) | copy-start | bytes 4612
  123.6 4.3 %copy-start.24 = (s32[1024]{0:T(1024)S(1)}, s32[1024]{0:T(1024)}, u32[]{:S(2)}) copy-start(s32[1024]{0:T(1024)} %copy-done.23) | copy-start | bytes 12292
  137.7 3.4 copy-start.28
  137.7 3.4 copy-start.30
  137.7 3.8 copy-start.22
  151.6 3.0 copy-start.2
  161.2 19.5 %copy-start.6 = (s32[384]{0:T(512)S(1)}, s32[384]{0:T(512)}, u32[]{:S(2)}) copy-start(s32[384]{0:T(512)} %fusion.83) | copy-start | bytes 4612
  161.5 38.7 %copy-start.5 = (s32[384]{0:T(512)S(1)}, s32[384]{0:T(512)}, u32[]{:S(2)}) copy-start(s32[384]{0:T(512)} %fusion.85) | copy-start | bytes 4612
  180.7 39.0 %copy-start.4 = (s32[384]{0:T(512)S(1)}, s32[384]{0:T(512)}, u32[]{:S(2)}) copy-start(s32[384]{0:T(512)} %fusion.87) | copy-start | bytes 4612
  243.7 142.0 %copy-start.12 = (bf16[32,2048]{1,0:T(8,128)(2,1)S(1)}, bf16[32,2048]{1,0:T(8,128)(2,1)}, u32[]{:S(2)}) copy-start(bf16[32,2048]{1,0:T(8,128)(2,1)} %param.10) | copy-start | bytes 393220
  246.2 141.0 %copy-start.13 = (bf16[16,128,128]{2,1,0:T(8,128)(2,1)}, bf16[16,128,128]{2,1,0:T(8,128)(2,1)S(1)}, u32[]{:S(2)}) copy-start(bf16[16,128,128]{2,1,0:T(8,128)(2,1)S(1)} %scatter_fusion.4) | copy-start | bytes 1572868
  (19 other events, 31.6 us)
Sparse Core Ops, SparseCore 0:
  11.4 64.3 all-gather.1
  243.8 141.8 reduce-scatter.1
where the time goes:
time: 401 us; the launch traced here: 395 us
  local copies, waits for them, and re-layouts  181 us (45%)
  waiting for transfers between devices  147 us (37%)
  other arithmetic  26.6 us (7%)
  matrix products  23.4 us (6%)
  between operations  15.3 us (4%)
    reduce_scatter x1, waiting for transfers between devices, local(): lax.psum_scatter(jnp.dot(flat_spread, out_weight, preferred_element_type=...  139 us
    scatter x4, local copies, waits for them, and re-layouts, local(): spread = spread.at[target, :, expert_slot].set(gated, mode='drop')  77.8 us
    gather x4, local copies, waits for them, and re-layouts, local(): normed[slot_tok]  31.1 us
    scatter x4, local copies, waits for them, and re-layouts, expert_slots(): jnp.zeros((capacity + 1,), jnp.int32).at[placed].set(index_row)[:capacity]  17.4 us
    gather x5, local copies, waits for them, and re-layouts, gate_table(): chosen = jnp.take_along_axis(logits, routes, axis=1)  13.7 us
    gather x4, local copies, waits for them, and re-layouts, local(): segment_ids[slot_tok][:, None] == segment_ids[None, :]  12.1 us
    gather x4, local copies, waits for them, and re-layouts, local(): gate_here = gates[slot_tok, expert] * is_valid.astype(jnp.float32)  10.9 us
    dot_general x4, matrix products, local(): jnp.einsum('cd,dhk->chk', normed[slot_tok], query_cols[:, :, expert_slot]...  9.93 us
  transfers between devices with their start and end apart: 3, of which 2 were waited for; matrix products, arithmetic and copies ran while one was open for 27% of the time, Pallas kernels for 0%

commit v1 on v0

v1 whole, which is shorter than its diff:
```python
import jax
import jax.numpy as jnp
from jax import lax
from jax.sharding import PartitionSpec as P

D = 2048
HD = 128
EA = 8
PAGE = 128
REDUCE_PARTS = 4


def swapped(array, axis, bit):
    return lax.ppermute(array, axis, [(i, i ^ 1 << bit) for i in range(lax.axis_size(axis))])


def normalize(hidden, norm_gain):
    values = hidden.astype(jnp.float32)
    factor = lax.rsqrt(jnp.mean(values * values, axis=-1, keepdims=True) + 1e-05)
    return (values * factor * norm_gain.astype(jnp.float32)).astype(jnp.bfloat16)


def gate_table(normed, router_weight, routes):
    logits = jnp.dot(normed, router_weight, preferred_element_type=jnp.float32)
    expert_ids = jnp.arange(router_weight.shape[1], dtype=jnp.int32)
    onehot = routes[:, :, None] == expert_ids[None, None, :]
    chosen = jnp.sum(jnp.where(onehot, logits[:, None, :], 0.0), axis=2)
    weights = jax.nn.softmax(chosen, axis=-1)
    return jnp.sum(jnp.where(onehot, weights[:, :, None], 0.0), axis=1)


def positions_of(segment_ids):
    index_row = jnp.arange(segment_ids.shape[0], dtype=jnp.int32)
    starts_here = jnp.concatenate([jnp.ones((1,), dtype=bool), segment_ids[1:] != segment_ids[:-1]])
    segment_start = lax.cummax(jnp.where(starts_here, index_row, 0), axis=0)
    return index_row - segment_start


def rotate(values, positions):
    half_width = values.shape[-1] // 2
    frequency = 10000.0 ** (-jnp.arange(half_width, dtype=jnp.float32) / half_width)
    angles = positions.astype(jnp.float32)[:, None] * frequency[None, :]
    angles = angles.reshape((values.shape[0],) + (1,) * (values.ndim - 2) + (half_width,))
    cosine = jnp.cos(angles)
    sine_part = jnp.sin(angles)
    leading = values[..., :half_width]
    trailing = values[..., half_width:]
    return jnp.concatenate(
        [leading * cosine - trailing * sine_part, trailing * cosine + leading * sine_part], axis=-1
    )


def project_kv(normed, weight, positions, first_block):
    projected = jnp.dot(normed, weight, preferred_element_type=jnp.float32)
    block_total = weight.shape[1] // HD
    blocks = projected.reshape(normed.shape[0], block_total, HD)
    block_index = first_block + jnp.arange(block_total, dtype=jnp.int32)
    turned = rotate(blocks, positions)
    chosen = jnp.where((block_index % 2 == 0)[None, :, None], turned, blocks)
    return chosen.astype(jnp.bfloat16).reshape(normed.shape[0], weight.shape[1])


def write_pages(kv_cache, page_table, rows):
    pages = jnp.arange(kv_cache.shape[0], dtype=jnp.int32)
    hit = page_table[None, :] == pages[:, None]
    placed = jnp.einsum(
        "pb,brc->prc", hit.astype(rows.dtype), rows, preferred_element_type=jnp.float32
    ).astype(kv_cache.dtype)
    return jnp.where(jnp.any(hit, axis=1)[:, None, None], placed, kv_cache)


def bit_orders(bits, parts):
    rest = list(range(1, bits))
    if not rest:
        return [[0]] * parts
    return [[0] + rest[j % len(rest):] + rest[:j % len(rest)] for j in range(parts)]


def reduce_to_owner(partial, axis):
    size = lax.axis_size(axis)
    bits = size.bit_length() - 1
    assert 1 << bits == size
    me = lax.axis_index(axis)
    rows, width = partial.shape
    block = rows // size
    parts = REDUCE_PARTS if width % REDUCE_PARTS == 0 else 1
    piece = width // parts
    outs = []
    for j, order in enumerate(bit_orders(bits, parts)):
        cols = partial[:, j * piece:(j + 1) * piece]
        cube = cols.reshape((2,) * bits + (block, piece))
        cube = jnp.transpose(cube, [bits - 1 - k for k in order] + [bits, bits + 1])
        current = cube.reshape(rows, piece)
        for k in order:
            half = current.shape[0] // 2
            mine = (me >> k) & 1
            keep = lax.dynamic_slice_in_dim(current, mine * half, half, 0)
            send = lax.dynamic_slice_in_dim(current, (1 - mine) * half, half, 0)
            got = lax.ppermute(send, axis, [(i, i ^ (1 << k)) for i in range(size)])
            current = (keep.astype(jnp.float32) + got.astype(jnp.float32)).astype(jnp.bfloat16)
        outs.append(current)
    return jnp.concatenate(outs, axis=1)


def local(
    hidden,
    norm_gain,
    router_weight,
    kv_weight,
    query_weight,
    out_weight,
    routes,
    segment_ids,
    page_table,
    kv_cache,
):
    device_index = lax.axis_index("tensor")
    token_count = routes.shape[0]
    normed = lax.all_gather(normalize(hidden, norm_gain), "tensor", axis=0, tiled=True)
    gates = gate_table(normed, router_weight, routes)
    positions = positions_of(segment_ids)
    kv_width = kv_weight.shape[1]
    block_count = kv_width // HD
    own_rows = project_kv(normed, kv_weight, positions, device_index * block_count)
    new_cache = write_pages(kv_cache, page_table, own_rows.reshape(page_table.shape[0], PAGE, kv_width))
    partner_rows = swapped(own_rows, "tensor", 0)
    leading_first = device_index % 2 == 0
    head_rows = jnp.where(
        leading_first,
        jnp.concatenate([own_rows, partner_rows], axis=1),
        jnp.concatenate([partner_rows, own_rows], axis=1),
    )
    local_heads = head_rows.shape[1] // (2 * HD)
    head_rows = head_rows.reshape(token_count, local_heads, 2, HD)
    pair_count = query_weight.shape[1] // HD
    local_experts = pair_count // local_heads
    index_row = jnp.arange(token_count, dtype=jnp.int32)
    scale_factor = HD ** (-0.5)
    queries = jnp.dot(normed, query_weight, preferred_element_type=jnp.float32)
    queries = queries.reshape(token_count, local_experts, HD)
    queries = (rotate(queries, positions) * scale_factor).astype(jnp.bfloat16)
    allowed = (segment_ids[:, None] == segment_ids[None, :]) & (index_row[None, :] <= index_row[:, None])
    scores = jnp.einsum(
        "teh,sh->ets", queries, head_rows[:, 0, 0], preferred_element_type=jnp.float32
    )
    scores = jnp.where(allowed[None], scores, -1e30)
    probabilities = jax.nn.softmax(scores, axis=-1).astype(jnp.bfloat16)
    attended = jnp.einsum(
        "ets,sh->teh", probabilities, head_rows[:, 0, 1], preferred_element_type=jnp.float32
    )
    first_expert = (device_index * pair_count) % EA
    gate_here = lax.dynamic_slice_in_dim(gates, first_expert, local_experts, 1)
    gated = (attended * gate_here[:, :, None]).astype(jnp.bfloat16)
    flat = gated.reshape(token_count, pair_count * HD)
    partial = jnp.dot(flat, out_weight, preferred_element_type=jnp.float32).astype(jnp.bfloat16)
    reduced = reduce_to_owner(partial, "tensor").astype(jnp.float32)
    attended_out = (hidden.astype(jnp.float32) + reduced).astype(jnp.bfloat16)
    return (attended_out, new_cache)


def solution(mesh):
    placed = (
        P(("dp", "tensor"), None),
        P(),
        P(),
        P(None, "tensor"),
        P(None, "tensor"),
        P("tensor", None),
        P("dp", None),
        P("dp"),
        P("dp"),
        P("dp", None, "tensor"),
    )
    return jax.shard_map(
        local,
        mesh=mesh,
        in_specs=placed,
        out_specs=(P(("dp", "tensor"), None), P("dp", None, "tensor")),
        check_vma=False,
    )
```

time: 401 us -> 194 us (0.48); the launches traced: 395 us -> 193 us
  local copies, waits for them, and re-layouts: 181 us -> 15.3 us
  waiting for transfers between devices: 147 us -> 76 us
  starting transfers between devices: 0.33 us -> 19.4 us
  other arithmetic: 26.6 us -> 37.4 us
  matrix products: 23.4 us -> 30.7 us
    reduce_scatter x1 -> x0, waiting for transfers between devices: 139 us -> none  [local(): lax.psum_scatter(jnp.dot(flat_spread, out_weight, preferred_element_type=...]
    scatter x9 -> x0, local copies, waits for them, and re-layouts: 96 us -> none  [the longest x4 77.8 us: local(): spread = spread.at[target, :, expert_slot].set(gated, mode='drop')]
    gather x21 -> x0, local copies, waits for them, and re-layouts: 75.3 us -> none  [the longest x4 31.1 us: local(): normed[slot_tok]]
    all_gather x1, waiting for transfers between devices: 7.98 us -> 58.4 us  [local(): lax.all_gather(normalize(hidden, norm_gain), 'tensor', axis=0, tiled=True)]
    sub x4 -> x2, other arithmetic: 0.3 us -> 23.1 us  [the longest x1 18.3 us: local(): probabilities = jax.nn.softmax(scores, axis=-1).astype(jnp.bfloat16)]
    ppermute x0 -> x20, starting transfers between devices: none -> 19 us  [reduce_to_owner(): got = lax.ppermute(send, axis, [(i, i ^ 1 << k) for i in range(size)])]
    ppermute x0 -> x20, waiting for transfers between devices: none -> 17.6 us  [reduce_to_owner(): got = lax.ppermute(send, axis, [(i, i ^ 1 << k) for i in range(size)])]
    dot_general x13 -> x5, matrix products: 18.4 us -> 25.8 us  [the longest x1 10.4 us: local(): jnp.einsum('teh,sh->ets', queries, head_rows[:, 0, 0], preferred_element_...]
  transfers between devices with their start and end apart: 3 -> 22, of which waited for: 2 -> 10; matrix products, arithmetic and copies ran while one was open for 27% -> 12% of each run, Pallas kernels for 0% -> 0%
where the time goes in v1:
time: 194 us; the launch traced here: 193 us
  waiting for transfers between devices  76 us (39%)
  other arithmetic  37.4 us (19%)
  matrix products  30.7 us (16%)
  starting transfers between devices  19.4 us (10%)
  local copies, waits for them, and re-layouts  15.3 us (8%)
  between operations  14.6 us (8%)
    all_gather x1, waiting for transfers between devices, local(): lax.all_gather(normalize(hidden, norm_gain), 'tensor', axis=0, tiled=True)  58.4 us
    ppermute x20, starting transfers between devices, reduce_to_owner(): got = lax.ppermute(send, axis, [(i, i ^ 1 << k) for i in range(size)])  19 us
    sub x1, other arithmetic, local(): probabilities = jax.nn.softmax(scores, axis=-1).astype(jnp.bfloat16)  18.3 us
    ppermute x20, waiting for transfers between devices, reduce_to_owner(): got = lax.ppermute(send, axis, [(i, i ^ 1 << k) for i in range(size)])  17.6 us
    unnamed x22, local copies, waits for them, and re-layouts  10.4 us
    dot_general x1, matrix products, local(): jnp.einsum('teh,sh->ets', queries, head_rows[:, 0, 0], preferred_element_...  10.4 us
    dot_general x1, matrix products, local(): jnp.einsum('ets,sh->teh', probabilities, head_rows[:, 0, 1], preferred_el...  7.2 us
    dot_general x1, matrix products, local(): queries = jnp.dot(normed, query_weight, preferred_element_type=jnp.float32)  5.28 us
  transfers between devices with their start and end apart: 22, of which 10 were waited for; matrix products, arithmetic and copies ran while one was open for 12% of the time, Pallas kernels for 0%

profile of v1, /device:TPU:0, one launch (start us, length us, event | category | flops | bytes accessed | tf_op | source)
XLA Modules:
  0.0 193.4 jit_solution(6031437300662054691)
XLA Ops:
  9.1 1.7 fusion.23
  13.1 3.0 %multiply_cosine_fusion = (f32[1024,64]{1,0:T(8,128)}, f32[1024,64]{1,0:T(8,128)}) fusion(f32[64]{0:T(128)S(1)} %multiply_power_fusion, f32[1024]{0:T(1024)S(1)} %fusion.27), kind=kLoop, calls=%fused_computation.26 | loop fusion | flops 65536 | bytes 528640 | tf_op jit(solution)/shard_map/cos | solution.py:44
  17.5 58.4 %all-gather.2.cloned.1.call-done = bf16[1024,2048]{1,0:T(8,128)(2,1)} async-done(((bf16[32,2048]{1,0:T(8,128)(2,1)}), bf16[1024,2048]{1,0:T(8,128)(2,1)}) %all-gather.2.cloned.1.call-update) | async-done | bytes 4194320 | tf_op jit(solution)/shard_map/all_gather | solution.py:119
  75.9 3.4 %fusion.40 = f32[1024,8]{0,1:T(8,128)S(1)} fusion(bf16[1024,2048]{1,0:T(8,128)(2,1)} %all-gather.2.cloned.1.call-done, bf16[2048,8]{0,1:T(8,128)(2,1)} %param.12), kind=kOutput, calls=%fused_computation.112 | convolution fusion | flops 33554432 | bytes 4259840 | tf_op jit(solution)/shard_map/dot_general | solution.py:24
  79.4 5.3 %fusion.39 = f32[1024,512]{0,1:T(8,128)S(1)} fusion(bf16[1024,2048]{1,0:T(8,128)(2,1)} %all-gather.2.cloned.1.call-done, bf16[2048,512]{1,0:T(8,128)(2,1)} %param.14), kind=kOutput, calls=%fused_computation.111 | convolution fusion | flops 2147483648 | bytes 8388608 | tf_op jit(solution)/shard_map/dot_general | solution.py:139
  84.7 1.6 fusion.36
  87.6 1.5 fusion.38
  90.7 3.2 %copy.52 = f32[1024,4,64]{2,0,1:T(8,128)} copy(f32[1024,4,64]{0,2,1:T(8,128)} %get-tuple-element.14) | data formatting | bytes 2097152
  93.9 3.1 %copy.51 = f32[1024,4,64]{2,0,1:T(8,128)} copy(f32[1024,4,64]{0,2,1:T(8,128)} %get-tuple-element.15) | data formatting | bytes 2097152
  97.0 4.9 %multiply_subtract_fusion = (f32[1024,4,64]{2,0,1:T(8,128)}, f32[1024,4,64]{2,0,1:T(8,128)}) fusion(f32[1024,4,64]{2,0,1:T(8,128)} %copy.52, f32[1024,4,64]{2,0,1:T(8,128)} %copy.51, f32[1024,64]{1,0:T(8,128)} %get-tuple-element.19, f32[1024,64]{1,0:T(8,128)} %get-tuple-element.18), kind=kLoop, calls=%fused_computation.16 | loop fusion | flops 1572864 | bytes 4718592 | tf_op jit(solution)/shard_map/sub | solution.py:49
  102.7 1.9 copy.46
  106.6 10.4 %fusion.9 = f32[1024,1024,4]{1,0,2:T(8,128)} fusion(f32[1024,4,64]{2,0,1:T(8,128)} %get-tuple-element.9, f32[1024,4,64]{2,0,1:T(8,128)} %get-tuple-element.8, bf16[1024,1,2,128]{0,3,2,1:T(8,128)(2,1)S(1)} %bitcast.91), kind=kOutput, calls=%fused_computation.19 | convolution fusion | flops 1075314688 | bytes 19136512 | tf_op jit(solution)/shard_map/teh,sh->ets/dot_general | solution.py:143
  117.0 18.3 %fusion.37 = (f32[4,1024]{1,0:T(4,128)S(1)}, f32[4,1024,1024]{1,2,0:T(8,128)}) fusion(f32[1024,1024,4]{1,0,2:T(8,128)} %fusion.9, pred[1024,1024]{0,1:T(8,128)(4,1)S(1)} %fusion.5), kind=kOutput, calls=%fused_computation.109 | output fusion | flops 16778240 | bytes 34619392 | tf_op jit(solution)/shard_map/sub | solution.py:147
  135.3 7.2 %fusion.7 = bf16[1024,4,128]{0,2,1:T(8,128)(2,1)S(1)} fusion(f32[4,1024,1024]{1,2,0:T(8,128)} %get-tuple-element.21, f32[4,1024]{1,0:T(4,128)S(1)} %get-tuple-element.20, f32[1024,4]{0,1:T(4,128)S(1)} %constant_dynamic-slice_fusion.20, bf16[1024,1,2,128]{0,3,2,1:T(8,128)(2,1)} %bitcast.92), kind=kOutput, calls=%fused_computation.14 | convolution fusion | flops 1083179008 | bytes 18120704 | tf_op jit(solution)/shard_map/ets,sh->teh/dot_general | solution.py:148
  142.5 2.4 %convolution_convert_fusion = bf16[1024,2048]{1,0:T(8,128)(2,1)S(1)} fusion(bf16[1024,512]{0,1:T(8,128)(2,1)S(1)} %bitcast.94, bf16[512,2048]{1,0:T(8,128)(2,1)S(1)} %copy-done), kind=kOutput, calls=%fused_computation.10 | convolution fusion | flops 2149580800 | bytes 7340032 | tf_op jit(solution)/shard_map/dot_general | solution.py:155
  150.6 1.7 collective-permute-start.17
  154.6 3.0 %collective-permute-done.2 = bf16[256,512]{1,0:T(8,128)(2,1)S(1)} collective-permute-done((bf16[256,512]{1,0:T(8,128)(2,1)S(1)}, bf16[256,512]{1,0:T(8,128)(2,1)S(1)}, u32[]{:S(2)}, u32[]{:S(2)}) %collective-permute-start.2) | collective-permute-done | bytes 262176 | tf_op jit(solution)/shard_map/ppermute | solution.py:99
  157.7 1.5 collective-permute-start.3
  159.2 6.1 %collective-permute-done.17 = bf16[256,512]{1,0:T(8,128)(2,1)S(1)} collective-permute-done((bf16[256,512]{1,0:T(8,128)(2,1)S(1)}, bf16[256,512]{1,0:T(8,128)(2,1)S(1)}, u32[]{:S(2)}, u32[]{:S(2)}) %collective-permute-start.17) | collective-permute-done | bytes 262176 | tf_op jit(solution)/shard_map/ppermute | solution.py:99
  167.1 2.3 %collective-permute-start.8 = (bf16[128,512]{1,0:T(8,128)(2,1)S(1)}, bf16[128,512]{1,0:T(8,128)(2,1)S(1)}, u32[]{:S(2)}, u32[]{:S(2)}) collective-permute-start(bf16[128,512]{1,0:T(8,128)(2,1)S(1)} %constant_dynamic-slice_fusion.12), channel_id=1, source_target_pairs={{0,8},{1,9},{2,10},{3,11},{4,12},{5,13},{6,14},{7,15},{8,0},{9,1},... | collective-permute-start | bytes 393224 | tf_op jit(solution)/shard_map/ppermute | solution.py:99
  171.6 2.9 %collective-permute-done.13 = bf16[128,512]{1,0:T(8,128)(2,1)S(1)} collective-permute-done((bf16[128,512]{1,0:T(8,128)(2,1)S(1)}, bf16[128,512]{1,0:T(8,128)(2,1)S(1)}, u32[]{:S(2)}, u32[]{:S(2)}) %collective-permute-start.13) | collective-permute-done | bytes 131104 | tf_op jit(solution)/shard_map/ppermute | solution.py:99
  176.3 2.8 %collective-permute-start.5 = (bf16[32,512]{1,0:T(8,128)(2,1)S(1)}, bf16[32,512]{1,0:T(8,128)(2,1)S(1)}, u32[]{:S(2)}, u32[]{:S(2)}) collective-permute-start(bf16[32,512]{1,0:T(8,128)(2,1)S(1)} %constant_dynamic-slice_fusion.15), channel_id=1, source_target_pairs={{0,16},{1,17},{2,18},{3,19},{4,20},{5,21},{6,22},{7,23},{8,24},{9,... | collective-permute-start | bytes 98312 | tf_op jit(solution)/shard_map/ppermute | solution.py:99
  180.5 1.4 collective-permute-done.9
  183.2 2.6 %collective-permute-done.10 = bf16[32,512]{1,0:T(8,128)(2,1)S(1)} collective-permute-done((bf16[32,512]{1,0:T(8,128)(2,1)S(1)}, bf16[32,512]{1,0:T(8,128)(2,1)S(1)}, u32[]{:S(2)}, u32[]{:S(2)}) %collective-permute-start.10) | collective-permute-done | bytes 32800 | tf_op jit(solution)/shard_map/ppermute | solution.py:99
  (124 shorter events, 28.3 us)
Async XLA Ops:
  7.2 135.3 %copy-start = (bf16[512,2048]{1,0:T(8,128)(2,1)S(1)}, bf16[512,2048]{1,0:T(8,128)(2,1)}, u32[]{:S(2)}) copy-start(bf16[512,2048]{1,0:T(8,128)(2,1)} %param.15) | copy-start | bytes 6291460
  7.2 72.1 %copy-start.7 = (s32[1024,2]{0,1:T(2,128)S(1)}, s32[1024,2]{0,1:T(2,128)}, u32[]{:S(2)}) copy-start(s32[1024,2]{0,1:T(2,128)} %param.16) | copy-start | bytes 24580
  7.2 68.7 %all-gather.2.cloned.1.call-start = ((), (), s32[]{:S(2)}) async-start(), calls=%async_computation | async-start | bytes 4325376 | tf_op jit(solution)/shard_map/all_gather | solution.py:119
  90.4 14.2 %collective-permute-start = (bf16[1024,128]{0,1:T(8,128)(2,1)S(1)}, bf16[1024,128]{0,1:T(8,128)(2,1)}, u32[]{:S(2)}, u32[]{:S(2)}) collective-permute-start(bf16[1024,128]{0,1:T(8,128)(2,1)S(1)} %fusion.12), channel_id=1, source_target_pairs={{0,1},{1,0},{2,3},{3,2},{4,5},{5,4},{6,7},{7,6},{8,9},{9,8},{10,11... | collective-permute-start | bytes 786440 | tf_op jit(solution)/shard_map/ppermute | solution.py:14
  145.5 3.4 %collective-permute-start.1 = (bf16[512,512]{1,0:T(8,128)(2,1)S(1)}, bf16[512,512]{1,0:T(8,128)(2,1)S(1)}, u32[]{:S(2)}, u32[]{:S(2)}) collective-permute-start(bf16[512,512]{1,0:T(8,128)(2,1)S(1)} %constant_dynamic-slice_fusion.19), channel_id=1, source_target_pairs={{0,1},{1,0},{2,3},{3,2},{4,5},{5,4},{6,7},{7,6},{8,9},{9,8},{10,11... | collective-permute-start | bytes 1572872 | tf_op jit(solution)/shard_map/ppermute | solution.py:99
  147.7 2.7 %collective-permute-start.16 = (bf16[512,512]{1,0:T(8,128)(2,1)S(1)}, bf16[512,512]{1,0:T(8,128)(2,1)S(1)}, u32[]{:S(2)}, u32[]{:S(2)}) collective-permute-start(bf16[512,512]{1,0:T(8,128)(2,1)S(1)} %constant_dynamic-slice_fusion.4), channel_id=1, source_target_pairs={{0,1},{1,0},{2,3},{3,2},{4,5},{5,4},{6,7},{7,6},{8,9},{9,8},{10,11... | collective-permute-start | bytes 1572872 | tf_op jit(solution)/shard_map/ppermute | solution.py:99
  148.1 4.1 %collective-permute-start.11 = (bf16[512,512]{1,0:T(8,128)(2,1)S(1)}, bf16[512,512]{1,0:T(8,128)(2,1)S(1)}, u32[]{:S(2)}, u32[]{:S(2)}) collective-permute-start(bf16[512,512]{1,0:T(8,128)(2,1)S(1)} %constant_dynamic-slice_fusion.9), channel_id=1, source_target_pairs={{0,1},{1,0},{2,3},{3,2},{4,5},{5,4},{6,7},{7,6},{8,9},{9,8},{10,11... | collective-permute-start | bytes 1572872 | tf_op jit(solution)/shard_map/ppermute | solution.py:99
  148.6 5.0 %collective-permute-start.6 = (bf16[512,512]{1,0:T(8,128)(2,1)S(1)}, bf16[512,512]{1,0:T(8,128)(2,1)S(1)}, u32[]{:S(2)}, u32[]{:S(2)}) collective-permute-start(bf16[512,512]{1,0:T(8,128)(2,1)S(1)} %constant_dynamic-slice_fusion.14), channel_id=1, source_target_pairs={{0,1},{1,0},{2,3},{3,2},{4,5},{5,4},{6,7},{7,6},{8,9},{9,8},{10,11... | collective-permute-start | bytes 1572872 | tf_op jit(solution)/shard_map/ppermute | solution.py:99
  149.1 8.5 %collective-permute-start.2 = (bf16[256,512]{1,0:T(8,128)(2,1)S(1)}, bf16[256,512]{1,0:T(8,128)(2,1)S(1)}, u32[]{:S(2)}, u32[]{:S(2)}) collective-permute-start(bf16[256,512]{1,0:T(8,128)(2,1)S(1)} %constant_dynamic-slice_fusion.18), channel_id=1, source_target_pairs={{0,2},{1,3},{2,0},{3,1},{4,6},{5,7},{6,4},{7,5},{8,10},{9,11},{10,... | collective-permute-start | bytes 786440 | tf_op jit(solution)/shard_map/ppermute | solution.py:99
  150.6 14.8 %collective-permute-start.17 = (bf16[256,512]{1,0:T(8,128)(2,1)S(1)}, bf16[256,512]{1,0:T(8,128)(2,1)S(1)}, u32[]{:S(2)}, u32[]{:S(2)}) collective-permute-start(bf16[256,512]{1,0:T(8,128)(2,1)S(1)} %constant_dynamic-slice_fusion.3), channel_id=1, source_target_pairs={{0,16},{1,17},{2,18},{3,19},{4,20},{5,21},{6,22},{7,23},{8,24},{9,... | collective-permute-start | bytes 786440 | tf_op jit(solution)/shard_map/ppermute | solution.py:99
  152.4 13.9 %collective-permute-start.12 = (bf16[256,512]{1,0:T(8,128)(2,1)S(1)}, bf16[256,512]{1,0:T(8,128)(2,1)S(1)}, u32[]{:S(2)}, u32[]{:S(2)}) collective-permute-start(bf16[256,512]{1,0:T(8,128)(2,1)S(1)} %constant_dynamic-slice_fusion.8), channel_id=1, source_target_pairs={{0,8},{1,9},{2,10},{3,11},{4,12},{5,13},{6,14},{7,15},{8,0},{9,1},... | collective-permute-start | bytes 786440 | tf_op jit(solution)/shard_map/ppermute | solution.py:99
  153.7 13.2 %collective-permute-start.7 = (bf16[256,512]{1,0:T(8,128)(2,1)S(1)}, bf16[256,512]{1,0:T(8,128)(2,1)S(1)}, u32[]{:S(2)}, u32[]{:S(2)}) collective-permute-start(bf16[256,512]{1,0:T(8,128)(2,1)S(1)} %constant_dynamic-slice_fusion.13), channel_id=1, source_target_pairs={{0,4},{1,5},{2,6},{3,7},{4,0},{5,1},{6,2},{7,3},{8,12},{9,13},{10,... | collective-permute-start | bytes 786440 | tf_op jit(solution)/shard_map/ppermute | solution.py:99
  157.7 11.7 %collective-permute-start.3 = (bf16[128,512]{1,0:T(8,128)(2,1)S(1)}, bf16[128,512]{1,0:T(8,128)(2,1)S(1)}, u32[]{:S(2)}, u32[]{:S(2)}) collective-permute-start(bf16[128,512]{1,0:T(8,128)(2,1)S(1)} %constant_dynamic-slice_fusion.17), channel_id=1, source_target_pairs={{0,4},{1,5},{2,6},{3,7},{4,0},{5,1},{6,2},{7,3},{8,12},{9,13},{10,... | collective-permute-start | bytes 393224 | tf_op jit(solution)/shard_map/ppermute | solution.py:99
  165.4 5.0 %collective-permute-start.18 = (bf16[128,512]{1,0:T(8,128)(2,1)S(1)}, bf16[128,512]{1,0:T(8,128)(2,1)S(1)}, u32[]{:S(2)}, u32[]{:S(2)}) collective-permute-start(bf16[128,512]{1,0:T(8,128)(2,1)S(1)} %constant_dynamic-slice_fusion.2), channel_id=1, source_target_pairs={{0,2},{1,3},{2,0},{3,1},{4,6},{5,7},{6,4},{7,5},{8,10},{9,11},{10,... | collective-permute-start | bytes 393224 | tf_op jit(solution)/shard_map/ppermute | solution.py:99
  166.4 8.1 %collective-permute-start.13 = (bf16[128,512]{1,0:T(8,128)(2,1)S(1)}, bf16[128,512]{1,0:T(8,128)(2,1)S(1)}, u32[]{:S(2)}, u32[]{:S(2)}) collective-permute-start(bf16[128,512]{1,0:T(8,128)(2,1)S(1)} %constant_dynamic-slice_fusion.7), channel_id=1, source_target_pairs={{0,16},{1,17},{2,18},{3,19},{4,20},{5,21},{6,22},{7,23},{8,24},{9,... | collective-permute-start | bytes 393224 | tf_op jit(solution)/shard_map/ppermute | solution.py:99
  167.1 8.8 %collective-permute-start.8 = (bf16[128,512]{1,0:T(8,128)(2,1)S(1)}, bf16[128,512]{1,0:T(8,128)(2,1)S(1)}, u32[]{:S(2)}, u32[]{:S(2)}) collective-permute-start(bf16[128,512]{1,0:T(8,128)(2,1)S(1)} %constant_dynamic-slice_fusion.12), channel_id=1, source_target_pairs={{0,8},{1,9},{2,10},{3,11},{4,12},{5,13},{6,14},{7,15},{8,0},{9,1},... | collective-permute-start | bytes 393224 | tf_op jit(solution)/shard_map/ppermute | solution.py:99
  169.5 6.8 %collective-permute-start.4 = (bf16[64,512]{1,0:T(8,128)(2,1)S(1)}, bf16[64,512]{1,0:T(8,128)(2,1)S(1)}, u32[]{:S(2)}, u32[]{:S(2)}) collective-permute-start(bf16[64,512]{1,0:T(8,128)(2,1)S(1)} %constant_dynamic-slice_fusion.16), channel_id=1, source_target_pairs={{0,8},{1,9},{2,10},{3,11},{4,12},{5,13},{6,14},{7,15},{8,0},{9,1},... | collective-permute-start | bytes 196616 | tf_op jit(solution)/shard_map/ppermute | solution.py:99
  170.5 8.5 %collective-permute-start.19 = (bf16[64,512]{1,0:T(8,128)(2,1)S(1)}, bf16[64,512]{1,0:T(8,128)(2,1)S(1)}, u32[]{:S(2)}, u32[]{:S(2)}) collective-permute-start(bf16[64,512]{1,0:T(8,128)(2,1)S(1)} %constant_dynamic-slice_fusion.1), channel_id=1, source_target_pairs={{0,4},{1,5},{2,6},{3,7},{4,0},{5,1},{6,2},{7,3},{8,12},{9,13},{10,... | collective-permute-start | bytes 196616 | tf_op jit(solution)/shard_map/ppermute | solution.py:99
  174.6 4.6 %collective-permute-start.14 = (bf16[64,512]{1,0:T(8,128)(2,1)S(1)}, bf16[64,512]{1,0:T(8,128)(2,1)S(1)}, u32[]{:S(2)}, u32[]{:S(2)}) collective-permute-start(bf16[64,512]{1,0:T(8,128)(2,1)S(1)} %constant_dynamic-slice_fusion.6), channel_id=1, source_target_pairs={{0,2},{1,3},{2,0},{3,1},{4,6},{5,7},{6,4},{7,5},{8,10},{9,11},{10,... | collective-permute-start | bytes 196616 | tf_op jit(solution)/shard_map/ppermute | solution.py:99
  176.0 5.9 %collective-permute-start.9 = (bf16[64,512]{1,0:T(8,128)(2,1)S(1)}, bf16[64,512]{1,0:T(8,128)(2,1)S(1)}, u32[]{:S(2)}, u32[]{:S(2)}) collective-permute-start(bf16[64,512]{1,0:T(8,128)(2,1)S(1)} %constant_dynamic-slice_fusion.11), channel_id=1, source_target_pairs={{0,16},{1,17},{2,18},{3,19},{4,20},{5,21},{6,22},{7,23},{8,24},{9,... | collective-permute-start | bytes 196616 | tf_op jit(solution)/shard_map/ppermute | solution.py:99
  176.3 6.5 %collective-permute-start.5 = (bf16[32,512]{1,0:T(8,128)(2,1)S(1)}, bf16[32,512]{1,0:T(8,128)(2,1)S(1)}, u32[]{:S(2)}, u32[]{:S(2)}) collective-permute-start(bf16[32,512]{1,0:T(8,128)(2,1)S(1)} %constant_dynamic-slice_fusion.15), channel_id=1, source_target_pairs={{0,16},{1,17},{2,18},{3,19},{4,20},{5,21},{6,22},{7,23},{8,24},{9,... | collective-permute-start | bytes 98312 | tf_op jit(solution)/shard_map/ppermute | solution.py:99
  179.1 4.0 %collective-permute-start.20 = (bf16[32,512]{1,0:T(8,128)(2,1)S(1)}, bf16[32,512]{1,0:T(8,128)(2,1)S(1)}, u32[]{:S(2)}, u32[]{:S(2)}) collective-permute-start(bf16[32,512]{1,0:T(8,128)(2,1)S(1)} %constant_dynamic-slice_fusion), channel_id=1, source_target_pairs={{0,8},{1,9},{2,10},{3,11},{4,12},{5,13},{6,14},{7,15},{8,0},{9,1},... | collective-permute-start | bytes 98312 | tf_op jit(solution)/shard_map/ppermute | solution.py:99
  179.2 4.0 %collective-permute-start.15 = (bf16[32,512]{1,0:T(8,128)(2,1)S(1)}, bf16[32,512]{1,0:T(8,128)(2,1)S(1)}, u32[]{:S(2)}, u32[]{:S(2)}) collective-permute-start(bf16[32,512]{1,0:T(8,128)(2,1)S(1)} %constant_dynamic-slice_fusion.5), channel_id=1, source_target_pairs={{0,4},{1,5},{2,6},{3,7},{4,0},{5,1},{6,2},{7,3},{8,12},{9,13},{10,... | collective-permute-start | bytes 98312 | tf_op jit(solution)/shard_map/ppermute | solution.py:99
  181.9 4.0 %collective-permute-start.10 = (bf16[32,512]{1,0:T(8,128)(2,1)S(1)}, bf16[32,512]{1,0:T(8,128)(2,1)S(1)}, u32[]{:S(2)}, u32[]{:S(2)}) collective-permute-start(bf16[32,512]{1,0:T(8,128)(2,1)S(1)} %constant_dynamic-slice_fusion.10), channel_id=1, source_target_pairs={{0,2},{1,3},{2,0},{3,1},{4,6},{5,7},{6,4},{7,5},{8,10},{9,11},{10,... | collective-permute-start | bytes 98312 | tf_op jit(solution)/shard_map/ppermute | solution.py:99
  (7 other events, 46.0 us)
Sparse Core Ops, SparseCore 0:
  11.4 64.4 all-gather.1

commit v2 on v1

--- a/solution.py
+++ b/solution.py
@@ -1,6 +1,8 @@
 import jax
 import jax.numpy as jnp
 from jax import lax
+from jax.experimental import pallas as pl
+from jax.experimental.pallas import tpu as pltpu
 from jax.sharding import PartitionSpec as P
 
 D = 2048
@@ -8,6 +10,8 @@
 EA = 8
 PAGE = 128
 REDUCE_PARTS = 4
+SEG_MOST = 512
+CHUNK = 128
 
 
 def swapped(array, axis, bit):
@@ -100,6 +104,62 @@
             current = (keep.astype(jnp.float32) + got.astype(jnp.float32)).astype(jnp.bfloat16)
         outs.append(current)
     return jnp.concatenate(outs, axis=1)
+
+
+def attention_kernel(window, q_ref, k_ref, v_ref, qseg_ref, kseg_ref, gate_ref, out_ref):
+    chunk = pl.program_id(0)
+    blocks = pl.num_programs(0)
+    start_block = jnp.clip(chunk - (window - 1), 0, blocks - window)
+    start = pl.multiple_of(start_block * CHUNK, CHUNK)
+    span = window * CHUNK
+    keys = k_ref[pl.ds(start, span), :]
+    values = v_ref[pl.ds(start, span), :]
+    key_seg = kseg_ref[:, pl.ds(start, span)]
+    query_seg = qseg_ref[...]
+    query_index = chunk * CHUNK + lax.broadcasted_iota(jnp.int32, (CHUNK, span), 0)
+    key_index = start + lax.broadcasted_iota(jnp.int32, (CHUNK, span), 1)
+    allowed = (query_seg == key_seg) & (key_index <= query_index)
+    experts = gate_ref.shape[0]
+    for e in range(experts):
+        queries = q_ref[:, e * HD:(e + 1) * HD]
+        scores = lax.dot_general(
+            queries, keys, (((1,), (1,)), ((), ())), preferred_element_type=jnp.float32
+        )
+        scores = jnp.where(allowed, scores, -1e30)
+        top = jnp.max(scores, axis=1, keepdims=True)
+        raised = jnp.exp(scores - top)
+        probabilities = (raised / jnp.sum(raised, axis=1, keepdims=True)).astype(jnp.bfloat16)
+        attended = jnp.dot(probabilities, values, preferred_element_type=jnp.float32)
+        out_ref[:, e * HD:(e + 1) * HD] = (attended * gate_ref[e]).astype(out_ref.dtype)
+
+
+def attend_window(queries, keys, values, segment_ids, gate_here):
+    tokens, width = queries.shape
+    experts = width // HD
+    blocks = tokens // CHUNK
+    window = min(blocks, SEG_MOST // CHUNK + 1)
+    gate_cols = jnp.transpose(gate_here).reshape(experts, tokens, 1)
+    seg_cols = segment_ids.reshape(tokens, 1)
+    seg_row = segment_ids.reshape(1, tokens)
+    return pl.pallas_call(
+        lambda *refs: attention_kernel(window, *refs),
+        grid=(blocks,),
+        in_specs=[
+            pl.BlockSpec((CHUNK, width), lambda i: (i, 0)),
+            pl.BlockSpec((tokens, HD), lambda i: (0, 0)),
+            pl.BlockSpec((tokens, HD), lambda i: (0, 0)),
+            pl.BlockSpec((CHUNK, 1), lambda i: (i, 0)),
+            pl.BlockSpec((1, tokens), lambda i: (0, 0)),
+            pl.BlockSpec((experts, CHUNK, 1), lambda i: (0, i, 0)),
+        ],
+        out_specs=pl.BlockSpec((CHUNK, width), lambda i: (i, 0)),
+        out_shape=jax.ShapeDtypeStruct((tokens, width), jnp.bfloat16),
+        cost_estimate=pl.CostEstimate(
+            flops=4 * tokens * window * CHUNK * width,
+            transcendentals=tokens * window * CHUNK * experts,
+            bytes_accessed=2 * tokens * width * 2 + 2 * tokens * HD * 2,
+        ),
+    )(queries, keys, values, seg_cols, seg_row, gate_cols)
 
 
 def local(
@@ -134,24 +194,19 @@
     head_rows = head_rows.reshape(token_count, local_heads, 2, HD)
     pair_count = query_weight.shape[1] // HD
     local_experts = pair_count // local_heads
-    index_row = jnp.arange(token_count, dtype=jnp.int32)
     scale_factor = HD ** (-0.5)
     queries = jnp.dot(normed, query_weight, preferred_element_type=jnp.float32)
     queries = queries.reshape(token_count, local_experts, HD)
     queries = (rotate(queries, positions) * scale_factor).astype(jnp.bfloat16)
-    allowed = (segment_ids[:, None] == segment_ids[None, :]) & (index_row[None, :] <= index_row[:, None])
-    scores = jnp.einsum(
-        "teh,sh->ets", queries, head_rows[:, 0, 0], preferred_element_type=jnp.float32
-    )
-    scores = jnp.where(allowed[None], scores, -1e30)
-    probabilities = jax.nn.softmax(scores, axis=-1).astype(jnp.bfloat16)
-    attended = jnp.einsum(
-        "ets,sh->teh", probabilities, head_rows[:, 0, 1], preferred_element_type=jnp.float32
-    )
     first_expert = (device_index * pair_count) % EA
     gate_here = lax.dynamic_slice_in_dim(gates, first_expert, local_experts, 1)
-    gated = (attended * gate_here[:, :, None]).astype(jnp.bfloat16)
-    flat = gated.reshape(token_count, pair_count * HD)
+    flat = attend_window(
+        queries.reshape(token_count, pair_count * HD),
+        head_rows[:, 0, 0],
+        head_rows[:, 0, 1],
+        segment_ids,
+        gate_here,
+    )
     partial = jnp.dot(flat, out_weight, preferred_element_type=jnp.float32).astype(jnp.bfloat16)
     reduced = reduce_to_owner(partial, "tensor").astype(jnp.float32)
     attended_out = (hidden.astype(jnp.float32) + reduced).astype(jnp.bfloat16)

time: 194 us -> 174 us (0.90)
  other arithmetic: 37.4 us -> 17 us
  Pallas kernels: 0 us -> 16.3 us
  matrix products: 30.7 us -> 14.5 us
    sub x1 -> x0, other arithmetic: 18.3 us -> none  [local(): probabilities = jax.nn.softmax(scores, axis=-1).astype(jnp.bfloat16)]
    dot_general x2 -> x0, matrix products: 17.6 us -> none  [the longest x1 10.4 us: local(): jnp.einsum('teh,sh->ets', queries, head_rows[:, 0, 0], preferred_element_...]
    pallas_call x0 -> x1, Pallas kernels: none -> 16.3 us  [attend_window(): pl.pallas_call(lambda *refs: attention_kernel(window, *refs), grid=(block...]
    reshape x0 -> x3, local copies, waits for them, and re-layouts: none -> 3.73 us  [the longest x2 1.99 us: attend_window(): gate_cols = jnp.transpose(gate_here).reshape(experts, tokens, 1)]
    dot_general x1, matrix products: 1.52 us -> 3.97 us  [project_kv(): projected = jnp.dot(normed, weight, preferred_element_type=jnp.float32)]
    dot_general x1, matrix products: 3.37 us -> 1.18 us  [gate_table(): logits = jnp.dot(normed, router_weight, preferred_element_type=jnp.float32)]
    sub x1, other arithmetic: 4.86 us -> 2.74 us  [rotate(): leading * cosine - trailing * sine_part]
    unnamed x22 -> x25, local copies, waits for them, and re-layouts: 10.4 us -> 8.92 us
  transfers between devices with their start and end apart: 22 -> 22, of which waited for: 10 -> 7; matrix products, arithmetic and copies ran while one was open for 12% -> 11% of each run, Pallas kernels for 0% -> 0%
where the time goes in v2:
time: 174 us
  waiting for transfers between devices  76.3 us (44%)
  starting transfers between devices  19.5 us (11%)
  other arithmetic  17 us (10%)
  Pallas kernels  16.3 us (9%)
  local copies, waits for them, and re-layouts  15.5 us (9%)
  between operations  14.6 us (8%)
  matrix products  14.5 us (8%)
    all_gather x1, waiting for transfers between devices, local(): lax.all_gather(normalize(hidden, norm_gain), 'tensor', axis=0, tiled=True)  58 us
    ppermute x20, starting transfers between devices, reduce_to_owner(): got = lax.ppermute(send, axis, [(i, i ^ 1 << k) for i in range(size)])  19.1 us
    ppermute x20, waiting for transfers between devices, reduce_to_owner(): got = lax.ppermute(send, axis, [(i, i ^ 1 << k) for i in range(size)])  18.2 us
    pallas_call x1, Pallas kernels, attend_window(): pl.pallas_call(lambda *refs: attention_kernel(window, *refs), grid=(block...  16.3 us
    unnamed x25, local copies, waits for them, and re-layouts  8.92 us
    dot_general x1, matrix products, local(): queries = jnp.dot(normed, query_weight, preferred_element_type=jnp.float32)  5.23 us
    dot_general x1, matrix products, project_kv(): projected = jnp.dot(normed, weight, preferred_element_type=jnp.float32)  3.97 us
    dot_general x1, matrix products, local(): jnp.dot(flat, out_weight, preferred_element_type=jnp.float32)  3.56 us
  transfers between devices with their start and end apart: 22, of which 7 were waited for; matrix products, arithmetic and copies ran while one was open for 11% of the time, Pallas kernels for 0%

profile of v2, /device:TPU:0, one launch (start us, length us, event | category | flops | bytes accessed | tf_op | source)
XLA Modules:
  0.0 173.7 jit_solution(16602702515051675107)
XLA Ops:
  9.1 1.7 fusion.13
  12.2 1.7 copy.42.refs_3_
  14.8 3.0 %multiply_cosine_fusion = (f32[1024,64]{1,0:T(8,128)}, f32[1024,64]{1,0:T(8,128)}) fusion(f32[64]{0:T(128)S(1)} %multiply_power_fusion, f32[1024]{0:T(1024)S(1)} %fusion.17), kind=kLoop, calls=%fused_computation.13 | loop fusion | flops 65536 | bytes 528640 | tf_op jit(solution)/shard_map/cos | solution.py:48
  17.9 58.0 %all-gather.2.cloned.1.call-done = bf16[1024,2048]{1,0:T(8,128)(2,1)} async-done(((bf16[32,2048]{1,0:T(8,128)(2,1)}), bf16[1024,2048]{1,0:T(8,128)(2,1)}) %all-gather.2.cloned.1.call-update) | async-done | bytes 4194320 | tf_op jit(solution)/shard_map/all_gather | solution.py:179
  75.9 5.2 %fusion.25 = f32[1024,512]{0,1:T(8,128)S(1)} fusion(bf16[1024,2048]{1,0:T(8,128)(2,1)} %all-gather.2.cloned.1.call-done, bf16[2048,512]{1,0:T(8,128)(2,1)} %param.14), kind=kOutput, calls=%fused_computation.92 | convolution fusion | flops 2147483648 | bytes 8388608 | tf_op jit(solution)/shard_map/dot_general | solution.py:198
  82.3 2.7 %copy.52 = f32[1024,4,64]{2,1,0:T(4,128)} copy(f32[1024,4,64]{0,2,1:T(8,128)} %get-tuple-element.14) | data formatting | bytes 2097152
  85.0 1.8 %copy.51 = f32[1024,4,64]{2,1,0:T(4,128)} copy(f32[1024,4,64]{0,2,1:T(8,128)S(1)} %get-tuple-element.15) | data formatting | bytes 2097152
  86.8 4.0 %fusion.26 = f32[1024,128]{0,1:T(8,128)S(1)} fusion(bf16[1024,2048]{1,0:T(8,128)(2,1)} %all-gather.2.cloned.1.call-done, bf16[2048,128]{1,0:T(8,128)(2,1)} %param.13), kind=kOutput, calls=%fused_computation.93 | convolution fusion | flops 536870912 | bytes 5242880 | tf_op jit(solution)/shard_map/dot_general | solution.py:58
  93.7 2.7 %multiply_subtract_fusion = (f32[1024,4,64]{2,1,0:T(4,128)S(1)}, f32[1024,4,64]{2,1,0:T(4,128)S(1)}) fusion(f32[1024,4,64]{2,1,0:T(4,128)} %copy.52, f32[1024,4,64]{2,1,0:T(4,128)} %copy.51, f32[1024,64]{1,0:T(8,128)S(1)} %copy-done.3, f32[1024,64]{1,0:T(8,128)S(1)} %copy-done.2), kind=kLoop, calls=%fused_computation.4 | loop fusion | flops 1572864 | bytes 4718592 | tf_op jit(solution)/shard_map/sub | solution.py:53
  96.5 1.3 fusion
  98.9 2.0 %copy.43.refs_5_ = f32[4,1024,1]{2,1,0:T(8,128)} copy(f32[4,1024,1]{1,0,2:T(4,128)S(1)} %dynamic-slice_bitcast_fusion) | data formatting | bytes 32768 | tf_op jit(solution)/shard_map/reshape | solution.py:141
  104.2 16.3 %shard_map.113 = bf16[1024,512]{1,0:T(8,128)(2,1)} custom-call(bf16[1024,512]{1,0:T(8,128)(2,1)} %bitcast.71, bf16[1024,128]{1,0:T(8,128)(2,1)} %bitcast.79, bf16[1024,128]{1,0:T(8,128)(2,1)} %bitcast.80, s32[1024,1]{1,0:T(8,128)} %copy.42.refs_3_, s32[1,1024]{1,0:T(1,128)} %bitcast.83, f32[4,1024,1]{2,1,0:T(8,128)} %copy.43.refs_5_), custom_call_target="tpu_custom_call" | custom-call | flops 1342177280 | bytes 2621440 | tf_op jit(solution)/shard_map/pallas_call | solution.py:144
  120.5 3.6 %convolution_convert_fusion = bf16[1024,2048]{1,0:T(8,128)(2,1)S(1)} fusion(bf16[1024,512]{1,0:T(8,128)(2,1)} %shard_map.113, bf16[512,2048]{1,0:T(8,128)(2,1)S(1)} %copy-done), kind=kOutput, calls=%fused_computation | convolution fusion | flops 2149580800 | bytes 7340032 | tf_op jit(solution)/shard_map/dot_general | solution.py:210
  128.5 1.7 collective-permute-start.17
  131.7 1.5 collective-permute-start.7
  134.1 9.5 %collective-permute-done.17 = bf16[256,512]{1,0:T(8,128)(2,1)S(1)} collective-permute-done((bf16[256,512]{1,0:T(8,128)(2,1)S(1)}, bf16[256,512]{1,0:T(8,128)(2,1)S(1)}, u32[]{:S(2)}, u32[]{:S(2)}) %collective-permute-start.17) | collective-permute-done | bytes 262176 | tf_op jit(solution)/shard_map/ppermute | solution.py:103
  143.7 1.3 collective-permute-start.18
  145.3 2.8 %collective-permute-start.8 = (bf16[128,512]{1,0:T(8,128)(2,1)S(1)}, bf16[128,512]{1,0:T(8,128)(2,1)S(1)}, u32[]{:S(2)}, u32[]{:S(2)}) collective-permute-start(bf16[128,512]{1,0:T(8,128)(2,1)S(1)} %constant_dynamic-slice_fusion.12), channel_id=1, source_target_pairs={{0,8},{1,9},{2,10},{3,11},{4,12},{5,13},{6,14},{7,15},{8,0},{9,1},... | collective-permute-start | bytes 393224 | tf_op jit(solution)/shard_map/ppermute | solution.py:103
  149.2 1.3 collective-permute-start.19
  150.5 2.8 %collective-permute-done.13 = bf16[128,512]{1,0:T(8,128)(2,1)S(1)} collective-permute-done((bf16[128,512]{1,0:T(8,128)(2,1)S(1)}, bf16[128,512]{1,0:T(8,128)(2,1)S(1)}, u32[]{:S(2)}, u32[]{:S(2)}) %collective-permute-start.13) | collective-permute-done | bytes 131104 | tf_op jit(solution)/shard_map/ppermute | solution.py:103
  154.4 2.6 %collective-permute-start.4 = (bf16[64,512]{1,0:T(8,128)(2,1)S(1)}, bf16[64,512]{1,0:T(8,128)(2,1)S(1)}, u32[]{:S(2)}, u32[]{:S(2)}) collective-permute-start(bf16[64,512]{1,0:T(8,128)(2,1)S(1)} %constant_dynamic-slice_fusion.16), channel_id=1, source_target_pairs={{0,8},{1,9},{2,10},{3,11},{4,12},{5,13},{6,14},{7,15},{8,0},{9,1},... | collective-permute-start | bytes 196616 | tf_op jit(solution)/shard_map/ppermute | solution.py:103
  159.5 1.3 collective-permute-start.10
  161.8 1.7 collective-permute-done.10
  163.5 2.6 %collective-permute-done.5 = bf16[32,512]{1,0:T(8,128)(2,1)S(1)} collective-permute-done((bf16[32,512]{1,0:T(8,128)(2,1)S(1)}, bf16[32,512]{1,0:T(8,128)(2,1)S(1)}, u32[]{:S(2)}, u32[]{:S(2)}) %collective-permute-start.5) | collective-permute-done | bytes 32800 | tf_op jit(solution)/shard_map/ppermute | solution.py:103
  (128 shorter events, 25.9 us)
Async XLA Ops:
  7.2 113.3 %copy-start = (bf16[512,2048]{1,0:T(8,128)(2,1)S(1)}, bf16[512,2048]{1,0:T(8,128)(2,1)}, u32[]{:S(2)}) copy-start(bf16[512,2048]{1,0:T(8,128)(2,1)} %param.15) | copy-start | bytes 6291460
  7.2 68.7 %all-gather.2.cloned.1.call-start = ((), (), s32[]{:S(2)}) async-start(), calls=%async_computation | async-start | bytes 4325376 | tf_op jit(solution)/shard_map/all_gather | solution.py:179
  92.1 9.1 %collective-permute-start = (bf16[1024,128]{0,1:T(8,128)(2,1)S(1)}, bf16[1024,128]{0,1:T(8,128)(2,1)}, u32[]{:S(2)}, u32[]{:S(2)}) collective-permute-start(bf16[1024,128]{0,1:T(8,128)(2,1)S(1)} %fusion.2), channel_id=1, source_target_pairs={{0,1},{1,0},{2,3},{3,2},{4,5},{5,4},{6,7},{7,6},{8,9},{9,8},{10,11... | collective-permute-start | bytes 786440 | tf_op jit(solution)/shard_map/ppermute | solution.py:18
  124.6 3.7 %collective-permute-start.16 = (bf16[512,512]{1,0:T(8,128)(2,1)S(1)}, bf16[512,512]{1,0:T(8,128)(2,1)S(1)}, u32[]{:S(2)}, u32[]{:S(2)}) collective-permute-start(bf16[512,512]{1,0:T(8,128)(2,1)S(1)} %constant_dynamic-slice_fusion.4), channel_id=1, source_target_pairs={{0,1},{1,0},{2,3},{3,2},{4,5},{5,4},{6,7},{7,6},{8,9},{9,8},{10,11... | collective-permute-start | bytes 1572872 | tf_op jit(solution)/shard_map/ppermute | solution.py:103
  127.1 3.1 %collective-permute-start.11 = (bf16[512,512]{1,0:T(8,128)(2,1)S(1)}, bf16[512,512]{1,0:T(8,128)(2,1)S(1)}, u32[]{:S(2)}, u32[]{:S(2)}) collective-permute-start(bf16[512,512]{1,0:T(8,128)(2,1)S(1)} %constant_dynamic-slice_fusion.9), channel_id=1, source_target_pairs={{0,1},{1,0},{2,3},{3,2},{4,5},{5,4},{6,7},{7,6},{8,9},{9,8},{10,11... | collective-permute-start | bytes 1572872 | tf_op jit(solution)/shard_map/ppermute | solution.py:103
  127.6 3.9 %collective-permute-start.6 = (bf16[512,512]{1,0:T(8,128)(2,1)S(1)}, bf16[512,512]{1,0:T(8,128)(2,1)S(1)}, u32[]{:S(2)}, u32[]{:S(2)}) collective-permute-start(bf16[512,512]{1,0:T(8,128)(2,1)S(1)} %constant_dynamic-slice_fusion.14), channel_id=1, source_target_pairs={{0,1},{1,0},{2,3},{3,2},{4,5},{5,4},{6,7},{7,6},{8,9},{9,8},{10,11... | collective-permute-start | bytes 1572872 | tf_op jit(solution)/shard_map/ppermute | solution.py:103
  128.0 5.2 %collective-permute-start.1 = (bf16[512,512]{1,0:T(8,128)(2,1)S(1)}, bf16[512,512]{1,0:T(8,128)(2,1)S(1)}, u32[]{:S(2)}, u32[]{:S(2)}) collective-permute-start(bf16[512,512]{1,0:T(8,128)(2,1)S(1)} %constant_dynamic-slice_fusion.19), channel_id=1, source_target_pairs={{0,1},{1,0},{2,3},{3,2},{4,5},{5,4},{6,7},{7,6},{8,9},{9,8},{10,11... | collective-permute-start | bytes 1572872 | tf_op jit(solution)/shard_map/ppermute | solution.py:103
  128.5 15.0 %collective-permute-start.17 = (bf16[256,512]{1,0:T(8,128)(2,1)S(1)}, bf16[256,512]{1,0:T(8,128)(2,1)S(1)}, u32[]{:S(2)}, u32[]{:S(2)}) collective-permute-start(bf16[256,512]{1,0:T(8,128)(2,1)S(1)} %constant_dynamic-slice_fusion.3), channel_id=1, source_target_pairs={{0,16},{1,17},{2,18},{3,19},{4,20},{5,21},{6,22},{7,23},{8,24},{9,... | collective-permute-start | bytes 786440 | tf_op jit(solution)/shard_map/ppermute | solution.py:103
  130.4 14.6 %collective-permute-start.12 = (bf16[256,512]{1,0:T(8,128)(2,1)S(1)}, bf16[256,512]{1,0:T(8,128)(2,1)S(1)}, u32[]{:S(2)}, u32[]{:S(2)}) collective-permute-start(bf16[256,512]{1,0:T(8,128)(2,1)S(1)} %constant_dynamic-slice_fusion.8), channel_id=1, source_target_pairs={{0,8},{1,9},{2,10},{3,11},{4,12},{5,13},{6,14},{7,15},{8,0},{9,1},... | collective-permute-start | bytes 786440 | tf_op jit(solution)/shard_map/ppermute | solution.py:103
  131.7 13.5 %collective-permute-start.7 = (bf16[256,512]{1,0:T(8,128)(2,1)S(1)}, bf16[256,512]{1,0:T(8,128)(2,1)S(1)}, u32[]{:S(2)}, u32[]{:S(2)}) collective-permute-start(bf16[256,512]{1,0:T(8,128)(2,1)S(1)} %constant_dynamic-slice_fusion.13), channel_id=1, source_target_pairs={{0,4},{1,5},{2,6},{3,7},{4,0},{5,1},{6,2},{7,3},{8,12},{9,13},{10,... | collective-permute-start | bytes 786440 | tf_op jit(solution)/shard_map/ppermute | solution.py:103
  133.4 14.7 %collective-permute-start.2 = (bf16[256,512]{1,0:T(8,128)(2,1)S(1)}, bf16[256,512]{1,0:T(8,128)(2,1)S(1)}, u32[]{:S(2)}, u32[]{:S(2)}) collective-permute-start(bf16[256,512]{1,0:T(8,128)(2,1)S(1)} %constant_dynamic-slice_fusion.18), channel_id=1, source_target_pairs={{0,2},{1,3},{2,0},{3,1},{4,6},{5,7},{6,4},{7,5},{8,10},{9,11},{10,... | collective-permute-start | bytes 786440 | tf_op jit(solution)/shard_map/ppermute | solution.py:103
  143.7 5.4 %collective-permute-start.18 = (bf16[128,512]{1,0:T(8,128)(2,1)S(1)}, bf16[128,512]{1,0:T(8,128)(2,1)S(1)}, u32[]{:S(2)}, u32[]{:S(2)}) collective-permute-start(bf16[128,512]{1,0:T(8,128)(2,1)S(1)} %constant_dynamic-slice_fusion.2), channel_id=1, source_target_pairs={{0,2},{1,3},{2,0},{3,1},{4,6},{5,7},{6,4},{7,5},{8,10},{9,11},{10,... | collective-permute-start | bytes 393224 | tf_op jit(solution)/shard_map/ppermute | solution.py:103
  145.1 8.1 %collective-permute-start.13 = (bf16[128,512]{1,0:T(8,128)(2,1)S(1)}, bf16[128,512]{1,0:T(8,128)(2,1)S(1)}, u32[]{:S(2)}, u32[]{:S(2)}) collective-permute-start(bf16[128,512]{1,0:T(8,128)(2,1)S(1)} %constant_dynamic-slice_fusion.7), channel_id=1, source_target_pairs={{0,16},{1,17},{2,18},{3,19},{4,20},{5,21},{6,22},{7,23},{8,24},{9,... | collective-permute-start | bytes 393224 | tf_op jit(solution)/shard_map/ppermute | solution.py:103
  145.3 8.8 %collective-permute-start.8 = (bf16[128,512]{1,0:T(8,128)(2,1)S(1)}, bf16[128,512]{1,0:T(8,128)(2,1)S(1)}, u32[]{:S(2)}, u32[]{:S(2)}) collective-permute-start(bf16[128,512]{1,0:T(8,128)(2,1)S(1)} %constant_dynamic-slice_fusion.12), channel_id=1, source_target_pairs={{0,8},{1,9},{2,10},{3,11},{4,12},{5,13},{6,14},{7,15},{8,0},{9,1},... | collective-permute-start | bytes 393224 | tf_op jit(solution)/shard_map/ppermute | solution.py:103
  148.2 17.9 %copy-start.4 = (bf16[32,2048]{1,0:T(8,128)(2,1)S(1)}, bf16[32,2048]{1,0:T(8,128)(2,1)}, u32[]{:S(2)}) copy-start(bf16[32,2048]{1,0:T(8,128)(2,1)} %param.10) | copy-start | bytes 393220
  148.3 6.0 %collective-permute-start.3 = (bf16[128,512]{1,0:T(8,128)(2,1)S(1)}, bf16[128,512]{1,0:T(8,128)(2,1)S(1)}, u32[]{:S(2)}, u32[]{:S(2)}) collective-permute-start(bf16[128,512]{1,0:T(8,128)(2,1)S(1)} %constant_dynamic-slice_fusion.17), channel_id=1, source_target_pairs={{0,4},{1,5},{2,6},{3,7},{4,0},{5,1},{6,2},{7,3},{8,12},{9,13},{10,... | collective-permute-start | bytes 393224 | tf_op jit(solution)/shard_map/ppermute | solution.py:103
  149.2 7.8 %collective-permute-start.19 = (bf16[64,512]{1,0:T(8,128)(2,1)S(1)}, bf16[64,512]{1,0:T(8,128)(2,1)S(1)}, u32[]{:S(2)}, u32[]{:S(2)}) collective-permute-start(bf16[64,512]{1,0:T(8,128)(2,1)S(1)} %constant_dynamic-slice_fusion.1), channel_id=1, source_target_pairs={{0,4},{1,5},{2,6},{3,7},{4,0},{5,1},{6,2},{7,3},{8,12},{9,13},{10,... | collective-permute-start | bytes 196616 | tf_op jit(solution)/shard_map/ppermute | solution.py:103
  153.3 4.3 %collective-permute-start.14 = (bf16[64,512]{1,0:T(8,128)(2,1)S(1)}, bf16[64,512]{1,0:T(8,128)(2,1)S(1)}, u32[]{:S(2)}, u32[]{:S(2)}) collective-permute-start(bf16[64,512]{1,0:T(8,128)(2,1)S(1)} %constant_dynamic-slice_fusion.6), channel_id=1, source_target_pairs={{0,2},{1,3},{2,0},{3,1},{4,6},{5,7},{6,4},{7,5},{8,10},{9,11},{10,... | collective-permute-start | bytes 196616 | tf_op jit(solution)/shard_map/ppermute | solution.py:103
  154.2 5.3 %collective-permute-start.9 = (bf16[64,512]{1,0:T(8,128)(2,1)S(1)}, bf16[64,512]{1,0:T(8,128)(2,1)S(1)}, u32[]{:S(2)}, u32[]{:S(2)}) collective-permute-start(bf16[64,512]{1,0:T(8,128)(2,1)S(1)} %constant_dynamic-slice_fusion.11), channel_id=1, source_target_pairs={{0,16},{1,17},{2,18},{3,19},{4,20},{5,21},{6,22},{7,23},{8,24},{9,... | collective-permute-start | bytes 196616 | tf_op jit(solution)/shard_map/ppermute | solution.py:103
  154.4 6.5 %collective-permute-start.4 = (bf16[64,512]{1,0:T(8,128)(2,1)S(1)}, bf16[64,512]{1,0:T(8,128)(2,1)S(1)}, u32[]{:S(2)}, u32[]{:S(2)}) collective-permute-start(bf16[64,512]{1,0:T(8,128)(2,1)S(1)} %constant_dynamic-slice_fusion.16), channel_id=1, source_target_pairs={{0,8},{1,9},{2,10},{3,11},{4,12},{5,13},{6,14},{7,15},{8,0},{9,1},... | collective-permute-start | bytes 196616 | tf_op jit(solution)/shard_map/ppermute | solution.py:103
  157.0 4.8 %collective-permute-start.20 = (bf16[32,512]{1,0:T(8,128)(2,1)S(1)}, bf16[32,512]{1,0:T(8,128)(2,1)S(1)}, u32[]{:S(2)}, u32[]{:S(2)}) collective-permute-start(bf16[32,512]{1,0:T(8,128)(2,1)S(1)} %constant_dynamic-slice_fusion), channel_id=1, source_target_pairs={{0,8},{1,9},{2,10},{3,11},{4,12},{5,13},{6,14},{7,15},{8,0},{9,1},... | collective-permute-start | bytes 98312 | tf_op jit(solution)/shard_map/ppermute | solution.py:103
  157.7 4.1 %collective-permute-start.15 = (bf16[32,512]{1,0:T(8,128)(2,1)S(1)}, bf16[32,512]{1,0:T(8,128)(2,1)S(1)}, u32[]{:S(2)}, u32[]{:S(2)}) collective-permute-start(bf16[32,512]{1,0:T(8,128)(2,1)S(1)} %constant_dynamic-slice_fusion.5), channel_id=1, source_target_pairs={{0,4},{1,5},{2,6},{3,7},{4,0},{5,1},{6,2},{7,3},{8,12},{9,13},{10,... | collective-permute-start | bytes 98312 | tf_op jit(solution)/shard_map/ppermute | solution.py:103
  159.5 4.0 %collective-permute-start.10 = (bf16[32,512]{1,0:T(8,128)(2,1)S(1)}, bf16[32,512]{1,0:T(8,128)(2,1)S(1)}, u32[]{:S(2)}, u32[]{:S(2)}) collective-permute-start(bf16[32,512]{1,0:T(8,128)(2,1)S(1)} %constant_dynamic-slice_fusion.10), channel_id=1, source_target_pairs={{0,2},{1,3},{2,0},{3,1},{4,6},{5,7},{6,4},{7,5},{8,10},{9,11},{10,... | collective-permute-start | bytes 98312 | tf_op jit(solution)/shard_map/ppermute | solution.py:103
  160.9 5.2 %collective-permute-start.5 = (bf16[32,512]{1,0:T(8,128)(2,1)S(1)}, bf16[32,512]{1,0:T(8,128)(2,1)S(1)}, u32[]{:S(2)}, u32[]{:S(2)}) collective-permute-start(bf16[32,512]{1,0:T(8,128)(2,1)S(1)} %constant_dynamic-slice_fusion.15), channel_id=1, source_target_pairs={{0,16},{1,17},{2,18},{3,19},{4,20},{5,21},{6,22},{7,23},{8,24},{9,... | collective-permute-start | bytes 98312 | tf_op jit(solution)/shard_map/ppermute | solution.py:103
  (7 other events, 18.0 us)
Sparse Core Ops, SparseCore 0:
  11.4 64.4 all-gather.1

commit v3 on v2

--- a/solution.py
+++ b/solution.py
@@ -162,6 +162,31 @@
     )(queries, keys, values, seg_cols, seg_row, gate_cols)
 
 
+def gather_from_all(block, axis):
+    size = lax.axis_size(axis)
+    bits = size.bit_length() - 1
+    assert 1 << bits == size
+    me = lax.axis_index(axis)
+    rows, width = block.shape
+    parts = REDUCE_PARTS if width % REDUCE_PARTS == 0 else 1
+    piece = width // parts
+    outs = []
+    for j, forward in enumerate(bit_orders(bits, parts)):
+        order = forward[::-1]
+        current = block[:, j * piece:(j + 1) * piece]
+        for k in order:
+            got = lax.ppermute(current, axis, [(i, i ^ (1 << k)) for i in range(size)])
+            upper = ((me >> k) & 1) == 1
+            current = jnp.concatenate(
+                [jnp.where(upper, got, current), jnp.where(upper, current, got)], axis=0
+            )
+        cube = current.reshape((2,) * bits + (rows, piece))
+        old_axis = {order[bits - 1 - a]: a for a in range(bits)}
+        cube = jnp.transpose(cube, [old_axis[bits - 1 - a] for a in range(bits)] + [bits, bits + 1])
+        outs.append(cube.reshape(size * rows, piece))
+    return jnp.concatenate(outs, axis=1)
+
+
 def local(
     hidden,
     norm_gain,
@@ -176,7 +201,7 @@
 ):
     device_index = lax.axis_index("tensor")
     token_count = routes.shape[0]
-    normed = lax.all_gather(normalize(hidden, norm_gain), "tensor", axis=0, tiled=True)
+    normed = gather_from_all(normalize(hidden, norm_gain), "tensor")
     gates = gate_table(normed, router_weight, routes)
     positions = positions_of(segment_ids)
     kv_width = kv_weight.shape[1]

time: 174 us -> 140 us (0.80)
  waiting for transfers between devices: 76.3 us -> 34 us
  starting transfers between devices: 19.5 us -> 37.4 us
  between operations: 14.6 us -> 1.55 us
  other arithmetic: 17 us -> 22.8 us
  matrix products: 14.5 us -> 11.6 us
    all_gather x1 -> x0, waiting for transfers between devices: 58 us -> none  [local(): lax.all_gather(normalize(hidden, norm_gain), 'tensor', axis=0, tiled=True)]
    ppermute x0 -> x20, starting transfers between devices: none -> 20.5 us  [gather_from_all(): got = lax.ppermute(current, axis, [(i, i ^ 1 << k) for i in range(size)])]
    ppermute x0 -> x20, waiting for transfers between devices: none -> 14.8 us  [gather_from_all(): got = lax.ppermute(current, axis, [(i, i ^ 1 << k) for i in range(size)])]
    dot_general x1, matrix products: 5.23 us -> 2.43 us  [local(): queries = jnp.dot(normed, query_weight, preferred_element_type=jnp.float32)]
    ppermute x20, starting transfers between devices: 19.1 us -> 16.7 us  [reduce_to_owner(): got = lax.ppermute(send, axis, [(i, i ^ 1 << k) for i in range(size)])]
    convert_element_type x1, other arithmetic: 1.27 us -> 3.49 us  [local(): queries = (rotate(queries, positions) * scale_factor).astype(jnp.bfloat16)]
    unnamed x25 -> x29, local copies, waits for them, and re-layouts: 8.92 us -> 9.73 us
  transfers between devices with their start and end apart: 22 -> 41, of which waited for: 7 -> 18; matrix products, arithmetic and copies ran while one was open for 11% -> 22% of each run, Pallas kernels for 0% -> 0%
where the time goes in v3:
time: 140 us
  starting transfers between devices  37.4 us (27%)
  waiting for transfers between devices  34 us (24%)
  other arithmetic  22.8 us (16%)
  Pallas kernels  16.3 us (12%)
  local copies, waits for them, and re-layouts  15.9 us (11%)
  matrix products  11.6 us (8%)
  between operations  1.55 us (1%)
    ppermute x20, starting transfers between devices, gather_from_all(): got = lax.ppermute(current, axis, [(i, i ^ 1 << k) for i in range(size)])  20.5 us
    ppermute x20, waiting for transfers between devices, reduce_to_owner(): got = lax.ppermute(send, axis, [(i, i ^ 1 << k) for i in range(size)])  19.3 us
    ppermute x20, starting transfers between devices, reduce_to_owner(): got = lax.ppermute(send, axis, [(i, i ^ 1 << k) for i in range(size)])  16.7 us
    pallas_call x1, Pallas kernels, attend_window(): pl.pallas_call(lambda *refs: attention_kernel(window, *refs), grid=(block...  16.3 us
    ppermute x20, waiting for transfers between devices, gather_from_all(): got = lax.ppermute(current, axis, [(i, i ^ 1 << k) for i in range(size)])  14.8 us
    unnamed x29, local copies, waits for them, and re-layouts  9.73 us
    sub x1, other arithmetic, rotate(): leading * cosine - trailing * sine_part  4.3 us
    dot_general x1, matrix products, project_kv(): projected = jnp.dot(normed, weight, preferred_element_type=jnp.float32)  3.85 us
  transfers between devices with their start and end apart: 41, of which 18 were waited for; matrix products, arithmetic and copies ran while one was open for 22% of the time, Pallas kernels for 0%

profile of v3, /device:TPU:0, one launch (start us, length us, event | category | flops | bytes accessed | tf_op | source)
XLA Modules:
  0.0 139.5 jit_solution(8726994797091541359)
XLA Ops:
  3.6 4.1 %collective-permute-start = (bf16[32,512]{1,0:T(8,128)(2,1)S(1)}, bf16[32,512]{1,0:T(8,128)(2,1)S(1)}, u32[]{:S(2)}, u32[]{:S(2)}) collective-permute-start(bf16[32,512]{1,0:T(8,128)(2,1)S(1)} %get-tuple-element.62), channel_id=1, source_target_pairs={{0,16},{1,17},{2,18},{3,19},{4,20},{5,21},{6,22},{7,23},{8,24},{9,... | collective-permute-start | bytes 98312 | tf_op jit(solution)/shard_map/ppermute | solution.py:178
  13.8 3.0 %multiply_cosine_fusion = (f32[1024,64]{1,0:T(8,128)}, f32[1024,64]{1,0:T(8,128)}) fusion(f32[64]{0:T(128)S(1)} %multiply_power_fusion, f32[1024]{0:T(1024)S(1)} %fusion.17), kind=kLoop, calls=%fused_computation.18 | loop fusion | flops 65536 | bytes 528640 | tf_op jit(solution)/shard_map/cos | solution.py:48
  20.3 2.7 %collective-permute-done.1 = bf16[64,512]{1,0:T(8,128)(2,1)S(1)} collective-permute-done((bf16[64,512]{1,0:T(8,128)(2,1)S(1)}, bf16[64,512]{1,0:T(8,128)(2,1)S(1)}, u32[]{:S(2)}, u32[]{:S(2)}) %collective-permute-start.1) | collective-permute-done | bytes 65568 | tf_op jit(solution)/shard_map/ppermute | solution.py:178
  25.0 1.6 %collective-permute-start.7 = (bf16[128,512]{1,0:T(8,128)(2,1)S(1)}, bf16[128,512]{1,0:T(8,128)(2,1)S(1)}, u32[]{:S(2)}, u32[]{:S(2)}) collective-permute-start(bf16[128,512]{1,0:T(8,128)(2,1)S(1)} %pad_maximum_fusion.14), channel_id=1, source_target_pairs={{0,8},{1,9},{2,10},{3,11},{4,12},{5,13},{6,14},{7,15},{8,0},{9,1},... | collective-permute-start | bytes 393224 | tf_op jit(solution)/shard_map/ppermute | solution.py:178
  31.4 1.6 %collective-permute-start.8 = (bf16[256,512]{1,0:T(8,128)(2,1)S(1)}, bf16[256,512]{1,0:T(8,128)(2,1)S(1)}, u32[]{:S(2)}, u32[]{:S(2)}) collective-permute-start(bf16[256,512]{1,0:T(8,128)(2,1)S(1)} %pad_maximum_fusion.10), channel_id=1, source_target_pairs={{0,4},{1,5},{2,6},{3,7},{4,0},{5,1},{6,2},{7,3},{8,12},{9,13},{10,... | collective-permute-start | bytes 786440 | tf_op jit(solution)/shard_map/ppermute | solution.py:178
  34.3 3.2 %collective-permute-start.18 = (bf16[256,512]{1,0:T(8,128)(2,1)S(1)}, bf16[256,512]{1,0:T(8,128)(2,1)S(1)}, u32[]{:S(2)}, u32[]{:S(2)}) collective-permute-start(bf16[256,512]{1,0:T(8,128)(2,1)S(1)} %pad_maximum_fusion.12), channel_id=1, source_target_pairs={{0,16},{1,17},{2,18},{3,19},{4,20},{5,21},{6,22},{7,23},{8,24},{9,... | collective-permute-start | bytes 786440 | tf_op jit(solution)/shard_map/ppermute | solution.py:178
  38.4 5.5 %collective-permute-done.13 = bf16[256,512]{1,0:T(8,128)(2,1)S(1)} collective-permute-done((bf16[256,512]{1,0:T(8,128)(2,1)S(1)}, bf16[256,512]{1,0:T(8,128)(2,1)S(1)}, u32[]{:S(2)}, u32[]{:S(2)}) %collective-permute-start.13) | collective-permute-done | bytes 262176 | tf_op jit(solution)/shard_map/ppermute | solution.py:178
  50.6 3.9 %fusion.27 = f32[1024,128]{0,1:T(8,128)S(1)} fusion(bf16[1024,2048]{1,0:T(8,128)(2,1)} %copy-done.1, bf16[2048,128]{1,0:T(8,128)(2,1)S(1)} %copy-done.4), kind=kOutput, calls=%fused_computation.155 | convolution fusion | flops 536870912 | bytes 5242880 | tf_op jit(solution)/shard_map/dot_general | solution.py:58
  55.9 2.4 %fusion.26 = f32[1024,512]{0,1:T(8,128)S(1)} fusion(bf16[1024,2048]{1,0:T(8,128)(2,1)S(1)} %copy-done.2, bf16[2048,512]{1,0:T(8,128)(2,1)S(1)} %copy-done.10), kind=kOutput, calls=%fused_computation.154 | convolution fusion | flops 2147483648 | bytes 8388608 | tf_op jit(solution)/shard_map/dot_general | solution.py:223
  59.6 2.7 %copy.74 = f32[1024,4,64]{2,1,0:T(4,128)} copy(f32[1024,4,64]{0,2,1:T(8,128)} %get-tuple-element.17) | data formatting | bytes 2097152
  62.3 1.8 %copy.75 = f32[1024,4,64]{2,1,0:T(4,128)} copy(f32[1024,4,64]{0,2,1:T(8,128)S(1)} %get-tuple-element.16) | data formatting | bytes 2097152
  64.1 4.3 %multiply_subtract_fusion = (f32[1024,4,64]{2,1,0:T(4,128)}, f32[1024,4,64]{2,1,0:T(4,128)}) fusion(f32[1024,4,64]{2,1,0:T(4,128)} %copy.75, f32[1024,4,64]{2,1,0:T(4,128)} %copy.74, f32[1024,64]{1,0:T(8,128)} %get-tuple-element.73, f32[1024,64]{1,0:T(8,128)} %get-tuple-element.72), kind=kLoop, calls=%fused_computation.5 | loop fusion | flops 1572864 | bytes 4718592 | tf_op jit(solution)/shard_map/sub | solution.py:53
  68.4 2.0 %copy.66.refs_5_ = f32[4,1024,1]{2,1,0:T(8,128)} copy(f32[4,1024,1]{1,0,2:T(4,128)S(1)} %dynamic-slice_bitcast_fusion) | data formatting | bytes 32768 | tf_op jit(solution)/shard_map/reshape | solution.py:141
  70.4 3.5 %fusion = bf16[1024,4,128]{2,1,0:T(4,128)(2,1)S(1)} fusion(f32[1024,4,64]{2,1,0:T(4,128)} %get-tuple-element.11, f32[1024,4,64]{2,1,0:T(4,128)} %get-tuple-element.10), kind=kLoop, calls=%fused_computation.3 | loop fusion | flops 1572864 | bytes 3145728 | tf_op jit(solution)/shard_map/convert_element_type | solution.py:225
  78.3 16.3 %shard_map.113 = bf16[1024,512]{1,0:T(8,128)(2,1)} custom-call(bf16[1024,512]{1,0:T(8,128)(2,1)} %bitcast.91, bf16[1024,128]{1,0:T(8,128)(2,1)} %bitcast.103, bf16[1024,128]{1,0:T(8,128)(2,1)} %bitcast.104, s32[1024,1]{1,0:T(8,128)} %copy.65.refs_3_, s32[1,1024]{1,0:T(1,128)} %bitcast.106, f32[4,1024,1]{2,1,0:T(8,128)} %copy.66.refs_5_), custom_call_target="tpu_custom_call" | custom-call | flops 1342177280 | bytes 2621440 | tf_op jit(solution)/shard_map/pallas_call | solution.py:144
  94.7 3.6 %convolution_convert_fusion = bf16[1024,2048]{1,0:T(8,128)(2,1)S(1)} fusion(bf16[1024,512]{1,0:T(8,128)(2,1)} %shard_map.113, bf16[512,2048]{1,0:T(8,128)(2,1)S(1)} %copy-done), kind=kOutput, calls=%fused_computation.1 | convolution fusion | flops 2149580800 | bytes 7340032 | tf_op jit(solution)/shard_map/dot_general | solution.py:235
  105.7 2.1 %collective-permute-start.37 = (bf16[256,512]{1,0:T(8,128)(2,1)S(1)}, bf16[256,512]{1,0:T(8,128)(2,1)S(1)}, u32[]{:S(2)}, u32[]{:S(2)}) collective-permute-start(bf16[256,512]{1,0:T(8,128)(2,1)S(1)} %constant_dynamic-slice_fusion.3), channel_id=1, source_target_pairs={{0,16},{1,17},{2,18},{3,19},{4,20},{5,21},{6,22},{7,23},{8,24},{9,... | collective-permute-start | bytes 786440 | tf_op jit(solution)/shard_map/ppermute | solution.py:103
  107.8 3.5 %collective-permute-done.22 = bf16[256,512]{1,0:T(8,128)(2,1)S(1)} collective-permute-done((bf16[256,512]{1,0:T(8,128)(2,1)S(1)}, bf16[256,512]{1,0:T(8,128)(2,1)S(1)}, u32[]{:S(2)}, u32[]{:S(2)}) %collective-permute-start.22) | collective-permute-done | bytes 262176 | tf_op jit(solution)/shard_map/ppermute | solution.py:103
  111.4 1.6 %collective-permute-start.23 = (bf16[128,512]{1,0:T(8,128)(2,1)S(1)}, bf16[128,512]{1,0:T(8,128)(2,1)S(1)}, u32[]{:S(2)}, u32[]{:S(2)}) collective-permute-start(bf16[128,512]{1,0:T(8,128)(2,1)S(1)} %constant_dynamic-slice_fusion.17), channel_id=1, source_target_pairs={{0,4},{1,5},{2,6},{3,7},{4,0},{5,1},{6,2},{7,3},{8,12},{9,13},{10,... | collective-permute-start | bytes 393224 | tf_op jit(solution)/shard_map/ppermute | solution.py:103
  113.1 6.5 %collective-permute-done.32 = bf16[256,512]{1,0:T(8,128)(2,1)S(1)} collective-permute-done((bf16[256,512]{1,0:T(8,128)(2,1)S(1)}, bf16[256,512]{1,0:T(8,128)(2,1)S(1)}, u32[]{:S(2)}, u32[]{:S(2)}) %collective-permute-start.32) | collective-permute-done | bytes 262176 | tf_op jit(solution)/shard_map/ppermute | solution.py:103
  122.0 2.1 %collective-permute-start.24 = (bf16[64,512]{1,0:T(8,128)(2,1)S(1)}, bf16[64,512]{1,0:T(8,128)(2,1)S(1)}, u32[]{:S(2)}, u32[]{:S(2)}) collective-permute-start(bf16[64,512]{1,0:T(8,128)(2,1)S(1)} %constant_dynamic-slice_fusion.16), channel_id=1, source_target_pairs={{0,8},{1,9},{2,10},{3,11},{4,12},{5,13},{6,14},{7,15},{8,0},{9,1},... | collective-permute-start | bytes 196616 | tf_op jit(solution)/shard_map/ppermute | solution.py:103
  125.1 2.8 %collective-permute-done.33 = bf16[128,512]{1,0:T(8,128)(2,1)S(1)} collective-permute-done((bf16[128,512]{1,0:T(8,128)(2,1)S(1)}, bf16[128,512]{1,0:T(8,128)(2,1)S(1)}, u32[]{:S(2)}, u32[]{:S(2)}) %collective-permute-start.33) | collective-permute-done | bytes 131104 | tf_op jit(solution)/shard_map/ppermute | solution.py:103
  128.0 2.4 %collective-permute-start.34 = (bf16[64,512]{1,0:T(8,128)(2,1)S(1)}, bf16[64,512]{1,0:T(8,128)(2,1)S(1)}, u32[]{:S(2)}, u32[]{:S(2)}) collective-permute-start(bf16[64,512]{1,0:T(8,128)(2,1)S(1)} %constant_dynamic-slice_fusion.6), channel_id=1, source_target_pairs={{0,2},{1,3},{2,0},{3,1},{4,6},{5,7},{6,4},{7,5},{8,10},{9,11},{10,... | collective-permute-start | bytes 196616 | tf_op jit(solution)/shard_map/ppermute | solution.py:103
  136.7 2.1 %collective-permute-done.40 = bf16[32,512]{1,0:T(8,128)(2,1)S(1)} collective-permute-done((bf16[32,512]{1,0:T(8,128)(2,1)S(1)}, bf16[32,512]{1,0:T(8,128)(2,1)S(1)}, u32[]{:S(2)}, u32[]{:S(2)}) %collective-permute-start.40) | collective-permute-done | bytes 32800 | tf_op jit(solution)/shard_map/ppermute | solution.py:103
  (210 shorter events, 52.7 us)
Async XLA Ops:
  3.6 15.0 %collective-permute-start = (bf16[32,512]{1,0:T(8,128)(2,1)S(1)}, bf16[32,512]{1,0:T(8,128)(2,1)S(1)}, u32[]{:S(2)}, u32[]{:S(2)}) collective-permute-start(bf16[32,512]{1,0:T(8,128)(2,1)S(1)} %get-tuple-element.62), channel_id=1, source_target_pairs={{0,16},{1,17},{2,18},{3,19},{4,20},{5,21},{6,22},{7,23},{8,24},{9,... | collective-permute-start | bytes 98312 | tf_op jit(solution)/shard_map/ppermute | solution.py:178
  7.7 10.9 %collective-permute-start.10 = (bf16[32,512]{1,0:T(8,128)(2,1)S(1)}, bf16[32,512]{1,0:T(8,128)(2,1)S(1)}, u32[]{:S(2)}, u32[]{:S(2)}) collective-permute-start(bf16[32,512]{1,0:T(8,128)(2,1)S(1)} %get-tuple-element.64), channel_id=1, source_target_pairs={{0,4},{1,5},{2,6},{3,7},{4,0},{5,1},{6,2},{7,3},{8,12},{9,13},{10,... | collective-permute-start | bytes 98312 | tf_op jit(solution)/shard_map/ppermute | solution.py:178
  9.2 9.4 %collective-permute-start.15 = (bf16[32,512]{1,0:T(8,128)(2,1)S(1)}, bf16[32,512]{1,0:T(8,128)(2,1)S(1)}, u32[]{:S(2)}, u32[]{:S(2)}) collective-permute-start(bf16[32,512]{1,0:T(8,128)(2,1)S(1)} %get-tuple-element.63), channel_id=1, source_target_pairs={{0,8},{1,9},{2,10},{3,11},{4,12},{5,13},{6,14},{7,15},{8,0},{9,1},... | collective-permute-start | bytes 98312 | tf_op jit(solution)/shard_map/ppermute | solution.py:178
  10.8 7.8 %collective-permute-start.5 = (bf16[32,512]{1,0:T(8,128)(2,1)S(1)}, bf16[32,512]{1,0:T(8,128)(2,1)S(1)}, u32[]{:S(2)}, u32[]{:S(2)}) collective-permute-start(bf16[32,512]{1,0:T(8,128)(2,1)S(1)} %get-tuple-element.65), channel_id=1, source_target_pairs={{0,2},{1,3},{2,0},{3,1},{4,6},{5,7},{6,4},{7,5},{8,10},{9,11},{10,... | collective-permute-start | bytes 98312 | tf_op jit(solution)/shard_map/ppermute | solution.py:178
  19.5 7.1 %collective-permute-start.11 = (bf16[64,512]{1,0:T(8,128)(2,1)S(1)}, bf16[64,512]{1,0:T(8,128)(2,1)S(1)}, u32[]{:S(2)}, u32[]{:S(2)}) collective-permute-start(bf16[64,512]{1,0:T(8,128)(2,1)S(1)} %pad_maximum_fusion.19), channel_id=1, source_target_pairs={{0,2},{1,3},{2,0},{3,1},{4,6},{5,7},{6,4},{7,5},{8,10},{9,11},{10,... | collective-permute-start | bytes 196616 | tf_op jit(solution)/shard_map/ppermute | solution.py:178
  20.1 6.6 %collective-permute-start.16 = (bf16[64,512]{1,0:T(8,128)(2,1)S(1)}, bf16[64,512]{1,0:T(8,128)(2,1)S(1)}, u32[]{:S(2)}, u32[]{:S(2)}) collective-permute-start(bf16[64,512]{1,0:T(8,128)(2,1)S(1)} %pad_maximum_fusion.20), channel_id=1, source_target_pairs={{0,4},{1,5},{2,6},{3,7},{4,0},{5,1},{6,2},{7,3},{8,12},{9,13},{10,... | collective-permute-start | bytes 196616 | tf_op jit(solution)/shard_map/ppermute | solution.py:178
  26.7 7.3 %collective-permute-start.12 = (bf16[128,512]{1,0:T(8,128)(2,1)S(1)}, bf16[128,512]{1,0:T(8,128)(2,1)S(1)}, u32[]{:S(2)}, u32[]{:S(2)}) collective-permute-start(bf16[128,512]{1,0:T(8,128)(2,1)S(1)} %pad_maximum_fusion.15), channel_id=1, source_target_pairs={{0,16},{1,17},{2,18},{3,19},{4,20},{5,21},{6,22},{7,23},{8,24},{9,... | collective-permute-start | bytes 393224 | tf_op jit(solution)/shard_map/ppermute | solution.py:178
  29.6 7.9 %collective-permute-start.3 = (bf16[256,512]{1,0:T(8,128)(2,1)S(1)}, bf16[256,512]{1,0:T(8,128)(2,1)S(1)}, u32[]{:S(2)}, u32[]{:S(2)}) collective-permute-start(bf16[256,512]{1,0:T(8,128)(2,1)S(1)} %pad_maximum_fusion.9), channel_id=1, source_target_pairs={{0,2},{1,3},{2,0},{3,1},{4,6},{5,7},{6,4},{7,5},{8,10},{9,11},{10,... | collective-permute-start | bytes 786440 | tf_op jit(solution)/shard_map/ppermute | solution.py:178
  31.4 6.4 %collective-permute-start.8 = (bf16[256,512]{1,0:T(8,128)(2,1)S(1)}, bf16[256,512]{1,0:T(8,128)(2,1)S(1)}, u32[]{:S(2)}, u32[]{:S(2)}) collective-permute-start(bf16[256,512]{1,0:T(8,128)(2,1)S(1)} %pad_maximum_fusion.10), channel_id=1, source_target_pairs={{0,4},{1,5},{2,6},{3,7},{4,0},{5,1},{6,2},{7,3},{8,12},{9,13},{10,... | collective-permute-start | bytes 786440 | tf_op jit(solution)/shard_map/ppermute | solution.py:178
  34.1 9.8 %collective-permute-start.13 = (bf16[256,512]{1,0:T(8,128)(2,1)S(1)}, bf16[256,512]{1,0:T(8,128)(2,1)S(1)}, u32[]{:S(2)}, u32[]{:S(2)}) collective-permute-start(bf16[256,512]{1,0:T(8,128)(2,1)S(1)} %pad_maximum_fusion.11), channel_id=1, source_target_pairs={{0,8},{1,9},{2,10},{3,11},{4,12},{5,13},{6,14},{7,15},{8,0},{9,1},... | collective-permute-start | bytes 786440 | tf_op jit(solution)/shard_map/ppermute | solution.py:178
  34.3 11.0 %collective-permute-start.18 = (bf16[256,512]{1,0:T(8,128)(2,1)S(1)}, bf16[256,512]{1,0:T(8,128)(2,1)S(1)}, u32[]{:S(2)}, u32[]{:S(2)}) collective-permute-start(bf16[256,512]{1,0:T(8,128)(2,1)S(1)} %pad_maximum_fusion.12), channel_id=1, source_target_pairs={{0,16},{1,17},{2,18},{3,19},{4,20},{5,21},{6,22},{7,23},{8,24},{9,... | collective-permute-start | bytes 786440 | tf_op jit(solution)/shard_map/ppermute | solution.py:178
  37.6 7.9 %collective-permute-start.4 = (bf16[512,512]{1,0:T(8,128)(2,1)S(1)}, bf16[512,512]{1,0:T(8,128)(2,1)S(1)}, u32[]{:S(2)}, u32[]{:S(2)}) collective-permute-start(bf16[512,512]{1,0:T(8,128)(2,1)S(1)} %pad_maximum_fusion.5), channel_id=1, source_target_pairs={{0,1},{1,0},{2,3},{3,2},{4,5},{5,4},{6,7},{7,6},{8,9},{9,8},{10,11... | collective-permute-start | bytes 1572872 | tf_op jit(solution)/shard_map/ppermute | solution.py:178
  38.0 7.8 %collective-permute-start.9 = (bf16[512,512]{1,0:T(8,128)(2,1)S(1)}, bf16[512,512]{1,0:T(8,128)(2,1)S(1)}, u32[]{:S(2)}, u32[]{:S(2)}) collective-permute-start(bf16[512,512]{1,0:T(8,128)(2,1)S(1)} %pad_maximum_fusion.6), channel_id=1, source_target_pairs={{0,1},{1,0},{2,3},{3,2},{4,5},{5,4},{6,7},{7,6},{8,9},{9,8},{10,11... | collective-permute-start | bytes 1572872 | tf_op jit(solution)/shard_map/ppermute | solution.py:178
  55.7 19.6 %collective-permute-start.20 = (bf16[1024,128]{0,1:T(8,128)(2,1)S(1)}, bf16[1024,128]{0,1:T(8,128)(2,1)}, u32[]{:S(2)}, u32[]{:S(2)}) collective-permute-start(bf16[1024,128]{0,1:T(8,128)(2,1)S(1)} %fusion.2), channel_id=1, source_target_pairs={{0,1},{1,0},{2,3},{3,2},{4,5},{5,4},{6,7},{7,6},{8,9},{9,8},{10,11... | collective-permute-start | bytes 786440 | tf_op jit(solution)/shard_map/ppermute | solution.py:18
  102.8 8.4 %collective-permute-start.22 = (bf16[256,512]{1,0:T(8,128)(2,1)S(1)}, bf16[256,512]{1,0:T(8,128)(2,1)S(1)}, u32[]{:S(2)}, u32[]{:S(2)}) collective-permute-start(bf16[256,512]{1,0:T(8,128)(2,1)S(1)} %constant_dynamic-slice_fusion.18), channel_id=1, source_target_pairs={{0,2},{1,3},{2,0},{3,1},{4,6},{5,7},{6,4},{7,5},{8,10},{9,11},{10,... | collective-permute-start | bytes 786440 | tf_op jit(solution)/shard_map/ppermute | solution.py:103
  103.7 9.3 %collective-permute-start.27 = (bf16[256,512]{1,0:T(8,128)(2,1)S(1)}, bf16[256,512]{1,0:T(8,128)(2,1)S(1)}, u32[]{:S(2)}, u32[]{:S(2)}) collective-permute-start(bf16[256,512]{1,0:T(8,128)(2,1)S(1)} %constant_dynamic-slice_fusion.13), channel_id=1, source_target_pairs={{0,4},{1,5},{2,6},{3,7},{4,0},{5,1},{6,2},{7,3},{8,12},{9,13},{10,... | collective-permute-start | bytes 786440 | tf_op jit(solution)/shard_map/ppermute | solution.py:103
  105.4 14.2 %collective-permute-start.32 = (bf16[256,512]{1,0:T(8,128)(2,1)S(1)}, bf16[256,512]{1,0:T(8,128)(2,1)S(1)}, u32[]{:S(2)}, u32[]{:S(2)}) collective-permute-start(bf16[256,512]{1,0:T(8,128)(2,1)S(1)} %constant_dynamic-slice_fusion.8), channel_id=1, source_target_pairs={{0,8},{1,9},{2,10},{3,11},{4,12},{5,13},{6,14},{7,15},{8,0},{9,1},... | collective-permute-start | bytes 786440 | tf_op jit(solution)/shard_map/ppermute | solution.py:103
  105.7 14.9 %collective-permute-start.37 = (bf16[256,512]{1,0:T(8,128)(2,1)S(1)}, bf16[256,512]{1,0:T(8,128)(2,1)S(1)}, u32[]{:S(2)}, u32[]{:S(2)}) collective-permute-start(bf16[256,512]{1,0:T(8,128)(2,1)S(1)} %constant_dynamic-slice_fusion.3), channel_id=1, source_target_pairs={{0,16},{1,17},{2,18},{3,19},{4,20},{5,21},{6,22},{7,23},{8,24},{9,... | collective-permute-start | bytes 786440 | tf_op jit(solution)/shard_map/ppermute | solution.py:103
  111.4 10.6 %collective-permute-start.23 = (bf16[128,512]{1,0:T(8,128)(2,1)S(1)}, bf16[128,512]{1,0:T(8,128)(2,1)S(1)}, u32[]{:S(2)}, u32[]{:S(2)}) collective-permute-start(bf16[128,512]{1,0:T(8,128)(2,1)S(1)} %constant_dynamic-slice_fusion.17), channel_id=1, source_target_pairs={{0,4},{1,5},{2,6},{3,7},{4,0},{5,1},{6,2},{7,3},{8,12},{9,13},{10,... | collective-permute-start | bytes 393224 | tf_op jit(solution)/shard_map/ppermute | solution.py:103
  113.0 11.1 %collective-permute-start.28 = (bf16[128,512]{1,0:T(8,128)(2,1)S(1)}, bf16[128,512]{1,0:T(8,128)(2,1)S(1)}, u32[]{:S(2)}, u32[]{:S(2)}) collective-permute-start(bf16[128,512]{1,0:T(8,128)(2,1)S(1)} %constant_dynamic-slice_fusion.12), channel_id=1, source_target_pairs={{0,8},{1,9},{2,10},{3,11},{4,12},{5,13},{6,14},{7,15},{8,0},{9,1},... | collective-permute-start | bytes 393224 | tf_op jit(solution)/shard_map/ppermute | solution.py:103
  119.7 8.2 %collective-permute-start.33 = (bf16[128,512]{1,0:T(8,128)(2,1)S(1)}, bf16[128,512]{1,0:T(8,128)(2,1)S(1)}, u32[]{:S(2)}, u32[]{:S(2)}) collective-permute-start(bf16[128,512]{1,0:T(8,128)(2,1)S(1)} %constant_dynamic-slice_fusion.7), channel_id=1, source_target_pairs={{0,16},{1,17},{2,18},{3,19},{4,20},{5,21},{6,22},{7,23},{8,24},{9,... | collective-permute-start | bytes 393224 | tf_op jit(solution)/shard_map/ppermute | solution.py:103
  120.7 9.8 %collective-permute-start.38 = (bf16[128,512]{1,0:T(8,128)(2,1)S(1)}, bf16[128,512]{1,0:T(8,128)(2,1)S(1)}, u32[]{:S(2)}, u32[]{:S(2)}) collective-permute-start(bf16[128,512]{1,0:T(8,128)(2,1)S(1)} %constant_dynamic-slice_fusion.2), channel_id=1, source_target_pairs={{0,2},{1,3},{2,0},{3,1},{4,6},{5,7},{6,4},{7,5},{8,10},{9,11},{10,... | collective-permute-start | bytes 393224 | tf_op jit(solution)/shard_map/ppermute | solution.py:103
  122.0 8.5 %collective-permute-start.24 = (bf16[64,512]{1,0:T(8,128)(2,1)S(1)}, bf16[64,512]{1,0:T(8,128)(2,1)S(1)}, u32[]{:S(2)}, u32[]{:S(2)}) collective-permute-start(bf16[64,512]{1,0:T(8,128)(2,1)S(1)} %constant_dynamic-slice_fusion.16), channel_id=1, source_target_pairs={{0,8},{1,9},{2,10},{3,11},{4,12},{5,13},{6,14},{7,15},{8,0},{9,1},... | collective-permute-start | bytes 196616 | tf_op jit(solution)/shard_map/ppermute | solution.py:103
  124.2 6.5 %collective-permute-start.29 = (bf16[64,512]{1,0:T(8,128)(2,1)S(1)}, bf16[64,512]{1,0:T(8,128)(2,1)S(1)}, u32[]{:S(2)}, u32[]{:S(2)}) collective-permute-start(bf16[64,512]{1,0:T(8,128)(2,1)S(1)} %constant_dynamic-slice_fusion.11), channel_id=1, source_target_pairs={{0,16},{1,17},{2,18},{3,19},{4,20},{5,21},{6,22},{7,23},{8,24},{9,... | collective-permute-start | bytes 196616 | tf_op jit(solution)/shard_map/ppermute | solution.py:103
  (28 other events, 220.0 us)

commit v4 on v3

--- a/solution.py
+++ b/solution.py
@@ -106,7 +106,7 @@
     return jnp.concatenate(outs, axis=1)
 
 
-def attention_kernel(window, q_ref, k_ref, v_ref, qseg_ref, kseg_ref, gate_ref, out_ref):
+def attention_kernel(window, q_ref, cos_ref, sin_ref, k_ref, v_ref, qseg_ref, kseg_ref, gate_ref, out_ref):
     chunk = pl.program_id(0)
     blocks = pl.num_programs(0)
     start_block = jnp.clip(chunk - (window - 1), 0, blocks - window)
@@ -119,9 +119,14 @@
     query_index = chunk * CHUNK + lax.broadcasted_iota(jnp.int32, (CHUNK, span), 0)
     key_index = start + lax.broadcasted_iota(jnp.int32, (CHUNK, span), 1)
     allowed = (query_seg == key_seg) & (key_index <= query_index)
-    experts = gate_ref.shape[0]
+    cosine = cos_ref[...]
+    sine_part = sin_ref[...]
+    scale_factor = HD ** (-0.5)
+    experts = gate_ref.shape[1]
     for e in range(experts):
-        queries = q_ref[:, e * HD:(e + 1) * HD]
+        raw = q_ref[:, e * HD:(e + 1) * HD]
+        turned = raw * cosine + pltpu.roll(raw, HD // 2, 1) * sine_part
+        queries = (turned * scale_factor).astype(jnp.bfloat16)
         scores = lax.dot_general(
             queries, keys, (((1,), (1,)), ((), ())), preferred_element_type=jnp.float32
         )
@@ -130,15 +135,27 @@
         raised = jnp.exp(scores - top)
         probabilities = (raised / jnp.sum(raised, axis=1, keepdims=True)).astype(jnp.bfloat16)
         attended = jnp.dot(probabilities, values, preferred_element_type=jnp.float32)
-        out_ref[:, e * HD:(e + 1) * HD] = (attended * gate_ref[e]).astype(out_ref.dtype)
-
-
-def attend_window(queries, keys, values, segment_ids, gate_here):
-    tokens, width = queries.shape
+        out_ref[:, e * HD:(e + 1) * HD] = (attended * gate_ref[:, e:e + 1]).astype(out_ref.dtype)
+
+
+def rope_tables(positions):
+    half_width = HD // 2
+    frequency = 10000.0 ** (-jnp.arange(half_width, dtype=jnp.float32) / half_width)
+    angles = positions.astype(jnp.float32)[:, None] * frequency[None, :]
+    cosine = jnp.cos(angles)
+    sine_part = jnp.sin(angles)
+    return (
+        jnp.concatenate([cosine, cosine], axis=1),
+        jnp.concatenate([-sine_part, sine_part], axis=1),
+    )
+
+
+def attend_window(raw_queries, positions, keys, values, segment_ids, gate_here):
+    tokens, width = raw_queries.shape
     experts = width // HD
     blocks = tokens // CHUNK
     window = min(blocks, SEG_MOST // CHUNK + 1)
-    gate_cols = jnp.transpose(gate_here).reshape(experts, tokens, 1)
+    cosine, sine_part = rope_tables(positions)
     seg_cols = segment_ids.reshape(tokens, 1)
     seg_row = segment_ids.reshape(1, tokens)
     return pl.pallas_call(
@@ -146,20 +163,22 @@
         grid=(blocks,),
         in_specs=[
             pl.BlockSpec((CHUNK, width), lambda i: (i, 0)),
+            pl.BlockSpec((CHUNK, HD), lambda i: (i, 0)),
+            pl.BlockSpec((CHUNK, HD), lambda i: (i, 0)),
             pl.BlockSpec((tokens, HD), lambda i: (0, 0)),
             pl.BlockSpec((tokens, HD), lambda i: (0, 0)),
             pl.BlockSpec((CHUNK, 1), lambda i: (i, 0)),
             pl.BlockSpec((1, tokens), lambda i: (0, 0)),
-            pl.BlockSpec((experts, CHUNK, 1), lambda i: (0, i, 0)),
+            pl.BlockSpec((CHUNK, experts), lambda i: (i, 0)),
         ],
         out_specs=pl.BlockSpec((CHUNK, width), lambda i: (i, 0)),
         out_shape=jax.ShapeDtypeStruct((tokens, width), jnp.bfloat16),
         cost_estimate=pl.CostEstimate(
             flops=4 * tokens * window * CHUNK * width,
             transcendentals=tokens * window * CHUNK * experts,
-            bytes_accessed=2 * tokens * width * 2 + 2 * tokens * HD * 2,
+            bytes_accessed=tokens * width * 6 + 2 * tokens * HD * 2 + 2 * tokens * HD * 4,
         ),
-    )(queries, keys, values, seg_cols, seg_row, gate_cols)
+    )(raw_queries, cosine, sine_part, keys, values, seg_cols, seg_row, gate_here)
 
 
 def gather_from_all(block, axis):
@@ -210,28 +229,13 @@
     new_cache = write_pages(kv_cache, page_table, own_rows.reshape(page_table.shape[0], PAGE, kv_width))
     partner_rows = swapped(own_rows, "tensor", 0)
     leading_first = device_index % 2 == 0
-    head_rows = jnp.where(
-        leading_first,
-        jnp.concatenate([own_rows, partner_rows], axis=1),
-        jnp.concatenate([partner_rows, own_rows], axis=1),
-    )
-    local_heads = head_rows.shape[1] // (2 * HD)
-    head_rows = head_rows.reshape(token_count, local_heads, 2, HD)
+    key_rows = jnp.where(leading_first, own_rows, partner_rows)
+    value_rows = jnp.where(leading_first, partner_rows, own_rows)
     pair_count = query_weight.shape[1] // HD
-    local_experts = pair_count // local_heads
-    scale_factor = HD ** (-0.5)
-    queries = jnp.dot(normed, query_weight, preferred_element_type=jnp.float32)
-    queries = queries.reshape(token_count, local_experts, HD)
-    queries = (rotate(queries, positions) * scale_factor).astype(jnp.bfloat16)
+    raw_queries = jnp.dot(normed, query_weight, preferred_element_type=jnp.float32)
     first_expert = (device_index * pair_count) % EA
-    gate_here = lax.dynamic_slice_in_dim(gates, first_expert, local_experts, 1)
-    flat = attend_window(
-        queries.reshape(token_count, pair_count * HD),
-        head_rows[:, 0, 0],
-        head_rows[:, 0, 1],
-        segment_ids,
-        gate_here,
-    )
+    gate_here = lax.dynamic_slice_in_dim(gates, first_expert, pair_count, 1)
+    flat = attend_window(raw_queries, positions, key_rows, value_rows, segment_ids, gate_here)
     partial = jnp.dot(flat, out_weight, preferred_element_type=jnp.float32).astype(jnp.bfloat16)
     reduced = reduce_to_owner(partial, "tensor").astype(jnp.float32)
     attended_out = (hidden.astype(jnp.float32) + reduced).astype(jnp.bfloat16)

time: 140 us -> 125 us (0.89)
  local copies, waits for them, and re-layouts: 15.9 us -> 6.74 us
  other arithmetic: 22.8 us -> 15.8 us
    unnamed x29 -> x24, local copies, waits for them, and re-layouts: 9.73 us -> 4.02 us
    sub x1 -> x0, other arithmetic: 4.3 us -> none  [rotate(): leading * cosine - trailing * sine_part]
    convert_element_type x2 -> x1, other arithmetic: 3.57 us -> 0.08 us  [rope_tables(): angles = positions.astype(jnp.float32)[:, None] * frequency[None, :]]
    cos x1 -> x0, other arithmetic: 3.01 us -> none  [rotate(): cosine = jnp.cos(angles)]
    reshape x2 -> x0, local copies, waits for them, and re-layouts: 2 us -> none  [attend_window(): gate_cols = jnp.transpose(gate_here).reshape(experts, tokens, 1)]
    neg x0 -> x1, other arithmetic: none -> 1.9 us  [rope_tables(): -sine_part]
  transfers between devices with their start and end apart: 41 -> 41, of which waited for: 18 -> 18; matrix products, arithmetic and copies ran while one was open for 22% -> 13% of each run, Pallas kernels for 0% -> 0%
where the time goes in v4:
time: 125 us
  starting transfers between devices  37.3 us (30%)
  waiting for transfers between devices  34 us (27%)
  Pallas kernels  17.1 us (14%)
  other arithmetic  15.8 us (13%)
  matrix products  12.6 us (10%)
  local copies, waits for them, and re-layouts  6.74 us (5%)
  between operations  1.51 us (1%)
    ppermute x20, starting transfers between devices, gather_from_all(): got = lax.ppermute(current, axis, [(i, i ^ 1 << k) for i in range(size)])  20.5 us
    ppermute x20, waiting for transfers between devices, reduce_to_owner(): got = lax.ppermute(send, axis, [(i, i ^ 1 << k) for i in range(size)])  19.3 us
    pallas_call x1, Pallas kernels, attend_window(): pl.pallas_call(lambda *refs: attention_kernel(window, *refs), grid=(block...  17.1 us
    ppermute x20, starting transfers between devices, reduce_to_owner(): got = lax.ppermute(send, axis, [(i, i ^ 1 << k) for i in range(size)])  16.6 us
    ppermute x20, waiting for transfers between devices, gather_from_all(): got = lax.ppermute(current, axis, [(i, i ^ 1 << k) for i in range(size)])  14.7 us
    unnamed x24, local copies, waits for them, and re-layouts  4.02 us
    dot_general x1, matrix products, local(): jnp.dot(normed, query_weight, preferred_element_type=jnp.float32)  3.69 us
    dot_general x1, matrix products, project_kv(): projected = jnp.dot(normed, weight, preferred_element_type=jnp.float32)  3.58 us
  transfers between devices with their start and end apart: 41, of which 18 were waited for; matrix products, arithmetic and copies ran while one was open for 13% of the time, Pallas kernels for 0%

profile of v4, /device:TPU:0, one launch (start us, length us, event | category | flops | bytes accessed | tf_op | source)
XLA Modules:
  0.0 125.1 jit_solution(16267523850741769354)
XLA Ops:
  3.6 4.1 %collective-permute-start = (bf16[32,512]{1,0:T(8,128)(2,1)S(1)}, bf16[32,512]{1,0:T(8,128)(2,1)S(1)}, u32[]{:S(2)}, u32[]{:S(2)}) collective-permute-start(bf16[32,512]{1,0:T(8,128)(2,1)S(1)} %get-tuple-element.58), channel_id=1, source_target_pairs={{0,16},{1,17},{2,18},{3,19},{4,20},{5,21},{6,22},{7,23},{8,24},{9,... | collective-permute-start | bytes 98312 | tf_op jit(solution)/shard_map/ppermute | solution.py:197
  7.7 1.5 %collective-permute-start.10 = (bf16[32,512]{1,0:T(8,128)(2,1)S(1)}, bf16[32,512]{1,0:T(8,128)(2,1)S(1)}, u32[]{:S(2)}, u32[]{:S(2)}) collective-permute-start(bf16[32,512]{1,0:T(8,128)(2,1)S(1)} %get-tuple-element.60), channel_id=1, source_target_pairs={{0,4},{1,5},{2,6},{3,7},{4,0},{5,1},{6,2},{7,3},{8,12},{9,13},{10,... | collective-permute-start | bytes 98312 | tf_op jit(solution)/shard_map/ppermute | solution.py:197
  9.2 1.6 %collective-permute-start.15 = (bf16[32,512]{1,0:T(8,128)(2,1)S(1)}, bf16[32,512]{1,0:T(8,128)(2,1)S(1)}, u32[]{:S(2)}, u32[]{:S(2)}) collective-permute-start(bf16[32,512]{1,0:T(8,128)(2,1)S(1)} %get-tuple-element.59), channel_id=1, source_target_pairs={{0,8},{1,9},{2,10},{3,11},{4,12},{5,13},{6,14},{7,15},{8,0},{9,1},... | collective-permute-start | bytes 98312 | tf_op jit(solution)/shard_map/ppermute | solution.py:197
  13.8 1.9 %fusion.15 = (f32[1024,64]{1,0:T(8,128)S(1)}, f32[1024,64]{1,0:T(8,128)S(1)}, f32[1024,64]{1,0:T(8,128)S(1)}) fusion(f32[64]{0:T(128)S(1)} %multiply_power_fusion, f32[1024]{0:T(1024)S(1)} %fusion.18), kind=kLoop, calls=%fused_computation.70 | loop fusion | flops 131072 | bytes 790784 | tf_op jit(solution)/shard_map/neg | solution.py:149
  19.9 2.7 %collective-permute-done.1 = bf16[64,512]{1,0:T(8,128)(2,1)S(1)} collective-permute-done((bf16[64,512]{1,0:T(8,128)(2,1)S(1)}, bf16[64,512]{1,0:T(8,128)(2,1)S(1)}, u32[]{:S(2)}, u32[]{:S(2)}) %collective-permute-start.1) | collective-permute-done | bytes 65568 | tf_op jit(solution)/shard_map/ppermute | solution.py:197
  24.6 1.6 %collective-permute-start.7 = (bf16[128,512]{1,0:T(8,128)(2,1)S(1)}, bf16[128,512]{1,0:T(8,128)(2,1)S(1)}, u32[]{:S(2)}, u32[]{:S(2)}) collective-permute-start(bf16[128,512]{1,0:T(8,128)(2,1)S(1)} %pad_maximum_fusion.16), channel_id=1, source_target_pairs={{0,8},{1,9},{2,10},{3,11},{4,12},{5,13},{6,14},{7,15},{8,0},{9,1},... | collective-permute-start | bytes 393224 | tf_op jit(solution)/shard_map/ppermute | solution.py:197
  31.1 1.6 %collective-permute-start.8 = (bf16[256,512]{1,0:T(8,128)(2,1)S(1)}, bf16[256,512]{1,0:T(8,128)(2,1)S(1)}, u32[]{:S(2)}, u32[]{:S(2)}) collective-permute-start(bf16[256,512]{1,0:T(8,128)(2,1)S(1)} %pad_maximum_fusion.12), channel_id=1, source_target_pairs={{0,4},{1,5},{2,6},{3,7},{4,0},{5,1},{6,2},{7,3},{8,12},{9,13},{10,... | collective-permute-start | bytes 786440 | tf_op jit(solution)/shard_map/ppermute | solution.py:197
  33.9 3.2 %collective-permute-start.18 = (bf16[256,512]{1,0:T(8,128)(2,1)S(1)}, bf16[256,512]{1,0:T(8,128)(2,1)S(1)}, u32[]{:S(2)}, u32[]{:S(2)}) collective-permute-start(bf16[256,512]{1,0:T(8,128)(2,1)S(1)} %pad_maximum_fusion.14), channel_id=1, source_target_pairs={{0,16},{1,17},{2,18},{3,19},{4,20},{5,21},{6,22},{7,23},{8,24},{9,... | collective-permute-start | bytes 786440 | tf_op jit(solution)/shard_map/ppermute | solution.py:197
  38.0 5.5 %collective-permute-done.13 = bf16[256,512]{1,0:T(8,128)(2,1)S(1)} collective-permute-done((bf16[256,512]{1,0:T(8,128)(2,1)S(1)}, bf16[256,512]{1,0:T(8,128)(2,1)S(1)}, u32[]{:S(2)}, u32[]{:S(2)}) %collective-permute-start.13) | collective-permute-done | bytes 262176 | tf_op jit(solution)/shard_map/ppermute | solution.py:197
  48.2 1.9 %copy-done.1 = bf16[1024,2048]{1,0:T(8,128)(2,1)} copy-done((bf16[1024,2048]{1,0:T(8,128)(2,1)}, bf16[1024,2048]{1,0:T(8,128)(2,1)S(1)}, u32[]{:S(2)}) %copy-start.1) | copy-done | bytes 4194328
  51.5 3.6 %fusion.26 = f32[1024,128]{1,0:T(8,128)S(1)} fusion(bf16[1024,2048]{1,0:T(8,128)(2,1)} %copy-done.1, bf16[2048,128]{1,0:T(8,128)(2,1)S(1)} %copy-done.4), kind=kOutput, calls=%fused_computation.153 | convolution fusion | flops 536870912 | bytes 5242880 | tf_op jit(solution)/shard_map/dot_general | solution.py:58
  55.1 2.4 %fusion.6 = (bf16[1024,64]{1,0:T(8,128)(2,1)S(1)}, bf16[1024,64]{1,0:T(8,128)(2,1)S(1)}) fusion(f32[1024,1,128]{2,0,1:T(8,128)S(1)} %bitcast.61, f32[64]{0:T(128)S(1)} %multiply_power_fusion, f32[1024]{0:T(1024)S(1)} %fusion.18), kind=kLoop, calls=%fused_computation.21 | loop fusion | flops 589824 | bytes 790784 | tf_op jit(solution)/shard_map/concatenate | solution.py:52
  57.9 3.7 %fusion.25.refs_0_ = f32[1024,512]{1,0:T(8,128)} fusion(bf16[1024,2048]{1,0:T(8,128)(2,1)S(1)} %copy-done.2, bf16[2048,512]{1,0:T(8,128)(2,1)S(1)} %copy-done.10), kind=kOutput, calls=%fused_computation.152 | convolution fusion | flops 2147483648 | bytes 8388608 | tf_op jit(solution)/shard_map/dot_general | solution.py:235
  63.5 17.1 %shard_map.113 = bf16[1024,512]{1,0:T(8,128)(2,1)} custom-call(f32[1024,512]{1,0:T(8,128)} %fusion.25.refs_0_, f32[1024,128]{1,0:T(8,128)} %get-tuple-element.75.refs_1_, f32[1024,128]{1,0:T(8,128)} %get-tuple-element.76.refs_2_, bf16[1024,128]{1,0:T(8,128)(2,1)} %get-tuple-element.25.refs_3_, bf16[1024,128]{1,0:T(8,128)(2,1)} %get-tuple-element.24.refs_4_, ...), custom_call_target="tpu_custom_call" | custom-call | flops 1342177280 | bytes 4718592 | tf_op jit(solution)/shard_map/pallas_call | solution.py:161
  80.6 3.6 %convolution_convert_fusion = bf16[1024,2048]{1,0:T(8,128)(2,1)S(1)} fusion(bf16[1024,512]{1,0:T(8,128)(2,1)} %shard_map.113, bf16[512,2048]{1,0:T(8,128)(2,1)S(1)} %copy-done), kind=kOutput, calls=%fused_computation.1 | convolution fusion | flops 2149580800 | bytes 7340032 | tf_op jit(solution)/shard_map/dot_general | solution.py:239
  89.2 1.5 %collective-permute-start.27 = (bf16[256,512]{1,0:T(8,128)(2,1)S(1)}, bf16[256,512]{1,0:T(8,128)(2,1)S(1)}, u32[]{:S(2)}, u32[]{:S(2)}) collective-permute-start(bf16[256,512]{1,0:T(8,128)(2,1)S(1)} %constant_dynamic-slice_fusion.13), channel_id=1, source_target_pairs={{0,4},{1,5},{2,6},{3,7},{4,0},{5,1},{6,2},{7,3},{8,12},{9,13},{10,... | collective-permute-start | bytes 786440 | tf_op jit(solution)/shard_map/ppermute | solution.py:103
  91.2 2.1 %collective-permute-start.37 = (bf16[256,512]{1,0:T(8,128)(2,1)S(1)}, bf16[256,512]{1,0:T(8,128)(2,1)S(1)}, u32[]{:S(2)}, u32[]{:S(2)}) collective-permute-start(bf16[256,512]{1,0:T(8,128)(2,1)S(1)} %constant_dynamic-slice_fusion.3), channel_id=1, source_target_pairs={{0,16},{1,17},{2,18},{3,19},{4,20},{5,21},{6,22},{7,23},{8,24},{9,... | collective-permute-start | bytes 786440 | tf_op jit(solution)/shard_map/ppermute | solution.py:103
  93.3 3.5 %collective-permute-done.22 = bf16[256,512]{1,0:T(8,128)(2,1)S(1)} collective-permute-done((bf16[256,512]{1,0:T(8,128)(2,1)S(1)}, bf16[256,512]{1,0:T(8,128)(2,1)S(1)}, u32[]{:S(2)}, u32[]{:S(2)}) %collective-permute-start.22) | collective-permute-done | bytes 262176 | tf_op jit(solution)/shard_map/ppermute | solution.py:103
  96.9 1.6 %collective-permute-start.23 = (bf16[128,512]{1,0:T(8,128)(2,1)S(1)}, bf16[128,512]{1,0:T(8,128)(2,1)S(1)}, u32[]{:S(2)}, u32[]{:S(2)}) collective-permute-start(bf16[128,512]{1,0:T(8,128)(2,1)S(1)} %constant_dynamic-slice_fusion.17), channel_id=1, source_target_pairs={{0,4},{1,5},{2,6},{3,7},{4,0},{5,1},{6,2},{7,3},{8,12},{9,13},{10,... | collective-permute-start | bytes 393224 | tf_op jit(solution)/shard_map/ppermute | solution.py:103
  98.6 6.4 %collective-permute-done.32 = bf16[256,512]{1,0:T(8,128)(2,1)S(1)} collective-permute-done((bf16[256,512]{1,0:T(8,128)(2,1)S(1)}, bf16[256,512]{1,0:T(8,128)(2,1)S(1)}, u32[]{:S(2)}, u32[]{:S(2)}) %collective-permute-start.32) | collective-permute-done | bytes 262176 | tf_op jit(solution)/shard_map/ppermute | solution.py:103
  107.6 2.0 %collective-permute-start.24 = (bf16[64,512]{1,0:T(8,128)(2,1)S(1)}, bf16[64,512]{1,0:T(8,128)(2,1)S(1)}, u32[]{:S(2)}, u32[]{:S(2)}) collective-permute-start(bf16[64,512]{1,0:T(8,128)(2,1)S(1)} %constant_dynamic-slice_fusion.16), channel_id=1, source_target_pairs={{0,8},{1,9},{2,10},{3,11},{4,12},{5,13},{6,14},{7,15},{8,0},{9,1},... | collective-permute-start | bytes 196616 | tf_op jit(solution)/shard_map/ppermute | solution.py:103
  110.6 2.8 %collective-permute-done.33 = bf16[128,512]{1,0:T(8,128)(2,1)S(1)} collective-permute-done((bf16[128,512]{1,0:T(8,128)(2,1)S(1)}, bf16[128,512]{1,0:T(8,128)(2,1)S(1)}, u32[]{:S(2)}, u32[]{:S(2)}) %collective-permute-start.33) | collective-permute-done | bytes 131104 | tf_op jit(solution)/shard_map/ppermute | solution.py:103
  113.4 2.5 %collective-permute-start.34 = (bf16[64,512]{1,0:T(8,128)(2,1)S(1)}, bf16[64,512]{1,0:T(8,128)(2,1)S(1)}, u32[]{:S(2)}, u32[]{:S(2)}) collective-permute-start(bf16[64,512]{1,0:T(8,128)(2,1)S(1)} %constant_dynamic-slice_fusion.6), channel_id=1, source_target_pairs={{0,2},{1,3},{2,0},{3,1},{4,6},{5,7},{6,4},{7,5},{8,10},{9,11},{10,... | collective-permute-start | bytes 196616 | tf_op jit(solution)/shard_map/ppermute | solution.py:103
  122.2 2.1 %collective-permute-done.40 = bf16[32,512]{1,0:T(8,128)(2,1)S(1)} collective-permute-done((bf16[32,512]{1,0:T(8,128)(2,1)S(1)}, bf16[32,512]{1,0:T(8,128)(2,1)S(1)}, u32[]{:S(2)}, u32[]{:S(2)}) %collective-permute-start.40) | collective-permute-done | bytes 32800 | tf_op jit(solution)/shard_map/ppermute | solution.py:103
  (200 shorter events, 43.0 us)
Async XLA Ops:
  3.6 14.6 %collective-permute-start = (bf16[32,512]{1,0:T(8,128)(2,1)S(1)}, bf16[32,512]{1,0:T(8,128)(2,1)S(1)}, u32[]{:S(2)}, u32[]{:S(2)}) collective-permute-start(bf16[32,512]{1,0:T(8,128)(2,1)S(1)} %get-tuple-element.58), channel_id=1, source_target_pairs={{0,16},{1,17},{2,18},{3,19},{4,20},{5,21},{6,22},{7,23},{8,24},{9,... | collective-permute-start | bytes 98312 | tf_op jit(solution)/shard_map/ppermute | solution.py:197
  7.7 10.5 %collective-permute-start.10 = (bf16[32,512]{1,0:T(8,128)(2,1)S(1)}, bf16[32,512]{1,0:T(8,128)(2,1)S(1)}, u32[]{:S(2)}, u32[]{:S(2)}) collective-permute-start(bf16[32,512]{1,0:T(8,128)(2,1)S(1)} %get-tuple-element.60), channel_id=1, source_target_pairs={{0,4},{1,5},{2,6},{3,7},{4,0},{5,1},{6,2},{7,3},{8,12},{9,13},{10,... | collective-permute-start | bytes 98312 | tf_op jit(solution)/shard_map/ppermute | solution.py:197
  9.2 9.0 %collective-permute-start.15 = (bf16[32,512]{1,0:T(8,128)(2,1)S(1)}, bf16[32,512]{1,0:T(8,128)(2,1)S(1)}, u32[]{:S(2)}, u32[]{:S(2)}) collective-permute-start(bf16[32,512]{1,0:T(8,128)(2,1)S(1)} %get-tuple-element.59), channel_id=1, source_target_pairs={{0,8},{1,9},{2,10},{3,11},{4,12},{5,13},{6,14},{7,15},{8,0},{9,1},... | collective-permute-start | bytes 98312 | tf_op jit(solution)/shard_map/ppermute | solution.py:197
  10.8 7.4 %collective-permute-start.5 = (bf16[32,512]{1,0:T(8,128)(2,1)S(1)}, bf16[32,512]{1,0:T(8,128)(2,1)S(1)}, u32[]{:S(2)}, u32[]{:S(2)}) collective-permute-start(bf16[32,512]{1,0:T(8,128)(2,1)S(1)} %get-tuple-element.61), channel_id=1, source_target_pairs={{0,2},{1,3},{2,0},{3,1},{4,6},{5,7},{6,4},{7,5},{8,10},{9,11},{10,... | collective-permute-start | bytes 98312 | tf_op jit(solution)/shard_map/ppermute | solution.py:197
  19.1 7.1 %collective-permute-start.11 = (bf16[64,512]{1,0:T(8,128)(2,1)S(1)}, bf16[64,512]{1,0:T(8,128)(2,1)S(1)}, u32[]{:S(2)}, u32[]{:S(2)}) collective-permute-start(bf16[64,512]{1,0:T(8,128)(2,1)S(1)} %pad_maximum_fusion.21), channel_id=1, source_target_pairs={{0,2},{1,3},{2,0},{3,1},{4,6},{5,7},{6,4},{7,5},{8,10},{9,11},{10,... | collective-permute-start | bytes 196616 | tf_op jit(solution)/shard_map/ppermute | solution.py:197
  19.7 6.6 %collective-permute-start.16 = (bf16[64,512]{1,0:T(8,128)(2,1)S(1)}, bf16[64,512]{1,0:T(8,128)(2,1)S(1)}, u32[]{:S(2)}, u32[]{:S(2)}) collective-permute-start(bf16[64,512]{1,0:T(8,128)(2,1)S(1)} %pad_maximum_fusion.22), channel_id=1, source_target_pairs={{0,4},{1,5},{2,6},{3,7},{4,0},{5,1},{6,2},{7,3},{8,12},{9,13},{10,... | collective-permute-start | bytes 196616 | tf_op jit(solution)/shard_map/ppermute | solution.py:197
  26.3 7.3 %collective-permute-start.12 = (bf16[128,512]{1,0:T(8,128)(2,1)S(1)}, bf16[128,512]{1,0:T(8,128)(2,1)S(1)}, u32[]{:S(2)}, u32[]{:S(2)}) collective-permute-start(bf16[128,512]{1,0:T(8,128)(2,1)S(1)} %pad_maximum_fusion.17), channel_id=1, source_target_pairs={{0,16},{1,17},{2,18},{3,19},{4,20},{5,21},{6,22},{7,23},{8,24},{9,... | collective-permute-start | bytes 393224 | tf_op jit(solution)/shard_map/ppermute | solution.py:197
  27.5 6.4 %collective-permute-start.17 = (bf16[128,512]{1,0:T(8,128)(2,1)S(1)}, bf16[128,512]{1,0:T(8,128)(2,1)S(1)}, u32[]{:S(2)}, u32[]{:S(2)}) collective-permute-start(bf16[128,512]{1,0:T(8,128)(2,1)S(1)} %pad_maximum_fusion.18), channel_id=1, source_target_pairs={{0,2},{1,3},{2,0},{3,1},{4,6},{5,7},{6,4},{7,5},{8,10},{9,11},{10,... | collective-permute-start | bytes 393224 | tf_op jit(solution)/shard_map/ppermute | solution.py:197
  29.2 7.9 %collective-permute-start.3 = (bf16[256,512]{1,0:T(8,128)(2,1)S(1)}, bf16[256,512]{1,0:T(8,128)(2,1)S(1)}, u32[]{:S(2)}, u32[]{:S(2)}) collective-permute-start(bf16[256,512]{1,0:T(8,128)(2,1)S(1)} %pad_maximum_fusion.11), channel_id=1, source_target_pairs={{0,2},{1,3},{2,0},{3,1},{4,6},{5,7},{6,4},{7,5},{8,10},{9,11},{10,... | collective-permute-start | bytes 786440 | tf_op jit(solution)/shard_map/ppermute | solution.py:197
  31.1 6.4 %collective-permute-start.8 = (bf16[256,512]{1,0:T(8,128)(2,1)S(1)}, bf16[256,512]{1,0:T(8,128)(2,1)S(1)}, u32[]{:S(2)}, u32[]{:S(2)}) collective-permute-start(bf16[256,512]{1,0:T(8,128)(2,1)S(1)} %pad_maximum_fusion.12), channel_id=1, source_target_pairs={{0,4},{1,5},{2,6},{3,7},{4,0},{5,1},{6,2},{7,3},{8,12},{9,13},{10,... | collective-permute-start | bytes 786440 | tf_op jit(solution)/shard_map/ppermute | solution.py:197
  33.7 9.8 %collective-permute-start.13 = (bf16[256,512]{1,0:T(8,128)(2,1)S(1)}, bf16[256,512]{1,0:T(8,128)(2,1)S(1)}, u32[]{:S(2)}, u32[]{:S(2)}) collective-permute-start(bf16[256,512]{1,0:T(8,128)(2,1)S(1)} %pad_maximum_fusion.13), channel_id=1, source_target_pairs={{0,8},{1,9},{2,10},{3,11},{4,12},{5,13},{6,14},{7,15},{8,0},{9,1},... | collective-permute-start | bytes 786440 | tf_op jit(solution)/shard_map/ppermute | solution.py:197
  33.9 11.0 %collective-permute-start.18 = (bf16[256,512]{1,0:T(8,128)(2,1)S(1)}, bf16[256,512]{1,0:T(8,128)(2,1)S(1)}, u32[]{:S(2)}, u32[]{:S(2)}) collective-permute-start(bf16[256,512]{1,0:T(8,128)(2,1)S(1)} %pad_maximum_fusion.14), channel_id=1, source_target_pairs={{0,16},{1,17},{2,18},{3,19},{4,20},{5,21},{6,22},{7,23},{8,24},{9,... | collective-permute-start | bytes 786440 | tf_op jit(solution)/shard_map/ppermute | solution.py:197
  37.2 7.9 %collective-permute-start.4 = (bf16[512,512]{1,0:T(8,128)(2,1)S(1)}, bf16[512,512]{1,0:T(8,128)(2,1)S(1)}, u32[]{:S(2)}, u32[]{:S(2)}) collective-permute-start(bf16[512,512]{1,0:T(8,128)(2,1)S(1)} %pad_maximum_fusion.5), channel_id=1, source_target_pairs={{0,1},{1,0},{2,3},{3,2},{4,5},{5,4},{6,7},{7,6},{8,9},{9,8},{10,11... | collective-permute-start | bytes 1572872 | tf_op jit(solution)/shard_map/ppermute | solution.py:197
  37.6 7.8 %collective-permute-start.9 = (bf16[512,512]{1,0:T(8,128)(2,1)S(1)}, bf16[512,512]{1,0:T(8,128)(2,1)S(1)}, u32[]{:S(2)}, u32[]{:S(2)}) collective-permute-start(bf16[512,512]{1,0:T(8,128)(2,1)S(1)} %pad_maximum_fusion.6), channel_id=1, source_target_pairs={{0,1},{1,0},{2,3},{3,2},{4,5},{5,4},{6,7},{7,6},{8,9},{9,8},{10,11... | collective-permute-start | bytes 1572872 | tf_op jit(solution)/shard_map/ppermute | solution.py:197
  88.3 8.4 %collective-permute-start.22 = (bf16[256,512]{1,0:T(8,128)(2,1)S(1)}, bf16[256,512]{1,0:T(8,128)(2,1)S(1)}, u32[]{:S(2)}, u32[]{:S(2)}) collective-permute-start(bf16[256,512]{1,0:T(8,128)(2,1)S(1)} %constant_dynamic-slice_fusion.18), channel_id=1, source_target_pairs={{0,2},{1,3},{2,0},{3,1},{4,6},{5,7},{6,4},{7,5},{8,10},{9,11},{10,... | collective-permute-start | bytes 786440 | tf_op jit(solution)/shard_map/ppermute | solution.py:103
  89.2 9.3 %collective-permute-start.27 = (bf16[256,512]{1,0:T(8,128)(2,1)S(1)}, bf16[256,512]{1,0:T(8,128)(2,1)S(1)}, u32[]{:S(2)}, u32[]{:S(2)}) collective-permute-start(bf16[256,512]{1,0:T(8,128)(2,1)S(1)} %constant_dynamic-slice_fusion.13), channel_id=1, source_target_pairs={{0,4},{1,5},{2,6},{3,7},{4,0},{5,1},{6,2},{7,3},{8,12},{9,13},{10,... | collective-permute-start | bytes 786440 | tf_op jit(solution)/shard_map/ppermute | solution.py:103
  90.9 14.2 %collective-permute-start.32 = (bf16[256,512]{1,0:T(8,128)(2,1)S(1)}, bf16[256,512]{1,0:T(8,128)(2,1)S(1)}, u32[]{:S(2)}, u32[]{:S(2)}) collective-permute-start(bf16[256,512]{1,0:T(8,128)(2,1)S(1)} %constant_dynamic-slice_fusion.8), channel_id=1, source_target_pairs={{0,8},{1,9},{2,10},{3,11},{4,12},{5,13},{6,14},{7,15},{8,0},{9,1},... | collective-permute-start | bytes 786440 | tf_op jit(solution)/shard_map/ppermute | solution.py:103
  91.2 14.9 %collective-permute-start.37 = (bf16[256,512]{1,0:T(8,128)(2,1)S(1)}, bf16[256,512]{1,0:T(8,128)(2,1)S(1)}, u32[]{:S(2)}, u32[]{:S(2)}) collective-permute-start(bf16[256,512]{1,0:T(8,128)(2,1)S(1)} %constant_dynamic-slice_fusion.3), channel_id=1, source_target_pairs={{0,16},{1,17},{2,18},{3,19},{4,20},{5,21},{6,22},{7,23},{8,24},{9,... | collective-permute-start | bytes 786440 | tf_op jit(solution)/shard_map/ppermute | solution.py:103
  96.9 10.7 %collective-permute-start.23 = (bf16[128,512]{1,0:T(8,128)(2,1)S(1)}, bf16[128,512]{1,0:T(8,128)(2,1)S(1)}, u32[]{:S(2)}, u32[]{:S(2)}) collective-permute-start(bf16[128,512]{1,0:T(8,128)(2,1)S(1)} %constant_dynamic-slice_fusion.17), channel_id=1, source_target_pairs={{0,4},{1,5},{2,6},{3,7},{4,0},{5,1},{6,2},{7,3},{8,12},{9,13},{10,... | collective-permute-start | bytes 393224 | tf_op jit(solution)/shard_map/ppermute | solution.py:103
  98.6 11.1 %collective-permute-start.28 = (bf16[128,512]{1,0:T(8,128)(2,1)S(1)}, bf16[128,512]{1,0:T(8,128)(2,1)S(1)}, u32[]{:S(2)}, u32[]{:S(2)}) collective-permute-start(bf16[128,512]{1,0:T(8,128)(2,1)S(1)} %constant_dynamic-slice_fusion.12), channel_id=1, source_target_pairs={{0,8},{1,9},{2,10},{3,11},{4,12},{5,13},{6,14},{7,15},{8,0},{9,1},... | collective-permute-start | bytes 393224 | tf_op jit(solution)/shard_map/ppermute | solution.py:103
  105.2 8.2 %collective-permute-start.33 = (bf16[128,512]{1,0:T(8,128)(2,1)S(1)}, bf16[128,512]{1,0:T(8,128)(2,1)S(1)}, u32[]{:S(2)}, u32[]{:S(2)}) collective-permute-start(bf16[128,512]{1,0:T(8,128)(2,1)S(1)} %constant_dynamic-slice_fusion.7), channel_id=1, source_target_pairs={{0,16},{1,17},{2,18},{3,19},{4,20},{5,21},{6,22},{7,23},{8,24},{9,... | collective-permute-start | bytes 393224 | tf_op jit(solution)/shard_map/ppermute | solution.py:103
  106.2 9.8 %collective-permute-start.38 = (bf16[128,512]{1,0:T(8,128)(2,1)S(1)}, bf16[128,512]{1,0:T(8,128)(2,1)S(1)}, u32[]{:S(2)}, u32[]{:S(2)}) collective-permute-start(bf16[128,512]{1,0:T(8,128)(2,1)S(1)} %constant_dynamic-slice_fusion.2), channel_id=1, source_target_pairs={{0,2},{1,3},{2,0},{3,1},{4,6},{5,7},{6,4},{7,5},{8,10},{9,11},{10,... | collective-permute-start | bytes 393224 | tf_op jit(solution)/shard_map/ppermute | solution.py:103
  107.6 8.4 %collective-permute-start.24 = (bf16[64,512]{1,0:T(8,128)(2,1)S(1)}, bf16[64,512]{1,0:T(8,128)(2,1)S(1)}, u32[]{:S(2)}, u32[]{:S(2)}) collective-permute-start(bf16[64,512]{1,0:T(8,128)(2,1)S(1)} %constant_dynamic-slice_fusion.16), channel_id=1, source_target_pairs={{0,8},{1,9},{2,10},{3,11},{4,12},{5,13},{6,14},{7,15},{8,0},{9,1},... | collective-permute-start | bytes 196616 | tf_op jit(solution)/shard_map/ppermute | solution.py:103
  109.7 6.5 %collective-permute-start.29 = (bf16[64,512]{1,0:T(8,128)(2,1)S(1)}, bf16[64,512]{1,0:T(8,128)(2,1)S(1)}, u32[]{:S(2)}, u32[]{:S(2)}) collective-permute-start(bf16[64,512]{1,0:T(8,128)(2,1)S(1)} %constant_dynamic-slice_fusion.11), channel_id=1, source_target_pairs={{0,16},{1,17},{2,18},{3,19},{4,20},{5,21},{6,22},{7,23},{8,24},{9,... | collective-permute-start | bytes 196616 | tf_op jit(solution)/shard_map/ppermute | solution.py:103
  (28 other events, 236.8 us)

commit v5 on v4

--- a/solution.py
+++ b/solution.py
@@ -75,26 +75,32 @@
 
 def bit_orders(bits, parts):
     rest = list(range(1, bits))
-    if not rest:
-        return [[0]] * parts
-    return [[0] + rest[j % len(rest):] + rest[:j % len(rest)] for j in range(parts)]
+    return [rest[j % len(rest):] + rest[:j % len(rest)] for j in range(parts)]
 
 
 def reduce_to_owner(partial, axis):
     size = lax.axis_size(axis)
     bits = size.bit_length() - 1
-    assert 1 << bits == size
+    assert 1 << bits == size and bits >= 1
     me = lax.axis_index(axis)
     rows, width = partial.shape
     block = rows // size
+    low = me & 1
+    paired = partial.reshape(size // 2, 2, block, width)
+    keep = lax.dynamic_index_in_dim(paired, low, 1, keepdims=False)
+    send = lax.dynamic_index_in_dim(paired, 1 - low, 1, keepdims=False)
+    got = lax.ppermute(send, axis, [(i, i ^ 1) for i in range(size)])
+    halved = (keep.astype(jnp.float32) + got.astype(jnp.float32)).astype(jnp.bfloat16)
+    if bits == 1:
+        return halved.reshape(block, width)
     parts = REDUCE_PARTS if width % REDUCE_PARTS == 0 else 1
     piece = width // parts
     outs = []
     for j, order in enumerate(bit_orders(bits, parts)):
-        cols = partial[:, j * piece:(j + 1) * piece]
-        cube = cols.reshape((2,) * bits + (block, piece))
-        cube = jnp.transpose(cube, [bits - 1 - k for k in order] + [bits, bits + 1])
-        current = cube.reshape(rows, piece)
+        cols = halved[:, :, j * piece:(j + 1) * piece]
+        cube = cols.reshape((2,) * (bits - 1) + (block, piece))
+        cube = jnp.transpose(cube, [bits - 1 - k for k in order] + [bits - 1, bits])
+        current = cube.reshape(rows // 2, piece)
         for k in order:
             half = current.shape[0] // 2
             mine = (me >> k) & 1
@@ -184,26 +190,34 @@
 def gather_from_all(block, axis):
     size = lax.axis_size(axis)
     bits = size.bit_length() - 1
-    assert 1 << bits == size
+    assert 1 << bits == size and bits >= 1
     me = lax.axis_index(axis)
     rows, width = block.shape
-    parts = REDUCE_PARTS if width % REDUCE_PARTS == 0 else 1
-    piece = width // parts
-    outs = []
-    for j, forward in enumerate(bit_orders(bits, parts)):
-        order = forward[::-1]
-        current = block[:, j * piece:(j + 1) * piece]
-        for k in order:
-            got = lax.ppermute(current, axis, [(i, i ^ (1 << k)) for i in range(size)])
-            upper = ((me >> k) & 1) == 1
-            current = jnp.concatenate(
-                [jnp.where(upper, got, current), jnp.where(upper, current, got)], axis=0
+    if bits > 1:
+        parts = REDUCE_PARTS if width % REDUCE_PARTS == 0 else 1
+        piece = width // parts
+        outs = []
+        for j, forward in enumerate(bit_orders(bits, parts)):
+            order = forward[::-1]
+            current = block[:, j * piece:(j + 1) * piece]
+            for k in order:
+                got = lax.ppermute(current, axis, [(i, i ^ (1 << k)) for i in range(size)])
+                upper = ((me >> k) & 1) == 1
+                current = jnp.concatenate(
+                    [jnp.where(upper, got, current), jnp.where(upper, current, got)], axis=0
+                )
+            cube = current.reshape((2,) * (bits - 1) + (rows, piece))
+            old_axis = {order[bits - 2 - a]: a for a in range(bits - 1)}
+            cube = jnp.transpose(
+                cube, [old_axis[bits - 1 - a] for a in range(bits - 1)] + [bits - 1, bits]
             )
-        cube = current.reshape((2,) * bits + (rows, piece))
-        old_axis = {order[bits - 1 - a]: a for a in range(bits)}
-        cube = jnp.transpose(cube, [old_axis[bits - 1 - a] for a in range(bits)] + [bits, bits + 1])
-        outs.append(cube.reshape(size * rows, piece))
-    return jnp.concatenate(outs, axis=1)
+            outs.append(cube.reshape(size // 2 * rows, piece))
+        block = jnp.concatenate(outs, axis=1)
+    got = lax.ppermute(block, axis, [(i, i ^ 1) for i in range(size)])
+    upper = (me & 1) == 1
+    lower_rows = jnp.where(upper, got, block).reshape(size // 2, 1, rows, width)
+    upper_rows = jnp.where(upper, block, got).reshape(size // 2, 1, rows, width)
+    return jnp.concatenate([lower_rows, upper_rows], axis=1).reshape(size * rows, width)
 
 
 def local(

time: 125 us -> 137 us (1.096)
  waiting for transfers between devices: 34 us -> 44.4 us
  other arithmetic: 15.8 us -> 19.9 us
  starting transfers between devices: 37.3 us -> 33.6 us
    ppermute x20 -> x16, waiting for transfers between devices: 14.7 us -> 22.5 us  [gather_from_all(): got = lax.ppermute(current, axis, [(i, i ^ 1 << k) for i in range(size)])]
    ppermute x0 -> x2, waiting for transfers between devices: none -> 2.84 us  [the longest x1 2.84 us: reduce_to_owner(): got = lax.ppermute(send, axis, [(i, i ^ 1) for i in range(size)])]
    convert_element_type x20 -> x17, other arithmetic: 1.14 us -> 3.6 us  [reduce_to_owner(): (keep.astype(jnp.float32) + got.astype(jnp.float32)).astype(jnp.bfloat16)]
    select_n x0 -> x1, other arithmetic: none -> 2.35 us  [gather_from_all(): lower_rows = jnp.where(upper, got, block).reshape(size // 2, 1, rows, width)]
    ppermute x20 -> x16, starting transfers between devices: 16.6 us -> 14.3 us  [reduce_to_owner(): got = lax.ppermute(send, axis, [(i, i ^ 1 << k) for i in range(size)])]
    ppermute x20 -> x16, starting transfers between devices: 20.5 us -> 18.7 us  [gather_from_all(): got = lax.ppermute(current, axis, [(i, i ^ 1 << k) for i in range(size)])]
    squeeze x0 -> x1, local copies, waits for them, and re-layouts: none -> 1.55 us  [reduce_to_owner(): send = lax.dynamic_index_in_dim(paired, 1 - low, 1, keepdims=False)]
    ppermute x20 -> x16, waiting for transfers between devices: 19.3 us -> 19 us  [reduce_to_owner(): got = lax.ppermute(send, axis, [(i, i ^ 1 << k) for i in range(size)])]
  transfers between devices with their start and end apart: 41 -> 35, of which waited for: 18 -> 18; matrix products, arithmetic and copies ran while one was open for 13% -> 10% of each run, Pallas kernels for 0% -> 0%
where the time goes in v5:
time: 137 us
  waiting for transfers between devices  44.4 us (32%)
  starting transfers between devices  33.6 us (25%)
  other arithmetic  19.9 us (15%)
  Pallas kernels  17.1 us (12%)
  matrix products  12.6 us (9%)
  local copies, waits for them, and re-layouts  7.52 us (5%)
  between operations  1.48 us (1%)
    ppermute x16, waiting for transfers between devices, gather_from_all(): got = lax.ppermute(current, axis, [(i, i ^ 1 << k) for i in range(size)])  22.5 us
    ppermute x16, waiting for transfers between devices, reduce_to_owner(): got = lax.ppermute(send, axis, [(i, i ^ 1 << k) for i in range(size)])  19 us
    ppermute x16, starting transfers between devices, gather_from_all(): got = lax.ppermute(current, axis, [(i, i ^ 1 << k) for i in range(size)])  18.7 us
    pallas_call x1, Pallas kernels, attend_window(): pl.pallas_call(lambda *refs: attention_kernel(window, *refs), grid=(block...  17.1 us
    ppermute x16, starting transfers between devices, reduce_to_owner(): got = lax.ppermute(send, axis, [(i, i ^ 1 << k) for i in range(size)])  14.3 us
    unnamed x34, local copies, waits for them, and re-layouts  3.86 us
    dot_general x1, matrix products, local(): jnp.dot(normed, query_weight, preferred_element_type=jnp.float32)  3.69 us
    convert_element_type x17, other arithmetic, reduce_to_owner(): (keep.astype(jnp.float32) + got.astype(jnp.float32)).astype(jnp.bfloat16)  3.6 us
  transfers between devices with their start and end apart: 35, of which 18 were waited for; matrix products, arithmetic and copies ran while one was open for 10% of the time, Pallas kernels for 0%

profile of v5, /device:TPU:0, one launch (start us, length us, event | category | flops | bytes accessed | tf_op | source)
XLA Modules:
  0.0 136.6 jit_solution(14770443377030944902)
XLA Ops:
  3.6 4.1 %collective-permute-start = (bf16[32,512]{1,0:T(8,128)(2,1)S(1)}, bf16[32,512]{1,0:T(8,128)(2,1)S(1)}, u32[]{:S(2)}, u32[]{:S(2)}) collective-permute-start(bf16[32,512]{1,0:T(8,128)(2,1)S(1)} %get-tuple-element.52), channel_id=1, source_target_pairs={{0,16},{1,17},{2,18},{3,19},{4,20},{5,21},{6,22},{7,23},{8,24},{9,... | collective-permute-start | bytes 98312 | tf_op jit(solution)/shard_map/ppermute | solution.py:204
  16.0 1.7 %collective-permute-start.13 = (bf16[64,512]{1,0:T(8,128)(2,1)S(1)}, bf16[64,512]{1,0:T(8,128)(2,1)S(1)}, u32[]{:S(2)}, u32[]{:S(2)}) collective-permute-start(bf16[64,512]{1,0:T(8,128)(2,1)S(1)} %pad_maximum_fusion.19), channel_id=1, source_target_pairs={{0,4},{1,5},{2,6},{3,7},{4,0},{5,1},{6,2},{7,3},{8,12},{9,13},{10,... | collective-permute-start | bytes 196616 | tf_op jit(solution)/shard_map/ppermute | solution.py:204
  22.1 2.3 %collective-permute-start.6 = (bf16[128,512]{1,0:T(8,128)(2,1)S(1)}, bf16[128,512]{1,0:T(8,128)(2,1)S(1)}, u32[]{:S(2)}, u32[]{:S(2)}) collective-permute-start(bf16[128,512]{1,0:T(8,128)(2,1)S(1)} %pad_maximum_fusion.13), channel_id=1, source_target_pairs={{0,8},{1,9},{2,10},{3,11},{4,12},{5,13},{6,14},{7,15},{8,0},{9,1},... | collective-permute-start | bytes 393224 | tf_op jit(solution)/shard_map/ppermute | solution.py:204
  28.2 7.3 %collective-permute-done.10 = bf16[128,512]{1,0:T(8,128)(2,1)S(1)} collective-permute-done((bf16[128,512]{1,0:T(8,128)(2,1)S(1)}, bf16[128,512]{1,0:T(8,128)(2,1)S(1)}, u32[]{:S(2)}, u32[]{:S(2)}) %collective-permute-start.10) | collective-permute-done | bytes 131104 | tf_op jit(solution)/shard_map/ppermute | solution.py:204
  36.2 7.3 %collective-permute-done.11 = bf16[256,512]{1,0:T(8,128)(2,1)S(1)} collective-permute-done((bf16[256,512]{1,0:T(8,128)(2,1)S(1)}, bf16[256,512]{1,0:T(8,128)(2,1)S(1)}, u32[]{:S(2)}, u32[]{:S(2)}) %collective-permute-start.11) | collective-permute-done | bytes 262176 | tf_op jit(solution)/shard_map/ppermute | solution.py:204
  43.7 2.2 %collective-permute-done.15 = bf16[256,512]{1,0:T(8,128)(2,1)S(1)} collective-permute-done((bf16[256,512]{1,0:T(8,128)(2,1)S(1)}, bf16[256,512]{1,0:T(8,128)(2,1)S(1)}, u32[]{:S(2)}, u32[]{:S(2)}) %collective-permute-start.15) | collective-permute-done | bytes 262176 | tf_op jit(solution)/shard_map/ppermute | solution.py:204
  49.6 1.9 %fusion.16 = (f32[1024,64]{1,0:T(8,128)S(1)}, f32[1024,64]{1,0:T(8,128)S(1)}, f32[1024,64]{1,0:T(8,128)S(1)}) fusion(f32[64]{0:T(128)S(1)} %multiply_power_fusion, f32[1024]{0:T(1024)S(1)} %fusion.19), kind=kLoop, calls=%fused_computation.60 | loop fusion | flops 131072 | bytes 790784 | tf_op jit(solution)/shard_map/neg | solution.py:155
  52.9 2.3 %broadcast_select_fusion.1 = (bf16[512,2048]{1,0:T(8,128)(2,1)S(1)}, bf16[512,2048]{1,0:T(8,128)(2,1)S(1)}) fusion(bf16[512,2048]{1,0:T(8,128)(2,1)} %collective-permute-done.16, pred[]{:T(512)S(6)} %eq.30, bf16[512,512]{1,0:T(8,128)(2,1)S(1)} %bitcast.87, bf16[512,512]{1,0:T(8,128)(2,1)S(1)} %bitcast.85, bf16[512,512]{1,0:T(8,128)(2,1)S(1)} %bitcast.83, ...), kind=kLoop, calls=%fused_computation.7 | loop fusion | flops 10485760 | bytes 8388609 | tf_op jit(solution)/shard_map/jit(_where)/select_n | solution.py:218
  57.8 3.6 %fusion.27 = f32[1024,128]{1,0:T(8,128)S(1)} fusion(bf16[1024,2048]{1,0:T(8,128)(2,1)} %bitcast.75, bf16[2048,128]{1,0:T(8,128)(2,1)S(1)} %copy-done.9), kind=kOutput, calls=%fused_computation.139 | convolution fusion | flops 536870912 | bytes 5242880 | tf_op jit(solution)/shard_map/dot_general | solution.py:58
  61.4 2.4 %fusion.7 = (bf16[1024,64]{1,0:T(8,128)(2,1)S(1)}, bf16[1024,64]{1,0:T(8,128)(2,1)S(1)}) fusion(f32[1024,1,128]{2,0,1:T(8,128)S(1)} %bitcast.77, f32[64]{0:T(128)S(1)} %multiply_power_fusion, f32[1024]{0:T(1024)S(1)} %fusion.19), kind=kLoop, calls=%fused_computation.19 | loop fusion | flops 589824 | bytes 790784 | tf_op jit(solution)/shard_map/concatenate | solution.py:52
  64.5 3.7 %fusion.26.refs_0_ = f32[1024,512]{1,0:T(8,128)} fusion(bf16[1024,2048]{1,0:T(8,128)(2,1)S(1)} %bitcast.76, bf16[2048,512]{1,0:T(8,128)(2,1)S(1)} %copy-done.15), kind=kOutput, calls=%fused_computation.138 | convolution fusion | flops 2147483648 | bytes 8388608 | tf_op jit(solution)/shard_map/dot_general | solution.py:249
  70.1 17.1 %shard_map.113 = bf16[1024,512]{1,0:T(8,128)(2,1)} custom-call(f32[1024,512]{1,0:T(8,128)} %fusion.26.refs_0_, f32[1024,128]{1,0:T(8,128)} %get-tuple-element.69.refs_1_, f32[1024,128]{1,0:T(8,128)} %get-tuple-element.70.refs_2_, bf16[1024,128]{1,0:T(8,128)(2,1)} %get-tuple-element.19.refs_3_, bf16[1024,128]{1,0:T(8,128)(2,1)} %get-tuple-element.18.refs_4_, ...), custom_call_target="tpu_custom_call" | custom-call | flops 1342177280 | bytes 4718592 | tf_op jit(solution)/shard_map/pallas_call | solution.py:167
  87.2 3.6 %convolution_convert_fusion = bf16[1024,2048]{1,0:T(8,128)(2,1)S(1)} fusion(bf16[1024,512]{1,0:T(8,128)(2,1)} %shard_map.113, bf16[512,2048]{1,0:T(8,128)(2,1)S(1)} %copy-done), kind=kOutput, calls=%fused_computation.3 | convolution fusion | flops 2149580800 | bytes 7340032 | tf_op jit(solution)/shard_map/dot_general | solution.py:253
  95.1 2.8 %collective-permute-done.18 = bf16[16,32,2048]{2,1,0:T(8,128)(2,1)} collective-permute-done((bf16[16,32,2048]{2,1,0:T(8,128)(2,1)}, bf16[16,32,2048]{2,1,0:T(8,128)(2,1)}, u32[]{:S(2)}, u32[]{:S(2)}) %collective-permute-start.18) | collective-permute-done | bytes 2097184 | tf_op jit(solution)/shard_map/ppermute | solution.py:92
  97.9 3.0 %fusion = bf16[16,32,2048]{2,1,0:T(8,128)(2,1)S(1)} fusion(bf16[16,32,2048]{2,1,0:T(8,128)(2,1)} %collective-permute-done.18, bf16[16,2,32,2048]{3,2,1,0:T(8,128)(2,1)} %bitcast.89, s32[]{:T(128)S(6)} %select_n.399), kind=kLoop, calls=%fused_computation.2 | loop fusion | flops 4194304 | bytes 6291460 | tf_op jit(solution)/shard_map/convert_element_type | solution.py:93
  102.3 2.0 %collective-permute-start.31 = (bf16[256,512]{1,0:T(8,128)(2,1)S(1)}, bf16[256,512]{1,0:T(8,128)(2,1)S(1)}, u32[]{:S(2)}, u32[]{:S(2)}) collective-permute-start(bf16[256,512]{1,0:T(8,128)(2,1)S(1)} %constant_dynamic-slice_fusion.3), channel_id=1, source_target_pairs={{0,16},{1,17},{2,18},{3,19},{4,20},{5,21},{6,22},{7,23},{8,24},{9,... | collective-permute-start | bytes 786440 | tf_op jit(solution)/shard_map/ppermute | solution.py:109
  104.3 5.4 %collective-permute-done.19 = bf16[256,512]{1,0:T(8,128)(2,1)S(1)} collective-permute-done((bf16[256,512]{1,0:T(8,128)(2,1)S(1)}, bf16[256,512]{1,0:T(8,128)(2,1)S(1)}, u32[]{:S(2)}, u32[]{:S(2)}) %collective-permute-start.19) | collective-permute-done | bytes 262176 | tf_op jit(solution)/shard_map/ppermute | solution.py:109
  110.3 6.1 %collective-permute-done.27 = bf16[256,512]{1,0:T(8,128)(2,1)S(1)} collective-permute-done((bf16[256,512]{1,0:T(8,128)(2,1)S(1)}, bf16[256,512]{1,0:T(8,128)(2,1)S(1)}, u32[]{:S(2)}, u32[]{:S(2)}) %collective-permute-start.27) | collective-permute-done | bytes 262176 | tf_op jit(solution)/shard_map/ppermute | solution.py:109
  118.8 2.1 %collective-permute-start.21 = (bf16[64,512]{1,0:T(8,128)(2,1)S(1)}, bf16[64,512]{1,0:T(8,128)(2,1)S(1)}, u32[]{:S(2)}, u32[]{:S(2)}) collective-permute-start(bf16[64,512]{1,0:T(8,128)(2,1)S(1)} %constant_dynamic-slice_fusion.13), channel_id=1, source_target_pairs={{0,8},{1,9},{2,10},{3,11},{4,12},{5,13},{6,14},{7,15},{8,0},{9,1},... | collective-permute-start | bytes 196616 | tf_op jit(solution)/shard_map/ppermute | solution.py:109
  121.4 3.4 %collective-permute-done.28 = bf16[128,512]{1,0:T(8,128)(2,1)S(1)} collective-permute-done((bf16[128,512]{1,0:T(8,128)(2,1)S(1)}, bf16[128,512]{1,0:T(8,128)(2,1)S(1)}, u32[]{:S(2)}, u32[]{:S(2)}) %collective-permute-start.28) | collective-permute-done | bytes 131104 | tf_op jit(solution)/shard_map/ppermute | solution.py:109
  124.9 2.5 %collective-permute-start.29 = (bf16[64,512]{1,0:T(8,128)(2,1)S(1)}, bf16[64,512]{1,0:T(8,128)(2,1)S(1)}, u32[]{:S(2)}, u32[]{:S(2)}) collective-permute-start(bf16[64,512]{1,0:T(8,128)(2,1)S(1)} %constant_dynamic-slice_fusion.5), channel_id=1, source_target_pairs={{0,2},{1,3},{2,0},{3,1},{4,6},{5,7},{6,4},{7,5},{8,10},{9,11},{10,... | collective-permute-start | bytes 196616 | tf_op jit(solution)/shard_map/ppermute | solution.py:109
  127.5 2.0 %collective-permute-start.33 = (bf16[64,512]{1,0:T(8,128)(2,1)S(1)}, bf16[64,512]{1,0:T(8,128)(2,1)S(1)}, u32[]{:S(2)}, u32[]{:S(2)}) collective-permute-start(bf16[64,512]{1,0:T(8,128)(2,1)S(1)} %constant_dynamic-slice_fusion.1), channel_id=1, source_target_pairs={{0,4},{1,5},{2,6},{3,7},{4,0},{5,1},{6,2},{7,3},{8,12},{9,13},{10,... | collective-permute-start | bytes 196616 | tf_op jit(solution)/shard_map/ppermute | solution.py:109
  129.9 1.9 %collective-permute-start.30 = (bf16[32,512]{1,0:T(8,128)(2,1)S(1)}, bf16[32,512]{1,0:T(8,128)(2,1)S(1)}, u32[]{:S(2)}, u32[]{:S(2)}) collective-permute-start(bf16[32,512]{1,0:T(8,128)(2,1)S(1)} %constant_dynamic-slice_fusion.4), channel_id=1, source_target_pairs={{0,4},{1,5},{2,6},{3,7},{4,0},{5,1},{6,2},{7,3},{8,12},{9,13},{10,... | collective-permute-start | bytes 98312 | tf_op jit(solution)/shard_map/ppermute | solution.py:109
  132.5 2.0 %collective-permute-done.22 = bf16[32,512]{1,0:T(8,128)(2,1)S(1)} collective-permute-done((bf16[32,512]{1,0:T(8,128)(2,1)S(1)}, bf16[32,512]{1,0:T(8,128)(2,1)S(1)}, u32[]{:S(2)}, u32[]{:S(2)}) %collective-permute-start.22) | collective-permute-done | bytes 32800 | tf_op jit(solution)/shard_map/ppermute | solution.py:109
  (186 shorter events, 42.3 us)
Async XLA Ops:
  3.6 8.7 %collective-permute-start = (bf16[32,512]{1,0:T(8,128)(2,1)S(1)}, bf16[32,512]{1,0:T(8,128)(2,1)S(1)}, u32[]{:S(2)}, u32[]{:S(2)}) collective-permute-start(bf16[32,512]{1,0:T(8,128)(2,1)S(1)} %get-tuple-element.52), channel_id=1, source_target_pairs={{0,16},{1,17},{2,18},{3,19},{4,20},{5,21},{6,22},{7,23},{8,24},{9,... | collective-permute-start | bytes 98312 | tf_op jit(solution)/shard_map/ppermute | solution.py:204
  15.2 5.2 %collective-permute-start.5 = (bf16[64,512]{1,0:T(8,128)(2,1)S(1)}, bf16[64,512]{1,0:T(8,128)(2,1)S(1)}, u32[]{:S(2)}, u32[]{:S(2)}) collective-permute-start(bf16[64,512]{1,0:T(8,128)(2,1)S(1)} %pad_maximum_fusion.17), channel_id=1, source_target_pairs={{0,16},{1,17},{2,18},{3,19},{4,20},{5,21},{6,22},{7,23},{8,24},{9,... | collective-permute-start | bytes 196616 | tf_op jit(solution)/shard_map/ppermute | solution.py:204
  15.6 8.8 %collective-permute-start.9 = (bf16[64,512]{1,0:T(8,128)(2,1)S(1)}, bf16[64,512]{1,0:T(8,128)(2,1)S(1)}, u32[]{:S(2)}, u32[]{:S(2)}) collective-permute-start(bf16[64,512]{1,0:T(8,128)(2,1)S(1)} %pad_maximum_fusion.18), channel_id=1, source_target_pairs={{0,2},{1,3},{2,0},{3,1},{4,6},{5,7},{6,4},{7,5},{8,10},{9,11},{10,... | collective-permute-start | bytes 196616 | tf_op jit(solution)/shard_map/ppermute | solution.py:204
  16.0 8.5 %collective-permute-start.13 = (bf16[64,512]{1,0:T(8,128)(2,1)S(1)}, bf16[64,512]{1,0:T(8,128)(2,1)S(1)}, u32[]{:S(2)}, u32[]{:S(2)}) collective-permute-start(bf16[64,512]{1,0:T(8,128)(2,1)S(1)} %pad_maximum_fusion.19), channel_id=1, source_target_pairs={{0,4},{1,5},{2,6},{3,7},{4,0},{5,1},{6,2},{7,3},{8,12},{9,13},{10,... | collective-permute-start | bytes 196616 | tf_op jit(solution)/shard_map/ppermute | solution.py:204
  20.5 5.4 %collective-permute-start.2 = (bf16[128,512]{1,0:T(8,128)(2,1)S(1)}, bf16[128,512]{1,0:T(8,128)(2,1)S(1)}, u32[]{:S(2)}, u32[]{:S(2)}) collective-permute-start(bf16[128,512]{1,0:T(8,128)(2,1)S(1)} %pad_maximum_fusion.12), channel_id=1, source_target_pairs={{0,4},{1,5},{2,6},{3,7},{4,0},{5,1},{6,2},{7,3},{8,12},{9,13},{10,... | collective-permute-start | bytes 393224 | tf_op jit(solution)/shard_map/ppermute | solution.py:204
  22.1 5.3 %collective-permute-start.6 = (bf16[128,512]{1,0:T(8,128)(2,1)S(1)}, bf16[128,512]{1,0:T(8,128)(2,1)S(1)}, u32[]{:S(2)}, u32[]{:S(2)}) collective-permute-start(bf16[128,512]{1,0:T(8,128)(2,1)S(1)} %pad_maximum_fusion.13), channel_id=1, source_target_pairs={{0,8},{1,9},{2,10},{3,11},{4,12},{5,13},{6,14},{7,15},{8,0},{9,1},... | collective-permute-start | bytes 393224 | tf_op jit(solution)/shard_map/ppermute | solution.py:204
  24.5 11.0 %collective-permute-start.10 = (bf16[128,512]{1,0:T(8,128)(2,1)S(1)}, bf16[128,512]{1,0:T(8,128)(2,1)S(1)}, u32[]{:S(2)}, u32[]{:S(2)}) collective-permute-start(bf16[128,512]{1,0:T(8,128)(2,1)S(1)} %pad_maximum_fusion.14), channel_id=1, source_target_pairs={{0,16},{1,17},{2,18},{3,19},{4,20},{5,21},{6,22},{7,23},{8,24},{9,... | collective-permute-start | bytes 393224 | tf_op jit(solution)/shard_map/ppermute | solution.py:204
  25.0 10.7 %collective-permute-start.14 = (bf16[128,512]{1,0:T(8,128)(2,1)S(1)}, bf16[128,512]{1,0:T(8,128)(2,1)S(1)}, u32[]{:S(2)}, u32[]{:S(2)}) collective-permute-start(bf16[128,512]{1,0:T(8,128)(2,1)S(1)} %pad_maximum_fusion.15), channel_id=1, source_target_pairs={{0,2},{1,3},{2,0},{3,1},{4,6},{5,7},{6,4},{7,5},{8,10},{9,11},{10,... | collective-permute-start | bytes 393224 | tf_op jit(solution)/shard_map/ppermute | solution.py:204
  26.0 9.9 %collective-permute-start.3 = (bf16[256,512]{1,0:T(8,128)(2,1)S(1)}, bf16[256,512]{1,0:T(8,128)(2,1)S(1)}, u32[]{:S(2)}, u32[]{:S(2)}) collective-permute-start(bf16[256,512]{1,0:T(8,128)(2,1)S(1)} %pad_maximum_fusion.8), channel_id=1, source_target_pairs={{0,2},{1,3},{2,0},{3,1},{4,6},{5,7},{6,4},{7,5},{8,10},{9,11},{10,... | collective-permute-start | bytes 786440 | tf_op jit(solution)/shard_map/ppermute | solution.py:204
  27.5 8.5 %collective-permute-start.7 = (bf16[256,512]{1,0:T(8,128)(2,1)S(1)}, bf16[256,512]{1,0:T(8,128)(2,1)S(1)}, u32[]{:S(2)}, u32[]{:S(2)}) collective-permute-start(bf16[256,512]{1,0:T(8,128)(2,1)S(1)} %pad_maximum_fusion.9), channel_id=1, source_target_pairs={{0,4},{1,5},{2,6},{3,7},{4,0},{5,1},{6,2},{7,3},{8,12},{9,13},{10,... | collective-permute-start | bytes 786440 | tf_op jit(solution)/shard_map/ppermute | solution.py:204
  35.6 7.9 %collective-permute-start.11 = (bf16[256,512]{1,0:T(8,128)(2,1)S(1)}, bf16[256,512]{1,0:T(8,128)(2,1)S(1)}, u32[]{:S(2)}, u32[]{:S(2)}) collective-permute-start(bf16[256,512]{1,0:T(8,128)(2,1)S(1)} %pad_maximum_fusion.10), channel_id=1, source_target_pairs={{0,8},{1,9},{2,10},{3,11},{4,12},{5,13},{6,14},{7,15},{8,0},{9,1},... | collective-permute-start | bytes 786440 | tf_op jit(solution)/shard_map/ppermute | solution.py:204
  35.8 10.2 %collective-permute-start.15 = (bf16[256,512]{1,0:T(8,128)(2,1)S(1)}, bf16[256,512]{1,0:T(8,128)(2,1)S(1)}, u32[]{:S(2)}, u32[]{:S(2)}) collective-permute-start(bf16[256,512]{1,0:T(8,128)(2,1)S(1)} %pad_maximum_fusion.11), channel_id=1, source_target_pairs={{0,16},{1,17},{2,18},{3,19},{4,20},{5,21},{6,22},{7,23},{8,24},{9,... | collective-permute-start | bytes 786440 | tf_op jit(solution)/shard_map/ppermute | solution.py:204
  47.8 5.1 %collective-permute-start.16 = (bf16[512,2048]{1,0:T(8,128)(2,1)}, bf16[512,2048]{1,0:T(8,128)(2,1)}, u32[]{:S(2)}, u32[]{:S(2)}) collective-permute-start(bf16[512,2048]{1,0:T(8,128)(2,1)} %pad_maximum_fusion.1), channel_id=1, source_target_pairs={{0,1},{1,0},{2,3},{3,2},{4,5},{5,4},{6,7},{7,6},{8,9},{9,8},{10,11... | collective-permute-start | bytes 6291464 | tf_op jit(solution)/shard_map/ppermute | solution.py:216
  64.0 5.3 %collective-permute-start.17 = (bf16[1024,128]{1,0:T(8,128)(2,1)S(1)}, bf16[1024,128]{1,0:T(8,128)(2,1)S(1)}, u32[]{:S(2)}, u32[]{:S(2)}) collective-permute-start(bf16[1024,128]{1,0:T(8,128)(2,1)S(1)} %fusion.10), channel_id=1, source_target_pairs={{0,1},{1,0},{2,3},{3,2},{4,5},{5,4},{6,7},{7,6},{8,9},{9,8},{10,11... | collective-permute-start | bytes 786440 | tf_op jit(solution)/shard_map/ppermute | solution.py:18
  101.3 8.4 %collective-permute-start.19 = (bf16[256,512]{1,0:T(8,128)(2,1)S(1)}, bf16[256,512]{1,0:T(8,128)(2,1)S(1)}, u32[]{:S(2)}, u32[]{:S(2)}) collective-permute-start(bf16[256,512]{1,0:T(8,128)(2,1)S(1)} %constant_dynamic-slice_fusion.15), channel_id=1, source_target_pairs={{0,2},{1,3},{2,0},{3,1},{4,6},{5,7},{6,4},{7,5},{8,10},{9,11},{10,... | collective-permute-start | bytes 786440 | tf_op jit(solution)/shard_map/ppermute | solution.py:109
  102.0 8.1 %collective-permute-start.23 = (bf16[256,512]{1,0:T(8,128)(2,1)S(1)}, bf16[256,512]{1,0:T(8,128)(2,1)S(1)}, u32[]{:S(2)}, u32[]{:S(2)}) collective-permute-start(bf16[256,512]{1,0:T(8,128)(2,1)S(1)} %constant_dynamic-slice_fusion.11), channel_id=1, source_target_pairs={{0,4},{1,5},{2,6},{3,7},{4,0},{5,1},{6,2},{7,3},{8,12},{9,13},{10,... | collective-permute-start | bytes 786440 | tf_op jit(solution)/shard_map/ppermute | solution.py:109
  102.1 14.3 %collective-permute-start.27 = (bf16[256,512]{1,0:T(8,128)(2,1)S(1)}, bf16[256,512]{1,0:T(8,128)(2,1)S(1)}, u32[]{:S(2)}, u32[]{:S(2)}) collective-permute-start(bf16[256,512]{1,0:T(8,128)(2,1)S(1)} %constant_dynamic-slice_fusion.7), channel_id=1, source_target_pairs={{0,8},{1,9},{2,10},{3,11},{4,12},{5,13},{6,14},{7,15},{8,0},{9,1},... | collective-permute-start | bytes 786440 | tf_op jit(solution)/shard_map/ppermute | solution.py:109
  102.3 14.8 %collective-permute-start.31 = (bf16[256,512]{1,0:T(8,128)(2,1)S(1)}, bf16[256,512]{1,0:T(8,128)(2,1)S(1)}, u32[]{:S(2)}, u32[]{:S(2)}) collective-permute-start(bf16[256,512]{1,0:T(8,128)(2,1)S(1)} %constant_dynamic-slice_fusion.3), channel_id=1, source_target_pairs={{0,16},{1,17},{2,18},{3,19},{4,20},{5,21},{6,22},{7,23},{8,24},{9,... | collective-permute-start | bytes 786440 | tf_op jit(solution)/shard_map/ppermute | solution.py:109
  109.8 9.0 %collective-permute-start.20 = (bf16[128,512]{1,0:T(8,128)(2,1)S(1)}, bf16[128,512]{1,0:T(8,128)(2,1)S(1)}, u32[]{:S(2)}, u32[]{:S(2)}) collective-permute-start(bf16[128,512]{1,0:T(8,128)(2,1)S(1)} %constant_dynamic-slice_fusion.14), channel_id=1, source_target_pairs={{0,4},{1,5},{2,6},{3,7},{4,0},{5,1},{6,2},{7,3},{8,12},{9,13},{10,... | collective-permute-start | bytes 393224 | tf_op jit(solution)/shard_map/ppermute | solution.py:109
  110.2 10.7 %collective-permute-start.24 = (bf16[128,512]{1,0:T(8,128)(2,1)S(1)}, bf16[128,512]{1,0:T(8,128)(2,1)S(1)}, u32[]{:S(2)}, u32[]{:S(2)}) collective-permute-start(bf16[128,512]{1,0:T(8,128)(2,1)S(1)} %constant_dynamic-slice_fusion.10), channel_id=1, source_target_pairs={{0,8},{1,9},{2,10},{3,11},{4,12},{5,13},{6,14},{7,15},{8,0},{9,1},... | collective-permute-start | bytes 393224 | tf_op jit(solution)/shard_map/ppermute | solution.py:109
  116.5 8.4 %collective-permute-start.28 = (bf16[128,512]{1,0:T(8,128)(2,1)S(1)}, bf16[128,512]{1,0:T(8,128)(2,1)S(1)}, u32[]{:S(2)}, u32[]{:S(2)}) collective-permute-start(bf16[128,512]{1,0:T(8,128)(2,1)S(1)} %constant_dynamic-slice_fusion.6), channel_id=1, source_target_pairs={{0,16},{1,17},{2,18},{3,19},{4,20},{5,21},{6,22},{7,23},{8,24},{9,... | collective-permute-start | bytes 393224 | tf_op jit(solution)/shard_map/ppermute | solution.py:109
  117.2 10.3 %collective-permute-start.32 = (bf16[128,512]{1,0:T(8,128)(2,1)S(1)}, bf16[128,512]{1,0:T(8,128)(2,1)S(1)}, u32[]{:S(2)}, u32[]{:S(2)}) collective-permute-start(bf16[128,512]{1,0:T(8,128)(2,1)S(1)} %constant_dynamic-slice_fusion.2), channel_id=1, source_target_pairs={{0,2},{1,3},{2,0},{3,1},{4,6},{5,7},{6,4},{7,5},{8,10},{9,11},{10,... | collective-permute-start | bytes 393224 | tf_op jit(solution)/shard_map/ppermute | solution.py:109
  118.8 10.8 %collective-permute-start.21 = (bf16[64,512]{1,0:T(8,128)(2,1)S(1)}, bf16[64,512]{1,0:T(8,128)(2,1)S(1)}, u32[]{:S(2)}, u32[]{:S(2)}) collective-permute-start(bf16[64,512]{1,0:T(8,128)(2,1)S(1)} %constant_dynamic-slice_fusion.13), channel_id=1, source_target_pairs={{0,8},{1,9},{2,10},{3,11},{4,12},{5,13},{6,14},{7,15},{8,0},{9,1},... | collective-permute-start | bytes 196616 | tf_op jit(solution)/shard_map/ppermute | solution.py:109
  121.0 8.7 %collective-permute-start.25 = (bf16[64,512]{1,0:T(8,128)(2,1)S(1)}, bf16[64,512]{1,0:T(8,128)(2,1)S(1)}, u32[]{:S(2)}, u32[]{:S(2)}) collective-permute-start(bf16[64,512]{1,0:T(8,128)(2,1)S(1)} %constant_dynamic-slice_fusion.9), channel_id=1, source_target_pairs={{0,16},{1,17},{2,18},{3,19},{4,20},{5,21},{6,22},{7,23},{8,24},{9,... | collective-permute-start | bytes 196616 | tf_op jit(solution)/shard_map/ppermute | solution.py:109
  (27 other events, 192.1 us)

commit v6 on v4

--- a/solution.py
+++ b/solution.py
@@ -112,7 +112,7 @@
     start_block = jnp.clip(chunk - (window - 1), 0, blocks - window)
     start = pl.multiple_of(start_block * CHUNK, CHUNK)
     span = window * CHUNK
-    keys = k_ref[pl.ds(start, span), :]
+    keys = k_ref[:, pl.ds(start, span)]
     values = v_ref[pl.ds(start, span), :]
     key_seg = kseg_ref[:, pl.ds(start, span)]
     query_seg = qseg_ref[...]
@@ -127,13 +127,12 @@
         raw = q_ref[:, e * HD:(e + 1) * HD]
         turned = raw * cosine + pltpu.roll(raw, HD // 2, 1) * sine_part
         queries = (turned * scale_factor).astype(jnp.bfloat16)
-        scores = lax.dot_general(
-            queries, keys, (((1,), (1,)), ((), ())), preferred_element_type=jnp.float32
-        )
+        scores = jnp.dot(queries, keys, preferred_element_type=jnp.float32)
         scores = jnp.where(allowed, scores, -1e30)
         top = jnp.max(scores, axis=1, keepdims=True)
         raised = jnp.exp(scores - top)
-        probabilities = (raised / jnp.sum(raised, axis=1, keepdims=True)).astype(jnp.bfloat16)
+        inverse = 1.0 / jnp.sum(raised, axis=1, keepdims=True)
+        probabilities = (raised * inverse).astype(jnp.bfloat16)
         attended = jnp.dot(probabilities, values, preferred_element_type=jnp.float32)
         out_ref[:, e * HD:(e + 1) * HD] = (attended * gate_ref[:, e:e + 1]).astype(out_ref.dtype)
 
@@ -165,7 +164,7 @@
             pl.BlockSpec((CHUNK, width), lambda i: (i, 0)),
             pl.BlockSpec((CHUNK, HD), lambda i: (i, 0)),
             pl.BlockSpec((CHUNK, HD), lambda i: (i, 0)),
-            pl.BlockSpec((tokens, HD), lambda i: (0, 0)),
+            pl.BlockSpec((HD, tokens), lambda i: (0, 0)),
             pl.BlockSpec((tokens, HD), lambda i: (0, 0)),
             pl.BlockSpec((CHUNK, 1), lambda i: (i, 0)),
             pl.BlockSpec((1, tokens), lambda i: (0, 0)),
@@ -178,7 +177,7 @@
             transcendentals=tokens * window * CHUNK * experts,
             bytes_accessed=tokens * width * 6 + 2 * tokens * HD * 2 + 2 * tokens * HD * 4,
         ),
-    )(raw_queries, cosine, sine_part, keys, values, seg_cols, seg_row, gate_here)
+    )(raw_queries, cosine, sine_part, jnp.transpose(keys), values, seg_cols, seg_row, gate_here)
 
 
 def gather_from_all(block, axis):

time: 125 us -> 126 us (level)
  no operation moved by 1% of the time
where the time goes in v6:
time: 126 us
  starting transfers between devices  37.4 us (30%)
  waiting for transfers between devices  34 us (27%)
  Pallas kernels  17 us (13%)
  other arithmetic  15.7 us (12%)
  matrix products  12.6 us (10%)
  local copies, waits for them, and re-layouts  7.58 us (6%)
  between operations  1.5 us (1%)
    ppermute x20, starting transfers between devices, gather_from_all(): got = lax.ppermute(current, axis, [(i, i ^ 1 << k) for i in range(size)])  20.5 us
    ppermute x20, waiting for transfers between devices, reduce_to_owner(): got = lax.ppermute(send, axis, [(i, i ^ 1 << k) for i in range(size)])  19.3 us
    pallas_call x1, Pallas kernels, attend_window(): pl.pallas_call(lambda *refs: attention_kernel(window, *refs), grid=(block...  17 us
    ppermute x20, starting transfers between devices, reduce_to_owner(): got = lax.ppermute(send, axis, [(i, i ^ 1 << k) for i in range(size)])  16.7 us
    ppermute x20, waiting for transfers between devices, gather_from_all(): got = lax.ppermute(current, axis, [(i, i ^ 1 << k) for i in range(size)])  14.7 us
    unnamed x24, local copies, waits for them, and re-layouts  4 us
    dot_general x1, matrix products, local(): jnp.dot(normed, query_weight, preferred_element_type=jnp.float32)  3.68 us
    dot_general x1, matrix products, project_kv(): projected = jnp.dot(normed, weight, preferred_element_type=jnp.float32)  3.58 us
  transfers between devices with their start and end apart: 41, of which 18 were waited for; matrix products, arithmetic and copies ran while one was open for 13% of the time, Pallas kernels for 0%

profile of v6, /device:TPU:0, one launch (start us, length us, event | category | flops | bytes accessed | tf_op | source)
XLA Modules:
  0.0 125.8 jit_solution(12623525449091872355)
XLA Ops:
  3.6 4.1 %collective-permute-start = (bf16[32,512]{1,0:T(8,128)(2,1)S(1)}, bf16[32,512]{1,0:T(8,128)(2,1)S(1)}, u32[]{:S(2)}, u32[]{:S(2)}) collective-permute-start(bf16[32,512]{1,0:T(8,128)(2,1)S(1)} %get-tuple-element.58), channel_id=1, source_target_pairs={{0,16},{1,17},{2,18},{3,19},{4,20},{5,21},{6,22},{7,23},{8,24},{9,... | collective-permute-start | bytes 98312 | tf_op jit(solution)/shard_map/ppermute | solution.py:196
  7.7 1.5 %collective-permute-start.10 = (bf16[32,512]{1,0:T(8,128)(2,1)S(1)}, bf16[32,512]{1,0:T(8,128)(2,1)S(1)}, u32[]{:S(2)}, u32[]{:S(2)}) collective-permute-start(bf16[32,512]{1,0:T(8,128)(2,1)S(1)} %get-tuple-element.60), channel_id=1, source_target_pairs={{0,4},{1,5},{2,6},{3,7},{4,0},{5,1},{6,2},{7,3},{8,12},{9,13},{10,... | collective-permute-start | bytes 98312 | tf_op jit(solution)/shard_map/ppermute | solution.py:196
  9.2 1.6 %collective-permute-start.15 = (bf16[32,512]{1,0:T(8,128)(2,1)S(1)}, bf16[32,512]{1,0:T(8,128)(2,1)S(1)}, u32[]{:S(2)}, u32[]{:S(2)}) collective-permute-start(bf16[32,512]{1,0:T(8,128)(2,1)S(1)} %get-tuple-element.59), channel_id=1, source_target_pairs={{0,8},{1,9},{2,10},{3,11},{4,12},{5,13},{6,14},{7,15},{8,0},{9,1},... | collective-permute-start | bytes 98312 | tf_op jit(solution)/shard_map/ppermute | solution.py:196
  13.8 1.9 %fusion.15 = (f32[1024,64]{1,0:T(8,128)S(1)}, f32[1024,64]{1,0:T(8,128)S(1)}, f32[1024,64]{1,0:T(8,128)S(1)}) fusion(f32[64]{0:T(128)S(1)} %multiply_power_fusion, f32[1024]{0:T(1024)S(1)} %fusion.18), kind=kLoop, calls=%fused_computation.70 | loop fusion | flops 131072 | bytes 790784 | tf_op jit(solution)/shard_map/neg | solution.py:148
  19.9 2.7 %collective-permute-done.1 = bf16[64,512]{1,0:T(8,128)(2,1)S(1)} collective-permute-done((bf16[64,512]{1,0:T(8,128)(2,1)S(1)}, bf16[64,512]{1,0:T(8,128)(2,1)S(1)}, u32[]{:S(2)}, u32[]{:S(2)}) %collective-permute-start.1) | collective-permute-done | bytes 65568 | tf_op jit(solution)/shard_map/ppermute | solution.py:196
  24.6 1.6 %collective-permute-start.7 = (bf16[128,512]{1,0:T(8,128)(2,1)S(1)}, bf16[128,512]{1,0:T(8,128)(2,1)S(1)}, u32[]{:S(2)}, u32[]{:S(2)}) collective-permute-start(bf16[128,512]{1,0:T(8,128)(2,1)S(1)} %pad_maximum_fusion.16), channel_id=1, source_target_pairs={{0,8},{1,9},{2,10},{3,11},{4,12},{5,13},{6,14},{7,15},{8,0},{9,1},... | collective-permute-start | bytes 393224 | tf_op jit(solution)/shard_map/ppermute | solution.py:196
  31.1 1.6 %collective-permute-start.8 = (bf16[256,512]{1,0:T(8,128)(2,1)S(1)}, bf16[256,512]{1,0:T(8,128)(2,1)S(1)}, u32[]{:S(2)}, u32[]{:S(2)}) collective-permute-start(bf16[256,512]{1,0:T(8,128)(2,1)S(1)} %pad_maximum_fusion.12), channel_id=1, source_target_pairs={{0,4},{1,5},{2,6},{3,7},{4,0},{5,1},{6,2},{7,3},{8,12},{9,13},{10,... | collective-permute-start | bytes 786440 | tf_op jit(solution)/shard_map/ppermute | solution.py:196
  33.9 3.2 %collective-permute-start.18 = (bf16[256,512]{1,0:T(8,128)(2,1)S(1)}, bf16[256,512]{1,0:T(8,128)(2,1)S(1)}, u32[]{:S(2)}, u32[]{:S(2)}) collective-permute-start(bf16[256,512]{1,0:T(8,128)(2,1)S(1)} %pad_maximum_fusion.14), channel_id=1, source_target_pairs={{0,16},{1,17},{2,18},{3,19},{4,20},{5,21},{6,22},{7,23},{8,24},{9,... | collective-permute-start | bytes 786440 | tf_op jit(solution)/shard_map/ppermute | solution.py:196
  38.0 5.5 %collective-permute-done.13 = bf16[256,512]{1,0:T(8,128)(2,1)S(1)} collective-permute-done((bf16[256,512]{1,0:T(8,128)(2,1)S(1)}, bf16[256,512]{1,0:T(8,128)(2,1)S(1)}, u32[]{:S(2)}, u32[]{:S(2)}) %collective-permute-start.13) | collective-permute-done | bytes 262176 | tf_op jit(solution)/shard_map/ppermute | solution.py:196
  48.2 1.9 %copy-done.1 = bf16[1024,2048]{1,0:T(8,128)(2,1)} copy-done((bf16[1024,2048]{1,0:T(8,128)(2,1)}, bf16[1024,2048]{1,0:T(8,128)(2,1)S(1)}, u32[]{:S(2)}) %copy-start.1) | copy-done | bytes 4194328
  51.5 3.6 %fusion.26 = f32[1024,128]{1,0:T(8,128)S(1)} fusion(bf16[1024,2048]{1,0:T(8,128)(2,1)} %copy-done.1, bf16[2048,128]{1,0:T(8,128)(2,1)S(1)} %copy-done.4), kind=kOutput, calls=%fused_computation.153 | convolution fusion | flops 536870912 | bytes 5242880 | tf_op jit(solution)/shard_map/dot_general | solution.py:58
  55.1 2.4 %fusion.6 = (bf16[1024,64]{1,0:T(8,128)(2,1)S(1)}, bf16[1024,64]{1,0:T(8,128)(2,1)S(1)}) fusion(f32[1024,1,128]{2,0,1:T(8,128)S(1)} %bitcast.63, f32[64]{0:T(128)S(1)} %multiply_power_fusion, f32[1024]{0:T(1024)S(1)} %fusion.18), kind=kLoop, calls=%fused_computation.21 | loop fusion | flops 589824 | bytes 790784 | tf_op jit(solution)/shard_map/concatenate | solution.py:52
  57.9 3.7 %fusion.25.refs_0_ = f32[1024,512]{1,0:T(8,128)} fusion(bf16[1024,2048]{1,0:T(8,128)(2,1)S(1)} %copy-done.2, bf16[2048,512]{1,0:T(8,128)(2,1)S(1)} %copy-done.10), kind=kOutput, calls=%fused_computation.152 | convolution fusion | flops 2147483648 | bytes 8388608 | tf_op jit(solution)/shard_map/dot_general | solution.py:234
  64.3 17.0 %shard_map.113 = bf16[1024,512]{1,0:T(8,128)(2,1)} custom-call(f32[1024,512]{1,0:T(8,128)} %fusion.25.refs_0_, f32[1024,128]{1,0:T(8,128)} %get-tuple-element.75.refs_1_, f32[1024,128]{1,0:T(8,128)} %get-tuple-element.76.refs_2_, bf16[128,1024]{1,0:T(8,128)(2,1)} %copy.61.refs_3_, bf16[1024,128]{1,0:T(8,128)(2,1)} %get-tuple-element.24.refs_4_, ...), custom_call_target="tpu_custom_call" | custom-call | flops 1342177280 | bytes 4718592 | tf_op jit(solution)/shard_map/pallas_call | solution.py:160
  81.3 3.6 %convolution_convert_fusion = bf16[1024,2048]{1,0:T(8,128)(2,1)S(1)} fusion(bf16[1024,512]{1,0:T(8,128)(2,1)} %shard_map.113, bf16[512,2048]{1,0:T(8,128)(2,1)S(1)} %copy-done), kind=kOutput, calls=%fused_computation.1 | convolution fusion | flops 2149580800 | bytes 7340032 | tf_op jit(solution)/shard_map/dot_general | solution.py:238
  89.9 1.5 %collective-permute-start.27 = (bf16[256,512]{1,0:T(8,128)(2,1)S(1)}, bf16[256,512]{1,0:T(8,128)(2,1)S(1)}, u32[]{:S(2)}, u32[]{:S(2)}) collective-permute-start(bf16[256,512]{1,0:T(8,128)(2,1)S(1)} %constant_dynamic-slice_fusion.13), channel_id=1, source_target_pairs={{0,4},{1,5},{2,6},{3,7},{4,0},{5,1},{6,2},{7,3},{8,12},{9,13},{10,... | collective-permute-start | bytes 786440 | tf_op jit(solution)/shard_map/ppermute | solution.py:103
  91.9 2.1 %collective-permute-start.37 = (bf16[256,512]{1,0:T(8,128)(2,1)S(1)}, bf16[256,512]{1,0:T(8,128)(2,1)S(1)}, u32[]{:S(2)}, u32[]{:S(2)}) collective-permute-start(bf16[256,512]{1,0:T(8,128)(2,1)S(1)} %constant_dynamic-slice_fusion.3), channel_id=1, source_target_pairs={{0,16},{1,17},{2,18},{3,19},{4,20},{5,21},{6,22},{7,23},{8,24},{9,... | collective-permute-start | bytes 786440 | tf_op jit(solution)/shard_map/ppermute | solution.py:103
  94.0 3.5 %collective-permute-done.22 = bf16[256,512]{1,0:T(8,128)(2,1)S(1)} collective-permute-done((bf16[256,512]{1,0:T(8,128)(2,1)S(1)}, bf16[256,512]{1,0:T(8,128)(2,1)S(1)}, u32[]{:S(2)}, u32[]{:S(2)}) %collective-permute-start.22) | collective-permute-done | bytes 262176 | tf_op jit(solution)/shard_map/ppermute | solution.py:103
  97.6 1.6 %collective-permute-start.23 = (bf16[128,512]{1,0:T(8,128)(2,1)S(1)}, bf16[128,512]{1,0:T(8,128)(2,1)S(1)}, u32[]{:S(2)}, u32[]{:S(2)}) collective-permute-start(bf16[128,512]{1,0:T(8,128)(2,1)S(1)} %constant_dynamic-slice_fusion.17), channel_id=1, source_target_pairs={{0,4},{1,5},{2,6},{3,7},{4,0},{5,1},{6,2},{7,3},{8,12},{9,13},{10,... | collective-permute-start | bytes 393224 | tf_op jit(solution)/shard_map/ppermute | solution.py:103
  99.4 6.4 %collective-permute-done.32 = bf16[256,512]{1,0:T(8,128)(2,1)S(1)} collective-permute-done((bf16[256,512]{1,0:T(8,128)(2,1)S(1)}, bf16[256,512]{1,0:T(8,128)(2,1)S(1)}, u32[]{:S(2)}, u32[]{:S(2)}) %collective-permute-start.32) | collective-permute-done | bytes 262176 | tf_op jit(solution)/shard_map/ppermute | solution.py:103
  108.3 2.1 %collective-permute-start.24 = (bf16[64,512]{1,0:T(8,128)(2,1)S(1)}, bf16[64,512]{1,0:T(8,128)(2,1)S(1)}, u32[]{:S(2)}, u32[]{:S(2)}) collective-permute-start(bf16[64,512]{1,0:T(8,128)(2,1)S(1)} %constant_dynamic-slice_fusion.16), channel_id=1, source_target_pairs={{0,8},{1,9},{2,10},{3,11},{4,12},{5,13},{6,14},{7,15},{8,0},{9,1},... | collective-permute-start | bytes 196616 | tf_op jit(solution)/shard_map/ppermute | solution.py:103
  111.3 2.8 %collective-permute-done.33 = bf16[128,512]{1,0:T(8,128)(2,1)S(1)} collective-permute-done((bf16[128,512]{1,0:T(8,128)(2,1)S(1)}, bf16[128,512]{1,0:T(8,128)(2,1)S(1)}, u32[]{:S(2)}, u32[]{:S(2)}) %collective-permute-start.33) | collective-permute-done | bytes 131104 | tf_op jit(solution)/shard_map/ppermute | solution.py:103
  114.2 2.5 %collective-permute-start.34 = (bf16[64,512]{1,0:T(8,128)(2,1)S(1)}, bf16[64,512]{1,0:T(8,128)(2,1)S(1)}, u32[]{:S(2)}, u32[]{:S(2)}) collective-permute-start(bf16[64,512]{1,0:T(8,128)(2,1)S(1)} %constant_dynamic-slice_fusion.6), channel_id=1, source_target_pairs={{0,2},{1,3},{2,0},{3,1},{4,6},{5,7},{6,4},{7,5},{8,10},{9,11},{10,... | collective-permute-start | bytes 196616 | tf_op jit(solution)/shard_map/ppermute | solution.py:103
  123.0 2.1 %collective-permute-done.40 = bf16[32,512]{1,0:T(8,128)(2,1)S(1)} collective-permute-done((bf16[32,512]{1,0:T(8,128)(2,1)S(1)}, bf16[32,512]{1,0:T(8,128)(2,1)S(1)}, u32[]{:S(2)}, u32[]{:S(2)}) %collective-permute-start.40) | collective-permute-done | bytes 32800 | tf_op jit(solution)/shard_map/ppermute | solution.py:103
  (201 shorter events, 43.8 us)
Async XLA Ops:
  3.6 14.6 %collective-permute-start = (bf16[32,512]{1,0:T(8,128)(2,1)S(1)}, bf16[32,512]{1,0:T(8,128)(2,1)S(1)}, u32[]{:S(2)}, u32[]{:S(2)}) collective-permute-start(bf16[32,512]{1,0:T(8,128)(2,1)S(1)} %get-tuple-element.58), channel_id=1, source_target_pairs={{0,16},{1,17},{2,18},{3,19},{4,20},{5,21},{6,22},{7,23},{8,24},{9,... | collective-permute-start | bytes 98312 | tf_op jit(solution)/shard_map/ppermute | solution.py:196
  7.7 10.5 %collective-permute-start.10 = (bf16[32,512]{1,0:T(8,128)(2,1)S(1)}, bf16[32,512]{1,0:T(8,128)(2,1)S(1)}, u32[]{:S(2)}, u32[]{:S(2)}) collective-permute-start(bf16[32,512]{1,0:T(8,128)(2,1)S(1)} %get-tuple-element.60), channel_id=1, source_target_pairs={{0,4},{1,5},{2,6},{3,7},{4,0},{5,1},{6,2},{7,3},{8,12},{9,13},{10,... | collective-permute-start | bytes 98312 | tf_op jit(solution)/shard_map/ppermute | solution.py:196
  9.2 9.0 %collective-permute-start.15 = (bf16[32,512]{1,0:T(8,128)(2,1)S(1)}, bf16[32,512]{1,0:T(8,128)(2,1)S(1)}, u32[]{:S(2)}, u32[]{:S(2)}) collective-permute-start(bf16[32,512]{1,0:T(8,128)(2,1)S(1)} %get-tuple-element.59), channel_id=1, source_target_pairs={{0,8},{1,9},{2,10},{3,11},{4,12},{5,13},{6,14},{7,15},{8,0},{9,1},... | collective-permute-start | bytes 98312 | tf_op jit(solution)/shard_map/ppermute | solution.py:196
  10.8 7.4 %collective-permute-start.5 = (bf16[32,512]{1,0:T(8,128)(2,1)S(1)}, bf16[32,512]{1,0:T(8,128)(2,1)S(1)}, u32[]{:S(2)}, u32[]{:S(2)}) collective-permute-start(bf16[32,512]{1,0:T(8,128)(2,1)S(1)} %get-tuple-element.61), channel_id=1, source_target_pairs={{0,2},{1,3},{2,0},{3,1},{4,6},{5,7},{6,4},{7,5},{8,10},{9,11},{10,... | collective-permute-start | bytes 98312 | tf_op jit(solution)/shard_map/ppermute | solution.py:196
  19.1 7.1 %collective-permute-start.11 = (bf16[64,512]{1,0:T(8,128)(2,1)S(1)}, bf16[64,512]{1,0:T(8,128)(2,1)S(1)}, u32[]{:S(2)}, u32[]{:S(2)}) collective-permute-start(bf16[64,512]{1,0:T(8,128)(2,1)S(1)} %pad_maximum_fusion.21), channel_id=1, source_target_pairs={{0,2},{1,3},{2,0},{3,1},{4,6},{5,7},{6,4},{7,5},{8,10},{9,11},{10,... | collective-permute-start | bytes 196616 | tf_op jit(solution)/shard_map/ppermute | solution.py:196
  19.7 6.6 %collective-permute-start.16 = (bf16[64,512]{1,0:T(8,128)(2,1)S(1)}, bf16[64,512]{1,0:T(8,128)(2,1)S(1)}, u32[]{:S(2)}, u32[]{:S(2)}) collective-permute-start(bf16[64,512]{1,0:T(8,128)(2,1)S(1)} %pad_maximum_fusion.22), channel_id=1, source_target_pairs={{0,4},{1,5},{2,6},{3,7},{4,0},{5,1},{6,2},{7,3},{8,12},{9,13},{10,... | collective-permute-start | bytes 196616 | tf_op jit(solution)/shard_map/ppermute | solution.py:196
  26.3 7.3 %collective-permute-start.12 = (bf16[128,512]{1,0:T(8,128)(2,1)S(1)}, bf16[128,512]{1,0:T(8,128)(2,1)S(1)}, u32[]{:S(2)}, u32[]{:S(2)}) collective-permute-start(bf16[128,512]{1,0:T(8,128)(2,1)S(1)} %pad_maximum_fusion.17), channel_id=1, source_target_pairs={{0,16},{1,17},{2,18},{3,19},{4,20},{5,21},{6,22},{7,23},{8,24},{9,... | collective-permute-start | bytes 393224 | tf_op jit(solution)/shard_map/ppermute | solution.py:196
  27.5 6.4 %collective-permute-start.17 = (bf16[128,512]{1,0:T(8,128)(2,1)S(1)}, bf16[128,512]{1,0:T(8,128)(2,1)S(1)}, u32[]{:S(2)}, u32[]{:S(2)}) collective-permute-start(bf16[128,512]{1,0:T(8,128)(2,1)S(1)} %pad_maximum_fusion.18), channel_id=1, source_target_pairs={{0,2},{1,3},{2,0},{3,1},{4,6},{5,7},{6,4},{7,5},{8,10},{9,11},{10,... | collective-permute-start | bytes 393224 | tf_op jit(solution)/shard_map/ppermute | solution.py:196
  29.2 7.9 %collective-permute-start.3 = (bf16[256,512]{1,0:T(8,128)(2,1)S(1)}, bf16[256,512]{1,0:T(8,128)(2,1)S(1)}, u32[]{:S(2)}, u32[]{:S(2)}) collective-permute-start(bf16[256,512]{1,0:T(8,128)(2,1)S(1)} %pad_maximum_fusion.11), channel_id=1, source_target_pairs={{0,2},{1,3},{2,0},{3,1},{4,6},{5,7},{6,4},{7,5},{8,10},{9,11},{10,... | collective-permute-start | bytes 786440 | tf_op jit(solution)/shard_map/ppermute | solution.py:196
  31.1 6.4 %collective-permute-start.8 = (bf16[256,512]{1,0:T(8,128)(2,1)S(1)}, bf16[256,512]{1,0:T(8,128)(2,1)S(1)}, u32[]{:S(2)}, u32[]{:S(2)}) collective-permute-start(bf16[256,512]{1,0:T(8,128)(2,1)S(1)} %pad_maximum_fusion.12), channel_id=1, source_target_pairs={{0,4},{1,5},{2,6},{3,7},{4,0},{5,1},{6,2},{7,3},{8,12},{9,13},{10,... | collective-permute-start | bytes 786440 | tf_op jit(solution)/shard_map/ppermute | solution.py:196
  33.7 9.8 %collective-permute-start.13 = (bf16[256,512]{1,0:T(8,128)(2,1)S(1)}, bf16[256,512]{1,0:T(8,128)(2,1)S(1)}, u32[]{:S(2)}, u32[]{:S(2)}) collective-permute-start(bf16[256,512]{1,0:T(8,128)(2,1)S(1)} %pad_maximum_fusion.13), channel_id=1, source_target_pairs={{0,8},{1,9},{2,10},{3,11},{4,12},{5,13},{6,14},{7,15},{8,0},{9,1},... | collective-permute-start | bytes 786440 | tf_op jit(solution)/shard_map/ppermute | solution.py:196
  33.9 11.0 %collective-permute-start.18 = (bf16[256,512]{1,0:T(8,128)(2,1)S(1)}, bf16[256,512]{1,0:T(8,128)(2,1)S(1)}, u32[]{:S(2)}, u32[]{:S(2)}) collective-permute-start(bf16[256,512]{1,0:T(8,128)(2,1)S(1)} %pad_maximum_fusion.14), channel_id=1, source_target_pairs={{0,16},{1,17},{2,18},{3,19},{4,20},{5,21},{6,22},{7,23},{8,24},{9,... | collective-permute-start | bytes 786440 | tf_op jit(solution)/shard_map/ppermute | solution.py:196
  37.2 7.9 %collective-permute-start.4 = (bf16[512,512]{1,0:T(8,128)(2,1)S(1)}, bf16[512,512]{1,0:T(8,128)(2,1)S(1)}, u32[]{:S(2)}, u32[]{:S(2)}) collective-permute-start(bf16[512,512]{1,0:T(8,128)(2,1)S(1)} %pad_maximum_fusion.5), channel_id=1, source_target_pairs={{0,1},{1,0},{2,3},{3,2},{4,5},{5,4},{6,7},{7,6},{8,9},{9,8},{10,11... | collective-permute-start | bytes 1572872 | tf_op jit(solution)/shard_map/ppermute | solution.py:196
  37.6 7.8 %collective-permute-start.9 = (bf16[512,512]{1,0:T(8,128)(2,1)S(1)}, bf16[512,512]{1,0:T(8,128)(2,1)S(1)}, u32[]{:S(2)}, u32[]{:S(2)}) collective-permute-start(bf16[512,512]{1,0:T(8,128)(2,1)S(1)} %pad_maximum_fusion.6), channel_id=1, source_target_pairs={{0,1},{1,0},{2,3},{3,2},{4,5},{5,4},{6,7},{7,6},{8,9},{9,8},{10,11... | collective-permute-start | bytes 1572872 | tf_op jit(solution)/shard_map/ppermute | solution.py:196
  89.1 8.4 %collective-permute-start.22 = (bf16[256,512]{1,0:T(8,128)(2,1)S(1)}, bf16[256,512]{1,0:T(8,128)(2,1)S(1)}, u32[]{:S(2)}, u32[]{:S(2)}) collective-permute-start(bf16[256,512]{1,0:T(8,128)(2,1)S(1)} %constant_dynamic-slice_fusion.18), channel_id=1, source_target_pairs={{0,2},{1,3},{2,0},{3,1},{4,6},{5,7},{6,4},{7,5},{8,10},{9,11},{10,... | collective-permute-start | bytes 786440 | tf_op jit(solution)/shard_map/ppermute | solution.py:103
  89.9 9.2 %collective-permute-start.27 = (bf16[256,512]{1,0:T(8,128)(2,1)S(1)}, bf16[256,512]{1,0:T(8,128)(2,1)S(1)}, u32[]{:S(2)}, u32[]{:S(2)}) collective-permute-start(bf16[256,512]{1,0:T(8,128)(2,1)S(1)} %constant_dynamic-slice_fusion.13), channel_id=1, source_target_pairs={{0,4},{1,5},{2,6},{3,7},{4,0},{5,1},{6,2},{7,3},{8,12},{9,13},{10,... | collective-permute-start | bytes 786440 | tf_op jit(solution)/shard_map/ppermute | solution.py:103
  91.6 14.1 %collective-permute-start.32 = (bf16[256,512]{1,0:T(8,128)(2,1)S(1)}, bf16[256,512]{1,0:T(8,128)(2,1)S(1)}, u32[]{:S(2)}, u32[]{:S(2)}) collective-permute-start(bf16[256,512]{1,0:T(8,128)(2,1)S(1)} %constant_dynamic-slice_fusion.8), channel_id=1, source_target_pairs={{0,8},{1,9},{2,10},{3,11},{4,12},{5,13},{6,14},{7,15},{8,0},{9,1},... | collective-permute-start | bytes 786440 | tf_op jit(solution)/shard_map/ppermute | solution.py:103
  91.9 14.9 %collective-permute-start.37 = (bf16[256,512]{1,0:T(8,128)(2,1)S(1)}, bf16[256,512]{1,0:T(8,128)(2,1)S(1)}, u32[]{:S(2)}, u32[]{:S(2)}) collective-permute-start(bf16[256,512]{1,0:T(8,128)(2,1)S(1)} %constant_dynamic-slice_fusion.3), channel_id=1, source_target_pairs={{0,16},{1,17},{2,18},{3,19},{4,20},{5,21},{6,22},{7,23},{8,24},{9,... | collective-permute-start | bytes 786440 | tf_op jit(solution)/shard_map/ppermute | solution.py:103
  97.6 10.7 %collective-permute-start.23 = (bf16[128,512]{1,0:T(8,128)(2,1)S(1)}, bf16[128,512]{1,0:T(8,128)(2,1)S(1)}, u32[]{:S(2)}, u32[]{:S(2)}) collective-permute-start(bf16[128,512]{1,0:T(8,128)(2,1)S(1)} %constant_dynamic-slice_fusion.17), channel_id=1, source_target_pairs={{0,4},{1,5},{2,6},{3,7},{4,0},{5,1},{6,2},{7,3},{8,12},{9,13},{10,... | collective-permute-start | bytes 393224 | tf_op jit(solution)/shard_map/ppermute | solution.py:103
  99.3 11.1 %collective-permute-start.28 = (bf16[128,512]{1,0:T(8,128)(2,1)S(1)}, bf16[128,512]{1,0:T(8,128)(2,1)S(1)}, u32[]{:S(2)}, u32[]{:S(2)}) collective-permute-start(bf16[128,512]{1,0:T(8,128)(2,1)S(1)} %constant_dynamic-slice_fusion.12), channel_id=1, source_target_pairs={{0,8},{1,9},{2,10},{3,11},{4,12},{5,13},{6,14},{7,15},{8,0},{9,1},... | collective-permute-start | bytes 393224 | tf_op jit(solution)/shard_map/ppermute | solution.py:103
  105.9 8.2 %collective-permute-start.33 = (bf16[128,512]{1,0:T(8,128)(2,1)S(1)}, bf16[128,512]{1,0:T(8,128)(2,1)S(1)}, u32[]{:S(2)}, u32[]{:S(2)}) collective-permute-start(bf16[128,512]{1,0:T(8,128)(2,1)S(1)} %constant_dynamic-slice_fusion.7), channel_id=1, source_target_pairs={{0,16},{1,17},{2,18},{3,19},{4,20},{5,21},{6,22},{7,23},{8,24},{9,... | collective-permute-start | bytes 393224 | tf_op jit(solution)/shard_map/ppermute | solution.py:103
  106.9 9.7 %collective-permute-start.38 = (bf16[128,512]{1,0:T(8,128)(2,1)S(1)}, bf16[128,512]{1,0:T(8,128)(2,1)S(1)}, u32[]{:S(2)}, u32[]{:S(2)}) collective-permute-start(bf16[128,512]{1,0:T(8,128)(2,1)S(1)} %constant_dynamic-slice_fusion.2), channel_id=1, source_target_pairs={{0,2},{1,3},{2,0},{3,1},{4,6},{5,7},{6,4},{7,5},{8,10},{9,11},{10,... | collective-permute-start | bytes 393224 | tf_op jit(solution)/shard_map/ppermute | solution.py:103
  108.3 8.5 %collective-permute-start.24 = (bf16[64,512]{1,0:T(8,128)(2,1)S(1)}, bf16[64,512]{1,0:T(8,128)(2,1)S(1)}, u32[]{:S(2)}, u32[]{:S(2)}) collective-permute-start(bf16[64,512]{1,0:T(8,128)(2,1)S(1)} %constant_dynamic-slice_fusion.16), channel_id=1, source_target_pairs={{0,8},{1,9},{2,10},{3,11},{4,12},{5,13},{6,14},{7,15},{8,0},{9,1},... | collective-permute-start | bytes 196616 | tf_op jit(solution)/shard_map/ppermute | solution.py:103
  110.5 6.5 %collective-permute-start.29 = (bf16[64,512]{1,0:T(8,128)(2,1)S(1)}, bf16[64,512]{1,0:T(8,128)(2,1)S(1)}, u32[]{:S(2)}, u32[]{:S(2)}) collective-permute-start(bf16[64,512]{1,0:T(8,128)(2,1)S(1)} %constant_dynamic-slice_fusion.11), channel_id=1, source_target_pairs={{0,16},{1,17},{2,18},{3,19},{4,20},{5,21},{6,22},{7,23},{8,24},{9,... | collective-permute-start | bytes 196616 | tf_op jit(solution)/shard_map/ppermute | solution.py:103
  (28 other events, 237.5 us)

commit v7 on v6

--- a/solution.py
+++ b/solution.py
@@ -11,7 +11,7 @@
 PAGE = 128
 REDUCE_PARTS = 4
 SEG_MOST = 512
-CHUNK = 128
+CHUNK = 256
 
 
 def swapped(array, axis, bit):

time: 126 us -> 121 us (0.960)
  Pallas kernels: 17 us -> 12.4 us
    pallas_call x1, Pallas kernels: 17 us -> 12.4 us  [attend_window(): pl.pallas_call(lambda *refs: attention_kernel(window, *refs), grid=(block...]
where the time goes in v7:
time: 121 us
  starting transfers between devices  37.4 us (31%)
  waiting for transfers between devices  34 us (28%)
  other arithmetic  15.7 us (13%)
  matrix products  12.6 us (10%)
  Pallas kernels  12.4 us (10%)
  local copies, waits for them, and re-layouts  7.59 us (6%)
  between operations  1.51 us (1%)
    ppermute x20, starting transfers between devices, gather_from_all(): got = lax.ppermute(current, axis, [(i, i ^ 1 << k) for i in range(size)])  20.5 us
    ppermute x20, waiting for transfers between devices, reduce_to_owner(): got = lax.ppermute(send, axis, [(i, i ^ 1 << k) for i in range(size)])  19.2 us
    ppermute x20, starting transfers between devices, reduce_to_owner(): got = lax.ppermute(send, axis, [(i, i ^ 1 << k) for i in range(size)])  16.7 us
    ppermute x20, waiting for transfers between devices, gather_from_all(): got = lax.ppermute(current, axis, [(i, i ^ 1 << k) for i in range(size)])  14.7 us
    pallas_call x1, Pallas kernels, attend_window(): pl.pallas_call(lambda *refs: attention_kernel(window, *refs), grid=(block...  12.4 us
    unnamed x24, local copies, waits for them, and re-layouts  4 us
    dot_general x1, matrix products, local(): jnp.dot(normed, query_weight, preferred_element_type=jnp.float32)  3.67 us
    dot_general x1, matrix products, project_kv(): projected = jnp.dot(normed, weight, preferred_element_type=jnp.float32)  3.58 us
  transfers between devices with their start and end apart: 41, of which 18 were waited for; matrix products, arithmetic and copies ran while one was open for 13% of the time, Pallas kernels for 0%

profile of v7, /device:TPU:0, one launch (start us, length us, event | category | flops | bytes accessed | tf_op | source)
XLA Modules:
  0.0 121.1 jit_solution(13762604881667523953)
XLA Ops:
  3.6 4.1 %collective-permute-start = (bf16[32,512]{1,0:T(8,128)(2,1)S(1)}, bf16[32,512]{1,0:T(8,128)(2,1)S(1)}, u32[]{:S(2)}, u32[]{:S(2)}) collective-permute-start(bf16[32,512]{1,0:T(8,128)(2,1)S(1)} %get-tuple-element.58), channel_id=1, source_target_pairs={{0,16},{1,17},{2,18},{3,19},{4,20},{5,21},{6,22},{7,23},{8,24},{9,... | collective-permute-start | bytes 98312 | tf_op jit(solution)/shard_map/ppermute | solution.py:196
  7.7 1.5 %collective-permute-start.10 = (bf16[32,512]{1,0:T(8,128)(2,1)S(1)}, bf16[32,512]{1,0:T(8,128)(2,1)S(1)}, u32[]{:S(2)}, u32[]{:S(2)}) collective-permute-start(bf16[32,512]{1,0:T(8,128)(2,1)S(1)} %get-tuple-element.60), channel_id=1, source_target_pairs={{0,4},{1,5},{2,6},{3,7},{4,0},{5,1},{6,2},{7,3},{8,12},{9,13},{10,... | collective-permute-start | bytes 98312 | tf_op jit(solution)/shard_map/ppermute | solution.py:196
  9.2 1.6 %collective-permute-start.15 = (bf16[32,512]{1,0:T(8,128)(2,1)S(1)}, bf16[32,512]{1,0:T(8,128)(2,1)S(1)}, u32[]{:S(2)}, u32[]{:S(2)}) collective-permute-start(bf16[32,512]{1,0:T(8,128)(2,1)S(1)} %get-tuple-element.59), channel_id=1, source_target_pairs={{0,8},{1,9},{2,10},{3,11},{4,12},{5,13},{6,14},{7,15},{8,0},{9,1},... | collective-permute-start | bytes 98312 | tf_op jit(solution)/shard_map/ppermute | solution.py:196
  13.8 1.9 %fusion.15 = (f32[1024,64]{1,0:T(8,128)S(1)}, f32[1024,64]{1,0:T(8,128)S(1)}, f32[1024,64]{1,0:T(8,128)S(1)}) fusion(f32[64]{0:T(128)S(1)} %multiply_power_fusion, f32[1024]{0:T(1024)S(1)} %fusion.18), kind=kLoop, calls=%fused_computation.70 | loop fusion | flops 131072 | bytes 790784 | tf_op jit(solution)/shard_map/neg | solution.py:148
  19.9 2.7 %collective-permute-done.1 = bf16[64,512]{1,0:T(8,128)(2,1)S(1)} collective-permute-done((bf16[64,512]{1,0:T(8,128)(2,1)S(1)}, bf16[64,512]{1,0:T(8,128)(2,1)S(1)}, u32[]{:S(2)}, u32[]{:S(2)}) %collective-permute-start.1) | collective-permute-done | bytes 65568 | tf_op jit(solution)/shard_map/ppermute | solution.py:196
  24.6 1.6 %collective-permute-start.7 = (bf16[128,512]{1,0:T(8,128)(2,1)S(1)}, bf16[128,512]{1,0:T(8,128)(2,1)S(1)}, u32[]{:S(2)}, u32[]{:S(2)}) collective-permute-start(bf16[128,512]{1,0:T(8,128)(2,1)S(1)} %pad_maximum_fusion.16), channel_id=1, source_target_pairs={{0,8},{1,9},{2,10},{3,11},{4,12},{5,13},{6,14},{7,15},{8,0},{9,1},... | collective-permute-start | bytes 393224 | tf_op jit(solution)/shard_map/ppermute | solution.py:196
  31.0 1.6 %collective-permute-start.8 = (bf16[256,512]{1,0:T(8,128)(2,1)S(1)}, bf16[256,512]{1,0:T(8,128)(2,1)S(1)}, u32[]{:S(2)}, u32[]{:S(2)}) collective-permute-start(bf16[256,512]{1,0:T(8,128)(2,1)S(1)} %pad_maximum_fusion.12), channel_id=1, source_target_pairs={{0,4},{1,5},{2,6},{3,7},{4,0},{5,1},{6,2},{7,3},{8,12},{9,13},{10,... | collective-permute-start | bytes 786440 | tf_op jit(solution)/shard_map/ppermute | solution.py:196
  33.9 3.2 %collective-permute-start.18 = (bf16[256,512]{1,0:T(8,128)(2,1)S(1)}, bf16[256,512]{1,0:T(8,128)(2,1)S(1)}, u32[]{:S(2)}, u32[]{:S(2)}) collective-permute-start(bf16[256,512]{1,0:T(8,128)(2,1)S(1)} %pad_maximum_fusion.14), channel_id=1, source_target_pairs={{0,16},{1,17},{2,18},{3,19},{4,20},{5,21},{6,22},{7,23},{8,24},{9,... | collective-permute-start | bytes 786440 | tf_op jit(solution)/shard_map/ppermute | solution.py:196
  38.0 5.5 %collective-permute-done.13 = bf16[256,512]{1,0:T(8,128)(2,1)S(1)} collective-permute-done((bf16[256,512]{1,0:T(8,128)(2,1)S(1)}, bf16[256,512]{1,0:T(8,128)(2,1)S(1)}, u32[]{:S(2)}, u32[]{:S(2)}) %collective-permute-start.13) | collective-permute-done | bytes 262176 | tf_op jit(solution)/shard_map/ppermute | solution.py:196
  48.2 1.9 %copy-done.1 = bf16[1024,2048]{1,0:T(8,128)(2,1)} copy-done((bf16[1024,2048]{1,0:T(8,128)(2,1)}, bf16[1024,2048]{1,0:T(8,128)(2,1)S(1)}, u32[]{:S(2)}) %copy-start.1) | copy-done | bytes 4194328
  51.5 3.6 %fusion.26 = f32[1024,128]{1,0:T(8,128)S(1)} fusion(bf16[1024,2048]{1,0:T(8,128)(2,1)} %copy-done.1, bf16[2048,128]{1,0:T(8,128)(2,1)S(1)} %copy-done.4), kind=kOutput, calls=%fused_computation.153 | convolution fusion | flops 536870912 | bytes 5242880 | tf_op jit(solution)/shard_map/dot_general | solution.py:58
  55.1 2.4 %fusion.6 = (bf16[1024,64]{1,0:T(8,128)(2,1)S(1)}, bf16[1024,64]{1,0:T(8,128)(2,1)S(1)}) fusion(f32[1024,1,128]{2,0,1:T(8,128)S(1)} %bitcast.63, f32[64]{0:T(128)S(1)} %multiply_power_fusion, f32[1024]{0:T(1024)S(1)} %fusion.18), kind=kLoop, calls=%fused_computation.21 | loop fusion | flops 589824 | bytes 790784 | tf_op jit(solution)/shard_map/concatenate | solution.py:52
  57.9 3.7 %fusion.25.refs_0_ = f32[1024,512]{1,0:T(8,128)} fusion(bf16[1024,2048]{1,0:T(8,128)(2,1)S(1)} %copy-done.2, bf16[2048,512]{1,0:T(8,128)(2,1)S(1)} %copy-done.10), kind=kOutput, calls=%fused_computation.152 | convolution fusion | flops 2147483648 | bytes 8388608 | tf_op jit(solution)/shard_map/dot_general | solution.py:234
  64.3 12.4 %shard_map.113 = bf16[1024,512]{1,0:T(8,128)(2,1)} custom-call(f32[1024,512]{1,0:T(8,128)} %fusion.25.refs_0_, f32[1024,128]{1,0:T(8,128)} %get-tuple-element.75.refs_1_, f32[1024,128]{1,0:T(8,128)} %get-tuple-element.76.refs_2_, bf16[128,1024]{1,0:T(8,128)(2,1)} %copy.61.refs_3_, bf16[1024,128]{1,0:T(8,128)(2,1)} %get-tuple-element.24.refs_4_, ...), custom_call_target="tpu_custom_call" | custom-call | flops 1610612736 | bytes 4718592 | tf_op jit(solution)/shard_map/pallas_call | solution.py:160
  76.6 3.6 %convolution_convert_fusion = bf16[1024,2048]{1,0:T(8,128)(2,1)S(1)} fusion(bf16[1024,512]{1,0:T(8,128)(2,1)} %shard_map.113, bf16[512,2048]{1,0:T(8,128)(2,1)S(1)} %copy-done), kind=kOutput, calls=%fused_computation.1 | convolution fusion | flops 2149580800 | bytes 7340032 | tf_op jit(solution)/shard_map/dot_general | solution.py:238
  85.2 1.5 %collective-permute-start.27 = (bf16[256,512]{1,0:T(8,128)(2,1)S(1)}, bf16[256,512]{1,0:T(8,128)(2,1)S(1)}, u32[]{:S(2)}, u32[]{:S(2)}) collective-permute-start(bf16[256,512]{1,0:T(8,128)(2,1)S(1)} %constant_dynamic-slice_fusion.13), channel_id=1, source_target_pairs={{0,4},{1,5},{2,6},{3,7},{4,0},{5,1},{6,2},{7,3},{8,12},{9,13},{10,... | collective-permute-start | bytes 786440 | tf_op jit(solution)/shard_map/ppermute | solution.py:103
  87.2 2.1 %collective-permute-start.37 = (bf16[256,512]{1,0:T(8,128)(2,1)S(1)}, bf16[256,512]{1,0:T(8,128)(2,1)S(1)}, u32[]{:S(2)}, u32[]{:S(2)}) collective-permute-start(bf16[256,512]{1,0:T(8,128)(2,1)S(1)} %constant_dynamic-slice_fusion.3), channel_id=1, source_target_pairs={{0,16},{1,17},{2,18},{3,19},{4,20},{5,21},{6,22},{7,23},{8,24},{9,... | collective-permute-start | bytes 786440 | tf_op jit(solution)/shard_map/ppermute | solution.py:103
  89.4 3.5 %collective-permute-done.22 = bf16[256,512]{1,0:T(8,128)(2,1)S(1)} collective-permute-done((bf16[256,512]{1,0:T(8,128)(2,1)S(1)}, bf16[256,512]{1,0:T(8,128)(2,1)S(1)}, u32[]{:S(2)}, u32[]{:S(2)}) %collective-permute-start.22) | collective-permute-done | bytes 262176 | tf_op jit(solution)/shard_map/ppermute | solution.py:103
  92.9 1.6 %collective-permute-start.23 = (bf16[128,512]{1,0:T(8,128)(2,1)S(1)}, bf16[128,512]{1,0:T(8,128)(2,1)S(1)}, u32[]{:S(2)}, u32[]{:S(2)}) collective-permute-start(bf16[128,512]{1,0:T(8,128)(2,1)S(1)} %constant_dynamic-slice_fusion.17), channel_id=1, source_target_pairs={{0,4},{1,5},{2,6},{3,7},{4,0},{5,1},{6,2},{7,3},{8,12},{9,13},{10,... | collective-permute-start | bytes 393224 | tf_op jit(solution)/shard_map/ppermute | solution.py:103
  94.7 6.4 %collective-permute-done.32 = bf16[256,512]{1,0:T(8,128)(2,1)S(1)} collective-permute-done((bf16[256,512]{1,0:T(8,128)(2,1)S(1)}, bf16[256,512]{1,0:T(8,128)(2,1)S(1)}, u32[]{:S(2)}, u32[]{:S(2)}) %collective-permute-start.32) | collective-permute-done | bytes 262176 | tf_op jit(solution)/shard_map/ppermute | solution.py:103
  103.7 2.0 %collective-permute-start.24 = (bf16[64,512]{1,0:T(8,128)(2,1)S(1)}, bf16[64,512]{1,0:T(8,128)(2,1)S(1)}, u32[]{:S(2)}, u32[]{:S(2)}) collective-permute-start(bf16[64,512]{1,0:T(8,128)(2,1)S(1)} %constant_dynamic-slice_fusion.16), channel_id=1, source_target_pairs={{0,8},{1,9},{2,10},{3,11},{4,12},{5,13},{6,14},{7,15},{8,0},{9,1},... | collective-permute-start | bytes 196616 | tf_op jit(solution)/shard_map/ppermute | solution.py:103
  106.6 2.8 %collective-permute-done.33 = bf16[128,512]{1,0:T(8,128)(2,1)S(1)} collective-permute-done((bf16[128,512]{1,0:T(8,128)(2,1)S(1)}, bf16[128,512]{1,0:T(8,128)(2,1)S(1)}, u32[]{:S(2)}, u32[]{:S(2)}) %collective-permute-start.33) | collective-permute-done | bytes 131104 | tf_op jit(solution)/shard_map/ppermute | solution.py:103
  109.5 2.5 %collective-permute-start.34 = (bf16[64,512]{1,0:T(8,128)(2,1)S(1)}, bf16[64,512]{1,0:T(8,128)(2,1)S(1)}, u32[]{:S(2)}, u32[]{:S(2)}) collective-permute-start(bf16[64,512]{1,0:T(8,128)(2,1)S(1)} %constant_dynamic-slice_fusion.6), channel_id=1, source_target_pairs={{0,2},{1,3},{2,0},{3,1},{4,6},{5,7},{6,4},{7,5},{8,10},{9,11},{10,... | collective-permute-start | bytes 196616 | tf_op jit(solution)/shard_map/ppermute | solution.py:103
  118.3 2.1 %collective-permute-done.40 = bf16[32,512]{1,0:T(8,128)(2,1)S(1)} collective-permute-done((bf16[32,512]{1,0:T(8,128)(2,1)S(1)}, bf16[32,512]{1,0:T(8,128)(2,1)S(1)}, u32[]{:S(2)}, u32[]{:S(2)}) %collective-permute-start.40) | collective-permute-done | bytes 32800 | tf_op jit(solution)/shard_map/ppermute | solution.py:103
  (201 shorter events, 43.8 us)
Async XLA Ops:
  3.6 14.6 %collective-permute-start = (bf16[32,512]{1,0:T(8,128)(2,1)S(1)}, bf16[32,512]{1,0:T(8,128)(2,1)S(1)}, u32[]{:S(2)}, u32[]{:S(2)}) collective-permute-start(bf16[32,512]{1,0:T(8,128)(2,1)S(1)} %get-tuple-element.58), channel_id=1, source_target_pairs={{0,16},{1,17},{2,18},{3,19},{4,20},{5,21},{6,22},{7,23},{8,24},{9,... | collective-permute-start | bytes 98312 | tf_op jit(solution)/shard_map/ppermute | solution.py:196
  7.7 10.5 %collective-permute-start.10 = (bf16[32,512]{1,0:T(8,128)(2,1)S(1)}, bf16[32,512]{1,0:T(8,128)(2,1)S(1)}, u32[]{:S(2)}, u32[]{:S(2)}) collective-permute-start(bf16[32,512]{1,0:T(8,128)(2,1)S(1)} %get-tuple-element.60), channel_id=1, source_target_pairs={{0,4},{1,5},{2,6},{3,7},{4,0},{5,1},{6,2},{7,3},{8,12},{9,13},{10,... | collective-permute-start | bytes 98312 | tf_op jit(solution)/shard_map/ppermute | solution.py:196
  9.2 9.0 %collective-permute-start.15 = (bf16[32,512]{1,0:T(8,128)(2,1)S(1)}, bf16[32,512]{1,0:T(8,128)(2,1)S(1)}, u32[]{:S(2)}, u32[]{:S(2)}) collective-permute-start(bf16[32,512]{1,0:T(8,128)(2,1)S(1)} %get-tuple-element.59), channel_id=1, source_target_pairs={{0,8},{1,9},{2,10},{3,11},{4,12},{5,13},{6,14},{7,15},{8,0},{9,1},... | collective-permute-start | bytes 98312 | tf_op jit(solution)/shard_map/ppermute | solution.py:196
  10.8 7.4 %collective-permute-start.5 = (bf16[32,512]{1,0:T(8,128)(2,1)S(1)}, bf16[32,512]{1,0:T(8,128)(2,1)S(1)}, u32[]{:S(2)}, u32[]{:S(2)}) collective-permute-start(bf16[32,512]{1,0:T(8,128)(2,1)S(1)} %get-tuple-element.61), channel_id=1, source_target_pairs={{0,2},{1,3},{2,0},{3,1},{4,6},{5,7},{6,4},{7,5},{8,10},{9,11},{10,... | collective-permute-start | bytes 98312 | tf_op jit(solution)/shard_map/ppermute | solution.py:196
  19.1 7.1 %collective-permute-start.11 = (bf16[64,512]{1,0:T(8,128)(2,1)S(1)}, bf16[64,512]{1,0:T(8,128)(2,1)S(1)}, u32[]{:S(2)}, u32[]{:S(2)}) collective-permute-start(bf16[64,512]{1,0:T(8,128)(2,1)S(1)} %pad_maximum_fusion.21), channel_id=1, source_target_pairs={{0,2},{1,3},{2,0},{3,1},{4,6},{5,7},{6,4},{7,5},{8,10},{9,11},{10,... | collective-permute-start | bytes 196616 | tf_op jit(solution)/shard_map/ppermute | solution.py:196
  19.7 6.6 %collective-permute-start.16 = (bf16[64,512]{1,0:T(8,128)(2,1)S(1)}, bf16[64,512]{1,0:T(8,128)(2,1)S(1)}, u32[]{:S(2)}, u32[]{:S(2)}) collective-permute-start(bf16[64,512]{1,0:T(8,128)(2,1)S(1)} %pad_maximum_fusion.22), channel_id=1, source_target_pairs={{0,4},{1,5},{2,6},{3,7},{4,0},{5,1},{6,2},{7,3},{8,12},{9,13},{10,... | collective-permute-start | bytes 196616 | tf_op jit(solution)/shard_map/ppermute | solution.py:196
  26.3 7.3 %collective-permute-start.12 = (bf16[128,512]{1,0:T(8,128)(2,1)S(1)}, bf16[128,512]{1,0:T(8,128)(2,1)S(1)}, u32[]{:S(2)}, u32[]{:S(2)}) collective-permute-start(bf16[128,512]{1,0:T(8,128)(2,1)S(1)} %pad_maximum_fusion.17), channel_id=1, source_target_pairs={{0,16},{1,17},{2,18},{3,19},{4,20},{5,21},{6,22},{7,23},{8,24},{9,... | collective-permute-start | bytes 393224 | tf_op jit(solution)/shard_map/ppermute | solution.py:196
  27.5 6.4 %collective-permute-start.17 = (bf16[128,512]{1,0:T(8,128)(2,1)S(1)}, bf16[128,512]{1,0:T(8,128)(2,1)S(1)}, u32[]{:S(2)}, u32[]{:S(2)}) collective-permute-start(bf16[128,512]{1,0:T(8,128)(2,1)S(1)} %pad_maximum_fusion.18), channel_id=1, source_target_pairs={{0,2},{1,3},{2,0},{3,1},{4,6},{5,7},{6,4},{7,5},{8,10},{9,11},{10,... | collective-permute-start | bytes 393224 | tf_op jit(solution)/shard_map/ppermute | solution.py:196
  29.2 7.9 %collective-permute-start.3 = (bf16[256,512]{1,0:T(8,128)(2,1)S(1)}, bf16[256,512]{1,0:T(8,128)(2,1)S(1)}, u32[]{:S(2)}, u32[]{:S(2)}) collective-permute-start(bf16[256,512]{1,0:T(8,128)(2,1)S(1)} %pad_maximum_fusion.11), channel_id=1, source_target_pairs={{0,2},{1,3},{2,0},{3,1},{4,6},{5,7},{6,4},{7,5},{8,10},{9,11},{10,... | collective-permute-start | bytes 786440 | tf_op jit(solution)/shard_map/ppermute | solution.py:196
  31.0 6.4 %collective-permute-start.8 = (bf16[256,512]{1,0:T(8,128)(2,1)S(1)}, bf16[256,512]{1,0:T(8,128)(2,1)S(1)}, u32[]{:S(2)}, u32[]{:S(2)}) collective-permute-start(bf16[256,512]{1,0:T(8,128)(2,1)S(1)} %pad_maximum_fusion.12), channel_id=1, source_target_pairs={{0,4},{1,5},{2,6},{3,7},{4,0},{5,1},{6,2},{7,3},{8,12},{9,13},{10,... | collective-permute-start | bytes 786440 | tf_op jit(solution)/shard_map/ppermute | solution.py:196
  33.7 9.8 %collective-permute-start.13 = (bf16[256,512]{1,0:T(8,128)(2,1)S(1)}, bf16[256,512]{1,0:T(8,128)(2,1)S(1)}, u32[]{:S(2)}, u32[]{:S(2)}) collective-permute-start(bf16[256,512]{1,0:T(8,128)(2,1)S(1)} %pad_maximum_fusion.13), channel_id=1, source_target_pairs={{0,8},{1,9},{2,10},{3,11},{4,12},{5,13},{6,14},{7,15},{8,0},{9,1},... | collective-permute-start | bytes 786440 | tf_op jit(solution)/shard_map/ppermute | solution.py:196
  33.9 11.0 %collective-permute-start.18 = (bf16[256,512]{1,0:T(8,128)(2,1)S(1)}, bf16[256,512]{1,0:T(8,128)(2,1)S(1)}, u32[]{:S(2)}, u32[]{:S(2)}) collective-permute-start(bf16[256,512]{1,0:T(8,128)(2,1)S(1)} %pad_maximum_fusion.14), channel_id=1, source_target_pairs={{0,16},{1,17},{2,18},{3,19},{4,20},{5,21},{6,22},{7,23},{8,24},{9,... | collective-permute-start | bytes 786440 | tf_op jit(solution)/shard_map/ppermute | solution.py:196
  37.2 7.9 %collective-permute-start.4 = (bf16[512,512]{1,0:T(8,128)(2,1)S(1)}, bf16[512,512]{1,0:T(8,128)(2,1)S(1)}, u32[]{:S(2)}, u32[]{:S(2)}) collective-permute-start(bf16[512,512]{1,0:T(8,128)(2,1)S(1)} %pad_maximum_fusion.5), channel_id=1, source_target_pairs={{0,1},{1,0},{2,3},{3,2},{4,5},{5,4},{6,7},{7,6},{8,9},{9,8},{10,11... | collective-permute-start | bytes 1572872 | tf_op jit(solution)/shard_map/ppermute | solution.py:196
  37.6 7.8 %collective-permute-start.9 = (bf16[512,512]{1,0:T(8,128)(2,1)S(1)}, bf16[512,512]{1,0:T(8,128)(2,1)S(1)}, u32[]{:S(2)}, u32[]{:S(2)}) collective-permute-start(bf16[512,512]{1,0:T(8,128)(2,1)S(1)} %pad_maximum_fusion.6), channel_id=1, source_target_pairs={{0,1},{1,0},{2,3},{3,2},{4,5},{5,4},{6,7},{7,6},{8,9},{9,8},{10,11... | collective-permute-start | bytes 1572872 | tf_op jit(solution)/shard_map/ppermute | solution.py:196
  84.4 8.4 %collective-permute-start.22 = (bf16[256,512]{1,0:T(8,128)(2,1)S(1)}, bf16[256,512]{1,0:T(8,128)(2,1)S(1)}, u32[]{:S(2)}, u32[]{:S(2)}) collective-permute-start(bf16[256,512]{1,0:T(8,128)(2,1)S(1)} %constant_dynamic-slice_fusion.18), channel_id=1, source_target_pairs={{0,2},{1,3},{2,0},{3,1},{4,6},{5,7},{6,4},{7,5},{8,10},{9,11},{10,... | collective-permute-start | bytes 786440 | tf_op jit(solution)/shard_map/ppermute | solution.py:103
  85.2 9.3 %collective-permute-start.27 = (bf16[256,512]{1,0:T(8,128)(2,1)S(1)}, bf16[256,512]{1,0:T(8,128)(2,1)S(1)}, u32[]{:S(2)}, u32[]{:S(2)}) collective-permute-start(bf16[256,512]{1,0:T(8,128)(2,1)S(1)} %constant_dynamic-slice_fusion.13), channel_id=1, source_target_pairs={{0,4},{1,5},{2,6},{3,7},{4,0},{5,1},{6,2},{7,3},{8,12},{9,13},{10,... | collective-permute-start | bytes 786440 | tf_op jit(solution)/shard_map/ppermute | solution.py:103
  87.0 14.2 %collective-permute-start.32 = (bf16[256,512]{1,0:T(8,128)(2,1)S(1)}, bf16[256,512]{1,0:T(8,128)(2,1)S(1)}, u32[]{:S(2)}, u32[]{:S(2)}) collective-permute-start(bf16[256,512]{1,0:T(8,128)(2,1)S(1)} %constant_dynamic-slice_fusion.8), channel_id=1, source_target_pairs={{0,8},{1,9},{2,10},{3,11},{4,12},{5,13},{6,14},{7,15},{8,0},{9,1},... | collective-permute-start | bytes 786440 | tf_op jit(solution)/shard_map/ppermute | solution.py:103
  87.2 14.9 %collective-permute-start.37 = (bf16[256,512]{1,0:T(8,128)(2,1)S(1)}, bf16[256,512]{1,0:T(8,128)(2,1)S(1)}, u32[]{:S(2)}, u32[]{:S(2)}) collective-permute-start(bf16[256,512]{1,0:T(8,128)(2,1)S(1)} %constant_dynamic-slice_fusion.3), channel_id=1, source_target_pairs={{0,16},{1,17},{2,18},{3,19},{4,20},{5,21},{6,22},{7,23},{8,24},{9,... | collective-permute-start | bytes 786440 | tf_op jit(solution)/shard_map/ppermute | solution.py:103
  92.9 10.7 %collective-permute-start.23 = (bf16[128,512]{1,0:T(8,128)(2,1)S(1)}, bf16[128,512]{1,0:T(8,128)(2,1)S(1)}, u32[]{:S(2)}, u32[]{:S(2)}) collective-permute-start(bf16[128,512]{1,0:T(8,128)(2,1)S(1)} %constant_dynamic-slice_fusion.17), channel_id=1, source_target_pairs={{0,4},{1,5},{2,6},{3,7},{4,0},{5,1},{6,2},{7,3},{8,12},{9,13},{10,... | collective-permute-start | bytes 393224 | tf_op jit(solution)/shard_map/ppermute | solution.py:103
  94.6 11.1 %collective-permute-start.28 = (bf16[128,512]{1,0:T(8,128)(2,1)S(1)}, bf16[128,512]{1,0:T(8,128)(2,1)S(1)}, u32[]{:S(2)}, u32[]{:S(2)}) collective-permute-start(bf16[128,512]{1,0:T(8,128)(2,1)S(1)} %constant_dynamic-slice_fusion.12), channel_id=1, source_target_pairs={{0,8},{1,9},{2,10},{3,11},{4,12},{5,13},{6,14},{7,15},{8,0},{9,1},... | collective-permute-start | bytes 393224 | tf_op jit(solution)/shard_map/ppermute | solution.py:103
  101.2 8.2 %collective-permute-start.33 = (bf16[128,512]{1,0:T(8,128)(2,1)S(1)}, bf16[128,512]{1,0:T(8,128)(2,1)S(1)}, u32[]{:S(2)}, u32[]{:S(2)}) collective-permute-start(bf16[128,512]{1,0:T(8,128)(2,1)S(1)} %constant_dynamic-slice_fusion.7), channel_id=1, source_target_pairs={{0,16},{1,17},{2,18},{3,19},{4,20},{5,21},{6,22},{7,23},{8,24},{9,... | collective-permute-start | bytes 393224 | tf_op jit(solution)/shard_map/ppermute | solution.py:103
  102.2 9.8 %collective-permute-start.38 = (bf16[128,512]{1,0:T(8,128)(2,1)S(1)}, bf16[128,512]{1,0:T(8,128)(2,1)S(1)}, u32[]{:S(2)}, u32[]{:S(2)}) collective-permute-start(bf16[128,512]{1,0:T(8,128)(2,1)S(1)} %constant_dynamic-slice_fusion.2), channel_id=1, source_target_pairs={{0,2},{1,3},{2,0},{3,1},{4,6},{5,7},{6,4},{7,5},{8,10},{9,11},{10,... | collective-permute-start | bytes 393224 | tf_op jit(solution)/shard_map/ppermute | solution.py:103
  103.7 8.4 %collective-permute-start.24 = (bf16[64,512]{1,0:T(8,128)(2,1)S(1)}, bf16[64,512]{1,0:T(8,128)(2,1)S(1)}, u32[]{:S(2)}, u32[]{:S(2)}) collective-permute-start(bf16[64,512]{1,0:T(8,128)(2,1)S(1)} %constant_dynamic-slice_fusion.16), channel_id=1, source_target_pairs={{0,8},{1,9},{2,10},{3,11},{4,12},{5,13},{6,14},{7,15},{8,0},{9,1},... | collective-permute-start | bytes 196616 | tf_op jit(solution)/shard_map/ppermute | solution.py:103
  105.8 6.5 %collective-permute-start.29 = (bf16[64,512]{1,0:T(8,128)(2,1)S(1)}, bf16[64,512]{1,0:T(8,128)(2,1)S(1)}, u32[]{:S(2)}, u32[]{:S(2)}) collective-permute-start(bf16[64,512]{1,0:T(8,128)(2,1)S(1)} %constant_dynamic-slice_fusion.11), channel_id=1, source_target_pairs={{0,16},{1,17},{2,18},{3,19},{4,20},{5,21},{6,22},{7,23},{8,24},{9,... | collective-permute-start | bytes 196616 | tf_op jit(solution)/shard_map/ppermute | solution.py:103
  (28 other events, 232.8 us)

commit v8 on v7

--- a/solution.py
+++ b/solution.py
@@ -11,7 +11,7 @@
 PAGE = 128
 REDUCE_PARTS = 4
 SEG_MOST = 512
-CHUNK = 256
+CHUNK = 512
 
 
 def swapped(array, axis, bit):

time: 121 us -> 123 us (1.017)
  no operation moved by 1% of the time
where the time goes in v8:
time: 123 us; the launch traced here: 122 us
  starting transfers between devices  37.4 us (30%)
  waiting for transfers between devices  34 us (28%)
  other arithmetic  15.7 us (13%)
  Pallas kernels  13.5 us (11%)
  matrix products  12.6 us (10%)
  local copies, waits for them, and re-layouts  7.59 us (6%)
  between operations  1.5 us (1%)
    ppermute x20, starting transfers between devices, gather_from_all(): got = lax.ppermute(current, axis, [(i, i ^ 1 << k) for i in range(size)])  20.5 us
    ppermute x20, waiting for transfers between devices, reduce_to_owner(): got = lax.ppermute(send, axis, [(i, i ^ 1 << k) for i in range(size)])  19.2 us
    ppermute x20, starting transfers between devices, reduce_to_owner(): got = lax.ppermute(send, axis, [(i, i ^ 1 << k) for i in range(size)])  16.8 us
    ppermute x20, waiting for transfers between devices, gather_from_all(): got = lax.ppermute(current, axis, [(i, i ^ 1 << k) for i in range(size)])  14.7 us
    pallas_call x1, Pallas kernels, attend_window(): pl.pallas_call(lambda *refs: attention_kernel(window, *refs), grid=(block...  13.5 us
    unnamed x24, local copies, waits for them, and re-layouts  4 us
    dot_general x1, matrix products, local(): jnp.dot(normed, query_weight, preferred_element_type=jnp.float32)  3.67 us
    dot_general x1, matrix products, project_kv(): projected = jnp.dot(normed, weight, preferred_element_type=jnp.float32)  3.58 us
  transfers between devices with their start and end apart: 41, of which 18 were waited for; matrix products, arithmetic and copies ran while one was open for 13% of the time, Pallas kernels for 0%

profile of v8, /device:TPU:0, one launch (start us, length us, event | category | flops | bytes accessed | tf_op | source)
XLA Modules:
  0.0 122.3 jit_solution(16174193313804486489)
XLA Ops:
  3.6 4.1 %collective-permute-start = (bf16[32,512]{1,0:T(8,128)(2,1)S(1)}, bf16[32,512]{1,0:T(8,128)(2,1)S(1)}, u32[]{:S(2)}, u32[]{:S(2)}) collective-permute-start(bf16[32,512]{1,0:T(8,128)(2,1)S(1)} %get-tuple-element.58), channel_id=1, source_target_pairs={{0,16},{1,17},{2,18},{3,19},{4,20},{5,21},{6,22},{7,23},{8,24},{9,... | collective-permute-start | bytes 98312 | tf_op jit(solution)/shard_map/ppermute | solution.py:196
  7.7 1.5 %collective-permute-start.10 = (bf16[32,512]{1,0:T(8,128)(2,1)S(1)}, bf16[32,512]{1,0:T(8,128)(2,1)S(1)}, u32[]{:S(2)}, u32[]{:S(2)}) collective-permute-start(bf16[32,512]{1,0:T(8,128)(2,1)S(1)} %get-tuple-element.60), channel_id=1, source_target_pairs={{0,4},{1,5},{2,6},{3,7},{4,0},{5,1},{6,2},{7,3},{8,12},{9,13},{10,... | collective-permute-start | bytes 98312 | tf_op jit(solution)/shard_map/ppermute | solution.py:196
  9.2 1.6 %collective-permute-start.15 = (bf16[32,512]{1,0:T(8,128)(2,1)S(1)}, bf16[32,512]{1,0:T(8,128)(2,1)S(1)}, u32[]{:S(2)}, u32[]{:S(2)}) collective-permute-start(bf16[32,512]{1,0:T(8,128)(2,1)S(1)} %get-tuple-element.59), channel_id=1, source_target_pairs={{0,8},{1,9},{2,10},{3,11},{4,12},{5,13},{6,14},{7,15},{8,0},{9,1},... | collective-permute-start | bytes 98312 | tf_op jit(solution)/shard_map/ppermute | solution.py:196
  13.8 1.9 %fusion.15 = (f32[1024,64]{1,0:T(8,128)S(1)}, f32[1024,64]{1,0:T(8,128)S(1)}, f32[1024,64]{1,0:T(8,128)S(1)}) fusion(f32[64]{0:T(128)S(1)} %multiply_power_fusion, f32[1024]{0:T(1024)S(1)} %fusion.18), kind=kLoop, calls=%fused_computation.70 | loop fusion | flops 131072 | bytes 790784 | tf_op jit(solution)/shard_map/neg | solution.py:148
  19.9 2.7 %collective-permute-done.1 = bf16[64,512]{1,0:T(8,128)(2,1)S(1)} collective-permute-done((bf16[64,512]{1,0:T(8,128)(2,1)S(1)}, bf16[64,512]{1,0:T(8,128)(2,1)S(1)}, u32[]{:S(2)}, u32[]{:S(2)}) %collective-permute-start.1) | collective-permute-done | bytes 65568 | tf_op jit(solution)/shard_map/ppermute | solution.py:196
  24.6 1.6 %collective-permute-start.7 = (bf16[128,512]{1,0:T(8,128)(2,1)S(1)}, bf16[128,512]{1,0:T(8,128)(2,1)S(1)}, u32[]{:S(2)}, u32[]{:S(2)}) collective-permute-start(bf16[128,512]{1,0:T(8,128)(2,1)S(1)} %pad_maximum_fusion.16), channel_id=1, source_target_pairs={{0,8},{1,9},{2,10},{3,11},{4,12},{5,13},{6,14},{7,15},{8,0},{9,1},... | collective-permute-start | bytes 393224 | tf_op jit(solution)/shard_map/ppermute | solution.py:196
  31.0 1.6 %collective-permute-start.8 = (bf16[256,512]{1,0:T(8,128)(2,1)S(1)}, bf16[256,512]{1,0:T(8,128)(2,1)S(1)}, u32[]{:S(2)}, u32[]{:S(2)}) collective-permute-start(bf16[256,512]{1,0:T(8,128)(2,1)S(1)} %pad_maximum_fusion.12), channel_id=1, source_target_pairs={{0,4},{1,5},{2,6},{3,7},{4,0},{5,1},{6,2},{7,3},{8,12},{9,13},{10,... | collective-permute-start | bytes 786440 | tf_op jit(solution)/shard_map/ppermute | solution.py:196
  33.9 3.2 %collective-permute-start.18 = (bf16[256,512]{1,0:T(8,128)(2,1)S(1)}, bf16[256,512]{1,0:T(8,128)(2,1)S(1)}, u32[]{:S(2)}, u32[]{:S(2)}) collective-permute-start(bf16[256,512]{1,0:T(8,128)(2,1)S(1)} %pad_maximum_fusion.14), channel_id=1, source_target_pairs={{0,16},{1,17},{2,18},{3,19},{4,20},{5,21},{6,22},{7,23},{8,24},{9,... | collective-permute-start | bytes 786440 | tf_op jit(solution)/shard_map/ppermute | solution.py:196
  38.0 5.5 %collective-permute-done.13 = bf16[256,512]{1,0:T(8,128)(2,1)S(1)} collective-permute-done((bf16[256,512]{1,0:T(8,128)(2,1)S(1)}, bf16[256,512]{1,0:T(8,128)(2,1)S(1)}, u32[]{:S(2)}, u32[]{:S(2)}) %collective-permute-start.13) | collective-permute-done | bytes 262176 | tf_op jit(solution)/shard_map/ppermute | solution.py:196
  48.2 1.9 %copy-done.1 = bf16[1024,2048]{1,0:T(8,128)(2,1)} copy-done((bf16[1024,2048]{1,0:T(8,128)(2,1)}, bf16[1024,2048]{1,0:T(8,128)(2,1)S(1)}, u32[]{:S(2)}) %copy-start.1) | copy-done | bytes 4194328
  51.5 3.6 %fusion.26 = f32[1024,128]{1,0:T(8,128)S(1)} fusion(bf16[1024,2048]{1,0:T(8,128)(2,1)} %copy-done.1, bf16[2048,128]{1,0:T(8,128)(2,1)S(1)} %copy-done.4), kind=kOutput, calls=%fused_computation.153 | convolution fusion | flops 536870912 | bytes 5242880 | tf_op jit(solution)/shard_map/dot_general | solution.py:58
  55.1 2.4 %fusion.6 = (bf16[1024,64]{1,0:T(8,128)(2,1)S(1)}, bf16[1024,64]{1,0:T(8,128)(2,1)S(1)}) fusion(f32[1024,1,128]{2,0,1:T(8,128)S(1)} %bitcast.63, f32[64]{0:T(128)S(1)} %multiply_power_fusion, f32[1024]{0:T(1024)S(1)} %fusion.18), kind=kLoop, calls=%fused_computation.21 | loop fusion | flops 589824 | bytes 790784 | tf_op jit(solution)/shard_map/concatenate | solution.py:52
  57.9 3.7 %fusion.25.refs_0_ = f32[1024,512]{1,0:T(8,128)} fusion(bf16[1024,2048]{1,0:T(8,128)(2,1)S(1)} %copy-done.2, bf16[2048,512]{1,0:T(8,128)(2,1)S(1)} %copy-done.10), kind=kOutput, calls=%fused_computation.152 | convolution fusion | flops 2147483648 | bytes 8388608 | tf_op jit(solution)/shard_map/dot_general | solution.py:234
  64.3 13.5 %shard_map.113 = bf16[1024,512]{1,0:T(8,128)(2,1)} custom-call(f32[1024,512]{1,0:T(8,128)} %fusion.25.refs_0_, f32[1024,128]{1,0:T(8,128)} %get-tuple-element.75.refs_1_, f32[1024,128]{1,0:T(8,128)} %get-tuple-element.76.refs_2_, bf16[128,1024]{1,0:T(8,128)(2,1)} %copy.61.refs_3_, bf16[1024,128]{1,0:T(8,128)(2,1)} %get-tuple-element.24.refs_4_, ...), custom_call_target="tpu_custom_call" | custom-call | flops 2147483648 | bytes 4718592 | tf_op jit(solution)/shard_map/pallas_call | solution.py:160
  77.7 3.6 %convolution_convert_fusion = bf16[1024,2048]{1,0:T(8,128)(2,1)S(1)} fusion(bf16[1024,512]{1,0:T(8,128)(2,1)} %shard_map.113, bf16[512,2048]{1,0:T(8,128)(2,1)S(1)} %copy-done), kind=kOutput, calls=%fused_computation.1 | convolution fusion | flops 2149580800 | bytes 7340032 | tf_op jit(solution)/shard_map/dot_general | solution.py:238
  86.4 1.5 %collective-permute-start.27 = (bf16[256,512]{1,0:T(8,128)(2,1)S(1)}, bf16[256,512]{1,0:T(8,128)(2,1)S(1)}, u32[]{:S(2)}, u32[]{:S(2)}) collective-permute-start(bf16[256,512]{1,0:T(8,128)(2,1)S(1)} %constant_dynamic-slice_fusion.13), channel_id=1, source_target_pairs={{0,4},{1,5},{2,6},{3,7},{4,0},{5,1},{6,2},{7,3},{8,12},{9,13},{10,... | collective-permute-start | bytes 786440 | tf_op jit(solution)/shard_map/ppermute | solution.py:103
  88.4 2.1 %collective-permute-start.37 = (bf16[256,512]{1,0:T(8,128)(2,1)S(1)}, bf16[256,512]{1,0:T(8,128)(2,1)S(1)}, u32[]{:S(2)}, u32[]{:S(2)}) collective-permute-start(bf16[256,512]{1,0:T(8,128)(2,1)S(1)} %constant_dynamic-slice_fusion.3), channel_id=1, source_target_pairs={{0,16},{1,17},{2,18},{3,19},{4,20},{5,21},{6,22},{7,23},{8,24},{9,... | collective-permute-start | bytes 786440 | tf_op jit(solution)/shard_map/ppermute | solution.py:103
  90.5 3.5 %collective-permute-done.22 = bf16[256,512]{1,0:T(8,128)(2,1)S(1)} collective-permute-done((bf16[256,512]{1,0:T(8,128)(2,1)S(1)}, bf16[256,512]{1,0:T(8,128)(2,1)S(1)}, u32[]{:S(2)}, u32[]{:S(2)}) %collective-permute-start.22) | collective-permute-done | bytes 262176 | tf_op jit(solution)/shard_map/ppermute | solution.py:103
  94.1 1.6 %collective-permute-start.23 = (bf16[128,512]{1,0:T(8,128)(2,1)S(1)}, bf16[128,512]{1,0:T(8,128)(2,1)S(1)}, u32[]{:S(2)}, u32[]{:S(2)}) collective-permute-start(bf16[128,512]{1,0:T(8,128)(2,1)S(1)} %constant_dynamic-slice_fusion.17), channel_id=1, source_target_pairs={{0,4},{1,5},{2,6},{3,7},{4,0},{5,1},{6,2},{7,3},{8,12},{9,13},{10,... | collective-permute-start | bytes 393224 | tf_op jit(solution)/shard_map/ppermute | solution.py:103
  95.8 6.4 %collective-permute-done.32 = bf16[256,512]{1,0:T(8,128)(2,1)S(1)} collective-permute-done((bf16[256,512]{1,0:T(8,128)(2,1)S(1)}, bf16[256,512]{1,0:T(8,128)(2,1)S(1)}, u32[]{:S(2)}, u32[]{:S(2)}) %collective-permute-start.32) | collective-permute-done | bytes 262176 | tf_op jit(solution)/shard_map/ppermute | solution.py:103
  104.9 2.0 %collective-permute-start.24 = (bf16[64,512]{1,0:T(8,128)(2,1)S(1)}, bf16[64,512]{1,0:T(8,128)(2,1)S(1)}, u32[]{:S(2)}, u32[]{:S(2)}) collective-permute-start(bf16[64,512]{1,0:T(8,128)(2,1)S(1)} %constant_dynamic-slice_fusion.16), channel_id=1, source_target_pairs={{0,8},{1,9},{2,10},{3,11},{4,12},{5,13},{6,14},{7,15},{8,0},{9,1},... | collective-permute-start | bytes 196616 | tf_op jit(solution)/shard_map/ppermute | solution.py:103
  107.8 2.8 %collective-permute-done.33 = bf16[128,512]{1,0:T(8,128)(2,1)S(1)} collective-permute-done((bf16[128,512]{1,0:T(8,128)(2,1)S(1)}, bf16[128,512]{1,0:T(8,128)(2,1)S(1)}, u32[]{:S(2)}, u32[]{:S(2)}) %collective-permute-start.33) | collective-permute-done | bytes 131104 | tf_op jit(solution)/shard_map/ppermute | solution.py:103
  110.6 2.5 %collective-permute-start.34 = (bf16[64,512]{1,0:T(8,128)(2,1)S(1)}, bf16[64,512]{1,0:T(8,128)(2,1)S(1)}, u32[]{:S(2)}, u32[]{:S(2)}) collective-permute-start(bf16[64,512]{1,0:T(8,128)(2,1)S(1)} %constant_dynamic-slice_fusion.6), channel_id=1, source_target_pairs={{0,2},{1,3},{2,0},{3,1},{4,6},{5,7},{6,4},{7,5},{8,10},{9,11},{10,... | collective-permute-start | bytes 196616 | tf_op jit(solution)/shard_map/ppermute | solution.py:103
  119.4 2.1 %collective-permute-done.40 = bf16[32,512]{1,0:T(8,128)(2,1)S(1)} collective-permute-done((bf16[32,512]{1,0:T(8,128)(2,1)S(1)}, bf16[32,512]{1,0:T(8,128)(2,1)S(1)}, u32[]{:S(2)}, u32[]{:S(2)}) %collective-permute-start.40) | collective-permute-done | bytes 32800 | tf_op jit(solution)/shard_map/ppermute | solution.py:103
  (201 shorter events, 43.9 us)
Async XLA Ops:
  3.6 14.6 %collective-permute-start = (bf16[32,512]{1,0:T(8,128)(2,1)S(1)}, bf16[32,512]{1,0:T(8,128)(2,1)S(1)}, u32[]{:S(2)}, u32[]{:S(2)}) collective-permute-start(bf16[32,512]{1,0:T(8,128)(2,1)S(1)} %get-tuple-element.58), channel_id=1, source_target_pairs={{0,16},{1,17},{2,18},{3,19},{4,20},{5,21},{6,22},{7,23},{8,24},{9,... | collective-permute-start | bytes 98312 | tf_op jit(solution)/shard_map/ppermute | solution.py:196
  7.7 10.5 %collective-permute-start.10 = (bf16[32,512]{1,0:T(8,128)(2,1)S(1)}, bf16[32,512]{1,0:T(8,128)(2,1)S(1)}, u32[]{:S(2)}, u32[]{:S(2)}) collective-permute-start(bf16[32,512]{1,0:T(8,128)(2,1)S(1)} %get-tuple-element.60), channel_id=1, source_target_pairs={{0,4},{1,5},{2,6},{3,7},{4,0},{5,1},{6,2},{7,3},{8,12},{9,13},{10,... | collective-permute-start | bytes 98312 | tf_op jit(solution)/shard_map/ppermute | solution.py:196
  9.2 9.0 %collective-permute-start.15 = (bf16[32,512]{1,0:T(8,128)(2,1)S(1)}, bf16[32,512]{1,0:T(8,128)(2,1)S(1)}, u32[]{:S(2)}, u32[]{:S(2)}) collective-permute-start(bf16[32,512]{1,0:T(8,128)(2,1)S(1)} %get-tuple-element.59), channel_id=1, source_target_pairs={{0,8},{1,9},{2,10},{3,11},{4,12},{5,13},{6,14},{7,15},{8,0},{9,1},... | collective-permute-start | bytes 98312 | tf_op jit(solution)/shard_map/ppermute | solution.py:196
  10.8 7.4 %collective-permute-start.5 = (bf16[32,512]{1,0:T(8,128)(2,1)S(1)}, bf16[32,512]{1,0:T(8,128)(2,1)S(1)}, u32[]{:S(2)}, u32[]{:S(2)}) collective-permute-start(bf16[32,512]{1,0:T(8,128)(2,1)S(1)} %get-tuple-element.61), channel_id=1, source_target_pairs={{0,2},{1,3},{2,0},{3,1},{4,6},{5,7},{6,4},{7,5},{8,10},{9,11},{10,... | collective-permute-start | bytes 98312 | tf_op jit(solution)/shard_map/ppermute | solution.py:196
  19.1 7.1 %collective-permute-start.11 = (bf16[64,512]{1,0:T(8,128)(2,1)S(1)}, bf16[64,512]{1,0:T(8,128)(2,1)S(1)}, u32[]{:S(2)}, u32[]{:S(2)}) collective-permute-start(bf16[64,512]{1,0:T(8,128)(2,1)S(1)} %pad_maximum_fusion.21), channel_id=1, source_target_pairs={{0,2},{1,3},{2,0},{3,1},{4,6},{5,7},{6,4},{7,5},{8,10},{9,11},{10,... | collective-permute-start | bytes 196616 | tf_op jit(solution)/shard_map/ppermute | solution.py:196
  19.7 6.6 %collective-permute-start.16 = (bf16[64,512]{1,0:T(8,128)(2,1)S(1)}, bf16[64,512]{1,0:T(8,128)(2,1)S(1)}, u32[]{:S(2)}, u32[]{:S(2)}) collective-permute-start(bf16[64,512]{1,0:T(8,128)(2,1)S(1)} %pad_maximum_fusion.22), channel_id=1, source_target_pairs={{0,4},{1,5},{2,6},{3,7},{4,0},{5,1},{6,2},{7,3},{8,12},{9,13},{10,... | collective-permute-start | bytes 196616 | tf_op jit(solution)/shard_map/ppermute | solution.py:196
  26.3 7.3 %collective-permute-start.12 = (bf16[128,512]{1,0:T(8,128)(2,1)S(1)}, bf16[128,512]{1,0:T(8,128)(2,1)S(1)}, u32[]{:S(2)}, u32[]{:S(2)}) collective-permute-start(bf16[128,512]{1,0:T(8,128)(2,1)S(1)} %pad_maximum_fusion.17), channel_id=1, source_target_pairs={{0,16},{1,17},{2,18},{3,19},{4,20},{5,21},{6,22},{7,23},{8,24},{9,... | collective-permute-start | bytes 393224 | tf_op jit(solution)/shard_map/ppermute | solution.py:196
  27.5 6.4 %collective-permute-start.17 = (bf16[128,512]{1,0:T(8,128)(2,1)S(1)}, bf16[128,512]{1,0:T(8,128)(2,1)S(1)}, u32[]{:S(2)}, u32[]{:S(2)}) collective-permute-start(bf16[128,512]{1,0:T(8,128)(2,1)S(1)} %pad_maximum_fusion.18), channel_id=1, source_target_pairs={{0,2},{1,3},{2,0},{3,1},{4,6},{5,7},{6,4},{7,5},{8,10},{9,11},{10,... | collective-permute-start | bytes 393224 | tf_op jit(solution)/shard_map/ppermute | solution.py:196
  29.2 7.9 %collective-permute-start.3 = (bf16[256,512]{1,0:T(8,128)(2,1)S(1)}, bf16[256,512]{1,0:T(8,128)(2,1)S(1)}, u32[]{:S(2)}, u32[]{:S(2)}) collective-permute-start(bf16[256,512]{1,0:T(8,128)(2,1)S(1)} %pad_maximum_fusion.11), channel_id=1, source_target_pairs={{0,2},{1,3},{2,0},{3,1},{4,6},{5,7},{6,4},{7,5},{8,10},{9,11},{10,... | collective-permute-start | bytes 786440 | tf_op jit(solution)/shard_map/ppermute | solution.py:196
  31.0 6.4 %collective-permute-start.8 = (bf16[256,512]{1,0:T(8,128)(2,1)S(1)}, bf16[256,512]{1,0:T(8,128)(2,1)S(1)}, u32[]{:S(2)}, u32[]{:S(2)}) collective-permute-start(bf16[256,512]{1,0:T(8,128)(2,1)S(1)} %pad_maximum_fusion.12), channel_id=1, source_target_pairs={{0,4},{1,5},{2,6},{3,7},{4,0},{5,1},{6,2},{7,3},{8,12},{9,13},{10,... | collective-permute-start | bytes 786440 | tf_op jit(solution)/shard_map/ppermute | solution.py:196
  33.7 9.8 %collective-permute-start.13 = (bf16[256,512]{1,0:T(8,128)(2,1)S(1)}, bf16[256,512]{1,0:T(8,128)(2,1)S(1)}, u32[]{:S(2)}, u32[]{:S(2)}) collective-permute-start(bf16[256,512]{1,0:T(8,128)(2,1)S(1)} %pad_maximum_fusion.13), channel_id=1, source_target_pairs={{0,8},{1,9},{2,10},{3,11},{4,12},{5,13},{6,14},{7,15},{8,0},{9,1},... | collective-permute-start | bytes 786440 | tf_op jit(solution)/shard_map/ppermute | solution.py:196
  33.9 11.0 %collective-permute-start.18 = (bf16[256,512]{1,0:T(8,128)(2,1)S(1)}, bf16[256,512]{1,0:T(8,128)(2,1)S(1)}, u32[]{:S(2)}, u32[]{:S(2)}) collective-permute-start(bf16[256,512]{1,0:T(8,128)(2,1)S(1)} %pad_maximum_fusion.14), channel_id=1, source_target_pairs={{0,16},{1,17},{2,18},{3,19},{4,20},{5,21},{6,22},{7,23},{8,24},{9,... | collective-permute-start | bytes 786440 | tf_op jit(solution)/shard_map/ppermute | solution.py:196
  37.2 7.9 %collective-permute-start.4 = (bf16[512,512]{1,0:T(8,128)(2,1)S(1)}, bf16[512,512]{1,0:T(8,128)(2,1)S(1)}, u32[]{:S(2)}, u32[]{:S(2)}) collective-permute-start(bf16[512,512]{1,0:T(8,128)(2,1)S(1)} %pad_maximum_fusion.5), channel_id=1, source_target_pairs={{0,1},{1,0},{2,3},{3,2},{4,5},{5,4},{6,7},{7,6},{8,9},{9,8},{10,11... | collective-permute-start | bytes 1572872 | tf_op jit(solution)/shard_map/ppermute | solution.py:196
  37.6 7.8 %collective-permute-start.9 = (bf16[512,512]{1,0:T(8,128)(2,1)S(1)}, bf16[512,512]{1,0:T(8,128)(2,1)S(1)}, u32[]{:S(2)}, u32[]{:S(2)}) collective-permute-start(bf16[512,512]{1,0:T(8,128)(2,1)S(1)} %pad_maximum_fusion.6), channel_id=1, source_target_pairs={{0,1},{1,0},{2,3},{3,2},{4,5},{5,4},{6,7},{7,6},{8,9},{9,8},{10,11... | collective-permute-start | bytes 1572872 | tf_op jit(solution)/shard_map/ppermute | solution.py:196
  85.5 8.4 %collective-permute-start.22 = (bf16[256,512]{1,0:T(8,128)(2,1)S(1)}, bf16[256,512]{1,0:T(8,128)(2,1)S(1)}, u32[]{:S(2)}, u32[]{:S(2)}) collective-permute-start(bf16[256,512]{1,0:T(8,128)(2,1)S(1)} %constant_dynamic-slice_fusion.18), channel_id=1, source_target_pairs={{0,2},{1,3},{2,0},{3,1},{4,6},{5,7},{6,4},{7,5},{8,10},{9,11},{10,... | collective-permute-start | bytes 786440 | tf_op jit(solution)/shard_map/ppermute | solution.py:103
  86.4 9.3 %collective-permute-start.27 = (bf16[256,512]{1,0:T(8,128)(2,1)S(1)}, bf16[256,512]{1,0:T(8,128)(2,1)S(1)}, u32[]{:S(2)}, u32[]{:S(2)}) collective-permute-start(bf16[256,512]{1,0:T(8,128)(2,1)S(1)} %constant_dynamic-slice_fusion.13), channel_id=1, source_target_pairs={{0,4},{1,5},{2,6},{3,7},{4,0},{5,1},{6,2},{7,3},{8,12},{9,13},{10,... | collective-permute-start | bytes 786440 | tf_op jit(solution)/shard_map/ppermute | solution.py:103
  88.1 14.2 %collective-permute-start.32 = (bf16[256,512]{1,0:T(8,128)(2,1)S(1)}, bf16[256,512]{1,0:T(8,128)(2,1)S(1)}, u32[]{:S(2)}, u32[]{:S(2)}) collective-permute-start(bf16[256,512]{1,0:T(8,128)(2,1)S(1)} %constant_dynamic-slice_fusion.8), channel_id=1, source_target_pairs={{0,8},{1,9},{2,10},{3,11},{4,12},{5,13},{6,14},{7,15},{8,0},{9,1},... | collective-permute-start | bytes 786440 | tf_op jit(solution)/shard_map/ppermute | solution.py:103
  88.4 14.9 %collective-permute-start.37 = (bf16[256,512]{1,0:T(8,128)(2,1)S(1)}, bf16[256,512]{1,0:T(8,128)(2,1)S(1)}, u32[]{:S(2)}, u32[]{:S(2)}) collective-permute-start(bf16[256,512]{1,0:T(8,128)(2,1)S(1)} %constant_dynamic-slice_fusion.3), channel_id=1, source_target_pairs={{0,16},{1,17},{2,18},{3,19},{4,20},{5,21},{6,22},{7,23},{8,24},{9,... | collective-permute-start | bytes 786440 | tf_op jit(solution)/shard_map/ppermute | solution.py:103
  94.1 10.7 %collective-permute-start.23 = (bf16[128,512]{1,0:T(8,128)(2,1)S(1)}, bf16[128,512]{1,0:T(8,128)(2,1)S(1)}, u32[]{:S(2)}, u32[]{:S(2)}) collective-permute-start(bf16[128,512]{1,0:T(8,128)(2,1)S(1)} %constant_dynamic-slice_fusion.17), channel_id=1, source_target_pairs={{0,4},{1,5},{2,6},{3,7},{4,0},{5,1},{6,2},{7,3},{8,12},{9,13},{10,... | collective-permute-start | bytes 393224 | tf_op jit(solution)/shard_map/ppermute | solution.py:103
  95.8 11.1 %collective-permute-start.28 = (bf16[128,512]{1,0:T(8,128)(2,1)S(1)}, bf16[128,512]{1,0:T(8,128)(2,1)S(1)}, u32[]{:S(2)}, u32[]{:S(2)}) collective-permute-start(bf16[128,512]{1,0:T(8,128)(2,1)S(1)} %constant_dynamic-slice_fusion.12), channel_id=1, source_target_pairs={{0,8},{1,9},{2,10},{3,11},{4,12},{5,13},{6,14},{7,15},{8,0},{9,1},... | collective-permute-start | bytes 393224 | tf_op jit(solution)/shard_map/ppermute | solution.py:103
  102.3 8.2 %collective-permute-start.33 = (bf16[128,512]{1,0:T(8,128)(2,1)S(1)}, bf16[128,512]{1,0:T(8,128)(2,1)S(1)}, u32[]{:S(2)}, u32[]{:S(2)}) collective-permute-start(bf16[128,512]{1,0:T(8,128)(2,1)S(1)} %constant_dynamic-slice_fusion.7), channel_id=1, source_target_pairs={{0,16},{1,17},{2,18},{3,19},{4,20},{5,21},{6,22},{7,23},{8,24},{9,... | collective-permute-start | bytes 393224 | tf_op jit(solution)/shard_map/ppermute | solution.py:103
  103.4 9.8 %collective-permute-start.38 = (bf16[128,512]{1,0:T(8,128)(2,1)S(1)}, bf16[128,512]{1,0:T(8,128)(2,1)S(1)}, u32[]{:S(2)}, u32[]{:S(2)}) collective-permute-start(bf16[128,512]{1,0:T(8,128)(2,1)S(1)} %constant_dynamic-slice_fusion.2), channel_id=1, source_target_pairs={{0,2},{1,3},{2,0},{3,1},{4,6},{5,7},{6,4},{7,5},{8,10},{9,11},{10,... | collective-permute-start | bytes 393224 | tf_op jit(solution)/shard_map/ppermute | solution.py:103
  104.9 8.4 %collective-permute-start.24 = (bf16[64,512]{1,0:T(8,128)(2,1)S(1)}, bf16[64,512]{1,0:T(8,128)(2,1)S(1)}, u32[]{:S(2)}, u32[]{:S(2)}) collective-permute-start(bf16[64,512]{1,0:T(8,128)(2,1)S(1)} %constant_dynamic-slice_fusion.16), channel_id=1, source_target_pairs={{0,8},{1,9},{2,10},{3,11},{4,12},{5,13},{6,14},{7,15},{8,0},{9,1},... | collective-permute-start | bytes 196616 | tf_op jit(solution)/shard_map/ppermute | solution.py:103
  106.9 6.5 %collective-permute-start.29 = (bf16[64,512]{1,0:T(8,128)(2,1)S(1)}, bf16[64,512]{1,0:T(8,128)(2,1)S(1)}, u32[]{:S(2)}, u32[]{:S(2)}) collective-permute-start(bf16[64,512]{1,0:T(8,128)(2,1)S(1)} %constant_dynamic-slice_fusion.11), channel_id=1, source_target_pairs={{0,16},{1,17},{2,18},{3,19},{4,20},{5,21},{6,22},{7,23},{8,24},{9,... | collective-permute-start | bytes 196616 | tf_op jit(solution)/shard_map/ppermute | solution.py:103
  (28 other events, 233.9 us)

commit v9 on v7

--- a/solution.py
+++ b/solution.py
@@ -106,7 +106,9 @@
     return jnp.concatenate(outs, axis=1)
 
 
-def attention_kernel(window, q_ref, cos_ref, sin_ref, k_ref, v_ref, qseg_ref, kseg_ref, gate_ref, out_ref):
+def attention_kernel(
+    window, x_ref, wq_ref, wo_ref, cos_ref, sin_ref, k_ref, v_ref, qseg_ref, kseg_ref, gate_ref, out_ref, gated_ref
+):
     chunk = pl.program_id(0)
     blocks = pl.num_programs(0)
     start_block = jnp.clip(chunk - (window - 1), 0, blocks - window)
@@ -122,9 +124,10 @@
     cosine = cos_ref[...]
     sine_part = sin_ref[...]
     scale_factor = HD ** (-0.5)
+    raw_all = jnp.dot(x_ref[...], wq_ref[...], preferred_element_type=jnp.float32)
     experts = gate_ref.shape[1]
     for e in range(experts):
-        raw = q_ref[:, e * HD:(e + 1) * HD]
+        raw = raw_all[:, e * HD:(e + 1) * HD]
         turned = raw * cosine + pltpu.roll(raw, HD // 2, 1) * sine_part
         queries = (turned * scale_factor).astype(jnp.bfloat16)
         scores = jnp.dot(queries, keys, preferred_element_type=jnp.float32)
@@ -134,7 +137,10 @@
         inverse = 1.0 / jnp.sum(raised, axis=1, keepdims=True)
         probabilities = (raised * inverse).astype(jnp.bfloat16)
         attended = jnp.dot(probabilities, values, preferred_element_type=jnp.float32)
-        out_ref[:, e * HD:(e + 1) * HD] = (attended * gate_ref[:, e:e + 1]).astype(out_ref.dtype)
+        gated_ref[:, e * HD:(e + 1) * HD] = (attended * gate_ref[:, e:e + 1]).astype(jnp.bfloat16)
+    out_ref[...] = jnp.dot(gated_ref[...], wo_ref[...], preferred_element_type=jnp.float32).astype(
+        out_ref.dtype
+    )
 
 
 def rope_tables(positions):
@@ -149,9 +155,10 @@
     )
 
 
-def attend_window(raw_queries, positions, keys, values, segment_ids, gate_here):
-    tokens, width = raw_queries.shape
-    experts = width // HD
+def attend_window(normed, query_weight, out_weight, positions, keys, values, segment_ids, gate_here):
+    tokens, width = normed.shape
+    pair_width = query_weight.shape[1]
+    experts = pair_width // HD
     blocks = tokens // CHUNK
     window = min(blocks, SEG_MOST // CHUNK + 1)
     cosine, sine_part = rope_tables(positions)
@@ -162,6 +169,8 @@
         grid=(blocks,),
         in_specs=[
             pl.BlockSpec((CHUNK, width), lambda i: (i, 0)),
+            pl.BlockSpec((width, pair_width), lambda i: (0, 0)),
+            pl.BlockSpec((pair_width, width), lambda i: (0, 0)),
             pl.BlockSpec((CHUNK, HD), lambda i: (i, 0)),
             pl.BlockSpec((CHUNK, HD), lambda i: (i, 0)),
             pl.BlockSpec((HD, tokens), lambda i: (0, 0)),
@@ -172,12 +181,13 @@
         ],
         out_specs=pl.BlockSpec((CHUNK, width), lambda i: (i, 0)),
         out_shape=jax.ShapeDtypeStruct((tokens, width), jnp.bfloat16),
+        scratch_shapes=[pltpu.VMEM((CHUNK, pair_width), jnp.bfloat16)],
         cost_estimate=pl.CostEstimate(
-            flops=4 * tokens * window * CHUNK * width,
+            flops=4 * tokens * window * CHUNK * pair_width + 4 * tokens * width * pair_width,
             transcendentals=tokens * window * CHUNK * experts,
-            bytes_accessed=tokens * width * 6 + 2 * tokens * HD * 2 + 2 * tokens * HD * 4,
+            bytes_accessed=2 * tokens * width * 2 + 2 * width * pair_width * 2 + 2 * tokens * HD * 4,
         ),
-    )(raw_queries, cosine, sine_part, jnp.transpose(keys), values, seg_cols, seg_row, gate_here)
+    )(normed, query_weight, out_weight, cosine, sine_part, jnp.transpose(keys), values, seg_cols, seg_row, gate_here)
 
 
 def gather_from_all(block, axis):
@@ -231,11 +241,11 @@
     key_rows = jnp.where(leading_first, own_rows, partner_rows)
     value_rows = jnp.where(leading_first, partner_rows, own_rows)
     pair_count = query_weight.shape[1] // HD
-    raw_queries = jnp.dot(normed, query_weight, preferred_element_type=jnp.float32)
     first_expert = (device_index * pair_count) % EA
     gate_here = lax.dynamic_slice_in_dim(gates, first_expert, pair_count, 1)
-    flat = attend_window(raw_queries, positions, key_rows, value_rows, segment_ids, gate_here)
-    partial = jnp.dot(flat, out_weight, preferred_element_type=jnp.float32).astype(jnp.bfloat16)
+    partial = attend_window(
+        normed, query_weight, out_weight, positions, key_rows, value_rows, segment_ids, gate_here
+    )
     reduced = reduce_to_owner(partial, "tensor").astype(jnp.float32)
     attended_out = (hidden.astype(jnp.float32) + reduced).astype(jnp.bfloat16)
     return (attended_out, new_cache)

time: 121 us -> 123 us (1.017)
  matrix products: 12.6 us -> 5.19 us
  Pallas kernels: 12.4 us -> 19.2 us
  local copies, waits for them, and re-layouts: 7.59 us -> 9.66 us
    dot_general x2 -> x0, matrix products: 7.23 us -> none  [the longest x1 3.67 us: local(): jnp.dot(normed, query_weight, preferred_element_type=jnp.float32)]
    pallas_call x1, Pallas kernels: 12.4 us -> 19.2 us  [attend_window(): pl.pallas_call(lambda *refs: attention_kernel(window, *refs), grid=(block...]
    slice x1, local copies, waits for them, and re-layouts: 0.39 us -> 2.53 us  [reduce_to_owner(): cols = partial[:, j * piece:(j + 1) * piece]]
    unnamed x24 -> x18, local copies, waits for them, and re-layouts: 4 us -> 3.97 us
  transfers between devices with their start and end apart: 41 -> 41, of which waited for: 18 -> 19; matrix products, arithmetic and copies ran while one was open for 13% -> 10% of each run, Pallas kernels for 0% -> 0%
where the time goes in v9:
time: 123 us
  starting transfers between devices  37.1 us (30%)
  waiting for transfers between devices  34.3 us (28%)
  Pallas kernels  19.2 us (16%)
  other arithmetic  15.6 us (13%)
  local copies, waits for them, and re-layouts  9.66 us (8%)
  matrix products  5.19 us (4%)
  between operations  1.46 us (1%)
    ppermute x20, starting transfers between devices, gather_from_all(): got = lax.ppermute(current, axis, [(i, i ^ 1 << k) for i in range(size)])  20.5 us
    ppermute x20, waiting for transfers between devices, reduce_to_owner(): got = lax.ppermute(send, axis, [(i, i ^ 1 << k) for i in range(size)])  19.3 us
    pallas_call x1, Pallas kernels, attend_window(): pl.pallas_call(lambda *refs: attention_kernel(window, *refs), grid=(block...  19.2 us
    ppermute x20, starting transfers between devices, reduce_to_owner(): got = lax.ppermute(send, axis, [(i, i ^ 1 << k) for i in range(size)])  16.5 us
    ppermute x20, waiting for transfers between devices, gather_from_all(): got = lax.ppermute(current, axis, [(i, i ^ 1 << k) for i in range(size)])  14.8 us
    unnamed x18, local copies, waits for them, and re-layouts  3.97 us
    dot_general x1, matrix products, project_kv(): projected = jnp.dot(normed, weight, preferred_element_type=jnp.float32)  3.43 us
    slice x1, local copies, waits for them, and re-layouts, reduce_to_owner(): cols = partial[:, j * piece:(j + 1) * piece]  2.53 us
  transfers between devices with their start and end apart: 41, of which 19 were waited for; matrix products, arithmetic and copies ran while one was open for 10% of the time, Pallas kernels for 0%

profile of v9, /device:TPU:0, one launch (start us, length us, event | category | flops | bytes accessed | tf_op | source)
XLA Modules:
  0.0 122.6 jit_solution(1479913648813024560)
XLA Ops:
  3.5 4.1 %collective-permute-start = (bf16[32,512]{1,0:T(8,128)(2,1)S(1)}, bf16[32,512]{1,0:T(8,128)(2,1)S(1)}, u32[]{:S(2)}, u32[]{:S(2)}) collective-permute-start(bf16[32,512]{1,0:T(8,128)(2,1)S(1)} %get-tuple-element.56), channel_id=1, source_target_pairs={{0,16},{1,17},{2,18},{3,19},{4,20},{5,21},{6,22},{7,23},{8,24},{9,... | collective-permute-start | bytes 98312 | tf_op jit(solution)/shard_map/ppermute | solution.py:206
  7.6 1.5 %collective-permute-start.10 = (bf16[32,512]{1,0:T(8,128)(2,1)S(1)}, bf16[32,512]{1,0:T(8,128)(2,1)S(1)}, u32[]{:S(2)}, u32[]{:S(2)}) collective-permute-start(bf16[32,512]{1,0:T(8,128)(2,1)S(1)} %get-tuple-element.58), channel_id=1, source_target_pairs={{0,4},{1,5},{2,6},{3,7},{4,0},{5,1},{6,2},{7,3},{8,12},{9,13},{10,... | collective-permute-start | bytes 98312 | tf_op jit(solution)/shard_map/ppermute | solution.py:206
  9.2 1.6 %collective-permute-start.15 = (bf16[32,512]{1,0:T(8,128)(2,1)S(1)}, bf16[32,512]{1,0:T(8,128)(2,1)S(1)}, u32[]{:S(2)}, u32[]{:S(2)}) collective-permute-start(bf16[32,512]{1,0:T(8,128)(2,1)S(1)} %get-tuple-element.57), channel_id=1, source_target_pairs={{0,8},{1,9},{2,10},{3,11},{4,12},{5,13},{6,14},{7,15},{8,0},{9,1},... | collective-permute-start | bytes 98312 | tf_op jit(solution)/shard_map/ppermute | solution.py:206
  10.7 1.5 %collective-permute-start.5 = (bf16[32,512]{1,0:T(8,128)(2,1)S(1)}, bf16[32,512]{1,0:T(8,128)(2,1)S(1)}, u32[]{:S(2)}, u32[]{:S(2)}) collective-permute-start(bf16[32,512]{1,0:T(8,128)(2,1)S(1)} %get-tuple-element.59), channel_id=1, source_target_pairs={{0,2},{1,3},{2,0},{3,1},{4,6},{5,7},{6,4},{7,5},{8,10},{9,11},{10,... | collective-permute-start | bytes 98312 | tf_op jit(solution)/shard_map/ppermute | solution.py:206
  13.7 1.9 %fusion.15 = (f32[1024,64]{1,0:T(8,128)S(1)}, f32[1024,64]{1,0:T(8,128)S(1)}, f32[1024,64]{1,0:T(8,128)S(1)}) fusion(f32[64]{0:T(128)S(1)} %multiply_power_fusion, f32[1024]{0:T(1024)S(1)} %fusion.18), kind=kLoop, calls=%fused_computation.69 | loop fusion | flops 131072 | bytes 790784 | tf_op jit(solution)/shard_map/neg | solution.py:154
  19.9 2.7 %collective-permute-done.1 = bf16[64,512]{1,0:T(8,128)(2,1)S(1)} collective-permute-done((bf16[64,512]{1,0:T(8,128)(2,1)S(1)}, bf16[64,512]{1,0:T(8,128)(2,1)S(1)}, u32[]{:S(2)}, u32[]{:S(2)}) %collective-permute-start.1) | collective-permute-done | bytes 65568 | tf_op jit(solution)/shard_map/ppermute | solution.py:206
  24.5 1.6 %collective-permute-start.7 = (bf16[128,512]{1,0:T(8,128)(2,1)S(1)}, bf16[128,512]{1,0:T(8,128)(2,1)S(1)}, u32[]{:S(2)}, u32[]{:S(2)}) collective-permute-start(bf16[128,512]{1,0:T(8,128)(2,1)S(1)} %pad_maximum_fusion.16), channel_id=1, source_target_pairs={{0,8},{1,9},{2,10},{3,11},{4,12},{5,13},{6,14},{7,15},{8,0},{9,1},... | collective-permute-start | bytes 393224 | tf_op jit(solution)/shard_map/ppermute | solution.py:206
  31.0 1.6 %collective-permute-start.8 = (bf16[256,512]{1,0:T(8,128)(2,1)S(1)}, bf16[256,512]{1,0:T(8,128)(2,1)S(1)}, u32[]{:S(2)}, u32[]{:S(2)}) collective-permute-start(bf16[256,512]{1,0:T(8,128)(2,1)S(1)} %pad_maximum_fusion.12), channel_id=1, source_target_pairs={{0,4},{1,5},{2,6},{3,7},{4,0},{5,1},{6,2},{7,3},{8,12},{9,13},{10,... | collective-permute-start | bytes 786440 | tf_op jit(solution)/shard_map/ppermute | solution.py:206
  33.8 3.2 %collective-permute-start.18 = (bf16[256,512]{1,0:T(8,128)(2,1)S(1)}, bf16[256,512]{1,0:T(8,128)(2,1)S(1)}, u32[]{:S(2)}, u32[]{:S(2)}) collective-permute-start(bf16[256,512]{1,0:T(8,128)(2,1)S(1)} %pad_maximum_fusion.14), channel_id=1, source_target_pairs={{0,16},{1,17},{2,18},{3,19},{4,20},{5,21},{6,22},{7,23},{8,24},{9,... | collective-permute-start | bytes 786440 | tf_op jit(solution)/shard_map/ppermute | solution.py:206
  37.9 5.5 %collective-permute-done.13 = bf16[256,512]{1,0:T(8,128)(2,1)S(1)} collective-permute-done((bf16[256,512]{1,0:T(8,128)(2,1)S(1)}, bf16[256,512]{1,0:T(8,128)(2,1)S(1)}, u32[]{:S(2)}, u32[]{:S(2)}) %collective-permute-start.13) | collective-permute-done | bytes 262176 | tf_op jit(solution)/shard_map/ppermute | solution.py:206
  48.1 2.0 %copy-done.1 = bf16[1024,2048]{1,0:T(8,128)(2,1)} copy-done((bf16[1024,2048]{1,0:T(8,128)(2,1)}, bf16[1024,2048]{1,0:T(8,128)(2,1)S(1)}, u32[]{:S(2)}) %copy-start.1) | copy-done | bytes 4194328
  51.4 3.4 %fusion.25 = f32[1024,128]{1,0:T(8,128)S(1)} fusion(bf16[1024,2048]{1,0:T(8,128)(2,1)} %copy-done.1, bf16[2048,128]{1,0:T(8,128)(2,1)S(1)} %copy-done), kind=kOutput, calls=%fused_computation.151 | convolution fusion | flops 536870912 | bytes 5242880 | tf_op jit(solution)/shard_map/dot_general | solution.py:58
  54.8 2.4 %fusion.6 = (bf16[1024,64]{1,0:T(8,128)(2,1)S(1)}, bf16[1024,64]{1,0:T(8,128)(2,1)S(1)}) fusion(f32[1024,1,128]{2,0,1:T(8,128)S(1)} %bitcast.59, f32[64]{0:T(128)S(1)} %multiply_power_fusion, f32[1024]{0:T(1024)S(1)} %fusion.18), kind=kLoop, calls=%fused_computation.20 | loop fusion | flops 589824 | bytes 790784 | tf_op jit(solution)/shard_map/concatenate | solution.py:52
  60.6 19.2 %shard_map.113 = bf16[1024,2048]{1,0:T(8,128)(2,1)} custom-call(bf16[1024,2048]{1,0:T(8,128)(2,1)} %copy-done.1, bf16[2048,512]{1,0:T(8,128)(2,1)} %refs_1_.1, bf16[512,2048]{1,0:T(8,128)(2,1)} %refs_2_.1, f32[1024,128]{1,0:T(8,128)} %get-tuple-element.73.refs_3_, f32[1024,128]{1,0:T(8,128)} %get-tuple-element.74.refs_4_, bf16[128,1024]{1,0:T(8,128)(2,1)} %copy.52.refs_5_, ...), custom_call_target="tpu_custom_call" | custom-call | flops 5905580032 | bytes 13631488 | tf_op jit(solution)/shard_map/pallas_call | solution.py:167
  79.8 2.5 %fusion.23 = (bf16[1024,512]{1,0:T(8,128)(2,1)S(1)}, bf16[1024,512]{1,0:T(8,128)(2,1)S(1)}, bf16[1024,512]{1,0:T(8,128)(2,1)S(1)}, bf16[1024,512]{1,0:T(8,128)(2,1)S(1)}) fusion(bf16[1024,2048]{1,0:T(8,128)(2,1)} %shard_map.113), kind=kLoop, calls=%fused_computation.149 | loop fusion | bytes 8388608 | tf_op jit(solution)/shard_map/slice | solution.py:94
  86.7 1.5 %collective-permute-start.27 = (bf16[256,512]{1,0:T(8,128)(2,1)S(1)}, bf16[256,512]{1,0:T(8,128)(2,1)S(1)}, u32[]{:S(2)}, u32[]{:S(2)}) collective-permute-start(bf16[256,512]{1,0:T(8,128)(2,1)S(1)} %constant_dynamic-slice_fusion.13), channel_id=1, source_target_pairs={{0,4},{1,5},{2,6},{3,7},{4,0},{5,1},{6,2},{7,3},{8,12},{9,13},{10,... | collective-permute-start | bytes 786440 | tf_op jit(solution)/shard_map/ppermute | solution.py:103
  88.7 2.1 %collective-permute-start.37 = (bf16[256,512]{1,0:T(8,128)(2,1)S(1)}, bf16[256,512]{1,0:T(8,128)(2,1)S(1)}, u32[]{:S(2)}, u32[]{:S(2)}) collective-permute-start(bf16[256,512]{1,0:T(8,128)(2,1)S(1)} %constant_dynamic-slice_fusion.3), channel_id=1, source_target_pairs={{0,16},{1,17},{2,18},{3,19},{4,20},{5,21},{6,22},{7,23},{8,24},{9,... | collective-permute-start | bytes 786440 | tf_op jit(solution)/shard_map/ppermute | solution.py:103
  90.8 3.5 %collective-permute-done.22 = bf16[256,512]{1,0:T(8,128)(2,1)S(1)} collective-permute-done((bf16[256,512]{1,0:T(8,128)(2,1)S(1)}, bf16[256,512]{1,0:T(8,128)(2,1)S(1)}, u32[]{:S(2)}, u32[]{:S(2)}) %collective-permute-start.22) | collective-permute-done | bytes 262176 | tf_op jit(solution)/shard_map/ppermute | solution.py:103
  94.4 1.6 %collective-permute-start.23 = (bf16[128,512]{1,0:T(8,128)(2,1)S(1)}, bf16[128,512]{1,0:T(8,128)(2,1)S(1)}, u32[]{:S(2)}, u32[]{:S(2)}) collective-permute-start(bf16[128,512]{1,0:T(8,128)(2,1)S(1)} %constant_dynamic-slice_fusion.17), channel_id=1, source_target_pairs={{0,4},{1,5},{2,6},{3,7},{4,0},{5,1},{6,2},{7,3},{8,12},{9,13},{10,... | collective-permute-start | bytes 393224 | tf_op jit(solution)/shard_map/ppermute | solution.py:103
  96.2 6.4 %collective-permute-done.32 = bf16[256,512]{1,0:T(8,128)(2,1)S(1)} collective-permute-done((bf16[256,512]{1,0:T(8,128)(2,1)S(1)}, bf16[256,512]{1,0:T(8,128)(2,1)S(1)}, u32[]{:S(2)}, u32[]{:S(2)}) %collective-permute-start.32) | collective-permute-done | bytes 262176 | tf_op jit(solution)/shard_map/ppermute | solution.py:103
  105.2 2.0 %collective-permute-start.24 = (bf16[64,512]{1,0:T(8,128)(2,1)S(1)}, bf16[64,512]{1,0:T(8,128)(2,1)S(1)}, u32[]{:S(2)}, u32[]{:S(2)}) collective-permute-start(bf16[64,512]{1,0:T(8,128)(2,1)S(1)} %constant_dynamic-slice_fusion.16), channel_id=1, source_target_pairs={{0,8},{1,9},{2,10},{3,11},{4,12},{5,13},{6,14},{7,15},{8,0},{9,1},... | collective-permute-start | bytes 196616 | tf_op jit(solution)/shard_map/ppermute | solution.py:103
  108.1 2.8 %collective-permute-done.33 = bf16[128,512]{1,0:T(8,128)(2,1)S(1)} collective-permute-done((bf16[128,512]{1,0:T(8,128)(2,1)S(1)}, bf16[128,512]{1,0:T(8,128)(2,1)S(1)}, u32[]{:S(2)}, u32[]{:S(2)}) %collective-permute-start.33) | collective-permute-done | bytes 131104 | tf_op jit(solution)/shard_map/ppermute | solution.py:103
  111.0 2.5 %collective-permute-start.34 = (bf16[64,512]{1,0:T(8,128)(2,1)S(1)}, bf16[64,512]{1,0:T(8,128)(2,1)S(1)}, u32[]{:S(2)}, u32[]{:S(2)}) collective-permute-start(bf16[64,512]{1,0:T(8,128)(2,1)S(1)} %constant_dynamic-slice_fusion.6), channel_id=1, source_target_pairs={{0,2},{1,3},{2,0},{3,1},{4,6},{5,7},{6,4},{7,5},{8,10},{9,11},{10,... | collective-permute-start | bytes 196616 | tf_op jit(solution)/shard_map/ppermute | solution.py:103
  119.8 2.1 %collective-permute-done.40 = bf16[32,512]{1,0:T(8,128)(2,1)S(1)} collective-permute-done((bf16[32,512]{1,0:T(8,128)(2,1)S(1)}, bf16[32,512]{1,0:T(8,128)(2,1)S(1)}, u32[]{:S(2)}, u32[]{:S(2)}) %collective-permute-start.40) | collective-permute-done | bytes 32800 | tf_op jit(solution)/shard_map/ppermute | solution.py:103
  (193 shorter events, 41.9 us)
Async XLA Ops:
  3.5 14.6 %collective-permute-start = (bf16[32,512]{1,0:T(8,128)(2,1)S(1)}, bf16[32,512]{1,0:T(8,128)(2,1)S(1)}, u32[]{:S(2)}, u32[]{:S(2)}) collective-permute-start(bf16[32,512]{1,0:T(8,128)(2,1)S(1)} %get-tuple-element.56), channel_id=1, source_target_pairs={{0,16},{1,17},{2,18},{3,19},{4,20},{5,21},{6,22},{7,23},{8,24},{9,... | collective-permute-start | bytes 98312 | tf_op jit(solution)/shard_map/ppermute | solution.py:206
  7.6 10.5 %collective-permute-start.10 = (bf16[32,512]{1,0:T(8,128)(2,1)S(1)}, bf16[32,512]{1,0:T(8,128)(2,1)S(1)}, u32[]{:S(2)}, u32[]{:S(2)}) collective-permute-start(bf16[32,512]{1,0:T(8,128)(2,1)S(1)} %get-tuple-element.58), channel_id=1, source_target_pairs={{0,4},{1,5},{2,6},{3,7},{4,0},{5,1},{6,2},{7,3},{8,12},{9,13},{10,... | collective-permute-start | bytes 98312 | tf_op jit(solution)/shard_map/ppermute | solution.py:206
  9.2 9.0 %collective-permute-start.15 = (bf16[32,512]{1,0:T(8,128)(2,1)S(1)}, bf16[32,512]{1,0:T(8,128)(2,1)S(1)}, u32[]{:S(2)}, u32[]{:S(2)}) collective-permute-start(bf16[32,512]{1,0:T(8,128)(2,1)S(1)} %get-tuple-element.57), channel_id=1, source_target_pairs={{0,8},{1,9},{2,10},{3,11},{4,12},{5,13},{6,14},{7,15},{8,0},{9,1},... | collective-permute-start | bytes 98312 | tf_op jit(solution)/shard_map/ppermute | solution.py:206
  10.7 7.4 %collective-permute-start.5 = (bf16[32,512]{1,0:T(8,128)(2,1)S(1)}, bf16[32,512]{1,0:T(8,128)(2,1)S(1)}, u32[]{:S(2)}, u32[]{:S(2)}) collective-permute-start(bf16[32,512]{1,0:T(8,128)(2,1)S(1)} %get-tuple-element.59), channel_id=1, source_target_pairs={{0,2},{1,3},{2,0},{3,1},{4,6},{5,7},{6,4},{7,5},{8,10},{9,11},{10,... | collective-permute-start | bytes 98312 | tf_op jit(solution)/shard_map/ppermute | solution.py:206
  19.1 7.1 %collective-permute-start.11 = (bf16[64,512]{1,0:T(8,128)(2,1)S(1)}, bf16[64,512]{1,0:T(8,128)(2,1)S(1)}, u32[]{:S(2)}, u32[]{:S(2)}) collective-permute-start(bf16[64,512]{1,0:T(8,128)(2,1)S(1)} %pad_maximum_fusion.21), channel_id=1, source_target_pairs={{0,2},{1,3},{2,0},{3,1},{4,6},{5,7},{6,4},{7,5},{8,10},{9,11},{10,... | collective-permute-start | bytes 196616 | tf_op jit(solution)/shard_map/ppermute | solution.py:206
  19.6 6.6 %collective-permute-start.16 = (bf16[64,512]{1,0:T(8,128)(2,1)S(1)}, bf16[64,512]{1,0:T(8,128)(2,1)S(1)}, u32[]{:S(2)}, u32[]{:S(2)}) collective-permute-start(bf16[64,512]{1,0:T(8,128)(2,1)S(1)} %pad_maximum_fusion.22), channel_id=1, source_target_pairs={{0,4},{1,5},{2,6},{3,7},{4,0},{5,1},{6,2},{7,3},{8,12},{9,13},{10,... | collective-permute-start | bytes 196616 | tf_op jit(solution)/shard_map/ppermute | solution.py:206
  26.3 7.3 %collective-permute-start.12 = (bf16[128,512]{1,0:T(8,128)(2,1)S(1)}, bf16[128,512]{1,0:T(8,128)(2,1)S(1)}, u32[]{:S(2)}, u32[]{:S(2)}) collective-permute-start(bf16[128,512]{1,0:T(8,128)(2,1)S(1)} %pad_maximum_fusion.17), channel_id=1, source_target_pairs={{0,16},{1,17},{2,18},{3,19},{4,20},{5,21},{6,22},{7,23},{8,24},{9,... | collective-permute-start | bytes 393224 | tf_op jit(solution)/shard_map/ppermute | solution.py:206
  27.4 6.4 %collective-permute-start.17 = (bf16[128,512]{1,0:T(8,128)(2,1)S(1)}, bf16[128,512]{1,0:T(8,128)(2,1)S(1)}, u32[]{:S(2)}, u32[]{:S(2)}) collective-permute-start(bf16[128,512]{1,0:T(8,128)(2,1)S(1)} %pad_maximum_fusion.18), channel_id=1, source_target_pairs={{0,2},{1,3},{2,0},{3,1},{4,6},{5,7},{6,4},{7,5},{8,10},{9,11},{10,... | collective-permute-start | bytes 393224 | tf_op jit(solution)/shard_map/ppermute | solution.py:206
  29.1 7.9 %collective-permute-start.3 = (bf16[256,512]{1,0:T(8,128)(2,1)S(1)}, bf16[256,512]{1,0:T(8,128)(2,1)S(1)}, u32[]{:S(2)}, u32[]{:S(2)}) collective-permute-start(bf16[256,512]{1,0:T(8,128)(2,1)S(1)} %pad_maximum_fusion.11), channel_id=1, source_target_pairs={{0,2},{1,3},{2,0},{3,1},{4,6},{5,7},{6,4},{7,5},{8,10},{9,11},{10,... | collective-permute-start | bytes 786440 | tf_op jit(solution)/shard_map/ppermute | solution.py:206
  31.0 6.4 %collective-permute-start.8 = (bf16[256,512]{1,0:T(8,128)(2,1)S(1)}, bf16[256,512]{1,0:T(8,128)(2,1)S(1)}, u32[]{:S(2)}, u32[]{:S(2)}) collective-permute-start(bf16[256,512]{1,0:T(8,128)(2,1)S(1)} %pad_maximum_fusion.12), channel_id=1, source_target_pairs={{0,4},{1,5},{2,6},{3,7},{4,0},{5,1},{6,2},{7,3},{8,12},{9,13},{10,... | collective-permute-start | bytes 786440 | tf_op jit(solution)/shard_map/ppermute | solution.py:206
  33.7 9.8 %collective-permute-start.13 = (bf16[256,512]{1,0:T(8,128)(2,1)S(1)}, bf16[256,512]{1,0:T(8,128)(2,1)S(1)}, u32[]{:S(2)}, u32[]{:S(2)}) collective-permute-start(bf16[256,512]{1,0:T(8,128)(2,1)S(1)} %pad_maximum_fusion.13), channel_id=1, source_target_pairs={{0,8},{1,9},{2,10},{3,11},{4,12},{5,13},{6,14},{7,15},{8,0},{9,1},... | collective-permute-start | bytes 786440 | tf_op jit(solution)/shard_map/ppermute | solution.py:206
  33.8 11.0 %collective-permute-start.18 = (bf16[256,512]{1,0:T(8,128)(2,1)S(1)}, bf16[256,512]{1,0:T(8,128)(2,1)S(1)}, u32[]{:S(2)}, u32[]{:S(2)}) collective-permute-start(bf16[256,512]{1,0:T(8,128)(2,1)S(1)} %pad_maximum_fusion.14), channel_id=1, source_target_pairs={{0,16},{1,17},{2,18},{3,19},{4,20},{5,21},{6,22},{7,23},{8,24},{9,... | collective-permute-start | bytes 786440 | tf_op jit(solution)/shard_map/ppermute | solution.py:206
  37.1 7.9 %collective-permute-start.4 = (bf16[512,512]{1,0:T(8,128)(2,1)S(1)}, bf16[512,512]{1,0:T(8,128)(2,1)S(1)}, u32[]{:S(2)}, u32[]{:S(2)}) collective-permute-start(bf16[512,512]{1,0:T(8,128)(2,1)S(1)} %pad_maximum_fusion.5), channel_id=1, source_target_pairs={{0,1},{1,0},{2,3},{3,2},{4,5},{5,4},{6,7},{7,6},{8,9},{9,8},{10,11... | collective-permute-start | bytes 1572872 | tf_op jit(solution)/shard_map/ppermute | solution.py:206
  37.5 7.8 %collective-permute-start.9 = (bf16[512,512]{1,0:T(8,128)(2,1)S(1)}, bf16[512,512]{1,0:T(8,128)(2,1)S(1)}, u32[]{:S(2)}, u32[]{:S(2)}) collective-permute-start(bf16[512,512]{1,0:T(8,128)(2,1)S(1)} %pad_maximum_fusion.6), channel_id=1, source_target_pairs={{0,1},{1,0},{2,3},{3,2},{4,5},{5,4},{6,7},{7,6},{8,9},{9,8},{10,11... | collective-permute-start | bytes 1572872 | tf_op jit(solution)/shard_map/ppermute | solution.py:206
  85.9 8.4 %collective-permute-start.22 = (bf16[256,512]{1,0:T(8,128)(2,1)S(1)}, bf16[256,512]{1,0:T(8,128)(2,1)S(1)}, u32[]{:S(2)}, u32[]{:S(2)}) collective-permute-start(bf16[256,512]{1,0:T(8,128)(2,1)S(1)} %constant_dynamic-slice_fusion.18), channel_id=1, source_target_pairs={{0,2},{1,3},{2,0},{3,1},{4,6},{5,7},{6,4},{7,5},{8,10},{9,11},{10,... | collective-permute-start | bytes 786440 | tf_op jit(solution)/shard_map/ppermute | solution.py:103
  86.7 9.3 %collective-permute-start.27 = (bf16[256,512]{1,0:T(8,128)(2,1)S(1)}, bf16[256,512]{1,0:T(8,128)(2,1)S(1)}, u32[]{:S(2)}, u32[]{:S(2)}) collective-permute-start(bf16[256,512]{1,0:T(8,128)(2,1)S(1)} %constant_dynamic-slice_fusion.13), channel_id=1, source_target_pairs={{0,4},{1,5},{2,6},{3,7},{4,0},{5,1},{6,2},{7,3},{8,12},{9,13},{10,... | collective-permute-start | bytes 786440 | tf_op jit(solution)/shard_map/ppermute | solution.py:103
  88.4 14.2 %collective-permute-start.32 = (bf16[256,512]{1,0:T(8,128)(2,1)S(1)}, bf16[256,512]{1,0:T(8,128)(2,1)S(1)}, u32[]{:S(2)}, u32[]{:S(2)}) collective-permute-start(bf16[256,512]{1,0:T(8,128)(2,1)S(1)} %constant_dynamic-slice_fusion.8), channel_id=1, source_target_pairs={{0,8},{1,9},{2,10},{3,11},{4,12},{5,13},{6,14},{7,15},{8,0},{9,1},... | collective-permute-start | bytes 786440 | tf_op jit(solution)/shard_map/ppermute | solution.py:103
  88.7 14.9 %collective-permute-start.37 = (bf16[256,512]{1,0:T(8,128)(2,1)S(1)}, bf16[256,512]{1,0:T(8,128)(2,1)S(1)}, u32[]{:S(2)}, u32[]{:S(2)}) collective-permute-start(bf16[256,512]{1,0:T(8,128)(2,1)S(1)} %constant_dynamic-slice_fusion.3), channel_id=1, source_target_pairs={{0,16},{1,17},{2,18},{3,19},{4,20},{5,21},{6,22},{7,23},{8,24},{9,... | collective-permute-start | bytes 786440 | tf_op jit(solution)/shard_map/ppermute | solution.py:103
  94.4 10.7 %collective-permute-start.23 = (bf16[128,512]{1,0:T(8,128)(2,1)S(1)}, bf16[128,512]{1,0:T(8,128)(2,1)S(1)}, u32[]{:S(2)}, u32[]{:S(2)}) collective-permute-start(bf16[128,512]{1,0:T(8,128)(2,1)S(1)} %constant_dynamic-slice_fusion.17), channel_id=1, source_target_pairs={{0,4},{1,5},{2,6},{3,7},{4,0},{5,1},{6,2},{7,3},{8,12},{9,13},{10,... | collective-permute-start | bytes 393224 | tf_op jit(solution)/shard_map/ppermute | solution.py:103
  96.1 11.1 %collective-permute-start.28 = (bf16[128,512]{1,0:T(8,128)(2,1)S(1)}, bf16[128,512]{1,0:T(8,128)(2,1)S(1)}, u32[]{:S(2)}, u32[]{:S(2)}) collective-permute-start(bf16[128,512]{1,0:T(8,128)(2,1)S(1)} %constant_dynamic-slice_fusion.12), channel_id=1, source_target_pairs={{0,8},{1,9},{2,10},{3,11},{4,12},{5,13},{6,14},{7,15},{8,0},{9,1},... | collective-permute-start | bytes 393224 | tf_op jit(solution)/shard_map/ppermute | solution.py:103
  102.7 8.2 %collective-permute-start.33 = (bf16[128,512]{1,0:T(8,128)(2,1)S(1)}, bf16[128,512]{1,0:T(8,128)(2,1)S(1)}, u32[]{:S(2)}, u32[]{:S(2)}) collective-permute-start(bf16[128,512]{1,0:T(8,128)(2,1)S(1)} %constant_dynamic-slice_fusion.7), channel_id=1, source_target_pairs={{0,16},{1,17},{2,18},{3,19},{4,20},{5,21},{6,22},{7,23},{8,24},{9,... | collective-permute-start | bytes 393224 | tf_op jit(solution)/shard_map/ppermute | solution.py:103
  103.7 9.8 %collective-permute-start.38 = (bf16[128,512]{1,0:T(8,128)(2,1)S(1)}, bf16[128,512]{1,0:T(8,128)(2,1)S(1)}, u32[]{:S(2)}, u32[]{:S(2)}) collective-permute-start(bf16[128,512]{1,0:T(8,128)(2,1)S(1)} %constant_dynamic-slice_fusion.2), channel_id=1, source_target_pairs={{0,2},{1,3},{2,0},{3,1},{4,6},{5,7},{6,4},{7,5},{8,10},{9,11},{10,... | collective-permute-start | bytes 393224 | tf_op jit(solution)/shard_map/ppermute | solution.py:103
  105.2 8.4 %collective-permute-start.24 = (bf16[64,512]{1,0:T(8,128)(2,1)S(1)}, bf16[64,512]{1,0:T(8,128)(2,1)S(1)}, u32[]{:S(2)}, u32[]{:S(2)}) collective-permute-start(bf16[64,512]{1,0:T(8,128)(2,1)S(1)} %constant_dynamic-slice_fusion.16), channel_id=1, source_target_pairs={{0,8},{1,9},{2,10},{3,11},{4,12},{5,13},{6,14},{7,15},{8,0},{9,1},... | collective-permute-start | bytes 196616 | tf_op jit(solution)/shard_map/ppermute | solution.py:103
  107.3 6.5 %collective-permute-start.29 = (bf16[64,512]{1,0:T(8,128)(2,1)S(1)}, bf16[64,512]{1,0:T(8,128)(2,1)S(1)}, u32[]{:S(2)}, u32[]{:S(2)}) collective-permute-start(bf16[64,512]{1,0:T(8,128)(2,1)S(1)} %constant_dynamic-slice_fusion.11), channel_id=1, source_target_pairs={{0,16},{1,17},{2,18},{3,19},{4,20},{5,21},{6,22},{7,23},{8,24},{9,... | collective-permute-start | bytes 196616 | tf_op jit(solution)/shard_map/ppermute | solution.py:103
  (25 other events, 191.6 us)

commit v10 on v7

--- a/solution.py
+++ b/solution.py
@@ -9,7 +9,7 @@
 HD = 128
 EA = 8
 PAGE = 128
-REDUCE_PARTS = 4
+REDUCE_PARTS = 2
 SEG_MOST = 512
 CHUNK = 256
 
@@ -77,7 +77,8 @@
     rest = list(range(1, bits))
     if not rest:
         return [[0]] * parts
-    return [[0] + rest[j % len(rest):] + rest[:j % len(rest)] for j in range(parts)]
+    stride = max(1, len(rest) // parts)
+    return [[0] + rest[j * stride % len(rest):] + rest[:j * stride % len(rest)] for j in range(parts)]
 
 
 def reduce_to_owner(partial, axis):

time: 121 us -> 137 us (1.13)
  waiting for transfers between devices: 34 us -> 55.4 us
  starting transfers between devices: 37.4 us -> 20.5 us
  other arithmetic: 15.7 us -> 23.8 us
  local copies, waits for them, and re-layouts: 7.59 us -> 10 us
    ppermute x20 -> x10, waiting for transfers between devices: 19.2 us -> 32 us  [reduce_to_owner(): got = lax.ppermute(send, axis, [(i, i ^ 1 << k) for i in range(size)])]
    ppermute x20 -> x10, starting transfers between devices: 16.7 us -> 6.06 us  [reduce_to_owner(): got = lax.ppermute(send, axis, [(i, i ^ 1 << k) for i in range(size)])]
    ppermute x20 -> x10, waiting for transfers between devices: 14.7 us -> 23.4 us  [gather_from_all(): got = lax.ppermute(current, axis, [(i, i ^ 1 << k) for i in range(size)])]
    ppermute x20 -> x10, starting transfers between devices: 20.5 us -> 13.8 us  [gather_from_all(): got = lax.ppermute(current, axis, [(i, i ^ 1 << k) for i in range(size)])]
    select_n x15 -> x8, other arithmetic: 1.51 us -> 6.31 us  [gather_from_all(): jnp.where(upper, got, current)]
    convert_element_type x20 -> x10, other arithmetic: 1.14 us -> 4.2 us  [reduce_to_owner(): (keep.astype(jnp.float32) + got.astype(jnp.float32)).astype(jnp.bfloat16)]
    concatenate x20 -> x10, other arithmetic: 0.57 us -> 2.44 us  [gather_from_all(): jnp.concatenate([jnp.where(upper, got, current), jnp.where(upper, current...]
    unnamed x24 -> x44, local copies, waits for them, and re-layouts: 4 us -> 5.07 us
  transfers between devices with their start and end apart: 41 -> 21, of which waited for: 18 -> 16; matrix products, arithmetic and copies ran while one was open for 13% -> 18% of each run, Pallas kernels for 0% -> 0%
where the time goes in v10:
time: 137 us; the launch traced here: 136 us
  waiting for transfers between devices  55.4 us (40%)
  other arithmetic  23.8 us (17%)
  starting transfers between devices  20.5 us (15%)
  matrix products  12.7 us (9%)
  Pallas kernels  12.4 us (9%)
  local copies, waits for them, and re-layouts  10 us (7%)
    ppermute x10, waiting for transfers between devices, reduce_to_owner(): got = lax.ppermute(send, axis, [(i, i ^ 1 << k) for i in range(size)])  32 us
    ppermute x10, waiting for transfers between devices, gather_from_all(): got = lax.ppermute(current, axis, [(i, i ^ 1 << k) for i in range(size)])  23.4 us
    ppermute x10, starting transfers between devices, gather_from_all(): got = lax.ppermute(current, axis, [(i, i ^ 1 << k) for i in range(size)])  13.8 us
    pallas_call x1, Pallas kernels, attend_window(): pl.pallas_call(lambda *refs: attention_kernel(window, *refs), grid=(block...  12.4 us
    select_n x8, other arithmetic, gather_from_all(): jnp.where(upper, got, current)  6.31 us
    ppermute x10, starting transfers between devices, reduce_to_owner(): got = lax.ppermute(send, axis, [(i, i ^ 1 << k) for i in range(size)])  6.06 us
    unnamed x44, local copies, waits for them, and re-layouts  5.07 us
    convert_element_type x10, other arithmetic, reduce_to_owner(): (keep.astype(jnp.float32) + got.astype(jnp.float32)).astype(jnp.bfloat16)  4.2 us
  transfers between devices with their start and end apart: 21, of which 16 were waited for; matrix products, arithmetic and copies ran while one was open for 18% of the time, Pallas kernels for 0%

profile of v10, /device:TPU:0, one launch (start us, length us, event | category | flops | bytes accessed | tf_op | source)
XLA Modules:
  0.0 136.0 jit_solution(13014433257500541239)
XLA Ops:
  3.6 4.1 %collective-permute-start = (bf16[32,1024]{1,0:T(8,128)(2,1)S(1)}, bf16[32,1024]{1,0:T(8,128)(2,1)S(1)}, u32[]{:S(2)}, u32[]{:S(2)}) collective-permute-start(bf16[32,1024]{1,0:T(8,128)(2,1)S(1)} %get-tuple-element.38), channel_id=1, source_target_pairs={{0,16},{1,17},{2,18},{3,19},{4,20},{5,21},{6,22},{7,23},{8,24},{9,... | collective-permute-start | bytes 196616 | tf_op jit(solution)/shard_map/ppermute | solution.py:197
  9.2 2.1 %collective-permute-done = bf16[32,1024]{1,0:T(8,128)(2,1)S(1)} collective-permute-done((bf16[32,1024]{1,0:T(8,128)(2,1)S(1)}, bf16[32,1024]{1,0:T(8,128)(2,1)S(1)}, u32[]{:S(2)}, u32[]{:S(2)}) %collective-permute-start) | collective-permute-done | bytes 65568 | tf_op jit(solution)/shard_map/ppermute | solution.py:197
  12.0 1.6 %collective-permute-start.1 = (bf16[64,1024]{1,0:T(8,128)(2,1)S(1)}, bf16[64,1024]{1,0:T(8,128)(2,1)S(1)}, u32[]{:S(2)}, u32[]{:S(2)}) collective-permute-start(bf16[64,1024]{1,0:T(8,128)(2,1)S(1)} %pad_maximum_fusion.14), channel_id=1, source_target_pairs={{0,8},{1,9},{2,10},{3,11},{4,12},{5,13},{6,14},{7,15},{8,0},{9,1},... | collective-permute-start | bytes 393224 | tf_op jit(solution)/shard_map/ppermute | solution.py:197
  15.2 1.8 %collective-permute-done.1 = bf16[64,1024]{1,0:T(8,128)(2,1)S(1)} collective-permute-done((bf16[64,1024]{1,0:T(8,128)(2,1)S(1)}, bf16[64,1024]{1,0:T(8,128)(2,1)S(1)}, u32[]{:S(2)}, u32[]{:S(2)}) %collective-permute-start.1) | collective-permute-done | bytes 131104 | tf_op jit(solution)/shard_map/ppermute | solution.py:197
  17.1 1.7 %collective-permute-done.6 = bf16[64,1024]{1,0:T(8,128)(2,1)S(1)} collective-permute-done((bf16[64,1024]{1,0:T(8,128)(2,1)S(1)}, bf16[64,1024]{1,0:T(8,128)(2,1)S(1)}, u32[]{:S(2)}, u32[]{:S(2)}) %collective-permute-start.6) | collective-permute-done | bytes 131104 | tf_op jit(solution)/shard_map/ppermute | solution.py:197
  20.5 1.8 %collective-permute-start.7 = (bf16[128,1024]{1,0:T(8,128)(2,1)S(1)}, bf16[128,1024]{1,0:T(8,128)(2,1)}, u32[]{:S(2)}, u32[]{:S(2)}) collective-permute-start(bf16[128,1024]{1,0:T(8,128)(2,1)S(1)} %pad_maximum_fusion.13), channel_id=1, source_target_pairs={{0,16},{1,17},{2,18},{3,19},{4,20},{5,21},{6,22},{7,23},{8,24},{9,... | collective-permute-start | bytes 786440 | tf_op jit(solution)/shard_map/ppermute | solution.py:197
  22.3 2.9 %collective-permute-done.2 = bf16[128,1024]{1,0:T(8,128)(2,1)S(1)} collective-permute-done((bf16[128,1024]{1,0:T(8,128)(2,1)S(1)}, bf16[128,1024]{1,0:T(8,128)(2,1)S(1)}, u32[]{:S(2)}, u32[]{:S(2)}) %collective-permute-start.2) | collective-permute-done | bytes 262176 | tf_op jit(solution)/shard_map/ppermute | solution.py:197
  28.2 4.5 %collective-permute-done.7 = bf16[128,1024]{1,0:T(8,128)(2,1)} collective-permute-done((bf16[128,1024]{1,0:T(8,128)(2,1)S(1)}, bf16[128,1024]{1,0:T(8,128)(2,1)}, u32[]{:S(2)}, u32[]{:S(2)}) %collective-permute-start.7) | collective-permute-done | bytes 262176 | tf_op jit(solution)/shard_map/ppermute | solution.py:197
  39.8 8.2 %collective-permute-done.8 = bf16[256,1024]{1,0:T(8,128)(2,1)} collective-permute-done((bf16[256,1024]{1,0:T(8,128)(2,1)}, bf16[256,1024]{1,0:T(8,128)(2,1)}, u32[]{:S(2)}, u32[]{:S(2)}) %collective-permute-start.8) | collective-permute-done | bytes 524320 | tf_op jit(solution)/shard_map/ppermute | solution.py:197
  49.6 1.9 %fusion.18 = (f32[1024,64]{1,0:T(8,128)S(1)}, f32[1024,64]{1,0:T(8,128)S(1)}, f32[1024,64]{1,0:T(8,128)S(1)}) fusion(f32[64]{0:T(128)S(1)} %multiply_power_fusion, f32[1024]{0:T(1024)S(1)} %fusion.21), kind=kLoop, calls=%fused_computation.61 | loop fusion | flops 131072 | bytes 790784 | tf_op jit(solution)/shard_map/neg | solution.py:149
  52.8 1.8 %broadcast_select_fusion.3 = (bf16[512,1024]{1,0:T(8,128)(2,1)S(1)}, bf16[512,1024]{1,0:T(8,128)(2,1)S(1)}) fusion(bf16[512,1024]{1,0:T(8,128)(2,1)} %collective-permute-done.4, pred[]{:T(512)S(6)} %eq.57, bf16[256,1024]{1,0:T(8,128)(2,1)S(1)} %get-tuple-element.17, bf16[256,1024]{1,0:T(8,128)(2,1)S(1)} %get-tuple-element.16), kind=kLoop, calls=%fused_computation.18 | loop fusion | flops 3145728 | bytes 4194305 | tf_op jit(solution)/shard_map/jit(_where)/select_n | solution.py:200
  58.0 3.6 %fusion.2 = f32[1024,128]{1,0:T(8,128)S(1)} fusion(bf16[2048,128]{1,0:T(8,128)(2,1)S(1)} %copy-done.19, bf16[1024,1024]{1,0:T(8,128)(2,1)} %bitcast.58, bf16[1024,1024]{1,0:T(8,128)(2,1)} %bitcast.55), kind=kOutput, calls=%fused_computation.9 | convolution fusion | flops 545259520 | bytes 5242880 | tf_op jit(solution)/shard_map/dot_general | solution.py:58
  61.7 2.4 %fusion.9 = (bf16[1024,64]{1,0:T(8,128)(2,1)S(1)}, bf16[1024,64]{1,0:T(8,128)(2,1)S(1)}) fusion(f32[1024,1,128]{2,0,1:T(8,128)S(1)} %bitcast.52, f32[64]{0:T(128)S(1)} %multiply_power_fusion, f32[1024]{0:T(1024)S(1)} %fusion.21), kind=kLoop, calls=%fused_computation.28 | loop fusion | flops 589824 | bytes 790784 | tf_op jit(solution)/shard_map/concatenate | solution.py:52
  64.8 3.7 %fusion.3.refs_0_ = f32[1024,512]{1,0:T(8,128)} fusion(bf16[2048,512]{1,0:T(8,128)(2,1)S(1)} %copy-done.18, bf16[1024,1024]{1,0:T(8,128)(2,1)S(1)} %bitcast.59, bf16[1024,1024]{1,0:T(8,128)(2,1)S(1)} %bitcast.56), kind=kOutput, calls=%fused_computation.10 | convolution fusion | flops 2155872256 | bytes 8388608 | tf_op jit(solution)/shard_map/dot_general | solution.py:235
  71.2 12.4 %shard_map.113 = bf16[1024,512]{1,0:T(8,128)(2,1)} custom-call(f32[1024,512]{1,0:T(8,128)} %fusion.3.refs_0_, f32[1024,128]{1,0:T(8,128)} %get-tuple-element.45.refs_1_, f32[1024,128]{1,0:T(8,128)} %get-tuple-element.46.refs_2_, bf16[128,1024]{1,0:T(8,128)(2,1)} %copy.51.refs_3_, bf16[1024,128]{1,0:T(8,128)(2,1)} %get-tuple-element.22.refs_4_, ...), custom_call_target="tpu_custom_call" | custom-call | flops 1610612736 | bytes 4718592 | tf_op jit(solution)/shard_map/pallas_call | solution.py:161
  83.5 3.6 %convolution_convert_fusion = bf16[1024,2048]{1,0:T(8,128)(2,1)S(1)} fusion(bf16[1024,512]{1,0:T(8,128)(2,1)} %shard_map.113, bf16[512,2048]{1,0:T(8,128)(2,1)S(1)} %copy-done), kind=kOutput, calls=%fused_computation.1 | convolution fusion | flops 2149580800 | bytes 7340032 | tf_op jit(solution)/shard_map/dot_general | solution.py:239
  92.0 1.9 %add_convert_fusion.1 = bf16[512,1024]{1,0:T(8,128)(2,1)S(1)} fusion(bf16[512,1024]{1,0:T(8,128)(2,1)} %collective-permute-done.11, bf16[1024,1024]{1,0:T(8,128)(2,1)} %bitcast.47, s32[]{:T(128)S(6)} %select_n.258), kind=kLoop, calls=%fused_computation.5 | loop fusion | flops 2097152 | bytes 3145732 | tf_op jit(solution)/shard_map/convert_element_type | solution.py:105
  95.6 1.6 %add_convert_fusion = bf16[512,1024]{1,0:T(8,128)(2,1)S(1)} fusion(bf16[512,1024]{1,0:T(8,128)(2,1)} %collective-permute-done.16, bf16[1024,1024]{1,0:T(8,128)(2,1)S(1)} %bitcast.45, s32[]{:T(128)S(6)} %select_n.258), kind=kLoop, calls=%fused_computation.4 | loop fusion | flops 2097152 | bytes 3145732 | tf_op jit(solution)/shard_map/convert_element_type | solution.py:105
  99.1 9.1 %collective-permute-done.12 = bf16[256,1024]{1,0:T(8,128)(2,1)S(1)} collective-permute-done((bf16[256,1024]{1,0:T(8,128)(2,1)S(1)}, bf16[256,1024]{1,0:T(8,128)(2,1)S(1)}, u32[]{:S(2)}, u32[]{:S(2)}) %collective-permute-start.12) | collective-permute-done | bytes 524320 | tf_op jit(solution)/shard_map/ppermute | solution.py:104
  109.0 2.2 %collective-permute-done.17 = bf16[256,1024]{1,0:T(8,128)(2,1)S(1)} collective-permute-done((bf16[256,1024]{1,0:T(8,128)(2,1)S(1)}, bf16[256,1024]{1,0:T(8,128)(2,1)S(1)}, u32[]{:S(2)}, u32[]{:S(2)}) %collective-permute-start.17) | collective-permute-done | bytes 524320 | tf_op jit(solution)/shard_map/ppermute | solution.py:104
  112.8 3.3 %collective-permute-done.13 = bf16[128,1024]{1,0:T(8,128)(2,1)S(1)} collective-permute-done((bf16[128,1024]{1,0:T(8,128)(2,1)S(1)}, bf16[128,1024]{1,0:T(8,128)(2,1)S(1)}, u32[]{:S(2)}, u32[]{:S(2)}) %collective-permute-start.13) | collective-permute-done | bytes 262176 | tf_op jit(solution)/shard_map/ppermute | solution.py:104
  116.6 8.7 %collective-permute-done.18 = bf16[128,1024]{1,0:T(8,128)(2,1)S(1)} collective-permute-done((bf16[128,1024]{1,0:T(8,128)(2,1)S(1)}, bf16[128,1024]{1,0:T(8,128)(2,1)S(1)}, u32[]{:S(2)}, u32[]{:S(2)}) %collective-permute-start.18) | collective-permute-done | bytes 262176 | tf_op jit(solution)/shard_map/ppermute | solution.py:104
  126.6 4.3 %collective-permute-done.19 = bf16[64,1024]{1,0:T(8,128)(2,1)S(1)} collective-permute-done((bf16[64,1024]{1,0:T(8,128)(2,1)S(1)}, bf16[64,1024]{1,0:T(8,128)(2,1)S(1)}, u32[]{:S(2)}, u32[]{:S(2)}) %collective-permute-start.19) | collective-permute-done | bytes 131104 | tf_op jit(solution)/shard_map/ppermute | solution.py:104
  131.9 3.4 %collective-permute-done.20 = bf16[32,1024]{1,0:T(8,128)(2,1)S(1)} collective-permute-done((bf16[32,1024]{1,0:T(8,128)(2,1)S(1)}, bf16[32,1024]{1,0:T(8,128)(2,1)S(1)}, u32[]{:S(2)}, u32[]{:S(2)}) %collective-permute-start.20) | collective-permute-done | bytes 65568 | tf_op jit(solution)/shard_map/ppermute | solution.py:104
  (139 shorter events, 42.2 us)
Async XLA Ops:
  0.6 82.9 %copy-start = (bf16[512,2048]{1,0:T(8,128)(2,1)S(1)}, bf16[512,2048]{1,0:T(8,128)(2,1)}, u32[]{:S(2)}) copy-start(bf16[512,2048]{1,0:T(8,128)(2,1)} %param.15) | copy-start | bytes 6291460
  0.6 19.8 %copy-start.15 = (s32[1024]{0:T(1024)S(1)}, s32[1024]{0:T(1024)}, u32[]{:S(2)}) copy-start(s32[1024]{0:T(1024)} %param.17) | copy-start | bytes 12292
  3.6 7.8 %collective-permute-start = (bf16[32,1024]{1,0:T(8,128)(2,1)S(1)}, bf16[32,1024]{1,0:T(8,128)(2,1)S(1)}, u32[]{:S(2)}, u32[]{:S(2)}) collective-permute-start(bf16[32,1024]{1,0:T(8,128)(2,1)S(1)} %get-tuple-element.38), channel_id=1, source_target_pairs={{0,16},{1,17},{2,18},{3,19},{4,20},{5,21},{6,22},{7,23},{8,24},{9,... | collective-permute-start | bytes 196616 | tf_op jit(solution)/shard_map/ppermute | solution.py:197
  7.7 4.3 %collective-permute-start.5 = (bf16[32,1024]{1,0:T(8,128)(2,1)S(1)}, bf16[32,1024]{1,0:T(8,128)(2,1)S(1)}, u32[]{:S(2)}, u32[]{:S(2)}) collective-permute-start(bf16[32,1024]{1,0:T(8,128)(2,1)S(1)} %get-tuple-element.39), channel_id=1, source_target_pairs={{0,4},{1,5},{2,6},{3,7},{4,0},{5,1},{6,2},{7,3},{8,12},{9,13},{10,... | collective-permute-start | bytes 196616 | tf_op jit(solution)/shard_map/ppermute | solution.py:197
  12.0 5.0 %collective-permute-start.1 = (bf16[64,1024]{1,0:T(8,128)(2,1)S(1)}, bf16[64,1024]{1,0:T(8,128)(2,1)S(1)}, u32[]{:S(2)}, u32[]{:S(2)}) collective-permute-start(bf16[64,1024]{1,0:T(8,128)(2,1)S(1)} %pad_maximum_fusion.14), channel_id=1, source_target_pairs={{0,8},{1,9},{2,10},{3,11},{4,12},{5,13},{6,14},{7,15},{8,0},{9,1},... | collective-permute-start | bytes 393224 | tf_op jit(solution)/shard_map/ppermute | solution.py:197
  13.7 5.0 %collective-permute-start.6 = (bf16[64,1024]{1,0:T(8,128)(2,1)S(1)}, bf16[64,1024]{1,0:T(8,128)(2,1)S(1)}, u32[]{:S(2)}, u32[]{:S(2)}) collective-permute-start(bf16[64,1024]{1,0:T(8,128)(2,1)S(1)} %pad_maximum_fusion.15), channel_id=1, source_target_pairs={{0,2},{1,3},{2,0},{3,1},{4,6},{5,7},{6,4},{7,5},{8,10},{9,11},{10,... | collective-permute-start | bytes 393224 | tf_op jit(solution)/shard_map/ppermute | solution.py:197
  18.8 6.4 %collective-permute-start.2 = (bf16[128,1024]{1,0:T(8,128)(2,1)S(1)}, bf16[128,1024]{1,0:T(8,128)(2,1)S(1)}, u32[]{:S(2)}, u32[]{:S(2)}) collective-permute-start(bf16[128,1024]{1,0:T(8,128)(2,1)S(1)} %pad_maximum_fusion.12), channel_id=1, source_target_pairs={{0,4},{1,5},{2,6},{3,7},{4,0},{5,1},{6,2},{7,3},{8,12},{9,13},{10,... | collective-permute-start | bytes 786440 | tf_op jit(solution)/shard_map/ppermute | solution.py:197
  20.5 12.1 %collective-permute-start.7 = (bf16[128,1024]{1,0:T(8,128)(2,1)S(1)}, bf16[128,1024]{1,0:T(8,128)(2,1)}, u32[]{:S(2)}, u32[]{:S(2)}) collective-permute-start(bf16[128,1024]{1,0:T(8,128)(2,1)S(1)} %pad_maximum_fusion.13), channel_id=1, source_target_pairs={{0,16},{1,17},{2,18},{3,19},{4,20},{5,21},{6,22},{7,23},{8,24},{9,... | collective-permute-start | bytes 786440 | tf_op jit(solution)/shard_map/ppermute | solution.py:197
  26.2 10.1 %collective-permute-start.3 = (bf16[256,1024]{1,0:T(8,128)(2,1)S(1)}, bf16[256,1024]{1,0:T(8,128)(2,1)}, u32[]{:S(2)}, u32[]{:S(2)}) collective-permute-start(bf16[256,1024]{1,0:T(8,128)(2,1)S(1)} %pad_maximum_fusion.8), channel_id=1, source_target_pairs={{0,2},{1,3},{2,0},{3,1},{4,6},{5,7},{6,4},{7,5},{8,10},{9,11},{10,... | collective-permute-start | bytes 1572872 | tf_op jit(solution)/shard_map/ppermute | solution.py:197
  34.6 13.4 %collective-permute-start.8 = (bf16[256,1024]{1,0:T(8,128)(2,1)}, bf16[256,1024]{1,0:T(8,128)(2,1)}, u32[]{:S(2)}, u32[]{:S(2)}) collective-permute-start(bf16[256,1024]{1,0:T(8,128)(2,1)} %pad_maximum_fusion.9), channel_id=1, source_target_pairs={{0,8},{1,9},{2,10},{3,11},{4,12},{5,13},{6,14},{7,15},{8,0},{9,1},... | collective-permute-start | bytes 1572872 | tf_op jit(solution)/shard_map/ppermute | solution.py:197
  38.7 14.1 %collective-permute-start.4 = (bf16[512,1024]{1,0:T(8,128)(2,1)}, bf16[512,1024]{1,0:T(8,128)(2,1)}, u32[]{:S(2)}, u32[]{:S(2)}) collective-permute-start(bf16[512,1024]{1,0:T(8,128)(2,1)} %pad_maximum_fusion.6), channel_id=1, source_target_pairs={{0,1},{1,0},{2,3},{3,2},{4,5},{5,4},{6,7},{7,6},{8,9},{9,8},{10,11... | collective-permute-start | bytes 3145736 | tf_op jit(solution)/shard_map/ppermute | solution.py:197
  49.4 5.6 %collective-permute-start.9 = (bf16[512,1024]{1,0:T(8,128)(2,1)S(1)}, bf16[512,1024]{1,0:T(8,128)(2,1)S(1)}, u32[]{:S(2)}, u32[]{:S(2)}) collective-permute-start(bf16[512,1024]{1,0:T(8,128)(2,1)S(1)} %pad_maximum_fusion.7), channel_id=1, source_target_pairs={{0,1},{1,0},{2,3},{3,2},{4,5},{5,4},{6,7},{7,6},{8,9},{9,8},{10,11... | collective-permute-start | bytes 3145736 | tf_op jit(solution)/shard_map/ppermute | solution.py:197
  64.3 5.3 %collective-permute-start.10 = (bf16[1024,128]{1,0:T(8,128)(2,1)S(1)}, bf16[1024,128]{1,0:T(8,128)(2,1)S(1)}, u32[]{:S(2)}, u32[]{:S(2)}) collective-permute-start(bf16[1024,128]{1,0:T(8,128)(2,1)S(1)} %fusion.12), channel_id=1, source_target_pairs={{0,1},{1,0},{2,3},{3,2},{4,5},{5,4},{6,7},{7,6},{8,9},{9,8},{10,11... | collective-permute-start | bytes 786440 | tf_op jit(solution)/shard_map/ppermute | solution.py:18
  89.0 3.0 %collective-permute-start.11 = (bf16[512,1024]{1,0:T(8,128)(2,1)}, bf16[512,1024]{1,0:T(8,128)(2,1)}, u32[]{:S(2)}, u32[]{:S(2)}) collective-permute-start(bf16[512,1024]{1,0:T(8,128)(2,1)} %constant_dynamic-slice_fusion.9), channel_id=1, source_target_pairs={{0,1},{1,0},{2,3},{3,2},{4,5},{5,4},{6,7},{7,6},{8,9},{9,8},{10,11... | collective-permute-start | bytes 3145736 | tf_op jit(solution)/shard_map/ppermute | solution.py:104
  91.1 4.5 %collective-permute-start.16 = (bf16[512,1024]{1,0:T(8,128)(2,1)S(1)}, bf16[512,1024]{1,0:T(8,128)(2,1)}, u32[]{:S(2)}, u32[]{:S(2)}) collective-permute-start(bf16[512,1024]{1,0:T(8,128)(2,1)S(1)} %constant_dynamic-slice_fusion.4), channel_id=1, source_target_pairs={{0,1},{1,0},{2,3},{3,2},{4,5},{5,4},{6,7},{7,6},{8,9},{9,8},{10,11... | collective-permute-start | bytes 3145736 | tf_op jit(solution)/shard_map/ppermute | solution.py:104
  94.0 14.2 %collective-permute-start.12 = (bf16[256,1024]{1,0:T(8,128)(2,1)S(1)}, bf16[256,1024]{1,0:T(8,128)(2,1)S(1)}, u32[]{:S(2)}, u32[]{:S(2)}) collective-permute-start(bf16[256,1024]{1,0:T(8,128)(2,1)S(1)} %constant_dynamic-slice_fusion.8), channel_id=1, source_target_pairs={{0,2},{1,3},{2,0},{3,1},{4,6},{5,7},{6,4},{7,5},{8,10},{9,11},{10,... | collective-permute-start | bytes 1572872 | tf_op jit(solution)/shard_map/ppermute | solution.py:104
  97.3 13.9 %collective-permute-start.17 = (bf16[256,1024]{1,0:T(8,128)(2,1)S(1)}, bf16[256,1024]{1,0:T(8,128)(2,1)S(1)}, u32[]{:S(2)}, u32[]{:S(2)}) collective-permute-start(bf16[256,1024]{1,0:T(8,128)(2,1)S(1)} %constant_dynamic-slice_fusion.3), channel_id=1, source_target_pairs={{0,8},{1,9},{2,10},{3,11},{4,12},{5,13},{6,14},{7,15},{8,0},{9,1},... | collective-permute-start | bytes 1572872 | tf_op jit(solution)/shard_map/ppermute | solution.py:104
  108.4 7.7 %collective-permute-start.13 = (bf16[128,1024]{1,0:T(8,128)(2,1)S(1)}, bf16[128,1024]{1,0:T(8,128)(2,1)S(1)}, u32[]{:S(2)}, u32[]{:S(2)}) collective-permute-start(bf16[128,1024]{1,0:T(8,128)(2,1)S(1)} %constant_dynamic-slice_fusion.7), channel_id=1, source_target_pairs={{0,4},{1,5},{2,6},{3,7},{4,0},{5,1},{6,2},{7,3},{8,12},{9,13},{10,... | collective-permute-start | bytes 786440 | tf_op jit(solution)/shard_map/ppermute | solution.py:104
  111.4 23.9 %copy-start.13 = (bf16[32,2048]{1,0:T(8,128)(2,1)S(1)}, bf16[32,2048]{1,0:T(8,128)(2,1)}, u32[]{:S(2)}) copy-start(bf16[32,2048]{1,0:T(8,128)(2,1)} %param.10) | copy-start | bytes 393220
  111.4 13.9 %collective-permute-start.18 = (bf16[128,1024]{1,0:T(8,128)(2,1)S(1)}, bf16[128,1024]{1,0:T(8,128)(2,1)S(1)}, u32[]{:S(2)}, u32[]{:S(2)}) collective-permute-start(bf16[128,1024]{1,0:T(8,128)(2,1)S(1)} %constant_dynamic-slice_fusion.2), channel_id=1, source_target_pairs={{0,16},{1,17},{2,18},{3,19},{4,20},{5,21},{6,22},{7,23},{8,24},{9,... | collective-permute-start | bytes 786440 | tf_op jit(solution)/shard_map/ppermute | solution.py:104
  116.3 9.8 %collective-permute-start.14 = (bf16[64,1024]{1,0:T(8,128)(2,1)S(1)}, bf16[64,1024]{1,0:T(8,128)(2,1)S(1)}, u32[]{:S(2)}, u32[]{:S(2)}) collective-permute-start(bf16[64,1024]{1,0:T(8,128)(2,1)S(1)} %constant_dynamic-slice_fusion.6), channel_id=1, source_target_pairs={{0,8},{1,9},{2,10},{3,11},{4,12},{5,13},{6,14},{7,15},{8,0},{9,1},... | collective-permute-start | bytes 393224 | tf_op jit(solution)/shard_map/ppermute | solution.py:104
  125.5 5.4 %collective-permute-start.19 = (bf16[64,1024]{1,0:T(8,128)(2,1)S(1)}, bf16[64,1024]{1,0:T(8,128)(2,1)S(1)}, u32[]{:S(2)}, u32[]{:S(2)}) collective-permute-start(bf16[64,1024]{1,0:T(8,128)(2,1)S(1)} %constant_dynamic-slice_fusion.1), channel_id=1, source_target_pairs={{0,2},{1,3},{2,0},{3,1},{4,6},{5,7},{6,4},{7,5},{8,10},{9,11},{10,... | collective-permute-start | bytes 393224 | tf_op jit(solution)/shard_map/ppermute | solution.py:104
  126.1 5.8 %collective-permute-start.15 = (bf16[32,1024]{1,0:T(8,128)(2,1)S(1)}, bf16[32,1024]{1,0:T(8,128)(2,1)S(1)}, u32[]{:S(2)}, u32[]{:S(2)}) collective-permute-start(bf16[32,1024]{1,0:T(8,128)(2,1)S(1)} %constant_dynamic-slice_fusion.5), channel_id=1, source_target_pairs={{0,16},{1,17},{2,18},{3,19},{4,20},{5,21},{6,22},{7,23},{8,24},{9,... | collective-permute-start | bytes 196616 | tf_op jit(solution)/shard_map/ppermute | solution.py:104
  131.0 4.3 %collective-permute-start.20 = (bf16[32,1024]{1,0:T(8,128)(2,1)S(1)}, bf16[32,1024]{1,0:T(8,128)(2,1)S(1)}, u32[]{:S(2)}, u32[]{:S(2)}) collective-permute-start(bf16[32,1024]{1,0:T(8,128)(2,1)S(1)} %constant_dynamic-slice_fusion), channel_id=1, source_target_pairs={{0,4},{1,5},{2,6},{3,7},{4,0},{5,1},{6,2},{7,3},{8,12},{9,13},{10,... | collective-permute-start | bytes 196616 | tf_op jit(solution)/shard_map/ppermute | solution.py:104
  (18 other events, 54.8 us)

commit v11 on v7

--- a/solution.py
+++ b/solution.py
@@ -54,12 +54,13 @@
     )
 
 
-def project_kv(normed, weight, positions, first_block):
+def project_kv(normed, weight, tables, first_block):
+    cosine, sine_part = tables
     projected = jnp.dot(normed, weight, preferred_element_type=jnp.float32)
     block_total = weight.shape[1] // HD
     blocks = projected.reshape(normed.shape[0], block_total, HD)
     block_index = first_block + jnp.arange(block_total, dtype=jnp.int32)
-    turned = rotate(blocks, positions)
+    turned = blocks * cosine[:, None, :] + jnp.roll(blocks, HD // 2, axis=2) * sine_part[:, None, :]
     chosen = jnp.where((block_index % 2 == 0)[None, :, None], turned, blocks)
     return chosen.astype(jnp.bfloat16).reshape(normed.shape[0], weight.shape[1])
 
@@ -149,12 +150,12 @@
     )
 
 
-def attend_window(raw_queries, positions, keys, values, segment_ids, gate_here):
+def attend_window(raw_queries, tables, keys, values, segment_ids, gate_here):
     tokens, width = raw_queries.shape
     experts = width // HD
     blocks = tokens // CHUNK
     window = min(blocks, SEG_MOST // CHUNK + 1)
-    cosine, sine_part = rope_tables(positions)
+    cosine, sine_part = tables
     seg_cols = segment_ids.reshape(tokens, 1)
     seg_row = segment_ids.reshape(1, tokens)
     return pl.pallas_call(
@@ -224,7 +225,8 @@
     positions = positions_of(segment_ids)
     kv_width = kv_weight.shape[1]
     block_count = kv_width // HD
-    own_rows = project_kv(normed, kv_weight, positions, device_index * block_count)
+    tables = rope_tables(positions)
+    own_rows = project_kv(normed, kv_weight, tables, device_index * block_count)
     new_cache = write_pages(kv_cache, page_table, own_rows.reshape(page_table.shape[0], PAGE, kv_width))
     partner_rows = swapped(own_rows, "tensor", 0)
     leading_first = device_index % 2 == 0
@@ -234,7 +236,7 @@
     raw_queries = jnp.dot(normed, query_weight, preferred_element_type=jnp.float32)
     first_expert = (device_index * pair_count) % EA
     gate_here = lax.dynamic_slice_in_dim(gates, first_expert, pair_count, 1)
-    flat = attend_window(raw_queries, positions, key_rows, value_rows, segment_ids, gate_here)
+    flat = attend_window(raw_queries, tables, key_rows, value_rows, segment_ids, gate_here)
     partial = jnp.dot(flat, out_weight, preferred_element_type=jnp.float32).astype(jnp.bfloat16)
     reduced = reduce_to_owner(partial, "tensor").astype(jnp.float32)
     attended_out = (hidden.astype(jnp.float32) + reduced).astype(jnp.bfloat16)

time: 121 us -> 123 us (1.017)
  local copies, waits for them, and re-layouts: 7.59 us -> 10.1 us
  starting transfers between devices: 37.4 us -> 36.1 us
    concatenate x2 -> x0, other arithmetic: 3.73 us -> none  [the longest x1 2.42 us: rotate(): jnp.concatenate([leading * cosine - trailing * sine_part, trailing * cosi...]
    unnamed x24 -> x22, local copies, waits for them, and re-layouts: 4 us -> 5.8 us
    convert_element_type x1, other arithmetic: 0.17 us -> 1.46 us  [project_kv(): return chosen.astype(jnp.bfloat16).reshape(normed.shape[0], weight.shape[1])]
    ppermute x20, starting transfers between devices: 16.7 us -> 15.5 us  [reduce_to_owner(): got = lax.ppermute(send, axis, [(i, i ^ 1 << k) for i in range(size)])]
  transfers between devices with their start and end apart: 41 -> 41, of which waited for: 18 -> 18; matrix products, arithmetic and copies ran while one was open for 13% -> 14% of each run, Pallas kernels for 0% -> 0%
where the time goes in v11:
time: 123 us
  starting transfers between devices  36.1 us (29%)
  waiting for transfers between devices  35 us (28%)
  other arithmetic  14.7 us (12%)
  matrix products  12.6 us (10%)
  Pallas kernels  12.5 us (10%)
  local copies, waits for them, and re-layouts  10.1 us (8%)
  between operations  1.5 us (1%)
    ppermute x20, starting transfers between devices, gather_from_all(): got = lax.ppermute(current, axis, [(i, i ^ 1 << k) for i in range(size)])  20.5 us
    ppermute x20, waiting for transfers between devices, reduce_to_owner(): got = lax.ppermute(send, axis, [(i, i ^ 1 << k) for i in range(size)])  20.2 us
    ppermute x20, starting transfers between devices, reduce_to_owner(): got = lax.ppermute(send, axis, [(i, i ^ 1 << k) for i in range(size)])  15.5 us
    ppermute x20, waiting for transfers between devices, gather_from_all(): got = lax.ppermute(current, axis, [(i, i ^ 1 << k) for i in range(size)])  14.8 us
    pallas_call x1, Pallas kernels, attend_window(): pl.pallas_call(lambda *refs: attention_kernel(window, *refs), grid=(block...  12.5 us
    unnamed x22, local copies, waits for them, and re-layouts  5.8 us
    dot_general x1, matrix products, local(): jnp.dot(normed, query_weight, preferred_element_type=jnp.float32)  3.69 us
    dot_general x1, matrix products, project_kv(): projected = jnp.dot(normed, weight, preferred_element_type=jnp.float32)  3.6 us
  transfers between devices with their start and end apart: 41, of which 18 were waited for; matrix products, arithmetic and copies ran while one was open for 14% of the time, Pallas kernels for 0%

profile of v11, /device:TPU:0, one launch (start us, length us, event | category | flops | bytes accessed | tf_op | source)
XLA Modules:
  0.0 122.5 jit_solution(87973693680112091)
XLA Ops:
  3.6 4.1 %collective-permute-start = (bf16[32,512]{1,0:T(8,128)(2,1)S(1)}, bf16[32,512]{1,0:T(8,128)(2,1)S(1)}, u32[]{:S(2)}, u32[]{:S(2)}) collective-permute-start(bf16[32,512]{1,0:T(8,128)(2,1)S(1)} %get-tuple-element.61), channel_id=1, source_target_pairs={{0,16},{1,17},{2,18},{3,19},{4,20},{5,21},{6,22},{7,23},{8,24},{9,... | collective-permute-start | bytes 98312 | tf_op jit(solution)/shard_map/ppermute | solution.py:197
  9.2 1.6 %collective-permute-start.15 = (bf16[32,512]{1,0:T(8,128)(2,1)S(1)}, bf16[32,512]{1,0:T(8,128)(2,1)S(1)}, u32[]{:S(2)}, u32[]{:S(2)}) collective-permute-start(bf16[32,512]{1,0:T(8,128)(2,1)S(1)} %get-tuple-element.62), channel_id=1, source_target_pairs={{0,8},{1,9},{2,10},{3,11},{4,12},{5,13},{6,14},{7,15},{8,0},{9,1},... | collective-permute-start | bytes 98312 | tf_op jit(solution)/shard_map/ppermute | solution.py:197
  13.8 2.9 %fusion.9 = (f32[1024,64]{1,0:T(8,128)S(1)}, f32[1024,64]{1,0:T(8,128)S(1)}, f32[1024,64]{1,0:T(8,128)}) fusion(f32[64]{0:T(128)S(1)} %multiply_power_fusion, f32[1024]{0:T(1024)S(1)} %fusion.12), kind=kLoop, calls=%fused_computation.64 | loop fusion | flops 131072 | bytes 790784 | tf_op jit(solution)/shard_map/neg | solution.py:149
  17.5 1.7 %copy.66.refs_5_ = s32[1024,1]{1,0:T(8,128)} copy(s32[1024,1]{0,1:T(1,128)} %bitcast.85) | data formatting | bytes 8192 | tf_op jit(solution)/shard_map/reshape | solution.py:159
  20.9 2.7 %collective-permute-done.1 = bf16[64,512]{1,0:T(8,128)(2,1)S(1)} collective-permute-done((bf16[64,512]{1,0:T(8,128)(2,1)S(1)}, bf16[64,512]{1,0:T(8,128)(2,1)S(1)}, u32[]{:S(2)}, u32[]{:S(2)}) %collective-permute-start.1) | collective-permute-done | bytes 65568 | tf_op jit(solution)/shard_map/ppermute | solution.py:197
  25.6 1.6 %collective-permute-start.7 = (bf16[128,512]{1,0:T(8,128)(2,1)S(1)}, bf16[128,512]{1,0:T(8,128)(2,1)S(1)}, u32[]{:S(2)}, u32[]{:S(2)}) collective-permute-start(bf16[128,512]{1,0:T(8,128)(2,1)S(1)} %pad_maximum_fusion.16), channel_id=1, source_target_pairs={{0,8},{1,9},{2,10},{3,11},{4,12},{5,13},{6,14},{7,15},{8,0},{9,1},... | collective-permute-start | bytes 393224 | tf_op jit(solution)/shard_map/ppermute | solution.py:197
  32.0 1.6 %collective-permute-start.8 = (bf16[256,512]{1,0:T(8,128)(2,1)S(1)}, bf16[256,512]{1,0:T(8,128)(2,1)S(1)}, u32[]{:S(2)}, u32[]{:S(2)}) collective-permute-start(bf16[256,512]{1,0:T(8,128)(2,1)S(1)} %pad_maximum_fusion.12), channel_id=1, source_target_pairs={{0,4},{1,5},{2,6},{3,7},{4,0},{5,1},{6,2},{7,3},{8,12},{9,13},{10,... | collective-permute-start | bytes 786440 | tf_op jit(solution)/shard_map/ppermute | solution.py:197
  34.9 3.2 %collective-permute-start.18 = (bf16[256,512]{1,0:T(8,128)(2,1)S(1)}, bf16[256,512]{1,0:T(8,128)(2,1)S(1)}, u32[]{:S(2)}, u32[]{:S(2)}) collective-permute-start(bf16[256,512]{1,0:T(8,128)(2,1)S(1)} %pad_maximum_fusion.14), channel_id=1, source_target_pairs={{0,16},{1,17},{2,18},{3,19},{4,20},{5,21},{6,22},{7,23},{8,24},{9,... | collective-permute-start | bytes 786440 | tf_op jit(solution)/shard_map/ppermute | solution.py:197
  39.0 5.5 %collective-permute-done.13 = bf16[256,512]{1,0:T(8,128)(2,1)S(1)} collective-permute-done((bf16[256,512]{1,0:T(8,128)(2,1)S(1)}, bf16[256,512]{1,0:T(8,128)(2,1)S(1)}, u32[]{:S(2)}, u32[]{:S(2)}) %collective-permute-start.13) | collective-permute-done | bytes 262176 | tf_op jit(solution)/shard_map/ppermute | solution.py:197
  49.0 2.0 %copy-done.1 = bf16[1024,2048]{1,0:T(8,128)(2,1)} copy-done((bf16[1024,2048]{1,0:T(8,128)(2,1)}, bf16[1024,2048]{1,0:T(8,128)(2,1)S(1)}, u32[]{:S(2)}) %copy-start.1) | copy-done | bytes 4194328
  52.3 3.6 %fusion.20 = f32[1024,128]{1,0:T(8,128)S(1)} fusion(bf16[1024,2048]{1,0:T(8,128)(2,1)} %copy-done.1, bf16[2048,128]{1,0:T(8,128)(2,1)} %param.13), kind=kOutput, calls=%fused_computation.147 | convolution fusion | flops 536870912 | bytes 5242880 | tf_op jit(solution)/shard_map/dot_general | solution.py:59
  59.1 3.7 %fusion.19.refs_0_ = f32[1024,512]{1,0:T(8,128)} fusion(bf16[1024,2048]{1,0:T(8,128)(2,1)S(1)} %copy-done.2, bf16[2048,512]{1,0:T(8,128)(2,1)S(1)} %copy-done.9), kind=kOutput, calls=%fused_computation.146 | convolution fusion | flops 2147483648 | bytes 8388608 | tf_op jit(solution)/shard_map/dot_general | solution.py:236
  65.5 12.5 %shard_map.113 = bf16[1024,512]{1,0:T(8,128)(2,1)} custom-call(f32[1024,512]{1,0:T(8,128)} %fusion.19.refs_0_, f32[1024,128]{1,0:T(8,128)} %get-tuple-element.26.refs_1_, f32[1024,128]{1,0:T(8,128)} %get-tuple-element.11.refs_2_, bf16[128,1024]{1,0:T(8,128)(2,1)} %copy.65.refs_3_, bf16[1024,128]{1,0:T(8,128)(2,1)} %get-tuple-element.24.refs_4_, ...), custom_call_target="tpu_custom_call" | custom-call | flops 1610612736 | bytes 4718592 | tf_op jit(solution)/shard_map/pallas_call | solution.py:161
  78.0 3.6 %convolution_convert_fusion = bf16[1024,2048]{1,0:T(8,128)(2,1)S(1)} fusion(bf16[1024,512]{1,0:T(8,128)(2,1)} %shard_map.113, bf16[512,2048]{1,0:T(8,128)(2,1)S(1)} %copy-done), kind=kOutput, calls=%fused_computation.1 | convolution fusion | flops 2149580800 | bytes 7340032 | tf_op jit(solution)/shard_map/dot_general | solution.py:240
  86.4 1.6 %collective-permute-start.27 = (bf16[256,512]{1,0:T(8,128)(2,1)S(1)}, bf16[256,512]{1,0:T(8,128)(2,1)S(1)}, u32[]{:S(2)}, u32[]{:S(2)}) collective-permute-start(bf16[256,512]{1,0:T(8,128)(2,1)S(1)} %constant_dynamic-slice_fusion.13), channel_id=1, source_target_pairs={{0,4},{1,5},{2,6},{3,7},{4,0},{5,1},{6,2},{7,3},{8,12},{9,13},{10,... | collective-permute-start | bytes 786440 | tf_op jit(solution)/shard_map/ppermute | solution.py:104
  88.5 2.1 %collective-permute-start.37 = (bf16[256,512]{1,0:T(8,128)(2,1)S(1)}, bf16[256,512]{1,0:T(8,128)(2,1)S(1)}, u32[]{:S(2)}, u32[]{:S(2)}) collective-permute-start(bf16[256,512]{1,0:T(8,128)(2,1)S(1)} %constant_dynamic-slice_fusion.3), channel_id=1, source_target_pairs={{0,16},{1,17},{2,18},{3,19},{4,20},{5,21},{6,22},{7,23},{8,24},{9,... | collective-permute-start | bytes 786440 | tf_op jit(solution)/shard_map/ppermute | solution.py:104
  90.5 3.7 %collective-permute-done.22 = bf16[256,512]{1,0:T(8,128)(2,1)S(1)} collective-permute-done((bf16[256,512]{1,0:T(8,128)(2,1)S(1)}, bf16[256,512]{1,0:T(8,128)(2,1)S(1)}, u32[]{:S(2)}, u32[]{:S(2)}) %collective-permute-start.22) | collective-permute-done | bytes 262176 | tf_op jit(solution)/shard_map/ppermute | solution.py:104
  94.3 1.6 %collective-permute-start.23 = (bf16[128,512]{1,0:T(8,128)(2,1)S(1)}, bf16[128,512]{1,0:T(8,128)(2,1)S(1)}, u32[]{:S(2)}, u32[]{:S(2)}) collective-permute-start(bf16[128,512]{1,0:T(8,128)(2,1)S(1)} %constant_dynamic-slice_fusion.17), channel_id=1, source_target_pairs={{0,4},{1,5},{2,6},{3,7},{4,0},{5,1},{6,2},{7,3},{8,12},{9,13},{10,... | collective-permute-start | bytes 393224 | tf_op jit(solution)/shard_map/ppermute | solution.py:104
  96.1 6.4 %collective-permute-done.32 = bf16[256,512]{1,0:T(8,128)(2,1)S(1)} collective-permute-done((bf16[256,512]{1,0:T(8,128)(2,1)S(1)}, bf16[256,512]{1,0:T(8,128)(2,1)S(1)}, u32[]{:S(2)}, u32[]{:S(2)}) %collective-permute-start.32) | collective-permute-done | bytes 262176 | tf_op jit(solution)/shard_map/ppermute | solution.py:104
  104.9 2.0 %collective-permute-start.24 = (bf16[64,512]{1,0:T(8,128)(2,1)S(1)}, bf16[64,512]{1,0:T(8,128)(2,1)S(1)}, u32[]{:S(2)}, u32[]{:S(2)}) collective-permute-start(bf16[64,512]{1,0:T(8,128)(2,1)S(1)} %constant_dynamic-slice_fusion.16), channel_id=1, source_target_pairs={{0,8},{1,9},{2,10},{3,11},{4,12},{5,13},{6,14},{7,15},{8,0},{9,1},... | collective-permute-start | bytes 196616 | tf_op jit(solution)/shard_map/ppermute | solution.py:104
  107.6 3.2 %collective-permute-done.33 = bf16[128,512]{1,0:T(8,128)(2,1)S(1)} collective-permute-done((bf16[128,512]{1,0:T(8,128)(2,1)S(1)}, bf16[128,512]{1,0:T(8,128)(2,1)S(1)}, u32[]{:S(2)}, u32[]{:S(2)}) %collective-permute-start.33) | collective-permute-done | bytes 131104 | tf_op jit(solution)/shard_map/ppermute | solution.py:104
  110.8 2.6 %collective-permute-start.34 = (bf16[64,512]{1,0:T(8,128)(2,1)S(1)}, bf16[64,512]{1,0:T(8,128)(2,1)S(1)}, u32[]{:S(2)}, u32[]{:S(2)}) collective-permute-start(bf16[64,512]{1,0:T(8,128)(2,1)S(1)} %constant_dynamic-slice_fusion.6), channel_id=1, source_target_pairs={{0,2},{1,3},{2,0},{3,1},{4,6},{5,7},{6,4},{7,5},{8,10},{9,11},{10,... | collective-permute-start | bytes 196616 | tf_op jit(solution)/shard_map/ppermute | solution.py:104
  116.0 1.7 %collective-permute-done.39 = bf16[64,512]{1,0:T(8,128)(2,1)S(1)} collective-permute-done((bf16[64,512]{1,0:T(8,128)(2,1)S(1)}, bf16[64,512]{1,0:T(8,128)(2,1)S(1)}, u32[]{:S(2)}, u32[]{:S(2)}) %collective-permute-start.39) | collective-permute-done | bytes 65568 | tf_op jit(solution)/shard_map/ppermute | solution.py:104
  119.7 2.1 %collective-permute-done.40 = bf16[32,512]{1,0:T(8,128)(2,1)S(1)} collective-permute-done((bf16[32,512]{1,0:T(8,128)(2,1)S(1)}, bf16[32,512]{1,0:T(8,128)(2,1)S(1)}, u32[]{:S(2)}, u32[]{:S(2)}) %collective-permute-start.40) | collective-permute-done | bytes 32800 | tf_op jit(solution)/shard_map/ppermute | solution.py:104
  (198 shorter events, 43.8 us)
Async XLA Ops:
  3.6 15.6 %collective-permute-start = (bf16[32,512]{1,0:T(8,128)(2,1)S(1)}, bf16[32,512]{1,0:T(8,128)(2,1)S(1)}, u32[]{:S(2)}, u32[]{:S(2)}) collective-permute-start(bf16[32,512]{1,0:T(8,128)(2,1)S(1)} %get-tuple-element.61), channel_id=1, source_target_pairs={{0,16},{1,17},{2,18},{3,19},{4,20},{5,21},{6,22},{7,23},{8,24},{9,... | collective-permute-start | bytes 98312 | tf_op jit(solution)/shard_map/ppermute | solution.py:197
  7.7 11.5 %collective-permute-start.10 = (bf16[32,512]{1,0:T(8,128)(2,1)S(1)}, bf16[32,512]{1,0:T(8,128)(2,1)S(1)}, u32[]{:S(2)}, u32[]{:S(2)}) collective-permute-start(bf16[32,512]{1,0:T(8,128)(2,1)S(1)} %get-tuple-element.63), channel_id=1, source_target_pairs={{0,4},{1,5},{2,6},{3,7},{4,0},{5,1},{6,2},{7,3},{8,12},{9,13},{10,... | collective-permute-start | bytes 98312 | tf_op jit(solution)/shard_map/ppermute | solution.py:197
  9.2 10.0 %collective-permute-start.15 = (bf16[32,512]{1,0:T(8,128)(2,1)S(1)}, bf16[32,512]{1,0:T(8,128)(2,1)S(1)}, u32[]{:S(2)}, u32[]{:S(2)}) collective-permute-start(bf16[32,512]{1,0:T(8,128)(2,1)S(1)} %get-tuple-element.62), channel_id=1, source_target_pairs={{0,8},{1,9},{2,10},{3,11},{4,12},{5,13},{6,14},{7,15},{8,0},{9,1},... | collective-permute-start | bytes 98312 | tf_op jit(solution)/shard_map/ppermute | solution.py:197
  10.8 8.4 %collective-permute-start.5 = (bf16[32,512]{1,0:T(8,128)(2,1)S(1)}, bf16[32,512]{1,0:T(8,128)(2,1)S(1)}, u32[]{:S(2)}, u32[]{:S(2)}) collective-permute-start(bf16[32,512]{1,0:T(8,128)(2,1)S(1)} %get-tuple-element.64), channel_id=1, source_target_pairs={{0,2},{1,3},{2,0},{3,1},{4,6},{5,7},{6,4},{7,5},{8,10},{9,11},{10,... | collective-permute-start | bytes 98312 | tf_op jit(solution)/shard_map/ppermute | solution.py:197
  20.1 7.1 %collective-permute-start.11 = (bf16[64,512]{1,0:T(8,128)(2,1)S(1)}, bf16[64,512]{1,0:T(8,128)(2,1)S(1)}, u32[]{:S(2)}, u32[]{:S(2)}) collective-permute-start(bf16[64,512]{1,0:T(8,128)(2,1)S(1)} %pad_maximum_fusion.21), channel_id=1, source_target_pairs={{0,2},{1,3},{2,0},{3,1},{4,6},{5,7},{6,4},{7,5},{8,10},{9,11},{10,... | collective-permute-start | bytes 196616 | tf_op jit(solution)/shard_map/ppermute | solution.py:197
  20.7 6.6 %collective-permute-start.16 = (bf16[64,512]{1,0:T(8,128)(2,1)S(1)}, bf16[64,512]{1,0:T(8,128)(2,1)S(1)}, u32[]{:S(2)}, u32[]{:S(2)}) collective-permute-start(bf16[64,512]{1,0:T(8,128)(2,1)S(1)} %pad_maximum_fusion.22), channel_id=1, source_target_pairs={{0,4},{1,5},{2,6},{3,7},{4,0},{5,1},{6,2},{7,3},{8,12},{9,13},{10,... | collective-permute-start | bytes 196616 | tf_op jit(solution)/shard_map/ppermute | solution.py:197
  27.3 7.3 %collective-permute-start.12 = (bf16[128,512]{1,0:T(8,128)(2,1)S(1)}, bf16[128,512]{1,0:T(8,128)(2,1)S(1)}, u32[]{:S(2)}, u32[]{:S(2)}) collective-permute-start(bf16[128,512]{1,0:T(8,128)(2,1)S(1)} %pad_maximum_fusion.17), channel_id=1, source_target_pairs={{0,16},{1,17},{2,18},{3,19},{4,20},{5,21},{6,22},{7,23},{8,24},{9,... | collective-permute-start | bytes 393224 | tf_op jit(solution)/shard_map/ppermute | solution.py:197
  28.4 6.4 %collective-permute-start.17 = (bf16[128,512]{1,0:T(8,128)(2,1)S(1)}, bf16[128,512]{1,0:T(8,128)(2,1)S(1)}, u32[]{:S(2)}, u32[]{:S(2)}) collective-permute-start(bf16[128,512]{1,0:T(8,128)(2,1)S(1)} %pad_maximum_fusion.18), channel_id=1, source_target_pairs={{0,2},{1,3},{2,0},{3,1},{4,6},{5,7},{6,4},{7,5},{8,10},{9,11},{10,... | collective-permute-start | bytes 393224 | tf_op jit(solution)/shard_map/ppermute | solution.py:197
  30.2 7.9 %collective-permute-start.3 = (bf16[256,512]{1,0:T(8,128)(2,1)S(1)}, bf16[256,512]{1,0:T(8,128)(2,1)S(1)}, u32[]{:S(2)}, u32[]{:S(2)}) collective-permute-start(bf16[256,512]{1,0:T(8,128)(2,1)S(1)} %pad_maximum_fusion.11), channel_id=1, source_target_pairs={{0,2},{1,3},{2,0},{3,1},{4,6},{5,7},{6,4},{7,5},{8,10},{9,11},{10,... | collective-permute-start | bytes 786440 | tf_op jit(solution)/shard_map/ppermute | solution.py:197
  32.0 6.4 %collective-permute-start.8 = (bf16[256,512]{1,0:T(8,128)(2,1)S(1)}, bf16[256,512]{1,0:T(8,128)(2,1)S(1)}, u32[]{:S(2)}, u32[]{:S(2)}) collective-permute-start(bf16[256,512]{1,0:T(8,128)(2,1)S(1)} %pad_maximum_fusion.12), channel_id=1, source_target_pairs={{0,4},{1,5},{2,6},{3,7},{4,0},{5,1},{6,2},{7,3},{8,12},{9,13},{10,... | collective-permute-start | bytes 786440 | tf_op jit(solution)/shard_map/ppermute | solution.py:197
  34.7 9.8 %collective-permute-start.13 = (bf16[256,512]{1,0:T(8,128)(2,1)S(1)}, bf16[256,512]{1,0:T(8,128)(2,1)S(1)}, u32[]{:S(2)}, u32[]{:S(2)}) collective-permute-start(bf16[256,512]{1,0:T(8,128)(2,1)S(1)} %pad_maximum_fusion.13), channel_id=1, source_target_pairs={{0,8},{1,9},{2,10},{3,11},{4,12},{5,13},{6,14},{7,15},{8,0},{9,1},... | collective-permute-start | bytes 786440 | tf_op jit(solution)/shard_map/ppermute | solution.py:197
  34.9 11.0 %collective-permute-start.18 = (bf16[256,512]{1,0:T(8,128)(2,1)S(1)}, bf16[256,512]{1,0:T(8,128)(2,1)S(1)}, u32[]{:S(2)}, u32[]{:S(2)}) collective-permute-start(bf16[256,512]{1,0:T(8,128)(2,1)S(1)} %pad_maximum_fusion.14), channel_id=1, source_target_pairs={{0,16},{1,17},{2,18},{3,19},{4,20},{5,21},{6,22},{7,23},{8,24},{9,... | collective-permute-start | bytes 786440 | tf_op jit(solution)/shard_map/ppermute | solution.py:197
  38.2 7.9 %collective-permute-start.4 = (bf16[512,512]{1,0:T(8,128)(2,1)S(1)}, bf16[512,512]{1,0:T(8,128)(2,1)S(1)}, u32[]{:S(2)}, u32[]{:S(2)}) collective-permute-start(bf16[512,512]{1,0:T(8,128)(2,1)S(1)} %pad_maximum_fusion.5), channel_id=1, source_target_pairs={{0,1},{1,0},{2,3},{3,2},{4,5},{5,4},{6,7},{7,6},{8,9},{9,8},{10,11... | collective-permute-start | bytes 1572872 | tf_op jit(solution)/shard_map/ppermute | solution.py:197
  38.6 7.9 %collective-permute-start.9 = (bf16[512,512]{1,0:T(8,128)(2,1)S(1)}, bf16[512,512]{1,0:T(8,128)(2,1)S(1)}, u32[]{:S(2)}, u32[]{:S(2)}) collective-permute-start(bf16[512,512]{1,0:T(8,128)(2,1)S(1)} %pad_maximum_fusion.6), channel_id=1, source_target_pairs={{0,1},{1,0},{2,3},{3,2},{4,5},{5,4},{6,7},{7,6},{8,9},{9,8},{10,11... | collective-permute-start | bytes 1572872 | tf_op jit(solution)/shard_map/ppermute | solution.py:197
  85.5 8.7 %collective-permute-start.22 = (bf16[256,512]{1,0:T(8,128)(2,1)S(1)}, bf16[256,512]{1,0:T(8,128)(2,1)S(1)}, u32[]{:S(2)}, u32[]{:S(2)}) collective-permute-start(bf16[256,512]{1,0:T(8,128)(2,1)S(1)} %constant_dynamic-slice_fusion.18), channel_id=1, source_target_pairs={{0,2},{1,3},{2,0},{3,1},{4,6},{5,7},{6,4},{7,5},{8,10},{9,11},{10,... | collective-permute-start | bytes 786440 | tf_op jit(solution)/shard_map/ppermute | solution.py:104
  86.4 9.5 %collective-permute-start.27 = (bf16[256,512]{1,0:T(8,128)(2,1)S(1)}, bf16[256,512]{1,0:T(8,128)(2,1)S(1)}, u32[]{:S(2)}, u32[]{:S(2)}) collective-permute-start(bf16[256,512]{1,0:T(8,128)(2,1)S(1)} %constant_dynamic-slice_fusion.13), channel_id=1, source_target_pairs={{0,4},{1,5},{2,6},{3,7},{4,0},{5,1},{6,2},{7,3},{8,12},{9,13},{10,... | collective-permute-start | bytes 786440 | tf_op jit(solution)/shard_map/ppermute | solution.py:104
  88.2 14.3 %collective-permute-start.32 = (bf16[256,512]{1,0:T(8,128)(2,1)S(1)}, bf16[256,512]{1,0:T(8,128)(2,1)S(1)}, u32[]{:S(2)}, u32[]{:S(2)}) collective-permute-start(bf16[256,512]{1,0:T(8,128)(2,1)S(1)} %constant_dynamic-slice_fusion.8), channel_id=1, source_target_pairs={{0,8},{1,9},{2,10},{3,11},{4,12},{5,13},{6,14},{7,15},{8,0},{9,1},... | collective-permute-start | bytes 786440 | tf_op jit(solution)/shard_map/ppermute | solution.py:104
  88.5 14.8 %collective-permute-start.37 = (bf16[256,512]{1,0:T(8,128)(2,1)S(1)}, bf16[256,512]{1,0:T(8,128)(2,1)S(1)}, u32[]{:S(2)}, u32[]{:S(2)}) collective-permute-start(bf16[256,512]{1,0:T(8,128)(2,1)S(1)} %constant_dynamic-slice_fusion.3), channel_id=1, source_target_pairs={{0,16},{1,17},{2,18},{3,19},{4,20},{5,21},{6,22},{7,23},{8,24},{9,... | collective-permute-start | bytes 786440 | tf_op jit(solution)/shard_map/ppermute | solution.py:104
  94.3 10.6 %collective-permute-start.23 = (bf16[128,512]{1,0:T(8,128)(2,1)S(1)}, bf16[128,512]{1,0:T(8,128)(2,1)S(1)}, u32[]{:S(2)}, u32[]{:S(2)}) collective-permute-start(bf16[128,512]{1,0:T(8,128)(2,1)S(1)} %constant_dynamic-slice_fusion.17), channel_id=1, source_target_pairs={{0,4},{1,5},{2,6},{3,7},{4,0},{5,1},{6,2},{7,3},{8,12},{9,13},{10,... | collective-permute-start | bytes 393224 | tf_op jit(solution)/shard_map/ppermute | solution.py:104
  96.0 11.0 %collective-permute-start.28 = (bf16[128,512]{1,0:T(8,128)(2,1)S(1)}, bf16[128,512]{1,0:T(8,128)(2,1)S(1)}, u32[]{:S(2)}, u32[]{:S(2)}) collective-permute-start(bf16[128,512]{1,0:T(8,128)(2,1)S(1)} %constant_dynamic-slice_fusion.12), channel_id=1, source_target_pairs={{0,8},{1,9},{2,10},{3,11},{4,12},{5,13},{6,14},{7,15},{8,0},{9,1},... | collective-permute-start | bytes 393224 | tf_op jit(solution)/shard_map/ppermute | solution.py:104
  102.6 8.2 %collective-permute-start.33 = (bf16[128,512]{1,0:T(8,128)(2,1)S(1)}, bf16[128,512]{1,0:T(8,128)(2,1)S(1)}, u32[]{:S(2)}, u32[]{:S(2)}) collective-permute-start(bf16[128,512]{1,0:T(8,128)(2,1)S(1)} %constant_dynamic-slice_fusion.7), channel_id=1, source_target_pairs={{0,16},{1,17},{2,18},{3,19},{4,20},{5,21},{6,22},{7,23},{8,24},{9,... | collective-permute-start | bytes 393224 | tf_op jit(solution)/shard_map/ppermute | solution.py:104
  103.4 10.0 %collective-permute-start.38 = (bf16[128,512]{1,0:T(8,128)(2,1)S(1)}, bf16[128,512]{1,0:T(8,128)(2,1)S(1)}, u32[]{:S(2)}, u32[]{:S(2)}) collective-permute-start(bf16[128,512]{1,0:T(8,128)(2,1)S(1)} %constant_dynamic-slice_fusion.2), channel_id=1, source_target_pairs={{0,2},{1,3},{2,0},{3,1},{4,6},{5,7},{6,4},{7,5},{8,10},{9,11},{10,... | collective-permute-start | bytes 393224 | tf_op jit(solution)/shard_map/ppermute | solution.py:104
  104.9 8.6 %collective-permute-start.24 = (bf16[64,512]{1,0:T(8,128)(2,1)S(1)}, bf16[64,512]{1,0:T(8,128)(2,1)S(1)}, u32[]{:S(2)}, u32[]{:S(2)}) collective-permute-start(bf16[64,512]{1,0:T(8,128)(2,1)S(1)} %constant_dynamic-slice_fusion.16), channel_id=1, source_target_pairs={{0,8},{1,9},{2,10},{3,11},{4,12},{5,13},{6,14},{7,15},{8,0},{9,1},... | collective-permute-start | bytes 196616 | tf_op jit(solution)/shard_map/ppermute | solution.py:104
  107.0 6.6 %collective-permute-start.29 = (bf16[64,512]{1,0:T(8,128)(2,1)S(1)}, bf16[64,512]{1,0:T(8,128)(2,1)S(1)}, u32[]{:S(2)}, u32[]{:S(2)}) collective-permute-start(bf16[64,512]{1,0:T(8,128)(2,1)S(1)} %constant_dynamic-slice_fusion.11), channel_id=1, source_target_pairs={{0,16},{1,17},{2,18},{3,19},{4,20},{5,21},{6,22},{7,23},{8,24},{9,... | collective-permute-start | bytes 196616 | tf_op jit(solution)/shard_map/ppermute | solution.py:104
  (27 other events, 198.7 us)

commit v12 on v7

--- a/solution.py
+++ b/solution.py
@@ -80,18 +80,21 @@
     return [[0] + rest[j % len(rest):] + rest[:j % len(rest)] for j in range(parts)]
 
 
-def reduce_to_owner(partial, axis):
+def reduce_to_owner(flat, out_weight, axis):
     size = lax.axis_size(axis)
     bits = size.bit_length() - 1
     assert 1 << bits == size
     me = lax.axis_index(axis)
-    rows, width = partial.shape
+    rows = flat.shape[0]
+    width = out_weight.shape[1]
     block = rows // size
     parts = REDUCE_PARTS if width % REDUCE_PARTS == 0 else 1
     piece = width // parts
     outs = []
     for j, order in enumerate(bit_orders(bits, parts)):
-        cols = partial[:, j * piece:(j + 1) * piece]
+        cols = jnp.dot(
+            flat, out_weight[:, j * piece:(j + 1) * piece], preferred_element_type=jnp.float32
+        ).astype(jnp.bfloat16)
         cube = cols.reshape((2,) * bits + (block, piece))
         cube = jnp.transpose(cube, [bits - 1 - k for k in order] + [bits, bits + 1])
         current = cube.reshape(rows, piece)
@@ -235,8 +238,7 @@
     first_expert = (device_index * pair_count) % EA
     gate_here = lax.dynamic_slice_in_dim(gates, first_expert, pair_count, 1)
     flat = attend_window(raw_queries, positions, key_rows, value_rows, segment_ids, gate_here)
-    partial = jnp.dot(flat, out_weight, preferred_element_type=jnp.float32).astype(jnp.bfloat16)
-    reduced = reduce_to_owner(partial, "tensor").astype(jnp.float32)
+    reduced = reduce_to_owner(flat, out_weight, "tensor").astype(jnp.float32)
     attended_out = (hidden.astype(jnp.float32) + reduced).astype(jnp.bfloat16)
     return (attended_out, new_cache)
 

time: 121 us -> 122 us (level)
  matrix products: 12.6 us -> 14.7 us
  local copies, waits for them, and re-layouts: 7.59 us -> 6.03 us
    dot_general x1 -> x4, matrix products: 3.56 us -> 5.65 us  [reduce_to_owner(): jnp.dot(flat, out_weight[:, j * piece:(j + 1) * piece], preferred_element...]
    unnamed x24 -> x26, local copies, waits for them, and re-layouts: 4 us -> 2.76 us
  transfers between devices with their start and end apart: 41 -> 41, of which waited for: 18 -> 18; matrix products, arithmetic and copies ran while one was open for 13% -> 14% of each run, Pallas kernels for 0% -> 0%
where the time goes in v12:
time: 122 us
  starting transfers between devices  37.6 us (31%)
  waiting for transfers between devices  34.2 us (28%)
  other arithmetic  15.7 us (13%)
  matrix products  14.7 us (12%)
  Pallas kernels  12.4 us (10%)
  local copies, waits for them, and re-layouts  6.03 us (5%)
  between operations  1.54 us (1%)
    ppermute x20, starting transfers between devices, gather_from_all(): got = lax.ppermute(current, axis, [(i, i ^ 1 << k) for i in range(size)])  20.5 us
    ppermute x20, waiting for transfers between devices, reduce_to_owner(): got = lax.ppermute(send, axis, [(i, i ^ 1 << k) for i in range(size)])  19.4 us
    ppermute x20, starting transfers between devices, reduce_to_owner(): got = lax.ppermute(send, axis, [(i, i ^ 1 << k) for i in range(size)])  16.9 us
    ppermute x20, waiting for transfers between devices, gather_from_all(): got = lax.ppermute(current, axis, [(i, i ^ 1 << k) for i in range(size)])  14.7 us
    pallas_call x1, Pallas kernels, attend_window(): pl.pallas_call(lambda *refs: attention_kernel(window, *refs), grid=(block...  12.4 us
    dot_general x4, matrix products, reduce_to_owner(): jnp.dot(flat, out_weight[:, j * piece:(j + 1) * piece], preferred_element...  5.65 us
    dot_general x1, matrix products, local(): jnp.dot(normed, query_weight, preferred_element_type=jnp.float32)  3.67 us
    dot_general x1, matrix products, project_kv(): projected = jnp.dot(normed, weight, preferred_element_type=jnp.float32)  3.59 us
  transfers between devices with their start and end apart: 41, of which 18 were waited for; matrix products, arithmetic and copies ran while one was open for 14% of the time, Pallas kernels for 0%

profile of v12, /device:TPU:0, one launch (start us, length us, event | category | flops | bytes accessed | tf_op | source)
XLA Modules:
  0.0 122.1 jit_solution(7847179419270074924)
XLA Ops:
  3.6 4.1 %collective-permute-start = (bf16[32,512]{1,0:T(8,128)(2,1)S(1)}, bf16[32,512]{1,0:T(8,128)(2,1)S(1)}, u32[]{:S(2)}, u32[]{:S(2)}) collective-permute-start(bf16[32,512]{1,0:T(8,128)(2,1)S(1)} %get-tuple-element.54), channel_id=1, source_target_pairs={{0,16},{1,17},{2,18},{3,19},{4,20},{5,21},{6,22},{7,23},{8,24},{9,... | collective-permute-start | bytes 98312 | tf_op jit(solution)/shard_map/ppermute | solution.py:199
  9.2 1.6 %collective-permute-start.15 = (bf16[32,512]{1,0:T(8,128)(2,1)S(1)}, bf16[32,512]{1,0:T(8,128)(2,1)S(1)}, u32[]{:S(2)}, u32[]{:S(2)}) collective-permute-start(bf16[32,512]{1,0:T(8,128)(2,1)S(1)} %get-tuple-element.55), channel_id=1, source_target_pairs={{0,8},{1,9},{2,10},{3,11},{4,12},{5,13},{6,14},{7,15},{8,0},{9,1},... | collective-permute-start | bytes 98312 | tf_op jit(solution)/shard_map/ppermute | solution.py:199
  13.8 1.9 %fusion.19 = (f32[1024,64]{1,0:T(8,128)S(1)}, f32[1024,64]{1,0:T(8,128)S(1)}, f32[1024,64]{1,0:T(8,128)S(1)}) fusion(f32[64]{0:T(128)S(1)} %multiply_power_fusion, f32[1024]{0:T(1024)S(1)} %fusion.22), kind=kLoop, calls=%fused_computation.77 | loop fusion | flops 131072 | bytes 790784 | tf_op jit(solution)/shard_map/neg | solution.py:151
  19.9 2.7 %collective-permute-done.1 = bf16[64,512]{1,0:T(8,128)(2,1)S(1)} collective-permute-done((bf16[64,512]{1,0:T(8,128)(2,1)S(1)}, bf16[64,512]{1,0:T(8,128)(2,1)S(1)}, u32[]{:S(2)}, u32[]{:S(2)}) %collective-permute-start.1) | collective-permute-done | bytes 65568 | tf_op jit(solution)/shard_map/ppermute | solution.py:199
  24.6 1.6 %collective-permute-start.7 = (bf16[128,512]{1,0:T(8,128)(2,1)S(1)}, bf16[128,512]{1,0:T(8,128)(2,1)S(1)}, u32[]{:S(2)}, u32[]{:S(2)}) collective-permute-start(bf16[128,512]{1,0:T(8,128)(2,1)S(1)} %pad_maximum_fusion.16), channel_id=1, source_target_pairs={{0,8},{1,9},{2,10},{3,11},{4,12},{5,13},{6,14},{7,15},{8,0},{9,1},... | collective-permute-start | bytes 393224 | tf_op jit(solution)/shard_map/ppermute | solution.py:199
  31.0 1.6 %collective-permute-start.8 = (bf16[256,512]{1,0:T(8,128)(2,1)S(1)}, bf16[256,512]{1,0:T(8,128)(2,1)S(1)}, u32[]{:S(2)}, u32[]{:S(2)}) collective-permute-start(bf16[256,512]{1,0:T(8,128)(2,1)S(1)} %pad_maximum_fusion.12), channel_id=1, source_target_pairs={{0,4},{1,5},{2,6},{3,7},{4,0},{5,1},{6,2},{7,3},{8,12},{9,13},{10,... | collective-permute-start | bytes 786440 | tf_op jit(solution)/shard_map/ppermute | solution.py:199
  33.9 3.2 %collective-permute-start.18 = (bf16[256,512]{1,0:T(8,128)(2,1)S(1)}, bf16[256,512]{1,0:T(8,128)(2,1)S(1)}, u32[]{:S(2)}, u32[]{:S(2)}) collective-permute-start(bf16[256,512]{1,0:T(8,128)(2,1)S(1)} %pad_maximum_fusion.14), channel_id=1, source_target_pairs={{0,16},{1,17},{2,18},{3,19},{4,20},{5,21},{6,22},{7,23},{8,24},{9,... | collective-permute-start | bytes 786440 | tf_op jit(solution)/shard_map/ppermute | solution.py:199
  38.0 5.5 %collective-permute-done.13 = bf16[256,512]{1,0:T(8,128)(2,1)S(1)} collective-permute-done((bf16[256,512]{1,0:T(8,128)(2,1)S(1)}, bf16[256,512]{1,0:T(8,128)(2,1)S(1)}, u32[]{:S(2)}, u32[]{:S(2)}) %collective-permute-start.13) | collective-permute-done | bytes 262176 | tf_op jit(solution)/shard_map/ppermute | solution.py:199
  50.3 3.6 %fusion.29 = f32[1024,128]{1,0:T(8,128)S(1)} fusion(bf16[1024,2048]{1,0:T(8,128)(2,1)} %copy-done.1, bf16[2048,128]{1,0:T(8,128)(2,1)S(1)} %copy-done.4), kind=kOutput, calls=%fused_computation.159 | convolution fusion | flops 536870912 | bytes 5242880 | tf_op jit(solution)/shard_map/dot_general | solution.py:58
  53.9 2.4 %fusion.6 = (bf16[1024,64]{1,0:T(8,128)(2,1)S(1)}, bf16[1024,64]{1,0:T(8,128)(2,1)S(1)}) fusion(f32[1024,1,128]{2,0,1:T(8,128)S(1)} %bitcast.65, f32[64]{0:T(128)S(1)} %multiply_power_fusion, f32[1024]{0:T(1024)S(1)} %fusion.22), kind=kLoop, calls=%fused_computation.24 | loop fusion | flops 589824 | bytes 790784 | tf_op jit(solution)/shard_map/concatenate | solution.py:52
  56.7 3.7 %fusion.28.refs_0_ = f32[1024,512]{1,0:T(8,128)} fusion(bf16[1024,2048]{1,0:T(8,128)(2,1)S(1)} %copy-done.2, bf16[2048,512]{1,0:T(8,128)(2,1)S(1)} %copy-done), kind=kOutput, calls=%fused_computation.158 | convolution fusion | flops 2147483648 | bytes 8388608 | tf_op jit(solution)/shard_map/dot_general | solution.py:237
  64.6 12.4 %shard_map.113 = bf16[1024,512]{1,0:T(8,128)(2,1)} custom-call(f32[1024,512]{1,0:T(8,128)} %fusion.28.refs_0_, f32[1024,128]{1,0:T(8,128)} %get-tuple-element.71.refs_1_, f32[1024,128]{1,0:T(8,128)} %get-tuple-element.72.refs_2_, bf16[128,1024]{1,0:T(8,128)(2,1)} %copy.61.refs_3_, bf16[1024,128]{1,0:T(8,128)(2,1)} %get-tuple-element.20.refs_4_, ...), custom_call_target="tpu_custom_call" | custom-call | flops 1610612736 | bytes 4718592 | tf_op jit(solution)/shard_map/pallas_call | solution.py:163
  76.9 2.2 %convolution_convert_fusion.3 = bf16[1024,512]{1,0:T(8,128)(2,1)S(1)} fusion(bf16[1024,512]{1,0:T(8,128)(2,1)} %shard_map.113, bf16[512,2048]{1,0:T(8,128)(2,1)} %param.15), kind=kOutput, calls=%fused_computation.4 | convolution fusion | flops 537395200 | bytes 2621440 | tf_op jit(solution)/shard_map/dot_general | solution.py:95
  79.2 2.0 %convolution_convert_fusion.2 = bf16[1024,512]{1,0:T(8,128)(2,1)S(1)} fusion(bf16[1024,512]{1,0:T(8,128)(2,1)} %shard_map.113, bf16[512,2048]{1,0:T(8,128)(2,1)S(1)} %copy-done.10), kind=kOutput, calls=%fused_computation.3 | convolution fusion | flops 537395200 | bytes 2621440 | tf_op jit(solution)/shard_map/dot_general | solution.py:95
  85.6 1.5 %collective-permute-start.27 = (bf16[256,512]{1,0:T(8,128)(2,1)S(1)}, bf16[256,512]{1,0:T(8,128)(2,1)S(1)}, u32[]{:S(2)}, u32[]{:S(2)}) collective-permute-start(bf16[256,512]{1,0:T(8,128)(2,1)S(1)} %constant_dynamic-slice_fusion.13), channel_id=1, source_target_pairs={{0,4},{1,5},{2,6},{3,7},{4,0},{5,1},{6,2},{7,3},{8,12},{9,13},{10,... | collective-permute-start | bytes 786440 | tf_op jit(solution)/shard_map/ppermute | solution.py:106
  87.6 2.1 %collective-permute-start.37 = (bf16[256,512]{1,0:T(8,128)(2,1)S(1)}, bf16[256,512]{1,0:T(8,128)(2,1)S(1)}, u32[]{:S(2)}, u32[]{:S(2)}) collective-permute-start(bf16[256,512]{1,0:T(8,128)(2,1)S(1)} %constant_dynamic-slice_fusion.3), channel_id=1, source_target_pairs={{0,16},{1,17},{2,18},{3,19},{4,20},{5,21},{6,22},{7,23},{8,24},{9,... | collective-permute-start | bytes 786440 | tf_op jit(solution)/shard_map/ppermute | solution.py:106
  89.7 3.7 %collective-permute-done.22 = bf16[256,512]{1,0:T(8,128)(2,1)S(1)} collective-permute-done((bf16[256,512]{1,0:T(8,128)(2,1)S(1)}, bf16[256,512]{1,0:T(8,128)(2,1)S(1)}, u32[]{:S(2)}, u32[]{:S(2)}) %collective-permute-start.22) | collective-permute-done | bytes 262176 | tf_op jit(solution)/shard_map/ppermute | solution.py:106
  93.5 1.6 %collective-permute-start.23 = (bf16[128,512]{1,0:T(8,128)(2,1)S(1)}, bf16[128,512]{1,0:T(8,128)(2,1)S(1)}, u32[]{:S(2)}, u32[]{:S(2)}) collective-permute-start(bf16[128,512]{1,0:T(8,128)(2,1)S(1)} %constant_dynamic-slice_fusion.17), channel_id=1, source_target_pairs={{0,4},{1,5},{2,6},{3,7},{4,0},{5,1},{6,2},{7,3},{8,12},{9,13},{10,... | collective-permute-start | bytes 393224 | tf_op jit(solution)/shard_map/ppermute | solution.py:106
  95.3 6.4 %collective-permute-done.32 = bf16[256,512]{1,0:T(8,128)(2,1)S(1)} collective-permute-done((bf16[256,512]{1,0:T(8,128)(2,1)S(1)}, bf16[256,512]{1,0:T(8,128)(2,1)S(1)}, u32[]{:S(2)}, u32[]{:S(2)}) %collective-permute-start.32) | collective-permute-done | bytes 262176 | tf_op jit(solution)/shard_map/ppermute | solution.py:106
  102.5 1.5 %collective-permute-start.38 = (bf16[128,512]{1,0:T(8,128)(2,1)S(1)}, bf16[128,512]{1,0:T(8,128)(2,1)S(1)}, u32[]{:S(2)}, u32[]{:S(2)}) collective-permute-start(bf16[128,512]{1,0:T(8,128)(2,1)S(1)} %constant_dynamic-slice_fusion.2), channel_id=1, source_target_pairs={{0,2},{1,3},{2,0},{3,1},{4,6},{5,7},{6,4},{7,5},{8,10},{9,11},{10,... | collective-permute-start | bytes 393224 | tf_op jit(solution)/shard_map/ppermute | solution.py:106
  104.1 2.1 %collective-permute-start.24 = (bf16[64,512]{1,0:T(8,128)(2,1)S(1)}, bf16[64,512]{1,0:T(8,128)(2,1)S(1)}, u32[]{:S(2)}, u32[]{:S(2)}) collective-permute-start(bf16[64,512]{1,0:T(8,128)(2,1)S(1)} %constant_dynamic-slice_fusion.16), channel_id=1, source_target_pairs={{0,8},{1,9},{2,10},{3,11},{4,12},{5,13},{6,14},{7,15},{8,0},{9,1},... | collective-permute-start | bytes 196616 | tf_op jit(solution)/shard_map/ppermute | solution.py:106
  106.8 3.3 %collective-permute-done.33 = bf16[128,512]{1,0:T(8,128)(2,1)S(1)} collective-permute-done((bf16[128,512]{1,0:T(8,128)(2,1)S(1)}, bf16[128,512]{1,0:T(8,128)(2,1)S(1)}, u32[]{:S(2)}, u32[]{:S(2)}) %collective-permute-start.33) | collective-permute-done | bytes 131104 | tf_op jit(solution)/shard_map/ppermute | solution.py:106
  110.1 2.8 %collective-permute-start.34 = (bf16[64,512]{1,0:T(8,128)(2,1)S(1)}, bf16[64,512]{1,0:T(8,128)(2,1)S(1)}, u32[]{:S(2)}, u32[]{:S(2)}) collective-permute-start(bf16[64,512]{1,0:T(8,128)(2,1)S(1)} %constant_dynamic-slice_fusion.6), channel_id=1, source_target_pairs={{0,2},{1,3},{2,0},{3,1},{4,6},{5,7},{6,4},{7,5},{8,10},{9,11},{10,... | collective-permute-start | bytes 196616 | tf_op jit(solution)/shard_map/ppermute | solution.py:106
  119.2 2.1 %collective-permute-done.40 = bf16[32,512]{1,0:T(8,128)(2,1)S(1)} collective-permute-done((bf16[32,512]{1,0:T(8,128)(2,1)S(1)}, bf16[32,512]{1,0:T(8,128)(2,1)S(1)}, u32[]{:S(2)}, u32[]{:S(2)}) %collective-permute-start.40) | collective-permute-done | bytes 32800 | tf_op jit(solution)/shard_map/ppermute | solution.py:106
  (205 shorter events, 44.8 us)
Async XLA Ops:
  3.6 14.6 %collective-permute-start = (bf16[32,512]{1,0:T(8,128)(2,1)S(1)}, bf16[32,512]{1,0:T(8,128)(2,1)S(1)}, u32[]{:S(2)}, u32[]{:S(2)}) collective-permute-start(bf16[32,512]{1,0:T(8,128)(2,1)S(1)} %get-tuple-element.54), channel_id=1, source_target_pairs={{0,16},{1,17},{2,18},{3,19},{4,20},{5,21},{6,22},{7,23},{8,24},{9,... | collective-permute-start | bytes 98312 | tf_op jit(solution)/shard_map/ppermute | solution.py:199
  7.7 10.5 %collective-permute-start.10 = (bf16[32,512]{1,0:T(8,128)(2,1)S(1)}, bf16[32,512]{1,0:T(8,128)(2,1)S(1)}, u32[]{:S(2)}, u32[]{:S(2)}) collective-permute-start(bf16[32,512]{1,0:T(8,128)(2,1)S(1)} %get-tuple-element.56), channel_id=1, source_target_pairs={{0,4},{1,5},{2,6},{3,7},{4,0},{5,1},{6,2},{7,3},{8,12},{9,13},{10,... | collective-permute-start | bytes 98312 | tf_op jit(solution)/shard_map/ppermute | solution.py:199
  9.2 9.0 %collective-permute-start.15 = (bf16[32,512]{1,0:T(8,128)(2,1)S(1)}, bf16[32,512]{1,0:T(8,128)(2,1)S(1)}, u32[]{:S(2)}, u32[]{:S(2)}) collective-permute-start(bf16[32,512]{1,0:T(8,128)(2,1)S(1)} %get-tuple-element.55), channel_id=1, source_target_pairs={{0,8},{1,9},{2,10},{3,11},{4,12},{5,13},{6,14},{7,15},{8,0},{9,1},... | collective-permute-start | bytes 98312 | tf_op jit(solution)/shard_map/ppermute | solution.py:199
  10.8 7.4 %collective-permute-start.5 = (bf16[32,512]{1,0:T(8,128)(2,1)S(1)}, bf16[32,512]{1,0:T(8,128)(2,1)S(1)}, u32[]{:S(2)}, u32[]{:S(2)}) collective-permute-start(bf16[32,512]{1,0:T(8,128)(2,1)S(1)} %get-tuple-element.57), channel_id=1, source_target_pairs={{0,2},{1,3},{2,0},{3,1},{4,6},{5,7},{6,4},{7,5},{8,10},{9,11},{10,... | collective-permute-start | bytes 98312 | tf_op jit(solution)/shard_map/ppermute | solution.py:199
  19.1 7.1 %collective-permute-start.11 = (bf16[64,512]{1,0:T(8,128)(2,1)S(1)}, bf16[64,512]{1,0:T(8,128)(2,1)S(1)}, u32[]{:S(2)}, u32[]{:S(2)}) collective-permute-start(bf16[64,512]{1,0:T(8,128)(2,1)S(1)} %pad_maximum_fusion.21), channel_id=1, source_target_pairs={{0,2},{1,3},{2,0},{3,1},{4,6},{5,7},{6,4},{7,5},{8,10},{9,11},{10,... | collective-permute-start | bytes 196616 | tf_op jit(solution)/shard_map/ppermute | solution.py:199
  19.7 6.6 %collective-permute-start.16 = (bf16[64,512]{1,0:T(8,128)(2,1)S(1)}, bf16[64,512]{1,0:T(8,128)(2,1)S(1)}, u32[]{:S(2)}, u32[]{:S(2)}) collective-permute-start(bf16[64,512]{1,0:T(8,128)(2,1)S(1)} %pad_maximum_fusion.22), channel_id=1, source_target_pairs={{0,4},{1,5},{2,6},{3,7},{4,0},{5,1},{6,2},{7,3},{8,12},{9,13},{10,... | collective-permute-start | bytes 196616 | tf_op jit(solution)/shard_map/ppermute | solution.py:199
  26.3 7.3 %collective-permute-start.12 = (bf16[128,512]{1,0:T(8,128)(2,1)S(1)}, bf16[128,512]{1,0:T(8,128)(2,1)S(1)}, u32[]{:S(2)}, u32[]{:S(2)}) collective-permute-start(bf16[128,512]{1,0:T(8,128)(2,1)S(1)} %pad_maximum_fusion.17), channel_id=1, source_target_pairs={{0,16},{1,17},{2,18},{3,19},{4,20},{5,21},{6,22},{7,23},{8,24},{9,... | collective-permute-start | bytes 393224 | tf_op jit(solution)/shard_map/ppermute | solution.py:199
  29.2 7.9 %collective-permute-start.3 = (bf16[256,512]{1,0:T(8,128)(2,1)S(1)}, bf16[256,512]{1,0:T(8,128)(2,1)S(1)}, u32[]{:S(2)}, u32[]{:S(2)}) collective-permute-start(bf16[256,512]{1,0:T(8,128)(2,1)S(1)} %pad_maximum_fusion.11), channel_id=1, source_target_pairs={{0,2},{1,3},{2,0},{3,1},{4,6},{5,7},{6,4},{7,5},{8,10},{9,11},{10,... | collective-permute-start | bytes 786440 | tf_op jit(solution)/shard_map/ppermute | solution.py:199
  31.0 6.4 %collective-permute-start.8 = (bf16[256,512]{1,0:T(8,128)(2,1)S(1)}, bf16[256,512]{1,0:T(8,128)(2,1)S(1)}, u32[]{:S(2)}, u32[]{:S(2)}) collective-permute-start(bf16[256,512]{1,0:T(8,128)(2,1)S(1)} %pad_maximum_fusion.12), channel_id=1, source_target_pairs={{0,4},{1,5},{2,6},{3,7},{4,0},{5,1},{6,2},{7,3},{8,12},{9,13},{10,... | collective-permute-start | bytes 786440 | tf_op jit(solution)/shard_map/ppermute | solution.py:199
  33.7 9.8 %collective-permute-start.13 = (bf16[256,512]{1,0:T(8,128)(2,1)S(1)}, bf16[256,512]{1,0:T(8,128)(2,1)S(1)}, u32[]{:S(2)}, u32[]{:S(2)}) collective-permute-start(bf16[256,512]{1,0:T(8,128)(2,1)S(1)} %pad_maximum_fusion.13), channel_id=1, source_target_pairs={{0,8},{1,9},{2,10},{3,11},{4,12},{5,13},{6,14},{7,15},{8,0},{9,1},... | collective-permute-start | bytes 786440 | tf_op jit(solution)/shard_map/ppermute | solution.py:199
  33.9 11.0 %collective-permute-start.18 = (bf16[256,512]{1,0:T(8,128)(2,1)S(1)}, bf16[256,512]{1,0:T(8,128)(2,1)S(1)}, u32[]{:S(2)}, u32[]{:S(2)}) collective-permute-start(bf16[256,512]{1,0:T(8,128)(2,1)S(1)} %pad_maximum_fusion.14), channel_id=1, source_target_pairs={{0,16},{1,17},{2,18},{3,19},{4,20},{5,21},{6,22},{7,23},{8,24},{9,... | collective-permute-start | bytes 786440 | tf_op jit(solution)/shard_map/ppermute | solution.py:199
  37.2 7.9 %collective-permute-start.4 = (bf16[512,512]{1,0:T(8,128)(2,1)S(1)}, bf16[512,512]{1,0:T(8,128)(2,1)S(1)}, u32[]{:S(2)}, u32[]{:S(2)}) collective-permute-start(bf16[512,512]{1,0:T(8,128)(2,1)S(1)} %pad_maximum_fusion.5), channel_id=1, source_target_pairs={{0,1},{1,0},{2,3},{3,2},{4,5},{5,4},{6,7},{7,6},{8,9},{9,8},{10,11... | collective-permute-start | bytes 1572872 | tf_op jit(solution)/shard_map/ppermute | solution.py:199
  37.6 7.8 %collective-permute-start.9 = (bf16[512,512]{1,0:T(8,128)(2,1)S(1)}, bf16[512,512]{1,0:T(8,128)(2,1)S(1)}, u32[]{:S(2)}, u32[]{:S(2)}) collective-permute-start(bf16[512,512]{1,0:T(8,128)(2,1)S(1)} %pad_maximum_fusion.6), channel_id=1, source_target_pairs={{0,1},{1,0},{2,3},{3,2},{4,5},{5,4},{6,7},{7,6},{8,9},{9,8},{10,11... | collective-permute-start | bytes 1572872 | tf_op jit(solution)/shard_map/ppermute | solution.py:199
  56.5 6.4 %collective-permute-start.20 = (bf16[1024,128]{1,0:T(8,128)(2,1)S(1)}, bf16[1024,128]{1,0:T(8,128)(2,1)S(1)}, u32[]{:S(2)}, u32[]{:S(2)}) collective-permute-start(bf16[1024,128]{1,0:T(8,128)(2,1)S(1)} %fusion.9), channel_id=1, source_target_pairs={{0,1},{1,0},{2,3},{3,2},{4,5},{5,4},{6,7},{7,6},{8,9},{9,8},{10,11... | collective-permute-start | bytes 786440 | tf_op jit(solution)/shard_map/ppermute | solution.py:18
  84.7 8.7 %collective-permute-start.22 = (bf16[256,512]{1,0:T(8,128)(2,1)S(1)}, bf16[256,512]{1,0:T(8,128)(2,1)S(1)}, u32[]{:S(2)}, u32[]{:S(2)}) collective-permute-start(bf16[256,512]{1,0:T(8,128)(2,1)S(1)} %constant_dynamic-slice_fusion.18), channel_id=1, source_target_pairs={{0,2},{1,3},{2,0},{3,1},{4,6},{5,7},{6,4},{7,5},{8,10},{9,11},{10,... | collective-permute-start | bytes 786440 | tf_op jit(solution)/shard_map/ppermute | solution.py:106
  85.6 9.5 %collective-permute-start.27 = (bf16[256,512]{1,0:T(8,128)(2,1)S(1)}, bf16[256,512]{1,0:T(8,128)(2,1)S(1)}, u32[]{:S(2)}, u32[]{:S(2)}) collective-permute-start(bf16[256,512]{1,0:T(8,128)(2,1)S(1)} %constant_dynamic-slice_fusion.13), channel_id=1, source_target_pairs={{0,4},{1,5},{2,6},{3,7},{4,0},{5,1},{6,2},{7,3},{8,12},{9,13},{10,... | collective-permute-start | bytes 786440 | tf_op jit(solution)/shard_map/ppermute | solution.py:106
  87.3 14.4 %collective-permute-start.32 = (bf16[256,512]{1,0:T(8,128)(2,1)S(1)}, bf16[256,512]{1,0:T(8,128)(2,1)S(1)}, u32[]{:S(2)}, u32[]{:S(2)}) collective-permute-start(bf16[256,512]{1,0:T(8,128)(2,1)S(1)} %constant_dynamic-slice_fusion.8), channel_id=1, source_target_pairs={{0,8},{1,9},{2,10},{3,11},{4,12},{5,13},{6,14},{7,15},{8,0},{9,1},... | collective-permute-start | bytes 786440 | tf_op jit(solution)/shard_map/ppermute | solution.py:106
  87.6 14.8 %collective-permute-start.37 = (bf16[256,512]{1,0:T(8,128)(2,1)S(1)}, bf16[256,512]{1,0:T(8,128)(2,1)S(1)}, u32[]{:S(2)}, u32[]{:S(2)}) collective-permute-start(bf16[256,512]{1,0:T(8,128)(2,1)S(1)} %constant_dynamic-slice_fusion.3), channel_id=1, source_target_pairs={{0,16},{1,17},{2,18},{3,19},{4,20},{5,21},{6,22},{7,23},{8,24},{9,... | collective-permute-start | bytes 786440 | tf_op jit(solution)/shard_map/ppermute | solution.py:106
  93.5 10.5 %collective-permute-start.23 = (bf16[128,512]{1,0:T(8,128)(2,1)S(1)}, bf16[128,512]{1,0:T(8,128)(2,1)S(1)}, u32[]{:S(2)}, u32[]{:S(2)}) collective-permute-start(bf16[128,512]{1,0:T(8,128)(2,1)S(1)} %constant_dynamic-slice_fusion.17), channel_id=1, source_target_pairs={{0,4},{1,5},{2,6},{3,7},{4,0},{5,1},{6,2},{7,3},{8,12},{9,13},{10,... | collective-permute-start | bytes 393224 | tf_op jit(solution)/shard_map/ppermute | solution.py:106
  95.2 11.0 %collective-permute-start.28 = (bf16[128,512]{1,0:T(8,128)(2,1)S(1)}, bf16[128,512]{1,0:T(8,128)(2,1)S(1)}, u32[]{:S(2)}, u32[]{:S(2)}) collective-permute-start(bf16[128,512]{1,0:T(8,128)(2,1)S(1)} %constant_dynamic-slice_fusion.12), channel_id=1, source_target_pairs={{0,8},{1,9},{2,10},{3,11},{4,12},{5,13},{6,14},{7,15},{8,0},{9,1},... | collective-permute-start | bytes 393224 | tf_op jit(solution)/shard_map/ppermute | solution.py:106
  101.8 8.3 %collective-permute-start.33 = (bf16[128,512]{1,0:T(8,128)(2,1)S(1)}, bf16[128,512]{1,0:T(8,128)(2,1)S(1)}, u32[]{:S(2)}, u32[]{:S(2)}) collective-permute-start(bf16[128,512]{1,0:T(8,128)(2,1)S(1)} %constant_dynamic-slice_fusion.7), channel_id=1, source_target_pairs={{0,16},{1,17},{2,18},{3,19},{4,20},{5,21},{6,22},{7,23},{8,24},{9,... | collective-permute-start | bytes 393224 | tf_op jit(solution)/shard_map/ppermute | solution.py:106
  102.5 10.5 %collective-permute-start.38 = (bf16[128,512]{1,0:T(8,128)(2,1)S(1)}, bf16[128,512]{1,0:T(8,128)(2,1)S(1)}, u32[]{:S(2)}, u32[]{:S(2)}) collective-permute-start(bf16[128,512]{1,0:T(8,128)(2,1)S(1)} %constant_dynamic-slice_fusion.2), channel_id=1, source_target_pairs={{0,2},{1,3},{2,0},{3,1},{4,6},{5,7},{6,4},{7,5},{8,10},{9,11},{10,... | collective-permute-start | bytes 393224 | tf_op jit(solution)/shard_map/ppermute | solution.py:106
  104.1 9.8 %collective-permute-start.24 = (bf16[64,512]{1,0:T(8,128)(2,1)S(1)}, bf16[64,512]{1,0:T(8,128)(2,1)S(1)}, u32[]{:S(2)}, u32[]{:S(2)}) collective-permute-start(bf16[64,512]{1,0:T(8,128)(2,1)S(1)} %constant_dynamic-slice_fusion.16), channel_id=1, source_target_pairs={{0,8},{1,9},{2,10},{3,11},{4,12},{5,13},{6,14},{7,15},{8,0},{9,1},... | collective-permute-start | bytes 196616 | tf_op jit(solution)/shard_map/ppermute | solution.py:106
  106.2 7.8 %collective-permute-start.29 = (bf16[64,512]{1,0:T(8,128)(2,1)S(1)}, bf16[64,512]{1,0:T(8,128)(2,1)S(1)}, u32[]{:S(2)}, u32[]{:S(2)}) collective-permute-start(bf16[64,512]{1,0:T(8,128)(2,1)S(1)} %constant_dynamic-slice_fusion.11), channel_id=1, source_target_pairs={{0,16},{1,17},{2,18},{3,19},{4,20},{5,21},{6,22},{7,23},{8,24},{9,... | collective-permute-start | bytes 196616 | tf_op jit(solution)/shard_map/ppermute | solution.py:106
  (29 other events, 174.0 us)

commit v13 on v7

--- a/solution.py
+++ b/solution.py
@@ -24,9 +24,19 @@
     return (values * factor * norm_gain.astype(jnp.float32)).astype(jnp.bfloat16)
 
 
-def gate_table(normed, router_weight, routes):
-    logits = jnp.dot(normed, router_weight, preferred_element_type=jnp.float32)
-    expert_ids = jnp.arange(router_weight.shape[1], dtype=jnp.int32)
+def split_dot(pieces, weight):
+    total = None
+    start = 0
+    for piece in pieces:
+        width = piece.shape[1]
+        term = jnp.dot(piece, weight[start:start + width], preferred_element_type=jnp.float32)
+        total = term if total is None else total + term
+        start += width
+    return total
+
+
+def gate_table(logits, routes):
+    expert_ids = jnp.arange(logits.shape[1], dtype=jnp.int32)
     onehot = routes[:, :, None] == expert_ids[None, None, :]
     chosen = jnp.sum(jnp.where(onehot, logits[:, None, :], 0.0), axis=2)
     weights = jax.nn.softmax(chosen, axis=-1)
@@ -54,14 +64,15 @@
     )
 
 
-def project_kv(normed, weight, positions, first_block):
-    projected = jnp.dot(normed, weight, preferred_element_type=jnp.float32)
+def project_kv(pieces, weight, positions, first_block):
+    projected = split_dot(pieces, weight)
+    tokens = projected.shape[0]
     block_total = weight.shape[1] // HD
-    blocks = projected.reshape(normed.shape[0], block_total, HD)
+    blocks = projected.reshape(tokens, block_total, HD)
     block_index = first_block + jnp.arange(block_total, dtype=jnp.int32)
     turned = rotate(blocks, positions)
     chosen = jnp.where((block_index % 2 == 0)[None, :, None], turned, blocks)
-    return chosen.astype(jnp.bfloat16).reshape(normed.shape[0], weight.shape[1])
+    return chosen.astype(jnp.bfloat16).reshape(tokens, weight.shape[1])
 
 
 def write_pages(kv_cache, page_table, rows):
@@ -202,7 +213,7 @@
         old_axis = {order[bits - 1 - a]: a for a in range(bits)}
         cube = jnp.transpose(cube, [old_axis[bits - 1 - a] for a in range(bits)] + [bits, bits + 1])
         outs.append(cube.reshape(size * rows, piece))
-    return jnp.concatenate(outs, axis=1)
+    return outs
 
 
 def local(
@@ -219,19 +230,19 @@
 ):
     device_index = lax.axis_index("tensor")
     token_count = routes.shape[0]
-    normed = gather_from_all(normalize(hidden, norm_gain), "tensor")
-    gates = gate_table(normed, router_weight, routes)
+    pieces = gather_from_all(normalize(hidden, norm_gain), "tensor")
+    gates = gate_table(split_dot(pieces, router_weight), routes)
     positions = positions_of(segment_ids)
     kv_width = kv_weight.shape[1]
     block_count = kv_width // HD
-    own_rows = project_kv(normed, kv_weight, positions, device_index * block_count)
+    own_rows = project_kv(pieces, kv_weight, positions, device_index * block_count)
     new_cache = write_pages(kv_cache, page_table, own_rows.reshape(page_table.shape[0], PAGE, kv_width))
     partner_rows = swapped(own_rows, "tensor", 0)
     leading_first = device_index % 2 == 0
     key_rows = jnp.where(leading_first, own_rows, partner_rows)
     value_rows = jnp.where(leading_first, partner_rows, own_rows)
     pair_count = query_weight.shape[1] // HD
-    raw_queries = jnp.dot(normed, query_weight, preferred_element_type=jnp.float32)
+    raw_queries = split_dot(pieces, query_weight)
     first_expert = (device_index * pair_count) % EA
     gate_here = lax.dynamic_slice_in_dim(gates, first_expert, pair_count, 1)
     flat = attend_window(raw_queries, positions, key_rows, value_rows, segment_ids, gate_here)

time: 121 us -> 128 us (1.058)
  matrix products: 12.6 us -> 19 us
  starting transfers between devices: 37.4 us -> 35.3 us
  local copies, waits for them, and re-layouts: 7.59 us -> 8.88 us
    dot_general x3 -> x12, matrix products: 8.43 us -> 14.8 us  [split_dot(): jnp.dot(piece, weight[start:start + width], preferred_element_type=jnp.fl...]
    ppermute x20, starting transfers between devices: 16.7 us -> 15.4 us  [reduce_to_owner(): got = lax.ppermute(send, axis, [(i, i ^ 1 << k) for i in range(size)])]
    unnamed x24 -> x36, local copies, waits for them, and re-layouts: 4 us -> 5.29 us
  transfers between devices with their start and end apart: 41 -> 41, of which waited for: 18 -> 18; matrix products, arithmetic and copies ran while one was open for 13% -> 17% of each run, Pallas kernels for 0% -> 0%
where the time goes in v13:
time: 128 us; the launch traced here: 127 us
  starting transfers between devices  35.3 us (28%)
  waiting for transfers between devices  35 us (27%)
  matrix products  19 us (15%)
  other arithmetic  15.1 us (12%)
  Pallas kernels  12.4 us (10%)
  local copies, waits for them, and re-layouts  8.88 us (7%)
  between operations  1.57 us (1%)
    ppermute x20, waiting for transfers between devices, reduce_to_owner(): got = lax.ppermute(send, axis, [(i, i ^ 1 << k) for i in range(size)])  19.9 us
    ppermute x20, starting transfers between devices, gather_from_all(): got = lax.ppermute(current, axis, [(i, i ^ 1 << k) for i in range(size)])  19.4 us
    ppermute x20, starting transfers between devices, reduce_to_owner(): got = lax.ppermute(send, axis, [(i, i ^ 1 << k) for i in range(size)])  15.4 us
    ppermute x20, waiting for transfers between devices, gather_from_all(): got = lax.ppermute(current, axis, [(i, i ^ 1 << k) for i in range(size)])  15.1 us
    dot_general x12, matrix products, split_dot(): jnp.dot(piece, weight[start:start + width], preferred_element_type=jnp.fl...  14.8 us
    pallas_call x1, Pallas kernels, attend_window(): pl.pallas_call(lambda *refs: attention_kernel(window, *refs), grid=(block...  12.4 us
    unnamed x36, local copies, waits for them, and re-layouts  5.29 us
    dot_general x1, matrix products, local(): jnp.dot(flat, out_weight, preferred_element_type=jnp.float32)  3.56 us
  transfers between devices with their start and end apart: 41, of which 18 were waited for; matrix products, arithmetic and copies ran while one was open for 17% of the time, Pallas kernels for 0%

profile of v13, /device:TPU:0, one launch (start us, length us, event | category | flops | bytes accessed | tf_op | source)
XLA Modules:
  0.0 127.2 jit_solution(10195947201683709262)
XLA Ops:
  3.6 4.1 %collective-permute-start = (bf16[32,512]{1,0:T(8,128)(2,1)S(1)}, bf16[32,512]{1,0:T(8,128)(2,1)S(1)}, u32[]{:S(2)}, u32[]{:S(2)}) collective-permute-start(bf16[32,512]{1,0:T(8,128)(2,1)S(1)} %get-tuple-element.61), channel_id=1, source_target_pairs={{0,16},{1,17},{2,18},{3,19},{4,20},{5,21},{6,22},{7,23},{8,24},{9,... | collective-permute-start | bytes 98312 | tf_op jit(solution)/shard_map/ppermute | solution.py:207
  13.8 1.9 %fusion.22 = (f32[1024,64]{1,0:T(8,128)S(1)}, f32[1024,64]{1,0:T(8,128)S(1)}, f32[1024,64]{1,0:T(8,128)S(1)}) fusion(f32[64]{0:T(128)S(1)} %multiply_power_fusion, f32[1024]{0:T(1024)S(1)} %fusion.35), kind=kLoop, calls=%fused_computation.83 | loop fusion | flops 131072 | bytes 790784 | tf_op jit(solution)/shard_map/neg | solution.py:159
  19.9 2.7 %collective-permute-done.1 = bf16[64,512]{1,0:T(8,128)(2,1)S(1)} collective-permute-done((bf16[64,512]{1,0:T(8,128)(2,1)S(1)}, bf16[64,512]{1,0:T(8,128)(2,1)S(1)}, u32[]{:S(2)}, u32[]{:S(2)}) %collective-permute-start.1) | collective-permute-done | bytes 65568 | tf_op jit(solution)/shard_map/ppermute | solution.py:207
  24.0 2.1 %collective-permute-start.7 = (bf16[128,512]{1,0:T(8,128)(2,1)S(1)}, bf16[128,512]{1,0:T(8,128)(2,1)S(1)}, u32[]{:S(2)}, u32[]{:S(2)}) collective-permute-start(bf16[128,512]{1,0:T(8,128)(2,1)S(1)} %pad_maximum_fusion.15), channel_id=1, source_target_pairs={{0,8},{1,9},{2,10},{3,11},{4,12},{5,13},{6,14},{7,15},{8,0},{9,1},... | collective-permute-start | bytes 393224 | tf_op jit(solution)/shard_map/ppermute | solution.py:207
  30.6 2.0 %collective-permute-done.2 = bf16[128,512]{1,0:T(8,128)(2,1)S(1)} collective-permute-done((bf16[128,512]{1,0:T(8,128)(2,1)S(1)}, bf16[128,512]{1,0:T(8,128)(2,1)S(1)}, u32[]{:S(2)}, u32[]{:S(2)}) %collective-permute-start.2) | collective-permute-done | bytes 131104 | tf_op jit(solution)/shard_map/ppermute | solution.py:207
  34.0 3.2 %collective-permute-start.18 = (bf16[256,512]{1,0:T(8,128)(2,1)S(1)}, bf16[256,512]{1,0:T(8,128)(2,1)S(1)}, u32[]{:S(2)}, u32[]{:S(2)}) collective-permute-start(bf16[256,512]{1,0:T(8,128)(2,1)S(1)} %pad_maximum_fusion.13), channel_id=1, source_target_pairs={{0,16},{1,17},{2,18},{3,19},{4,20},{5,21},{6,22},{7,23},{8,24},{9,... | collective-permute-start | bytes 786440 | tf_op jit(solution)/shard_map/ppermute | solution.py:207
  37.5 1.6 %collective-permute-done.3 = bf16[256,512]{1,0:T(8,128)(2,1)S(1)} collective-permute-done((bf16[256,512]{1,0:T(8,128)(2,1)S(1)}, bf16[256,512]{1,0:T(8,128)(2,1)S(1)}, u32[]{:S(2)}, u32[]{:S(2)}) %collective-permute-start.3) | collective-permute-done | bytes 262176 | tf_op jit(solution)/shard_map/ppermute | solution.py:207
  39.3 4.4 %collective-permute-done.13 = bf16[256,512]{1,0:T(8,128)(2,1)S(1)} collective-permute-done((bf16[256,512]{1,0:T(8,128)(2,1)S(1)}, bf16[256,512]{1,0:T(8,128)(2,1)S(1)}, u32[]{:S(2)}, u32[]{:S(2)}) %collective-permute-start.13) | collective-permute-done | bytes 262176 | tf_op jit(solution)/shard_map/ppermute | solution.py:207
  47.8 2.0 %fusion.13 = f32[1024,512]{1,0:T(8,128)} fusion(bf16[1024,512]{1,0:T(8,128)(2,1)S(1)} %bitcast.69, bf16[2048,512]{1,0:T(8,128)(2,1)S(1)} %copy-done.9), kind=kOutput, calls=%fused_computation.45 | convolution fusion | flops 536870912 | bytes 3670016 | tf_op jit(solution)/shard_map/dot_general | solution.py:32
  50.2 2.1 %fusion.15 = f32[1024,512]{1,0:T(8,128)} fusion(bf16[1024,512]{1,0:T(8,128)(2,1)S(1)} %bitcast.73, bf16[2048,512]{1,0:T(8,128)(2,1)S(1)} %copy-done.9), kind=kOutput, calls=%fused_computation.47 | convolution fusion | flops 536870912 | bytes 3670016 | tf_op jit(solution)/shard_map/dot_general | solution.py:32
  53.0 2.1 %fusion.11 = f32[1024,512]{1,0:T(8,128)} fusion(bf16[1024,512]{1,0:T(8,128)(2,1)S(1)} %bitcast.79, bf16[2048,512]{1,0:T(8,128)(2,1)S(1)} %copy-done.9), kind=kOutput, calls=%fused_computation.43 | convolution fusion | flops 536870912 | bytes 3670016 | tf_op jit(solution)/shard_map/dot_general | solution.py:32
  58.1 1.8 %fusion.26 = f32[1024,128]{1,0:T(8,128)S(1)} fusion(bf16[1024,512]{1,0:T(8,128)(2,1)} %bitcast.74, bf16[2048,128]{1,0:T(8,128)(2,1)} %param.13), kind=kOutput, calls=%fused_computation.95 | convolution fusion | flops 134217728 | bytes 1703936 | tf_op jit(solution)/shard_map/dot_general | solution.py:32
  62.2 2.6 %fusion.6 = (bf16[1024,64]{1,0:T(8,128)(2,1)S(1)}, bf16[1024,64]{1,0:T(8,128)(2,1)S(1)}) fusion(f32[1024,1,128]{2,0,1:T(8,128)S(1)} %bitcast.81, f32[64]{0:T(128)S(1)} %multiply_power_fusion, f32[1024]{0:T(1024)S(1)} %fusion.35), kind=kLoop, calls=%fused_computation.27 | loop fusion | flops 589824 | bytes 790784 | tf_op jit(solution)/shard_map/concatenate | solution.py:62
  65.6 3.1 %add_add_fusion.refs_0_ = f32[1024,512]{1,0:T(8,128)} fusion(f32[1024,512]{1,0:T(8,128)S(1)} %copy-done.8, f32[1024,512]{1,0:T(8,128)S(1)} %copy-done.7, f32[1024,512]{1,0:T(8,128)S(1)} %copy-done.6, bf16[1024,512]{1,0:T(8,128)(2,1)S(1)} %bitcast.77, bf16[2048,512]{1,0:T(8,128)(2,1)} %param.14), kind=kOutput, calls=%fused_computation.1 | convolution fusion | flops 538443776 | bytes 9961472 | tf_op jit(solution)/shard_map/dot_general | solution.py:32
  70.2 12.4 %shard_map.113 = bf16[1024,512]{1,0:T(8,128)(2,1)} custom-call(f32[1024,512]{1,0:T(8,128)} %add_add_fusion.refs_0_, f32[1024,128]{1,0:T(8,128)} %get-tuple-element.75.refs_1_, f32[1024,128]{1,0:T(8,128)} %get-tuple-element.76.refs_2_, bf16[128,1024]{1,0:T(8,128)(2,1)} %copy.69.refs_3_, bf16[1024,128]{1,0:T(8,128)(2,1)} %get-tuple-element.24.refs_4_, ...), custom_call_target="tpu_custom_call" | custom-call | flops 1610612736 | bytes 4718592 | tf_op jit(solution)/shard_map/pallas_call | solution.py:171
  82.6 3.6 %convolution_convert_fusion = bf16[1024,2048]{1,0:T(8,128)(2,1)S(1)} fusion(bf16[1024,512]{1,0:T(8,128)(2,1)} %shard_map.113, bf16[512,2048]{1,0:T(8,128)(2,1)S(1)} %copy-done), kind=kOutput, calls=%fused_computation | convolution fusion | flops 2149580800 | bytes 7340032 | tf_op jit(solution)/shard_map/dot_general | solution.py:249
  93.5 2.0 %collective-permute-start.37 = (bf16[256,512]{1,0:T(8,128)(2,1)S(1)}, bf16[256,512]{1,0:T(8,128)(2,1)S(1)}, u32[]{:S(2)}, u32[]{:S(2)}) collective-permute-start(bf16[256,512]{1,0:T(8,128)(2,1)S(1)} %constant_dynamic-slice_fusion.3), channel_id=1, source_target_pairs={{0,16},{1,17},{2,18},{3,19},{4,20},{5,21},{6,22},{7,23},{8,24},{9,... | collective-permute-start | bytes 786440 | tf_op jit(solution)/shard_map/ppermute | solution.py:114
  95.5 3.7 %collective-permute-done.22 = bf16[256,512]{1,0:T(8,128)(2,1)S(1)} collective-permute-done((bf16[256,512]{1,0:T(8,128)(2,1)S(1)}, bf16[256,512]{1,0:T(8,128)(2,1)S(1)}, u32[]{:S(2)}, u32[]{:S(2)}) %collective-permute-start.22) | collective-permute-done | bytes 262176 | tf_op jit(solution)/shard_map/ppermute | solution.py:114
  99.3 1.6 %collective-permute-start.23 = (bf16[128,512]{1,0:T(8,128)(2,1)S(1)}, bf16[128,512]{1,0:T(8,128)(2,1)S(1)}, u32[]{:S(2)}, u32[]{:S(2)}) collective-permute-start(bf16[128,512]{1,0:T(8,128)(2,1)S(1)} %constant_dynamic-slice_fusion.17), channel_id=1, source_target_pairs={{0,4},{1,5},{2,6},{3,7},{4,0},{5,1},{6,2},{7,3},{8,12},{9,13},{10,... | collective-permute-start | bytes 393224 | tf_op jit(solution)/shard_map/ppermute | solution.py:114
  101.1 6.4 %collective-permute-done.32 = bf16[256,512]{1,0:T(8,128)(2,1)S(1)} collective-permute-done((bf16[256,512]{1,0:T(8,128)(2,1)S(1)}, bf16[256,512]{1,0:T(8,128)(2,1)S(1)}, u32[]{:S(2)}, u32[]{:S(2)}) %collective-permute-start.32) | collective-permute-done | bytes 262176 | tf_op jit(solution)/shard_map/ppermute | solution.py:114
  109.9 2.0 %collective-permute-start.24 = (bf16[64,512]{1,0:T(8,128)(2,1)S(1)}, bf16[64,512]{1,0:T(8,128)(2,1)S(1)}, u32[]{:S(2)}, u32[]{:S(2)}) collective-permute-start(bf16[64,512]{1,0:T(8,128)(2,1)S(1)} %constant_dynamic-slice_fusion.16), channel_id=1, source_target_pairs={{0,8},{1,9},{2,10},{3,11},{4,12},{5,13},{6,14},{7,15},{8,0},{9,1},... | collective-permute-start | bytes 196616 | tf_op jit(solution)/shard_map/ppermute | solution.py:114
  112.3 3.5 %collective-permute-done.33 = bf16[128,512]{1,0:T(8,128)(2,1)S(1)} collective-permute-done((bf16[128,512]{1,0:T(8,128)(2,1)S(1)}, bf16[128,512]{1,0:T(8,128)(2,1)S(1)}, u32[]{:S(2)}, u32[]{:S(2)}) %collective-permute-start.33) | collective-permute-done | bytes 131104 | tf_op jit(solution)/shard_map/ppermute | solution.py:114
  115.9 2.2 %collective-permute-start.34 = (bf16[64,512]{1,0:T(8,128)(2,1)S(1)}, bf16[64,512]{1,0:T(8,128)(2,1)S(1)}, u32[]{:S(2)}, u32[]{:S(2)}) collective-permute-start(bf16[64,512]{1,0:T(8,128)(2,1)S(1)} %constant_dynamic-slice_fusion.6), channel_id=1, source_target_pairs={{0,2},{1,3},{2,0},{3,1},{4,6},{5,7},{6,4},{7,5},{8,10},{9,11},{10,... | collective-permute-start | bytes 196616 | tf_op jit(solution)/shard_map/ppermute | solution.py:114
  124.3 2.1 %collective-permute-done.40 = bf16[32,512]{1,0:T(8,128)(2,1)S(1)} collective-permute-done((bf16[32,512]{1,0:T(8,128)(2,1)S(1)}, bf16[32,512]{1,0:T(8,128)(2,1)S(1)}, u32[]{:S(2)}, u32[]{:S(2)}) %collective-permute-start.40) | collective-permute-done | bytes 32800 | tf_op jit(solution)/shard_map/ppermute | solution.py:114
  (221 shorter events, 50.5 us)
Async XLA Ops:
  3.6 14.6 %collective-permute-start = (bf16[32,512]{1,0:T(8,128)(2,1)S(1)}, bf16[32,512]{1,0:T(8,128)(2,1)S(1)}, u32[]{:S(2)}, u32[]{:S(2)}) collective-permute-start(bf16[32,512]{1,0:T(8,128)(2,1)S(1)} %get-tuple-element.61), channel_id=1, source_target_pairs={{0,16},{1,17},{2,18},{3,19},{4,20},{5,21},{6,22},{7,23},{8,24},{9,... | collective-permute-start | bytes 98312 | tf_op jit(solution)/shard_map/ppermute | solution.py:207
  7.7 10.5 %collective-permute-start.10 = (bf16[32,512]{1,0:T(8,128)(2,1)S(1)}, bf16[32,512]{1,0:T(8,128)(2,1)S(1)}, u32[]{:S(2)}, u32[]{:S(2)}) collective-permute-start(bf16[32,512]{1,0:T(8,128)(2,1)S(1)} %get-tuple-element.59), channel_id=1, source_target_pairs={{0,4},{1,5},{2,6},{3,7},{4,0},{5,1},{6,2},{7,3},{8,12},{9,13},{10,... | collective-permute-start | bytes 98312 | tf_op jit(solution)/shard_map/ppermute | solution.py:207
  9.2 9.0 %collective-permute-start.15 = (bf16[32,512]{1,0:T(8,128)(2,1)S(1)}, bf16[32,512]{1,0:T(8,128)(2,1)S(1)}, u32[]{:S(2)}, u32[]{:S(2)}) collective-permute-start(bf16[32,512]{1,0:T(8,128)(2,1)S(1)} %get-tuple-element.58), channel_id=1, source_target_pairs={{0,8},{1,9},{2,10},{3,11},{4,12},{5,13},{6,14},{7,15},{8,0},{9,1},... | collective-permute-start | bytes 98312 | tf_op jit(solution)/shard_map/ppermute | solution.py:207
  10.8 7.4 %collective-permute-start.5 = (bf16[32,512]{1,0:T(8,128)(2,1)S(1)}, bf16[32,512]{1,0:T(8,128)(2,1)S(1)}, u32[]{:S(2)}, u32[]{:S(2)}) collective-permute-start(bf16[32,512]{1,0:T(8,128)(2,1)S(1)} %get-tuple-element.60), channel_id=1, source_target_pairs={{0,2},{1,3},{2,0},{3,1},{4,6},{5,7},{6,4},{7,5},{8,10},{9,11},{10,... | collective-permute-start | bytes 98312 | tf_op jit(solution)/shard_map/ppermute | solution.py:207
  19.1 7.6 %collective-permute-start.11 = (bf16[64,512]{1,0:T(8,128)(2,1)S(1)}, bf16[64,512]{1,0:T(8,128)(2,1)S(1)}, u32[]{:S(2)}, u32[]{:S(2)}) collective-permute-start(bf16[64,512]{1,0:T(8,128)(2,1)S(1)} %pad_maximum_fusion.20), channel_id=1, source_target_pairs={{0,2},{1,3},{2,0},{3,1},{4,6},{5,7},{6,4},{7,5},{8,10},{9,11},{10,... | collective-permute-start | bytes 196616 | tf_op jit(solution)/shard_map/ppermute | solution.py:207
  19.6 7.1 %collective-permute-start.16 = (bf16[64,512]{1,0:T(8,128)(2,1)S(1)}, bf16[64,512]{1,0:T(8,128)(2,1)S(1)}, u32[]{:S(2)}, u32[]{:S(2)}) collective-permute-start(bf16[64,512]{1,0:T(8,128)(2,1)S(1)} %pad_maximum_fusion.21), channel_id=1, source_target_pairs={{0,4},{1,5},{2,6},{3,7},{4,0},{5,1},{6,2},{7,3},{8,12},{9,13},{10,... | collective-permute-start | bytes 196616 | tf_op jit(solution)/shard_map/ppermute | solution.py:207
  26.8 7.0 %collective-permute-start.12 = (bf16[128,512]{1,0:T(8,128)(2,1)S(1)}, bf16[128,512]{1,0:T(8,128)(2,1)S(1)}, u32[]{:S(2)}, u32[]{:S(2)}) collective-permute-start(bf16[128,512]{1,0:T(8,128)(2,1)S(1)} %pad_maximum_fusion.16), channel_id=1, source_target_pairs={{0,16},{1,17},{2,18},{3,19},{4,20},{5,21},{6,22},{7,23},{8,24},{9,... | collective-permute-start | bytes 393224 | tf_op jit(solution)/shard_map/ppermute | solution.py:207
  27.4 6.5 %collective-permute-start.17 = (bf16[128,512]{1,0:T(8,128)(2,1)S(1)}, bf16[128,512]{1,0:T(8,128)(2,1)S(1)}, u32[]{:S(2)}, u32[]{:S(2)}) collective-permute-start(bf16[128,512]{1,0:T(8,128)(2,1)S(1)} %pad_maximum_fusion.17), channel_id=1, source_target_pairs={{0,2},{1,3},{2,0},{3,1},{4,6},{5,7},{6,4},{7,5},{8,10},{9,11},{10,... | collective-permute-start | bytes 393224 | tf_op jit(solution)/shard_map/ppermute | solution.py:207
  30.5 6.7 %collective-permute-start.8 = (bf16[256,512]{1,0:T(8,128)(2,1)S(1)}, bf16[256,512]{1,0:T(8,128)(2,1)S(1)}, u32[]{:S(2)}, u32[]{:S(2)}) collective-permute-start(bf16[256,512]{1,0:T(8,128)(2,1)S(1)} %pad_maximum_fusion.11), channel_id=1, source_target_pairs={{0,4},{1,5},{2,6},{3,7},{4,0},{5,1},{6,2},{7,3},{8,12},{9,13},{10,... | collective-permute-start | bytes 786440 | tf_op jit(solution)/shard_map/ppermute | solution.py:207
  33.9 9.8 %collective-permute-start.13 = (bf16[256,512]{1,0:T(8,128)(2,1)S(1)}, bf16[256,512]{1,0:T(8,128)(2,1)S(1)}, u32[]{:S(2)}, u32[]{:S(2)}) collective-permute-start(bf16[256,512]{1,0:T(8,128)(2,1)S(1)} %pad_maximum_fusion.12), channel_id=1, source_target_pairs={{0,8},{1,9},{2,10},{3,11},{4,12},{5,13},{6,14},{7,15},{8,0},{9,1},... | collective-permute-start | bytes 786440 | tf_op jit(solution)/shard_map/ppermute | solution.py:207
  34.0 10.9 %collective-permute-start.18 = (bf16[256,512]{1,0:T(8,128)(2,1)S(1)}, bf16[256,512]{1,0:T(8,128)(2,1)S(1)}, u32[]{:S(2)}, u32[]{:S(2)}) collective-permute-start(bf16[256,512]{1,0:T(8,128)(2,1)S(1)} %pad_maximum_fusion.13), channel_id=1, source_target_pairs={{0,16},{1,17},{2,18},{3,19},{4,20},{5,21},{6,22},{7,23},{8,24},{9,... | collective-permute-start | bytes 786440 | tf_op jit(solution)/shard_map/ppermute | solution.py:207
  37.4 7.7 %collective-permute-start.9 = (bf16[512,512]{1,0:T(8,128)(2,1)S(1)}, bf16[512,512]{1,0:T(8,128)(2,1)S(1)}, u32[]{:S(2)}, u32[]{:S(2)}) collective-permute-start(bf16[512,512]{1,0:T(8,128)(2,1)S(1)} %pad_maximum_fusion.5), channel_id=1, source_target_pairs={{0,1},{1,0},{2,3},{3,2},{4,5},{5,4},{6,7},{7,6},{8,9},{9,8},{10,11... | collective-permute-start | bytes 1572872 | tf_op jit(solution)/shard_map/ppermute | solution.py:207
  43.8 8.4 %collective-permute-start.14 = (bf16[512,512]{1,0:T(8,128)(2,1)S(1)}, bf16[512,512]{1,0:T(8,128)(2,1)S(1)}, u32[]{:S(2)}, u32[]{:S(2)}) collective-permute-start(bf16[512,512]{1,0:T(8,128)(2,1)S(1)} %pad_maximum_fusion.6), channel_id=1, source_target_pairs={{0,1},{1,0},{2,3},{3,2},{4,5},{5,4},{6,7},{7,6},{8,9},{9,8},{10,11... | collective-permute-start | bytes 1572872 | tf_op jit(solution)/shard_map/ppermute | solution.py:207
  45.0 10.1 %collective-permute-start.19 = (bf16[512,512]{1,0:T(8,128)(2,1)S(1)}, bf16[512,512]{1,0:T(8,128)(2,1)S(1)}, u32[]{:S(2)}, u32[]{:S(2)}) collective-permute-start(bf16[512,512]{1,0:T(8,128)(2,1)S(1)} %pad_maximum_fusion.7), channel_id=1, source_target_pairs={{0,1},{1,0},{2,3},{3,2},{4,5},{5,4},{6,7},{7,6},{8,9},{9,8},{10,11... | collective-permute-start | bytes 1572872 | tf_op jit(solution)/shard_map/ppermute | solution.py:207
  90.5 8.7 %collective-permute-start.22 = (bf16[256,512]{1,0:T(8,128)(2,1)S(1)}, bf16[256,512]{1,0:T(8,128)(2,1)S(1)}, u32[]{:S(2)}, u32[]{:S(2)}) collective-permute-start(bf16[256,512]{1,0:T(8,128)(2,1)S(1)} %constant_dynamic-slice_fusion.18), channel_id=1, source_target_pairs={{0,2},{1,3},{2,0},{3,1},{4,6},{5,7},{6,4},{7,5},{8,10},{9,11},{10,... | collective-permute-start | bytes 786440 | tf_op jit(solution)/shard_map/ppermute | solution.py:114
  91.4 9.5 %collective-permute-start.27 = (bf16[256,512]{1,0:T(8,128)(2,1)S(1)}, bf16[256,512]{1,0:T(8,128)(2,1)S(1)}, u32[]{:S(2)}, u32[]{:S(2)}) collective-permute-start(bf16[256,512]{1,0:T(8,128)(2,1)S(1)} %constant_dynamic-slice_fusion.13), channel_id=1, source_target_pairs={{0,4},{1,5},{2,6},{3,7},{4,0},{5,1},{6,2},{7,3},{8,12},{9,13},{10,... | collective-permute-start | bytes 786440 | tf_op jit(solution)/shard_map/ppermute | solution.py:114
  93.2 14.3 %collective-permute-start.32 = (bf16[256,512]{1,0:T(8,128)(2,1)S(1)}, bf16[256,512]{1,0:T(8,128)(2,1)S(1)}, u32[]{:S(2)}, u32[]{:S(2)}) collective-permute-start(bf16[256,512]{1,0:T(8,128)(2,1)S(1)} %constant_dynamic-slice_fusion.8), channel_id=1, source_target_pairs={{0,8},{1,9},{2,10},{3,11},{4,12},{5,13},{6,14},{7,15},{8,0},{9,1},... | collective-permute-start | bytes 786440 | tf_op jit(solution)/shard_map/ppermute | solution.py:114
  93.5 14.8 %collective-permute-start.37 = (bf16[256,512]{1,0:T(8,128)(2,1)S(1)}, bf16[256,512]{1,0:T(8,128)(2,1)S(1)}, u32[]{:S(2)}, u32[]{:S(2)}) collective-permute-start(bf16[256,512]{1,0:T(8,128)(2,1)S(1)} %constant_dynamic-slice_fusion.3), channel_id=1, source_target_pairs={{0,16},{1,17},{2,18},{3,19},{4,20},{5,21},{6,22},{7,23},{8,24},{9,... | collective-permute-start | bytes 786440 | tf_op jit(solution)/shard_map/ppermute | solution.py:114
  99.3 10.5 %collective-permute-start.23 = (bf16[128,512]{1,0:T(8,128)(2,1)S(1)}, bf16[128,512]{1,0:T(8,128)(2,1)S(1)}, u32[]{:S(2)}, u32[]{:S(2)}) collective-permute-start(bf16[128,512]{1,0:T(8,128)(2,1)S(1)} %constant_dynamic-slice_fusion.17), channel_id=1, source_target_pairs={{0,4},{1,5},{2,6},{3,7},{4,0},{5,1},{6,2},{7,3},{8,12},{9,13},{10,... | collective-permute-start | bytes 393224 | tf_op jit(solution)/shard_map/ppermute | solution.py:114
  101.1 10.8 %collective-permute-start.28 = (bf16[128,512]{1,0:T(8,128)(2,1)S(1)}, bf16[128,512]{1,0:T(8,128)(2,1)S(1)}, u32[]{:S(2)}, u32[]{:S(2)}) collective-permute-start(bf16[128,512]{1,0:T(8,128)(2,1)S(1)} %constant_dynamic-slice_fusion.12), channel_id=1, source_target_pairs={{0,8},{1,9},{2,10},{3,11},{4,12},{5,13},{6,14},{7,15},{8,0},{9,1},... | collective-permute-start | bytes 393224 | tf_op jit(solution)/shard_map/ppermute | solution.py:114
  107.7 8.1 %collective-permute-start.33 = (bf16[128,512]{1,0:T(8,128)(2,1)S(1)}, bf16[128,512]{1,0:T(8,128)(2,1)S(1)}, u32[]{:S(2)}, u32[]{:S(2)}) collective-permute-start(bf16[128,512]{1,0:T(8,128)(2,1)S(1)} %constant_dynamic-slice_fusion.7), channel_id=1, source_target_pairs={{0,16},{1,17},{2,18},{3,19},{4,20},{5,21},{6,22},{7,23},{8,24},{9,... | collective-permute-start | bytes 393224 | tf_op jit(solution)/shard_map/ppermute | solution.py:114
  108.4 9.6 %collective-permute-start.38 = (bf16[128,512]{1,0:T(8,128)(2,1)S(1)}, bf16[128,512]{1,0:T(8,128)(2,1)S(1)}, u32[]{:S(2)}, u32[]{:S(2)}) collective-permute-start(bf16[128,512]{1,0:T(8,128)(2,1)S(1)} %constant_dynamic-slice_fusion.2), channel_id=1, source_target_pairs={{0,2},{1,3},{2,0},{3,1},{4,6},{5,7},{6,4},{7,5},{8,10},{9,11},{10,... | collective-permute-start | bytes 393224 | tf_op jit(solution)/shard_map/ppermute | solution.py:114
  109.9 8.4 %collective-permute-start.24 = (bf16[64,512]{1,0:T(8,128)(2,1)S(1)}, bf16[64,512]{1,0:T(8,128)(2,1)S(1)}, u32[]{:S(2)}, u32[]{:S(2)}) collective-permute-start(bf16[64,512]{1,0:T(8,128)(2,1)S(1)} %constant_dynamic-slice_fusion.16), channel_id=1, source_target_pairs={{0,8},{1,9},{2,10},{3,11},{4,12},{5,13},{6,14},{7,15},{8,0},{9,1},... | collective-permute-start | bytes 196616 | tf_op jit(solution)/shard_map/ppermute | solution.py:114
  112.0 6.4 %collective-permute-start.29 = (bf16[64,512]{1,0:T(8,128)(2,1)S(1)}, bf16[64,512]{1,0:T(8,128)(2,1)S(1)}, u32[]{:S(2)}, u32[]{:S(2)}) collective-permute-start(bf16[64,512]{1,0:T(8,128)(2,1)S(1)} %constant_dynamic-slice_fusion.11), channel_id=1, source_target_pairs={{0,16},{1,17},{2,18},{3,19},{4,20},{5,21},{6,22},{7,23},{8,24},{9,... | collective-permute-start | bytes 196616 | tf_op jit(solution)/shard_map/ppermute | solution.py:114
  (34 other events, 217.1 us)

commit v14 on v7

--- a/solution.py
+++ b/solution.py
@@ -233,7 +233,13 @@
     pair_count = query_weight.shape[1] // HD
     raw_queries = jnp.dot(normed, query_weight, preferred_element_type=jnp.float32)
     first_expert = (device_index * pair_count) % EA
-    gate_here = lax.dynamic_slice_in_dim(gates, first_expert, pair_count, 1)
+    gate_here = gates[:, :pair_count]
+    for group in range(1, EA // pair_count):
+        gate_here = jnp.where(
+            first_expert == group * pair_count,
+            gates[:, group * pair_count:(group + 1) * pair_count],
+            gate_here,
+        )
     flat = attend_window(raw_queries, positions, key_rows, value_rows, segment_ids, gate_here)
     partial = jnp.dot(flat, out_weight, preferred_element_type=jnp.float32).astype(jnp.bfloat16)
     reduced = reduce_to_owner(partial, "tensor").astype(jnp.float32)

time: 121 us -> 121 us (level)
    unnamed x24 -> x21, local copies, waits for them, and re-layouts: 4 us -> 2.99 us
where the time goes in v14:
time: 121 us
  starting transfers between devices  38.1 us (31%)
  waiting for transfers between devices  33 us (27%)
  other arithmetic  16.5 us (14%)
  matrix products  12.7 us (10%)
  Pallas kernels  12.4 us (10%)
  local copies, waits for them, and re-layouts  7.01 us (6%)
  between operations  1.51 us (1%)
    ppermute x20, starting transfers between devices, gather_from_all(): got = lax.ppermute(current, axis, [(i, i ^ 1 << k) for i in range(size)])  20.5 us
    ppermute x20, waiting for transfers between devices, reduce_to_owner(): got = lax.ppermute(send, axis, [(i, i ^ 1 << k) for i in range(size)])  18.2 us
    ppermute x20, starting transfers between devices, reduce_to_owner(): got = lax.ppermute(send, axis, [(i, i ^ 1 << k) for i in range(size)])  17.4 us
    ppermute x20, waiting for transfers between devices, gather_from_all(): got = lax.ppermute(current, axis, [(i, i ^ 1 << k) for i in range(size)])  14.7 us
    pallas_call x1, Pallas kernels, attend_window(): pl.pallas_call(lambda *refs: attention_kernel(window, *refs), grid=(block...  12.4 us
    dot_general x1, matrix products, project_kv(): projected = jnp.dot(normed, weight, preferred_element_type=jnp.float32)  3.69 us
    dot_general x1, matrix products, local(): jnp.dot(normed, query_weight, preferred_element_type=jnp.float32)  3.67 us
    dot_general x1, matrix products, local(): jnp.dot(flat, out_weight, preferred_element_type=jnp.float32)  3.56 us
  transfers between devices with their start and end apart: 41, of which 18 were waited for; matrix products, arithmetic and copies ran while one was open for 13% of the time, Pallas kernels for 0%

profile of v14, /device:TPU:0, one launch (start us, length us, event | category | flops | bytes accessed | tf_op | source)
XLA Modules:
  0.0 121.2 jit_solution(13072598614351601628)
XLA Ops:
  3.6 4.1 %collective-permute-start = (bf16[32,512]{1,0:T(8,128)(2,1)S(1)}, bf16[32,512]{1,0:T(8,128)(2,1)S(1)}, u32[]{:S(2)}, u32[]{:S(2)}) collective-permute-start(bf16[32,512]{1,0:T(8,128)(2,1)S(1)} %get-tuple-element.58), channel_id=1, source_target_pairs={{0,16},{1,17},{2,18},{3,19},{4,20},{5,21},{6,22},{7,23},{8,24},{9,... | collective-permute-start | bytes 98312 | tf_op jit(solution)/shard_map/ppermute | solution.py:196
  7.7 1.5 %collective-permute-start.10 = (bf16[32,512]{1,0:T(8,128)(2,1)S(1)}, bf16[32,512]{1,0:T(8,128)(2,1)S(1)}, u32[]{:S(2)}, u32[]{:S(2)}) collective-permute-start(bf16[32,512]{1,0:T(8,128)(2,1)S(1)} %get-tuple-element.60), channel_id=1, source_target_pairs={{0,4},{1,5},{2,6},{3,7},{4,0},{5,1},{6,2},{7,3},{8,12},{9,13},{10,... | collective-permute-start | bytes 98312 | tf_op jit(solution)/shard_map/ppermute | solution.py:196
  9.2 1.6 %collective-permute-start.15 = (bf16[32,512]{1,0:T(8,128)(2,1)S(1)}, bf16[32,512]{1,0:T(8,128)(2,1)S(1)}, u32[]{:S(2)}, u32[]{:S(2)}) collective-permute-start(bf16[32,512]{1,0:T(8,128)(2,1)S(1)} %get-tuple-element.59), channel_id=1, source_target_pairs={{0,8},{1,9},{2,10},{3,11},{4,12},{5,13},{6,14},{7,15},{8,0},{9,1},... | collective-permute-start | bytes 98312 | tf_op jit(solution)/shard_map/ppermute | solution.py:196
  13.8 1.9 %fusion.15 = (f32[1024,64]{1,0:T(8,128)S(1)}, f32[1024,64]{1,0:T(8,128)S(1)}, f32[1024,64]{1,0:T(8,128)S(1)}) fusion(f32[64]{0:T(128)S(1)} %multiply_power_fusion, f32[1024]{0:T(1024)S(1)} %fusion.18), kind=kLoop, calls=%fused_computation.71 | loop fusion | flops 131072 | bytes 790784 | tf_op jit(solution)/shard_map/neg | solution.py:148
  19.9 2.7 %collective-permute-done.1 = bf16[64,512]{1,0:T(8,128)(2,1)S(1)} collective-permute-done((bf16[64,512]{1,0:T(8,128)(2,1)S(1)}, bf16[64,512]{1,0:T(8,128)(2,1)S(1)}, u32[]{:S(2)}, u32[]{:S(2)}) %collective-permute-start.1) | collective-permute-done | bytes 65568 | tf_op jit(solution)/shard_map/ppermute | solution.py:196
  24.6 1.6 %collective-permute-start.7 = (bf16[128,512]{1,0:T(8,128)(2,1)S(1)}, bf16[128,512]{1,0:T(8,128)(2,1)S(1)}, u32[]{:S(2)}, u32[]{:S(2)}) collective-permute-start(bf16[128,512]{1,0:T(8,128)(2,1)S(1)} %pad_maximum_fusion.16), channel_id=1, source_target_pairs={{0,8},{1,9},{2,10},{3,11},{4,12},{5,13},{6,14},{7,15},{8,0},{9,1},... | collective-permute-start | bytes 393224 | tf_op jit(solution)/shard_map/ppermute | solution.py:196
  31.0 1.6 %collective-permute-start.8 = (bf16[256,512]{1,0:T(8,128)(2,1)S(1)}, bf16[256,512]{1,0:T(8,128)(2,1)S(1)}, u32[]{:S(2)}, u32[]{:S(2)}) collective-permute-start(bf16[256,512]{1,0:T(8,128)(2,1)S(1)} %pad_maximum_fusion.12), channel_id=1, source_target_pairs={{0,4},{1,5},{2,6},{3,7},{4,0},{5,1},{6,2},{7,3},{8,12},{9,13},{10,... | collective-permute-start | bytes 786440 | tf_op jit(solution)/shard_map/ppermute | solution.py:196
  33.9 3.2 %collective-permute-start.18 = (bf16[256,512]{1,0:T(8,128)(2,1)S(1)}, bf16[256,512]{1,0:T(8,128)(2,1)S(1)}, u32[]{:S(2)}, u32[]{:S(2)}) collective-permute-start(bf16[256,512]{1,0:T(8,128)(2,1)S(1)} %pad_maximum_fusion.14), channel_id=1, source_target_pairs={{0,16},{1,17},{2,18},{3,19},{4,20},{5,21},{6,22},{7,23},{8,24},{9,... | collective-permute-start | bytes 786440 | tf_op jit(solution)/shard_map/ppermute | solution.py:196
  38.0 5.5 %collective-permute-done.13 = bf16[256,512]{1,0:T(8,128)(2,1)S(1)} collective-permute-done((bf16[256,512]{1,0:T(8,128)(2,1)S(1)}, bf16[256,512]{1,0:T(8,128)(2,1)S(1)}, u32[]{:S(2)}, u32[]{:S(2)}) %collective-permute-start.13) | collective-permute-done | bytes 262176 | tf_op jit(solution)/shard_map/ppermute | solution.py:196
  48.2 1.9 %copy-done.1 = bf16[1024,2048]{1,0:T(8,128)(2,1)} copy-done((bf16[1024,2048]{1,0:T(8,128)(2,1)}, bf16[1024,2048]{1,0:T(8,128)(2,1)S(1)}, u32[]{:S(2)}) %copy-start.1) | copy-done | bytes 4194328
  52.0 3.7 %fusion.27 = f32[1024,128]{1,0:T(8,128)S(1)} fusion(bf16[1024,2048]{1,0:T(8,128)(2,1)} %copy-done.1, bf16[2048,128]{1,0:T(8,128)(2,1)} %param.13), kind=kOutput, calls=%fused_computation.154 | convolution fusion | flops 536870912 | bytes 5242880 | tf_op jit(solution)/shard_map/dot_general | solution.py:58
  55.7 2.4 %fusion.6 = (bf16[1024,64]{1,0:T(8,128)(2,1)S(1)}, bf16[1024,64]{1,0:T(8,128)(2,1)S(1)}) fusion(f32[1024,1,128]{2,0,1:T(8,128)S(1)} %bitcast.63, f32[64]{0:T(128)S(1)} %multiply_power_fusion, f32[1024]{0:T(1024)S(1)} %fusion.18), kind=kLoop, calls=%fused_computation.21 | loop fusion | flops 589824 | bytes 790784 | tf_op jit(solution)/shard_map/concatenate | solution.py:52
  58.5 3.7 %fusion.26.refs_0_ = f32[1024,512]{1,0:T(8,128)} fusion(bf16[1024,2048]{1,0:T(8,128)(2,1)S(1)} %copy-done.2, bf16[2048,512]{1,0:T(8,128)(2,1)S(1)} %copy-done.9), kind=kOutput, calls=%fused_computation.153 | convolution fusion | flops 2147483648 | bytes 8388608 | tf_op jit(solution)/shard_map/dot_general | solution.py:234
  64.6 12.4 %shard_map.113 = bf16[1024,512]{1,0:T(8,128)(2,1)} custom-call(f32[1024,512]{1,0:T(8,128)} %fusion.26.refs_0_, f32[1024,128]{1,0:T(8,128)} %get-tuple-element.77.refs_1_, f32[1024,128]{1,0:T(8,128)} %get-tuple-element.78.refs_2_, bf16[128,1024]{1,0:T(8,128)(2,1)} %copy.62.refs_3_, bf16[1024,128]{1,0:T(8,128)(2,1)} %get-tuple-element.24.refs_4_, ...), custom_call_target="tpu_custom_call" | custom-call | flops 1610612736 | bytes 4718592 | tf_op jit(solution)/shard_map/pallas_call | solution.py:160
  77.0 3.6 %convolution_convert_fusion = bf16[1024,2048]{1,0:T(8,128)(2,1)S(1)} fusion(bf16[1024,512]{1,0:T(8,128)(2,1)} %shard_map.113, bf16[512,2048]{1,0:T(8,128)(2,1)S(1)} %copy-done), kind=kOutput, calls=%fused_computation.1 | convolution fusion | flops 2149580800 | bytes 7340032 | tf_op jit(solution)/shard_map/dot_general | solution.py:244
  85.6 1.5 %collective-permute-start.27 = (bf16[256,512]{1,0:T(8,128)(2,1)S(1)}, bf16[256,512]{1,0:T(8,128)(2,1)S(1)}, u32[]{:S(2)}, u32[]{:S(2)}) collective-permute-start(bf16[256,512]{1,0:T(8,128)(2,1)S(1)} %constant_dynamic-slice_fusion.13), channel_id=1, source_target_pairs={{0,4},{1,5},{2,6},{3,7},{4,0},{5,1},{6,2},{7,3},{8,12},{9,13},{10,... | collective-permute-start | bytes 786440 | tf_op jit(solution)/shard_map/ppermute | solution.py:103
  87.6 2.1 %collective-permute-start.37 = (bf16[256,512]{1,0:T(8,128)(2,1)S(1)}, bf16[256,512]{1,0:T(8,128)(2,1)S(1)}, u32[]{:S(2)}, u32[]{:S(2)}) collective-permute-start(bf16[256,512]{1,0:T(8,128)(2,1)S(1)} %constant_dynamic-slice_fusion.3), channel_id=1, source_target_pairs={{0,16},{1,17},{2,18},{3,19},{4,20},{5,21},{6,22},{7,23},{8,24},{9,... | collective-permute-start | bytes 786440 | tf_op jit(solution)/shard_map/ppermute | solution.py:103
  89.7 3.5 %collective-permute-done.22 = bf16[256,512]{1,0:T(8,128)(2,1)S(1)} collective-permute-done((bf16[256,512]{1,0:T(8,128)(2,1)S(1)}, bf16[256,512]{1,0:T(8,128)(2,1)S(1)}, u32[]{:S(2)}, u32[]{:S(2)}) %collective-permute-start.22) | collective-permute-done | bytes 262176 | tf_op jit(solution)/shard_map/ppermute | solution.py:103
  93.3 1.6 %collective-permute-start.23 = (bf16[128,512]{1,0:T(8,128)(2,1)S(1)}, bf16[128,512]{1,0:T(8,128)(2,1)S(1)}, u32[]{:S(2)}, u32[]{:S(2)}) collective-permute-start(bf16[128,512]{1,0:T(8,128)(2,1)S(1)} %constant_dynamic-slice_fusion.17), channel_id=1, source_target_pairs={{0,4},{1,5},{2,6},{3,7},{4,0},{5,1},{6,2},{7,3},{8,12},{9,13},{10,... | collective-permute-start | bytes 393224 | tf_op jit(solution)/shard_map/ppermute | solution.py:103
  95.1 6.4 %collective-permute-done.32 = bf16[256,512]{1,0:T(8,128)(2,1)S(1)} collective-permute-done((bf16[256,512]{1,0:T(8,128)(2,1)S(1)}, bf16[256,512]{1,0:T(8,128)(2,1)S(1)}, u32[]{:S(2)}, u32[]{:S(2)}) %collective-permute-start.32) | collective-permute-done | bytes 262176 | tf_op jit(solution)/shard_map/ppermute | solution.py:103
  104.1 2.0 %collective-permute-start.24 = (bf16[64,512]{1,0:T(8,128)(2,1)S(1)}, bf16[64,512]{1,0:T(8,128)(2,1)S(1)}, u32[]{:S(2)}, u32[]{:S(2)}) collective-permute-start(bf16[64,512]{1,0:T(8,128)(2,1)S(1)} %constant_dynamic-slice_fusion.16), channel_id=1, source_target_pairs={{0,8},{1,9},{2,10},{3,11},{4,12},{5,13},{6,14},{7,15},{8,0},{9,1},... | collective-permute-start | bytes 196616 | tf_op jit(solution)/shard_map/ppermute | solution.py:103
  107.0 2.8 %collective-permute-done.33 = bf16[128,512]{1,0:T(8,128)(2,1)S(1)} collective-permute-done((bf16[128,512]{1,0:T(8,128)(2,1)S(1)}, bf16[128,512]{1,0:T(8,128)(2,1)S(1)}, u32[]{:S(2)}, u32[]{:S(2)}) %collective-permute-start.33) | collective-permute-done | bytes 131104 | tf_op jit(solution)/shard_map/ppermute | solution.py:103
  109.9 2.2 %collective-permute-start.34 = (bf16[64,512]{1,0:T(8,128)(2,1)S(1)}, bf16[64,512]{1,0:T(8,128)(2,1)S(1)}, u32[]{:S(2)}, u32[]{:S(2)}) collective-permute-start(bf16[64,512]{1,0:T(8,128)(2,1)S(1)} %constant_dynamic-slice_fusion.6), channel_id=1, source_target_pairs={{0,2},{1,3},{2,0},{3,1},{4,6},{5,7},{6,4},{7,5},{8,10},{9,11},{10,... | collective-permute-start | bytes 196616 | tf_op jit(solution)/shard_map/ppermute | solution.py:103
  118.3 2.1 %collective-permute-done.40 = bf16[32,512]{1,0:T(8,128)(2,1)S(1)} collective-permute-done((bf16[32,512]{1,0:T(8,128)(2,1)S(1)}, bf16[32,512]{1,0:T(8,128)(2,1)S(1)}, u32[]{:S(2)}, u32[]{:S(2)}) %collective-permute-start.40) | collective-permute-done | bytes 32800 | tf_op jit(solution)/shard_map/ppermute | solution.py:103
  (201 shorter events, 44.1 us)
Async XLA Ops:
  3.6 14.6 %collective-permute-start = (bf16[32,512]{1,0:T(8,128)(2,1)S(1)}, bf16[32,512]{1,0:T(8,128)(2,1)S(1)}, u32[]{:S(2)}, u32[]{:S(2)}) collective-permute-start(bf16[32,512]{1,0:T(8,128)(2,1)S(1)} %get-tuple-element.58), channel_id=1, source_target_pairs={{0,16},{1,17},{2,18},{3,19},{4,20},{5,21},{6,22},{7,23},{8,24},{9,... | collective-permute-start | bytes 98312 | tf_op jit(solution)/shard_map/ppermute | solution.py:196
  7.7 10.5 %collective-permute-start.10 = (bf16[32,512]{1,0:T(8,128)(2,1)S(1)}, bf16[32,512]{1,0:T(8,128)(2,1)S(1)}, u32[]{:S(2)}, u32[]{:S(2)}) collective-permute-start(bf16[32,512]{1,0:T(8,128)(2,1)S(1)} %get-tuple-element.60), channel_id=1, source_target_pairs={{0,4},{1,5},{2,6},{3,7},{4,0},{5,1},{6,2},{7,3},{8,12},{9,13},{10,... | collective-permute-start | bytes 98312 | tf_op jit(solution)/shard_map/ppermute | solution.py:196
  9.2 9.0 %collective-permute-start.15 = (bf16[32,512]{1,0:T(8,128)(2,1)S(1)}, bf16[32,512]{1,0:T(8,128)(2,1)S(1)}, u32[]{:S(2)}, u32[]{:S(2)}) collective-permute-start(bf16[32,512]{1,0:T(8,128)(2,1)S(1)} %get-tuple-element.59), channel_id=1, source_target_pairs={{0,8},{1,9},{2,10},{3,11},{4,12},{5,13},{6,14},{7,15},{8,0},{9,1},... | collective-permute-start | bytes 98312 | tf_op jit(solution)/shard_map/ppermute | solution.py:196
  10.8 7.4 %collective-permute-start.5 = (bf16[32,512]{1,0:T(8,128)(2,1)S(1)}, bf16[32,512]{1,0:T(8,128)(2,1)S(1)}, u32[]{:S(2)}, u32[]{:S(2)}) collective-permute-start(bf16[32,512]{1,0:T(8,128)(2,1)S(1)} %get-tuple-element.61), channel_id=1, source_target_pairs={{0,2},{1,3},{2,0},{3,1},{4,6},{5,7},{6,4},{7,5},{8,10},{9,11},{10,... | collective-permute-start | bytes 98312 | tf_op jit(solution)/shard_map/ppermute | solution.py:196
  19.1 7.1 %collective-permute-start.11 = (bf16[64,512]{1,0:T(8,128)(2,1)S(1)}, bf16[64,512]{1,0:T(8,128)(2,1)S(1)}, u32[]{:S(2)}, u32[]{:S(2)}) collective-permute-start(bf16[64,512]{1,0:T(8,128)(2,1)S(1)} %pad_maximum_fusion.21), channel_id=1, source_target_pairs={{0,2},{1,3},{2,0},{3,1},{4,6},{5,7},{6,4},{7,5},{8,10},{9,11},{10,... | collective-permute-start | bytes 196616 | tf_op jit(solution)/shard_map/ppermute | solution.py:196
  19.7 6.6 %collective-permute-start.16 = (bf16[64,512]{1,0:T(8,128)(2,1)S(1)}, bf16[64,512]{1,0:T(8,128)(2,1)S(1)}, u32[]{:S(2)}, u32[]{:S(2)}) collective-permute-start(bf16[64,512]{1,0:T(8,128)(2,1)S(1)} %pad_maximum_fusion.22), channel_id=1, source_target_pairs={{0,4},{1,5},{2,6},{3,7},{4,0},{5,1},{6,2},{7,3},{8,12},{9,13},{10,... | collective-permute-start | bytes 196616 | tf_op jit(solution)/shard_map/ppermute | solution.py:196
  26.3 7.3 %collective-permute-start.12 = (bf16[128,512]{1,0:T(8,128)(2,1)S(1)}, bf16[128,512]{1,0:T(8,128)(2,1)S(1)}, u32[]{:S(2)}, u32[]{:S(2)}) collective-permute-start(bf16[128,512]{1,0:T(8,128)(2,1)S(1)} %pad_maximum_fusion.17), channel_id=1, source_target_pairs={{0,16},{1,17},{2,18},{3,19},{4,20},{5,21},{6,22},{7,23},{8,24},{9,... | collective-permute-start | bytes 393224 | tf_op jit(solution)/shard_map/ppermute | solution.py:196
  27.5 6.4 %collective-permute-start.17 = (bf16[128,512]{1,0:T(8,128)(2,1)S(1)}, bf16[128,512]{1,0:T(8,128)(2,1)S(1)}, u32[]{:S(2)}, u32[]{:S(2)}) collective-permute-start(bf16[128,512]{1,0:T(8,128)(2,1)S(1)} %pad_maximum_fusion.18), channel_id=1, source_target_pairs={{0,2},{1,3},{2,0},{3,1},{4,6},{5,7},{6,4},{7,5},{8,10},{9,11},{10,... | collective-permute-start | bytes 393224 | tf_op jit(solution)/shard_map/ppermute | solution.py:196
  29.2 7.9 %collective-permute-start.3 = (bf16[256,512]{1,0:T(8,128)(2,1)S(1)}, bf16[256,512]{1,0:T(8,128)(2,1)S(1)}, u32[]{:S(2)}, u32[]{:S(2)}) collective-permute-start(bf16[256,512]{1,0:T(8,128)(2,1)S(1)} %pad_maximum_fusion.11), channel_id=1, source_target_pairs={{0,2},{1,3},{2,0},{3,1},{4,6},{5,7},{6,4},{7,5},{8,10},{9,11},{10,... | collective-permute-start | bytes 786440 | tf_op jit(solution)/shard_map/ppermute | solution.py:196
  31.0 6.4 %collective-permute-start.8 = (bf16[256,512]{1,0:T(8,128)(2,1)S(1)}, bf16[256,512]{1,0:T(8,128)(2,1)S(1)}, u32[]{:S(2)}, u32[]{:S(2)}) collective-permute-start(bf16[256,512]{1,0:T(8,128)(2,1)S(1)} %pad_maximum_fusion.12), channel_id=1, source_target_pairs={{0,4},{1,5},{2,6},{3,7},{4,0},{5,1},{6,2},{7,3},{8,12},{9,13},{10,... | collective-permute-start | bytes 786440 | tf_op jit(solution)/shard_map/ppermute | solution.py:196
  33.7 9.8 %collective-permute-start.13 = (bf16[256,512]{1,0:T(8,128)(2,1)S(1)}, bf16[256,512]{1,0:T(8,128)(2,1)S(1)}, u32[]{:S(2)}, u32[]{:S(2)}) collective-permute-start(bf16[256,512]{1,0:T(8,128)(2,1)S(1)} %pad_maximum_fusion.13), channel_id=1, source_target_pairs={{0,8},{1,9},{2,10},{3,11},{4,12},{5,13},{6,14},{7,15},{8,0},{9,1},... | collective-permute-start | bytes 786440 | tf_op jit(solution)/shard_map/ppermute | solution.py:196
  33.9 11.0 %collective-permute-start.18 = (bf16[256,512]{1,0:T(8,128)(2,1)S(1)}, bf16[256,512]{1,0:T(8,128)(2,1)S(1)}, u32[]{:S(2)}, u32[]{:S(2)}) collective-permute-start(bf16[256,512]{1,0:T(8,128)(2,1)S(1)} %pad_maximum_fusion.14), channel_id=1, source_target_pairs={{0,16},{1,17},{2,18},{3,19},{4,20},{5,21},{6,22},{7,23},{8,24},{9,... | collective-permute-start | bytes 786440 | tf_op jit(solution)/shard_map/ppermute | solution.py:196
  37.2 7.9 %collective-permute-start.4 = (bf16[512,512]{1,0:T(8,128)(2,1)S(1)}, bf16[512,512]{1,0:T(8,128)(2,1)S(1)}, u32[]{:S(2)}, u32[]{:S(2)}) collective-permute-start(bf16[512,512]{1,0:T(8,128)(2,1)S(1)} %pad_maximum_fusion.5), channel_id=1, source_target_pairs={{0,1},{1,0},{2,3},{3,2},{4,5},{5,4},{6,7},{7,6},{8,9},{9,8},{10,11... | collective-permute-start | bytes 1572872 | tf_op jit(solution)/shard_map/ppermute | solution.py:196
  37.6 7.8 %collective-permute-start.9 = (bf16[512,512]{1,0:T(8,128)(2,1)S(1)}, bf16[512,512]{1,0:T(8,128)(2,1)S(1)}, u32[]{:S(2)}, u32[]{:S(2)}) collective-permute-start(bf16[512,512]{1,0:T(8,128)(2,1)S(1)} %pad_maximum_fusion.6), channel_id=1, source_target_pairs={{0,1},{1,0},{2,3},{3,2},{4,5},{5,4},{6,7},{7,6},{8,9},{9,8},{10,11... | collective-permute-start | bytes 1572872 | tf_op jit(solution)/shard_map/ppermute | solution.py:196
  84.8 8.4 %collective-permute-start.22 = (bf16[256,512]{1,0:T(8,128)(2,1)S(1)}, bf16[256,512]{1,0:T(8,128)(2,1)S(1)}, u32[]{:S(2)}, u32[]{:S(2)}) collective-permute-start(bf16[256,512]{1,0:T(8,128)(2,1)S(1)} %constant_dynamic-slice_fusion.18), channel_id=1, source_target_pairs={{0,2},{1,3},{2,0},{3,1},{4,6},{5,7},{6,4},{7,5},{8,10},{9,11},{10,... | collective-permute-start | bytes 786440 | tf_op jit(solution)/shard_map/ppermute | solution.py:103
  85.6 9.3 %collective-permute-start.27 = (bf16[256,512]{1,0:T(8,128)(2,1)S(1)}, bf16[256,512]{1,0:T(8,128)(2,1)S(1)}, u32[]{:S(2)}, u32[]{:S(2)}) collective-permute-start(bf16[256,512]{1,0:T(8,128)(2,1)S(1)} %constant_dynamic-slice_fusion.13), channel_id=1, source_target_pairs={{0,4},{1,5},{2,6},{3,7},{4,0},{5,1},{6,2},{7,3},{8,12},{9,13},{10,... | collective-permute-start | bytes 786440 | tf_op jit(solution)/shard_map/ppermute | solution.py:103
  87.4 14.1 %collective-permute-start.32 = (bf16[256,512]{1,0:T(8,128)(2,1)S(1)}, bf16[256,512]{1,0:T(8,128)(2,1)S(1)}, u32[]{:S(2)}, u32[]{:S(2)}) collective-permute-start(bf16[256,512]{1,0:T(8,128)(2,1)S(1)} %constant_dynamic-slice_fusion.8), channel_id=1, source_target_pairs={{0,8},{1,9},{2,10},{3,11},{4,12},{5,13},{6,14},{7,15},{8,0},{9,1},... | collective-permute-start | bytes 786440 | tf_op jit(solution)/shard_map/ppermute | solution.py:103
  87.6 14.9 %collective-permute-start.37 = (bf16[256,512]{1,0:T(8,128)(2,1)S(1)}, bf16[256,512]{1,0:T(8,128)(2,1)S(1)}, u32[]{:S(2)}, u32[]{:S(2)}) collective-permute-start(bf16[256,512]{1,0:T(8,128)(2,1)S(1)} %constant_dynamic-slice_fusion.3), channel_id=1, source_target_pairs={{0,16},{1,17},{2,18},{3,19},{4,20},{5,21},{6,22},{7,23},{8,24},{9,... | collective-permute-start | bytes 786440 | tf_op jit(solution)/shard_map/ppermute | solution.py:103
  93.3 10.7 %collective-permute-start.23 = (bf16[128,512]{1,0:T(8,128)(2,1)S(1)}, bf16[128,512]{1,0:T(8,128)(2,1)S(1)}, u32[]{:S(2)}, u32[]{:S(2)}) collective-permute-start(bf16[128,512]{1,0:T(8,128)(2,1)S(1)} %constant_dynamic-slice_fusion.17), channel_id=1, source_target_pairs={{0,4},{1,5},{2,6},{3,7},{4,0},{5,1},{6,2},{7,3},{8,12},{9,13},{10,... | collective-permute-start | bytes 393224 | tf_op jit(solution)/shard_map/ppermute | solution.py:103
  95.0 11.1 %collective-permute-start.28 = (bf16[128,512]{1,0:T(8,128)(2,1)S(1)}, bf16[128,512]{1,0:T(8,128)(2,1)S(1)}, u32[]{:S(2)}, u32[]{:S(2)}) collective-permute-start(bf16[128,512]{1,0:T(8,128)(2,1)S(1)} %constant_dynamic-slice_fusion.12), channel_id=1, source_target_pairs={{0,8},{1,9},{2,10},{3,11},{4,12},{5,13},{6,14},{7,15},{8,0},{9,1},... | collective-permute-start | bytes 393224 | tf_op jit(solution)/shard_map/ppermute | solution.py:103
  101.6 8.2 %collective-permute-start.33 = (bf16[128,512]{1,0:T(8,128)(2,1)S(1)}, bf16[128,512]{1,0:T(8,128)(2,1)S(1)}, u32[]{:S(2)}, u32[]{:S(2)}) collective-permute-start(bf16[128,512]{1,0:T(8,128)(2,1)S(1)} %constant_dynamic-slice_fusion.7), channel_id=1, source_target_pairs={{0,16},{1,17},{2,18},{3,19},{4,20},{5,21},{6,22},{7,23},{8,24},{9,... | collective-permute-start | bytes 393224 | tf_op jit(solution)/shard_map/ppermute | solution.py:103
  102.6 9.4 %collective-permute-start.38 = (bf16[128,512]{1,0:T(8,128)(2,1)S(1)}, bf16[128,512]{1,0:T(8,128)(2,1)S(1)}, u32[]{:S(2)}, u32[]{:S(2)}) collective-permute-start(bf16[128,512]{1,0:T(8,128)(2,1)S(1)} %constant_dynamic-slice_fusion.2), channel_id=1, source_target_pairs={{0,2},{1,3},{2,0},{3,1},{4,6},{5,7},{6,4},{7,5},{8,10},{9,11},{10,... | collective-permute-start | bytes 393224 | tf_op jit(solution)/shard_map/ppermute | solution.py:103
  104.1 8.4 %collective-permute-start.24 = (bf16[64,512]{1,0:T(8,128)(2,1)S(1)}, bf16[64,512]{1,0:T(8,128)(2,1)S(1)}, u32[]{:S(2)}, u32[]{:S(2)}) collective-permute-start(bf16[64,512]{1,0:T(8,128)(2,1)S(1)} %constant_dynamic-slice_fusion.16), channel_id=1, source_target_pairs={{0,8},{1,9},{2,10},{3,11},{4,12},{5,13},{6,14},{7,15},{8,0},{9,1},... | collective-permute-start | bytes 196616 | tf_op jit(solution)/shard_map/ppermute | solution.py:103
  106.2 6.5 %collective-permute-start.29 = (bf16[64,512]{1,0:T(8,128)(2,1)S(1)}, bf16[64,512]{1,0:T(8,128)(2,1)S(1)}, u32[]{:S(2)}, u32[]{:S(2)}) collective-permute-start(bf16[64,512]{1,0:T(8,128)(2,1)S(1)} %constant_dynamic-slice_fusion.11), channel_id=1, source_target_pairs={{0,16},{1,17},{2,18},{3,19},{4,20},{5,21},{6,22},{7,23},{8,24},{9,... | collective-permute-start | bytes 196616 | tf_op jit(solution)/shard_map/ppermute | solution.py:103
  (27 other events, 231.2 us)

commit v15 on v14

--- a/solution.py
+++ b/solution.py
@@ -112,7 +112,7 @@
     start_block = jnp.clip(chunk - (window - 1), 0, blocks - window)
     start = pl.multiple_of(start_block * CHUNK, CHUNK)
     span = window * CHUNK
-    keys = k_ref[:, pl.ds(start, span)]
+    keys = k_ref[pl.ds(start, span), :]
     values = v_ref[pl.ds(start, span), :]
     key_seg = kseg_ref[:, pl.ds(start, span)]
     query_seg = qseg_ref[...]
@@ -127,7 +127,9 @@
         raw = q_ref[:, e * HD:(e + 1) * HD]
         turned = raw * cosine + pltpu.roll(raw, HD // 2, 1) * sine_part
         queries = (turned * scale_factor).astype(jnp.bfloat16)
-        scores = jnp.dot(queries, keys, preferred_element_type=jnp.float32)
+        scores = lax.dot_general(
+            queries, keys, (((1,), (1,)), ((), ())), preferred_element_type=jnp.float32
+        )
         scores = jnp.where(allowed, scores, -1e30)
         top = jnp.max(scores, axis=1, keepdims=True)
         raised = jnp.exp(scores - top)
@@ -164,7 +166,7 @@
             pl.BlockSpec((CHUNK, width), lambda i: (i, 0)),
             pl.BlockSpec((CHUNK, HD), lambda i: (i, 0)),
             pl.BlockSpec((CHUNK, HD), lambda i: (i, 0)),
-            pl.BlockSpec((HD, tokens), lambda i: (0, 0)),
+            pl.BlockSpec((tokens, HD), lambda i: (0, 0)),
             pl.BlockSpec((tokens, HD), lambda i: (0, 0)),
             pl.BlockSpec((CHUNK, 1), lambda i: (i, 0)),
             pl.BlockSpec((1, tokens), lambda i: (0, 0)),
@@ -177,7 +179,7 @@
             transcendentals=tokens * window * CHUNK * experts,
             bytes_accessed=tokens * width * 6 + 2 * tokens * HD * 2 + 2 * tokens * HD * 4,
         ),
-    )(raw_queries, cosine, sine_part, jnp.transpose(keys), values, seg_cols, seg_row, gate_here)
+    )(raw_queries, cosine, sine_part, keys, values, seg_cols, seg_row, gate_here)
 
 
 def gather_from_all(block, axis):

time: 121 us -> 121 us (level)
  no operation moved by 1% of the time
where the time goes in v15:
time: 121 us; the launch traced here: 120 us
  starting transfers between devices  38.1 us (31%)
  waiting for transfers between devices  33 us (27%)
  other arithmetic  16.6 us (14%)
  matrix products  12.7 us (10%)
  Pallas kernels  12.3 us (10%)
  local copies, waits for them, and re-layouts  6.15 us (5%)
  between operations  1.51 us (1%)
    ppermute x20, starting transfers between devices, gather_from_all(): got = lax.ppermute(current, axis, [(i, i ^ 1 << k) for i in range(size)])  20.5 us
    ppermute x20, waiting for transfers between devices, reduce_to_owner(): got = lax.ppermute(send, axis, [(i, i ^ 1 << k) for i in range(size)])  18.2 us
    ppermute x20, starting transfers between devices, reduce_to_owner(): got = lax.ppermute(send, axis, [(i, i ^ 1 << k) for i in range(size)])  17.4 us
    ppermute x20, waiting for transfers between devices, gather_from_all(): got = lax.ppermute(current, axis, [(i, i ^ 1 << k) for i in range(size)])  14.7 us
    pallas_call x1, Pallas kernels, attend_window(): pl.pallas_call(lambda *refs: attention_kernel(window, *refs), grid=(block...  12.3 us
    dot_general x1, matrix products, project_kv(): projected = jnp.dot(normed, weight, preferred_element_type=jnp.float32)  3.69 us
    dot_general x1, matrix products, local(): jnp.dot(normed, query_weight, preferred_element_type=jnp.float32)  3.67 us
    dot_general x1, matrix products, local(): jnp.dot(flat, out_weight, preferred_element_type=jnp.float32)  3.56 us
  transfers between devices with their start and end apart: 41, of which 18 were waited for; matrix products, arithmetic and copies ran while one was open for 13% of the time, Pallas kernels for 0%

profile of v15, /device:TPU:0, one launch (start us, length us, event | category | flops | bytes accessed | tf_op | source)
XLA Modules:
  0.0 120.4 jit_solution(11115726183605589705)
XLA Ops:
  3.6 4.1 %collective-permute-start = (bf16[32,512]{1,0:T(8,128)(2,1)S(1)}, bf16[32,512]{1,0:T(8,128)(2,1)S(1)}, u32[]{:S(2)}, u32[]{:S(2)}) collective-permute-start(bf16[32,512]{1,0:T(8,128)(2,1)S(1)} %get-tuple-element.58), channel_id=1, source_target_pairs={{0,16},{1,17},{2,18},{3,19},{4,20},{5,21},{6,22},{7,23},{8,24},{9,... | collective-permute-start | bytes 98312 | tf_op jit(solution)/shard_map/ppermute | solution.py:198
  7.7 1.5 %collective-permute-start.10 = (bf16[32,512]{1,0:T(8,128)(2,1)S(1)}, bf16[32,512]{1,0:T(8,128)(2,1)S(1)}, u32[]{:S(2)}, u32[]{:S(2)}) collective-permute-start(bf16[32,512]{1,0:T(8,128)(2,1)S(1)} %get-tuple-element.60), channel_id=1, source_target_pairs={{0,4},{1,5},{2,6},{3,7},{4,0},{5,1},{6,2},{7,3},{8,12},{9,13},{10,... | collective-permute-start | bytes 98312 | tf_op jit(solution)/shard_map/ppermute | solution.py:198
  9.2 1.6 %collective-permute-start.15 = (bf16[32,512]{1,0:T(8,128)(2,1)S(1)}, bf16[32,512]{1,0:T(8,128)(2,1)S(1)}, u32[]{:S(2)}, u32[]{:S(2)}) collective-permute-start(bf16[32,512]{1,0:T(8,128)(2,1)S(1)} %get-tuple-element.59), channel_id=1, source_target_pairs={{0,8},{1,9},{2,10},{3,11},{4,12},{5,13},{6,14},{7,15},{8,0},{9,1},... | collective-permute-start | bytes 98312 | tf_op jit(solution)/shard_map/ppermute | solution.py:198
  13.8 1.9 %fusion.15 = (f32[1024,64]{1,0:T(8,128)S(1)}, f32[1024,64]{1,0:T(8,128)S(1)}, f32[1024,64]{1,0:T(8,128)S(1)}) fusion(f32[64]{0:T(128)S(1)} %multiply_power_fusion, f32[1024]{0:T(1024)S(1)} %fusion.18), kind=kLoop, calls=%fused_computation.71 | loop fusion | flops 131072 | bytes 790784 | tf_op jit(solution)/shard_map/neg | solution.py:150
  19.9 2.7 %collective-permute-done.1 = bf16[64,512]{1,0:T(8,128)(2,1)S(1)} collective-permute-done((bf16[64,512]{1,0:T(8,128)(2,1)S(1)}, bf16[64,512]{1,0:T(8,128)(2,1)S(1)}, u32[]{:S(2)}, u32[]{:S(2)}) %collective-permute-start.1) | collective-permute-done | bytes 65568 | tf_op jit(solution)/shard_map/ppermute | solution.py:198
  24.6 1.6 %collective-permute-start.7 = (bf16[128,512]{1,0:T(8,128)(2,1)S(1)}, bf16[128,512]{1,0:T(8,128)(2,1)S(1)}, u32[]{:S(2)}, u32[]{:S(2)}) collective-permute-start(bf16[128,512]{1,0:T(8,128)(2,1)S(1)} %pad_maximum_fusion.16), channel_id=1, source_target_pairs={{0,8},{1,9},{2,10},{3,11},{4,12},{5,13},{6,14},{7,15},{8,0},{9,1},... | collective-permute-start | bytes 393224 | tf_op jit(solution)/shard_map/ppermute | solution.py:198
  31.0 1.6 %collective-permute-start.8 = (bf16[256,512]{1,0:T(8,128)(2,1)S(1)}, bf16[256,512]{1,0:T(8,128)(2,1)S(1)}, u32[]{:S(2)}, u32[]{:S(2)}) collective-permute-start(bf16[256,512]{1,0:T(8,128)(2,1)S(1)} %pad_maximum_fusion.12), channel_id=1, source_target_pairs={{0,4},{1,5},{2,6},{3,7},{4,0},{5,1},{6,2},{7,3},{8,12},{9,13},{10,... | collective-permute-start | bytes 786440 | tf_op jit(solution)/shard_map/ppermute | solution.py:198
  33.9 3.2 %collective-permute-start.18 = (bf16[256,512]{1,0:T(8,128)(2,1)S(1)}, bf16[256,512]{1,0:T(8,128)(2,1)S(1)}, u32[]{:S(2)}, u32[]{:S(2)}) collective-permute-start(bf16[256,512]{1,0:T(8,128)(2,1)S(1)} %pad_maximum_fusion.14), channel_id=1, source_target_pairs={{0,16},{1,17},{2,18},{3,19},{4,20},{5,21},{6,22},{7,23},{8,24},{9,... | collective-permute-start | bytes 786440 | tf_op jit(solution)/shard_map/ppermute | solution.py:198
  38.0 5.5 %collective-permute-done.13 = bf16[256,512]{1,0:T(8,128)(2,1)S(1)} collective-permute-done((bf16[256,512]{1,0:T(8,128)(2,1)S(1)}, bf16[256,512]{1,0:T(8,128)(2,1)S(1)}, u32[]{:S(2)}, u32[]{:S(2)}) %collective-permute-start.13) | collective-permute-done | bytes 262176 | tf_op jit(solution)/shard_map/ppermute | solution.py:198
  48.2 1.9 %copy-done.1 = bf16[1024,2048]{1,0:T(8,128)(2,1)} copy-done((bf16[1024,2048]{1,0:T(8,128)(2,1)}, bf16[1024,2048]{1,0:T(8,128)(2,1)S(1)}, u32[]{:S(2)}) %copy-start.1) | copy-done | bytes 4194328
  52.0 3.7 %fusion.27 = f32[1024,128]{1,0:T(8,128)S(1)} fusion(bf16[1024,2048]{1,0:T(8,128)(2,1)} %copy-done.1, bf16[2048,128]{1,0:T(8,128)(2,1)} %param.13), kind=kOutput, calls=%fused_computation.154 | convolution fusion | flops 536870912 | bytes 5242880 | tf_op jit(solution)/shard_map/dot_general | solution.py:58
  55.7 2.4 %fusion.6 = (bf16[1024,64]{1,0:T(8,128)(2,1)S(1)}, bf16[1024,64]{1,0:T(8,128)(2,1)S(1)}) fusion(f32[1024,1,128]{2,0,1:T(8,128)S(1)} %bitcast.61, f32[64]{0:T(128)S(1)} %multiply_power_fusion, f32[1024]{0:T(1024)S(1)} %fusion.18), kind=kLoop, calls=%fused_computation.21 | loop fusion | flops 589824 | bytes 790784 | tf_op jit(solution)/shard_map/concatenate | solution.py:52
  58.5 3.7 %fusion.26.refs_0_ = f32[1024,512]{1,0:T(8,128)} fusion(bf16[1024,2048]{1,0:T(8,128)(2,1)S(1)} %copy-done.2, bf16[2048,512]{1,0:T(8,128)(2,1)S(1)} %copy-done.9), kind=kOutput, calls=%fused_computation.153 | convolution fusion | flops 2147483648 | bytes 8388608 | tf_op jit(solution)/shard_map/dot_general | solution.py:236
  63.9 12.3 %shard_map.113 = bf16[1024,512]{1,0:T(8,128)(2,1)} custom-call(f32[1024,512]{1,0:T(8,128)} %fusion.26.refs_0_, f32[1024,128]{1,0:T(8,128)} %get-tuple-element.77.refs_1_, f32[1024,128]{1,0:T(8,128)} %get-tuple-element.78.refs_2_, bf16[1024,128]{1,0:T(8,128)(2,1)} %get-tuple-element.25.refs_3_, bf16[1024,128]{1,0:T(8,128)(2,1)} %get-tuple-element.24.refs_4_, ...), custom_call_target="tpu_custom_call" | custom-call | flops 1610612736 | bytes 4718592 | tf_op jit(solution)/shard_map/pallas_call | solution.py:162
  76.2 3.6 %convolution_convert_fusion = bf16[1024,2048]{1,0:T(8,128)(2,1)S(1)} fusion(bf16[1024,512]{1,0:T(8,128)(2,1)} %shard_map.113, bf16[512,2048]{1,0:T(8,128)(2,1)S(1)} %copy-done), kind=kOutput, calls=%fused_computation.1 | convolution fusion | flops 2149580800 | bytes 7340032 | tf_op jit(solution)/shard_map/dot_general | solution.py:246
  84.8 1.5 %collective-permute-start.27 = (bf16[256,512]{1,0:T(8,128)(2,1)S(1)}, bf16[256,512]{1,0:T(8,128)(2,1)S(1)}, u32[]{:S(2)}, u32[]{:S(2)}) collective-permute-start(bf16[256,512]{1,0:T(8,128)(2,1)S(1)} %constant_dynamic-slice_fusion.13), channel_id=1, source_target_pairs={{0,4},{1,5},{2,6},{3,7},{4,0},{5,1},{6,2},{7,3},{8,12},{9,13},{10,... | collective-permute-start | bytes 786440 | tf_op jit(solution)/shard_map/ppermute | solution.py:103
  86.8 2.1 %collective-permute-start.37 = (bf16[256,512]{1,0:T(8,128)(2,1)S(1)}, bf16[256,512]{1,0:T(8,128)(2,1)S(1)}, u32[]{:S(2)}, u32[]{:S(2)}) collective-permute-start(bf16[256,512]{1,0:T(8,128)(2,1)S(1)} %constant_dynamic-slice_fusion.3), channel_id=1, source_target_pairs={{0,16},{1,17},{2,18},{3,19},{4,20},{5,21},{6,22},{7,23},{8,24},{9,... | collective-permute-start | bytes 786440 | tf_op jit(solution)/shard_map/ppermute | solution.py:103
  89.0 3.5 %collective-permute-done.22 = bf16[256,512]{1,0:T(8,128)(2,1)S(1)} collective-permute-done((bf16[256,512]{1,0:T(8,128)(2,1)S(1)}, bf16[256,512]{1,0:T(8,128)(2,1)S(1)}, u32[]{:S(2)}, u32[]{:S(2)}) %collective-permute-start.22) | collective-permute-done | bytes 262176 | tf_op jit(solution)/shard_map/ppermute | solution.py:103
  92.5 1.6 %collective-permute-start.23 = (bf16[128,512]{1,0:T(8,128)(2,1)S(1)}, bf16[128,512]{1,0:T(8,128)(2,1)S(1)}, u32[]{:S(2)}, u32[]{:S(2)}) collective-permute-start(bf16[128,512]{1,0:T(8,128)(2,1)S(1)} %constant_dynamic-slice_fusion.17), channel_id=1, source_target_pairs={{0,4},{1,5},{2,6},{3,7},{4,0},{5,1},{6,2},{7,3},{8,12},{9,13},{10,... | collective-permute-start | bytes 393224 | tf_op jit(solution)/shard_map/ppermute | solution.py:103
  94.3 6.4 %collective-permute-done.32 = bf16[256,512]{1,0:T(8,128)(2,1)S(1)} collective-permute-done((bf16[256,512]{1,0:T(8,128)(2,1)S(1)}, bf16[256,512]{1,0:T(8,128)(2,1)S(1)}, u32[]{:S(2)}, u32[]{:S(2)}) %collective-permute-start.32) | collective-permute-done | bytes 262176 | tf_op jit(solution)/shard_map/ppermute | solution.py:103
  103.3 2.0 %collective-permute-start.24 = (bf16[64,512]{1,0:T(8,128)(2,1)S(1)}, bf16[64,512]{1,0:T(8,128)(2,1)S(1)}, u32[]{:S(2)}, u32[]{:S(2)}) collective-permute-start(bf16[64,512]{1,0:T(8,128)(2,1)S(1)} %constant_dynamic-slice_fusion.16), channel_id=1, source_target_pairs={{0,8},{1,9},{2,10},{3,11},{4,12},{5,13},{6,14},{7,15},{8,0},{9,1},... | collective-permute-start | bytes 196616 | tf_op jit(solution)/shard_map/ppermute | solution.py:103
  106.2 2.8 %collective-permute-done.33 = bf16[128,512]{1,0:T(8,128)(2,1)S(1)} collective-permute-done((bf16[128,512]{1,0:T(8,128)(2,1)S(1)}, bf16[128,512]{1,0:T(8,128)(2,1)S(1)}, u32[]{:S(2)}, u32[]{:S(2)}) %collective-permute-start.33) | collective-permute-done | bytes 131104 | tf_op jit(solution)/shard_map/ppermute | solution.py:103
  109.1 2.1 %collective-permute-start.34 = (bf16[64,512]{1,0:T(8,128)(2,1)S(1)}, bf16[64,512]{1,0:T(8,128)(2,1)S(1)}, u32[]{:S(2)}, u32[]{:S(2)}) collective-permute-start(bf16[64,512]{1,0:T(8,128)(2,1)S(1)} %constant_dynamic-slice_fusion.6), channel_id=1, source_target_pairs={{0,2},{1,3},{2,0},{3,1},{4,6},{5,7},{6,4},{7,5},{8,10},{9,11},{10,... | collective-permute-start | bytes 196616 | tf_op jit(solution)/shard_map/ppermute | solution.py:103
  117.5 2.1 %collective-permute-done.40 = bf16[32,512]{1,0:T(8,128)(2,1)S(1)} collective-permute-done((bf16[32,512]{1,0:T(8,128)(2,1)S(1)}, bf16[32,512]{1,0:T(8,128)(2,1)S(1)}, u32[]{:S(2)}, u32[]{:S(2)}) %collective-permute-start.40) | collective-permute-done | bytes 32800 | tf_op jit(solution)/shard_map/ppermute | solution.py:103
  (200 shorter events, 43.3 us)
Async XLA Ops:
  3.6 14.6 %collective-permute-start = (bf16[32,512]{1,0:T(8,128)(2,1)S(1)}, bf16[32,512]{1,0:T(8,128)(2,1)S(1)}, u32[]{:S(2)}, u32[]{:S(2)}) collective-permute-start(bf16[32,512]{1,0:T(8,128)(2,1)S(1)} %get-tuple-element.58), channel_id=1, source_target_pairs={{0,16},{1,17},{2,18},{3,19},{4,20},{5,21},{6,22},{7,23},{8,24},{9,... | collective-permute-start | bytes 98312 | tf_op jit(solution)/shard_map/ppermute | solution.py:198
  7.7 10.5 %collective-permute-start.10 = (bf16[32,512]{1,0:T(8,128)(2,1)S(1)}, bf16[32,512]{1,0:T(8,128)(2,1)S(1)}, u32[]{:S(2)}, u32[]{:S(2)}) collective-permute-start(bf16[32,512]{1,0:T(8,128)(2,1)S(1)} %get-tuple-element.60), channel_id=1, source_target_pairs={{0,4},{1,5},{2,6},{3,7},{4,0},{5,1},{6,2},{7,3},{8,12},{9,13},{10,... | collective-permute-start | bytes 98312 | tf_op jit(solution)/shard_map/ppermute | solution.py:198
  9.2 9.0 %collective-permute-start.15 = (bf16[32,512]{1,0:T(8,128)(2,1)S(1)}, bf16[32,512]{1,0:T(8,128)(2,1)S(1)}, u32[]{:S(2)}, u32[]{:S(2)}) collective-permute-start(bf16[32,512]{1,0:T(8,128)(2,1)S(1)} %get-tuple-element.59), channel_id=1, source_target_pairs={{0,8},{1,9},{2,10},{3,11},{4,12},{5,13},{6,14},{7,15},{8,0},{9,1},... | collective-permute-start | bytes 98312 | tf_op jit(solution)/shard_map/ppermute | solution.py:198
  10.8 7.4 %collective-permute-start.5 = (bf16[32,512]{1,0:T(8,128)(2,1)S(1)}, bf16[32,512]{1,0:T(8,128)(2,1)S(1)}, u32[]{:S(2)}, u32[]{:S(2)}) collective-permute-start(bf16[32,512]{1,0:T(8,128)(2,1)S(1)} %get-tuple-element.61), channel_id=1, source_target_pairs={{0,2},{1,3},{2,0},{3,1},{4,6},{5,7},{6,4},{7,5},{8,10},{9,11},{10,... | collective-permute-start | bytes 98312 | tf_op jit(solution)/shard_map/ppermute | solution.py:198
  19.1 7.1 %collective-permute-start.11 = (bf16[64,512]{1,0:T(8,128)(2,1)S(1)}, bf16[64,512]{1,0:T(8,128)(2,1)S(1)}, u32[]{:S(2)}, u32[]{:S(2)}) collective-permute-start(bf16[64,512]{1,0:T(8,128)(2,1)S(1)} %pad_maximum_fusion.21), channel_id=1, source_target_pairs={{0,2},{1,3},{2,0},{3,1},{4,6},{5,7},{6,4},{7,5},{8,10},{9,11},{10,... | collective-permute-start | bytes 196616 | tf_op jit(solution)/shard_map/ppermute | solution.py:198
  19.7 6.6 %collective-permute-start.16 = (bf16[64,512]{1,0:T(8,128)(2,1)S(1)}, bf16[64,512]{1,0:T(8,128)(2,1)S(1)}, u32[]{:S(2)}, u32[]{:S(2)}) collective-permute-start(bf16[64,512]{1,0:T(8,128)(2,1)S(1)} %pad_maximum_fusion.22), channel_id=1, source_target_pairs={{0,4},{1,5},{2,6},{3,7},{4,0},{5,1},{6,2},{7,3},{8,12},{9,13},{10,... | collective-permute-start | bytes 196616 | tf_op jit(solution)/shard_map/ppermute | solution.py:198
  26.3 7.3 %collective-permute-start.12 = (bf16[128,512]{1,0:T(8,128)(2,1)S(1)}, bf16[128,512]{1,0:T(8,128)(2,1)S(1)}, u32[]{:S(2)}, u32[]{:S(2)}) collective-permute-start(bf16[128,512]{1,0:T(8,128)(2,1)S(1)} %pad_maximum_fusion.17), channel_id=1, source_target_pairs={{0,16},{1,17},{2,18},{3,19},{4,20},{5,21},{6,22},{7,23},{8,24},{9,... | collective-permute-start | bytes 393224 | tf_op jit(solution)/shard_map/ppermute | solution.py:198
  27.5 6.4 %collective-permute-start.17 = (bf16[128,512]{1,0:T(8,128)(2,1)S(1)}, bf16[128,512]{1,0:T(8,128)(2,1)S(1)}, u32[]{:S(2)}, u32[]{:S(2)}) collective-permute-start(bf16[128,512]{1,0:T(8,128)(2,1)S(1)} %pad_maximum_fusion.18), channel_id=1, source_target_pairs={{0,2},{1,3},{2,0},{3,1},{4,6},{5,7},{6,4},{7,5},{8,10},{9,11},{10,... | collective-permute-start | bytes 393224 | tf_op jit(solution)/shard_map/ppermute | solution.py:198
  29.2 7.9 %collective-permute-start.3 = (bf16[256,512]{1,0:T(8,128)(2,1)S(1)}, bf16[256,512]{1,0:T(8,128)(2,1)S(1)}, u32[]{:S(2)}, u32[]{:S(2)}) collective-permute-start(bf16[256,512]{1,0:T(8,128)(2,1)S(1)} %pad_maximum_fusion.11), channel_id=1, source_target_pairs={{0,2},{1,3},{2,0},{3,1},{4,6},{5,7},{6,4},{7,5},{8,10},{9,11},{10,... | collective-permute-start | bytes 786440 | tf_op jit(solution)/shard_map/ppermute | solution.py:198
  31.0 6.4 %collective-permute-start.8 = (bf16[256,512]{1,0:T(8,128)(2,1)S(1)}, bf16[256,512]{1,0:T(8,128)(2,1)S(1)}, u32[]{:S(2)}, u32[]{:S(2)}) collective-permute-start(bf16[256,512]{1,0:T(8,128)(2,1)S(1)} %pad_maximum_fusion.12), channel_id=1, source_target_pairs={{0,4},{1,5},{2,6},{3,7},{4,0},{5,1},{6,2},{7,3},{8,12},{9,13},{10,... | collective-permute-start | bytes 786440 | tf_op jit(solution)/shard_map/ppermute | solution.py:198
  33.7 9.8 %collective-permute-start.13 = (bf16[256,512]{1,0:T(8,128)(2,1)S(1)}, bf16[256,512]{1,0:T(8,128)(2,1)S(1)}, u32[]{:S(2)}, u32[]{:S(2)}) collective-permute-start(bf16[256,512]{1,0:T(8,128)(2,1)S(1)} %pad_maximum_fusion.13), channel_id=1, source_target_pairs={{0,8},{1,9},{2,10},{3,11},{4,12},{5,13},{6,14},{7,15},{8,0},{9,1},... | collective-permute-start | bytes 786440 | tf_op jit(solution)/shard_map/ppermute | solution.py:198
  33.9 11.0 %collective-permute-start.18 = (bf16[256,512]{1,0:T(8,128)(2,1)S(1)}, bf16[256,512]{1,0:T(8,128)(2,1)S(1)}, u32[]{:S(2)}, u32[]{:S(2)}) collective-permute-start(bf16[256,512]{1,0:T(8,128)(2,1)S(1)} %pad_maximum_fusion.14), channel_id=1, source_target_pairs={{0,16},{1,17},{2,18},{3,19},{4,20},{5,21},{6,22},{7,23},{8,24},{9,... | collective-permute-start | bytes 786440 | tf_op jit(solution)/shard_map/ppermute | solution.py:198
  37.2 7.9 %collective-permute-start.4 = (bf16[512,512]{1,0:T(8,128)(2,1)S(1)}, bf16[512,512]{1,0:T(8,128)(2,1)S(1)}, u32[]{:S(2)}, u32[]{:S(2)}) collective-permute-start(bf16[512,512]{1,0:T(8,128)(2,1)S(1)} %pad_maximum_fusion.5), channel_id=1, source_target_pairs={{0,1},{1,0},{2,3},{3,2},{4,5},{5,4},{6,7},{7,6},{8,9},{9,8},{10,11... | collective-permute-start | bytes 1572872 | tf_op jit(solution)/shard_map/ppermute | solution.py:198
  37.6 7.8 %collective-permute-start.9 = (bf16[512,512]{1,0:T(8,128)(2,1)S(1)}, bf16[512,512]{1,0:T(8,128)(2,1)S(1)}, u32[]{:S(2)}, u32[]{:S(2)}) collective-permute-start(bf16[512,512]{1,0:T(8,128)(2,1)S(1)} %pad_maximum_fusion.6), channel_id=1, source_target_pairs={{0,1},{1,0},{2,3},{3,2},{4,5},{5,4},{6,7},{7,6},{8,9},{9,8},{10,11... | collective-permute-start | bytes 1572872 | tf_op jit(solution)/shard_map/ppermute | solution.py:198
  84.0 8.4 %collective-permute-start.22 = (bf16[256,512]{1,0:T(8,128)(2,1)S(1)}, bf16[256,512]{1,0:T(8,128)(2,1)S(1)}, u32[]{:S(2)}, u32[]{:S(2)}) collective-permute-start(bf16[256,512]{1,0:T(8,128)(2,1)S(1)} %constant_dynamic-slice_fusion.18), channel_id=1, source_target_pairs={{0,2},{1,3},{2,0},{3,1},{4,6},{5,7},{6,4},{7,5},{8,10},{9,11},{10,... | collective-permute-start | bytes 786440 | tf_op jit(solution)/shard_map/ppermute | solution.py:103
  84.8 9.3 %collective-permute-start.27 = (bf16[256,512]{1,0:T(8,128)(2,1)S(1)}, bf16[256,512]{1,0:T(8,128)(2,1)S(1)}, u32[]{:S(2)}, u32[]{:S(2)}) collective-permute-start(bf16[256,512]{1,0:T(8,128)(2,1)S(1)} %constant_dynamic-slice_fusion.13), channel_id=1, source_target_pairs={{0,4},{1,5},{2,6},{3,7},{4,0},{5,1},{6,2},{7,3},{8,12},{9,13},{10,... | collective-permute-start | bytes 786440 | tf_op jit(solution)/shard_map/ppermute | solution.py:103
  86.6 14.2 %collective-permute-start.32 = (bf16[256,512]{1,0:T(8,128)(2,1)S(1)}, bf16[256,512]{1,0:T(8,128)(2,1)S(1)}, u32[]{:S(2)}, u32[]{:S(2)}) collective-permute-start(bf16[256,512]{1,0:T(8,128)(2,1)S(1)} %constant_dynamic-slice_fusion.8), channel_id=1, source_target_pairs={{0,8},{1,9},{2,10},{3,11},{4,12},{5,13},{6,14},{7,15},{8,0},{9,1},... | collective-permute-start | bytes 786440 | tf_op jit(solution)/shard_map/ppermute | solution.py:103
  86.8 14.9 %collective-permute-start.37 = (bf16[256,512]{1,0:T(8,128)(2,1)S(1)}, bf16[256,512]{1,0:T(8,128)(2,1)S(1)}, u32[]{:S(2)}, u32[]{:S(2)}) collective-permute-start(bf16[256,512]{1,0:T(8,128)(2,1)S(1)} %constant_dynamic-slice_fusion.3), channel_id=1, source_target_pairs={{0,16},{1,17},{2,18},{3,19},{4,20},{5,21},{6,22},{7,23},{8,24},{9,... | collective-permute-start | bytes 786440 | tf_op jit(solution)/shard_map/ppermute | solution.py:103
  92.5 10.7 %collective-permute-start.23 = (bf16[128,512]{1,0:T(8,128)(2,1)S(1)}, bf16[128,512]{1,0:T(8,128)(2,1)S(1)}, u32[]{:S(2)}, u32[]{:S(2)}) collective-permute-start(bf16[128,512]{1,0:T(8,128)(2,1)S(1)} %constant_dynamic-slice_fusion.17), channel_id=1, source_target_pairs={{0,4},{1,5},{2,6},{3,7},{4,0},{5,1},{6,2},{7,3},{8,12},{9,13},{10,... | collective-permute-start | bytes 393224 | tf_op jit(solution)/shard_map/ppermute | solution.py:103
  94.2 11.1 %collective-permute-start.28 = (bf16[128,512]{1,0:T(8,128)(2,1)S(1)}, bf16[128,512]{1,0:T(8,128)(2,1)S(1)}, u32[]{:S(2)}, u32[]{:S(2)}) collective-permute-start(bf16[128,512]{1,0:T(8,128)(2,1)S(1)} %constant_dynamic-slice_fusion.12), channel_id=1, source_target_pairs={{0,8},{1,9},{2,10},{3,11},{4,12},{5,13},{6,14},{7,15},{8,0},{9,1},... | collective-permute-start | bytes 393224 | tf_op jit(solution)/shard_map/ppermute | solution.py:103
  100.8 8.2 %collective-permute-start.33 = (bf16[128,512]{1,0:T(8,128)(2,1)S(1)}, bf16[128,512]{1,0:T(8,128)(2,1)S(1)}, u32[]{:S(2)}, u32[]{:S(2)}) collective-permute-start(bf16[128,512]{1,0:T(8,128)(2,1)S(1)} %constant_dynamic-slice_fusion.7), channel_id=1, source_target_pairs={{0,16},{1,17},{2,18},{3,19},{4,20},{5,21},{6,22},{7,23},{8,24},{9,... | collective-permute-start | bytes 393224 | tf_op jit(solution)/shard_map/ppermute | solution.py:103
  101.8 9.4 %collective-permute-start.38 = (bf16[128,512]{1,0:T(8,128)(2,1)S(1)}, bf16[128,512]{1,0:T(8,128)(2,1)S(1)}, u32[]{:S(2)}, u32[]{:S(2)}) collective-permute-start(bf16[128,512]{1,0:T(8,128)(2,1)S(1)} %constant_dynamic-slice_fusion.2), channel_id=1, source_target_pairs={{0,2},{1,3},{2,0},{3,1},{4,6},{5,7},{6,4},{7,5},{8,10},{9,11},{10,... | collective-permute-start | bytes 393224 | tf_op jit(solution)/shard_map/ppermute | solution.py:103
  103.3 8.4 %collective-permute-start.24 = (bf16[64,512]{1,0:T(8,128)(2,1)S(1)}, bf16[64,512]{1,0:T(8,128)(2,1)S(1)}, u32[]{:S(2)}, u32[]{:S(2)}) collective-permute-start(bf16[64,512]{1,0:T(8,128)(2,1)S(1)} %constant_dynamic-slice_fusion.16), channel_id=1, source_target_pairs={{0,8},{1,9},{2,10},{3,11},{4,12},{5,13},{6,14},{7,15},{8,0},{9,1},... | collective-permute-start | bytes 196616 | tf_op jit(solution)/shard_map/ppermute | solution.py:103
  105.4 6.5 %collective-permute-start.29 = (bf16[64,512]{1,0:T(8,128)(2,1)S(1)}, bf16[64,512]{1,0:T(8,128)(2,1)S(1)}, u32[]{:S(2)}, u32[]{:S(2)}) collective-permute-start(bf16[64,512]{1,0:T(8,128)(2,1)S(1)} %constant_dynamic-slice_fusion.11), channel_id=1, source_target_pairs={{0,16},{1,17},{2,18},{3,19},{4,20},{5,21},{6,22},{7,23},{8,24},{9,... | collective-permute-start | bytes 196616 | tf_op jit(solution)/shard_map/ppermute | solution.py:103
  (27 other events, 230.4 us)

commit v16 on v15

--- a/solution.py
+++ b/solution.py
@@ -65,12 +65,9 @@
 
 
 def write_pages(kv_cache, page_table, rows):
-    pages = jnp.arange(kv_cache.shape[0], dtype=jnp.int32)
-    hit = page_table[None, :] == pages[:, None]
-    placed = jnp.einsum(
-        "pb,brc->prc", hit.astype(rows.dtype), rows, preferred_element_type=jnp.float32
-    ).astype(kv_cache.dtype)
-    return jnp.where(jnp.any(hit, axis=1)[:, None, None], placed, kv_cache)
+    for block in range(rows.shape[0]):
+        kv_cache = lax.dynamic_update_slice_in_dim(kv_cache, rows[block:block + 1], page_table[block], 0)
+    return kv_cache
 
 
 def bit_orders(bits, parts):

time: 121 us -> 137 us (1.13)
  between operations: 1.51 us -> 16.6 us
  other arithmetic: 16.6 us -> 18.4 us
  waiting for transfers between devices: 33 us -> 34.5 us
    dot_general x1, matrix products: 3.67 us -> 6.62 us  [local(): jnp.dot(normed, query_weight, preferred_element_type=jnp.float32)]
    unnamed x21 -> x26, local copies, waits for them, and re-layouts: 2.98 us -> 0.46 us
    dot_general x1, matrix products: 3.69 us -> 1.24 us  [project_kv(): projected = jnp.dot(normed, weight, preferred_element_type=jnp.float32)]
    ppermute x20, waiting for transfers between devices: 18.2 us -> 19.8 us  [reduce_to_owner(): got = lax.ppermute(send, axis, [(i, i ^ 1 << k) for i in range(size)])]
  transfers between devices with their start and end apart: 41 -> 41, of which waited for: 18 -> 19; matrix products, arithmetic and copies ran while one was open for 13% -> 13% of each run, Pallas kernels for 0% -> 0%
where the time goes in v16:
time: 137 us
  starting transfers between devices  36.9 us (27%)
  waiting for transfers between devices  34.5 us (25%)
  other arithmetic  18.4 us (13%)
  between operations  16.6 us (12%)
  matrix products  12.6 us (9%)
  Pallas kernels  12.3 us (9%)
  local copies, waits for them, and re-layouts  5.25 us (4%)
    ppermute x20, starting transfers between devices, gather_from_all(): got = lax.ppermute(current, axis, [(i, i ^ 1 << k) for i in range(size)])  20.5 us
    ppermute x20, waiting for transfers between devices, reduce_to_owner(): got = lax.ppermute(send, axis, [(i, i ^ 1 << k) for i in range(size)])  19.8 us
    ppermute x20, starting transfers between devices, reduce_to_owner(): got = lax.ppermute(send, axis, [(i, i ^ 1 << k) for i in range(size)])  16.2 us
    ppermute x20, waiting for transfers between devices, gather_from_all(): got = lax.ppermute(current, axis, [(i, i ^ 1 << k) for i in range(size)])  14.7 us
    pallas_call x1, Pallas kernels, attend_window(): pl.pallas_call(lambda *refs: attention_kernel(window, *refs), grid=(block...  12.3 us
    dot_general x1, matrix products, local(): jnp.dot(normed, query_weight, preferred_element_type=jnp.float32)  6.62 us
    dot_general x1, matrix products, local(): jnp.dot(flat, out_weight, preferred_element_type=jnp.float32)  3.56 us
    concatenate x1, other arithmetic, rotate(): jnp.concatenate([leading * cosine - trailing * sine_part, trailing * cosi...  3.11 us
  transfers between devices with their start and end apart: 41, of which 19 were waited for; matrix products, arithmetic and copies ran while one was open for 13% of the time, Pallas kernels for 0%

profile of v16, /device:TPU:0, one launch (start us, length us, event | category | flops | bytes accessed | tf_op | source)
XLA Modules:
  0.0 136.6 jit_solution(4360787344407958758)
XLA Ops:
  3.6 4.1 %collective-permute-start = (bf16[32,512]{1,0:T(8,128)(2,1)S(1)}, bf16[32,512]{1,0:T(8,128)(2,1)S(1)}, u32[]{:S(2)}, u32[]{:S(2)}) collective-permute-start(bf16[32,512]{1,0:T(8,128)(2,1)S(1)} %get-tuple-element.50), channel_id=1, source_target_pairs={{0,16},{1,17},{2,18},{3,19},{4,20},{5,21},{6,22},{7,23},{8,24},{9,... | collective-permute-start | bytes 98312 | tf_op jit(solution)/shard_map/ppermute | solution.py:195
  7.7 1.5 %collective-permute-start.10 = (bf16[32,512]{1,0:T(8,128)(2,1)S(1)}, bf16[32,512]{1,0:T(8,128)(2,1)S(1)}, u32[]{:S(2)}, u32[]{:S(2)}) collective-permute-start(bf16[32,512]{1,0:T(8,128)(2,1)S(1)} %get-tuple-element.52), channel_id=1, source_target_pairs={{0,4},{1,5},{2,6},{3,7},{4,0},{5,1},{6,2},{7,3},{8,12},{9,13},{10,... | collective-permute-start | bytes 98312 | tf_op jit(solution)/shard_map/ppermute | solution.py:195
  9.2 1.6 %collective-permute-start.15 = (bf16[32,512]{1,0:T(8,128)(2,1)S(1)}, bf16[32,512]{1,0:T(8,128)(2,1)S(1)}, u32[]{:S(2)}, u32[]{:S(2)}) collective-permute-start(bf16[32,512]{1,0:T(8,128)(2,1)S(1)} %get-tuple-element.51), channel_id=1, source_target_pairs={{0,8},{1,9},{2,10},{3,11},{4,12},{5,13},{6,14},{7,15},{8,0},{9,1},... | collective-permute-start | bytes 98312 | tf_op jit(solution)/shard_map/ppermute | solution.py:195
  10.8 1.5 %collective-permute-start.5 = (bf16[32,512]{1,0:T(8,128)(2,1)S(1)}, bf16[32,512]{1,0:T(8,128)(2,1)S(1)}, u32[]{:S(2)}, u32[]{:S(2)}) collective-permute-start(bf16[32,512]{1,0:T(8,128)(2,1)S(1)} %get-tuple-element.53), channel_id=1, source_target_pairs={{0,2},{1,3},{2,0},{3,1},{4,6},{5,7},{6,4},{7,5},{8,10},{9,11},{10,... | collective-permute-start | bytes 98312 | tf_op jit(solution)/shard_map/ppermute | solution.py:195
  13.8 1.9 %fusion.13 = (f32[1024,64]{1,0:T(8,128)S(1)}, f32[1024,64]{1,0:T(8,128)S(1)}, f32[1024,64]{1,0:T(8,128)S(1)}) fusion(f32[64]{0:T(128)S(1)} %multiply_power_fusion, f32[1024]{0:T(1024)S(1)} %fusion.24), kind=kLoop, calls=%fused_computation.68 | loop fusion | flops 131072 | bytes 790784 | tf_op jit(solution)/shard_map/neg | solution.py:147
  35.5 2.7 %collective-permute-done.1 = bf16[64,512]{1,0:T(8,128)(2,1)S(1)} collective-permute-done((bf16[64,512]{1,0:T(8,128)(2,1)S(1)}, bf16[64,512]{1,0:T(8,128)(2,1)S(1)}, u32[]{:S(2)}, u32[]{:S(2)}) %collective-permute-start.1) | collective-permute-done | bytes 65568 | tf_op jit(solution)/shard_map/ppermute | solution.py:195
  40.2 1.6 %collective-permute-start.7 = (bf16[128,512]{1,0:T(8,128)(2,1)S(1)}, bf16[128,512]{1,0:T(8,128)(2,1)S(1)}, u32[]{:S(2)}, u32[]{:S(2)}) collective-permute-start(bf16[128,512]{1,0:T(8,128)(2,1)S(1)} %pad_maximum_fusion.16), channel_id=1, source_target_pairs={{0,8},{1,9},{2,10},{3,11},{4,12},{5,13},{6,14},{7,15},{8,0},{9,1},... | collective-permute-start | bytes 393224 | tf_op jit(solution)/shard_map/ppermute | solution.py:195
  46.6 1.6 %collective-permute-start.8 = (bf16[256,512]{1,0:T(8,128)(2,1)S(1)}, bf16[256,512]{1,0:T(8,128)(2,1)S(1)}, u32[]{:S(2)}, u32[]{:S(2)}) collective-permute-start(bf16[256,512]{1,0:T(8,128)(2,1)S(1)} %pad_maximum_fusion.12), channel_id=1, source_target_pairs={{0,4},{1,5},{2,6},{3,7},{4,0},{5,1},{6,2},{7,3},{8,12},{9,13},{10,... | collective-permute-start | bytes 786440 | tf_op jit(solution)/shard_map/ppermute | solution.py:195
  49.5 3.2 %collective-permute-start.18 = (bf16[256,512]{1,0:T(8,128)(2,1)S(1)}, bf16[256,512]{1,0:T(8,128)(2,1)S(1)}, u32[]{:S(2)}, u32[]{:S(2)}) collective-permute-start(bf16[256,512]{1,0:T(8,128)(2,1)S(1)} %pad_maximum_fusion.14), channel_id=1, source_target_pairs={{0,16},{1,17},{2,18},{3,19},{4,20},{5,21},{6,22},{7,23},{8,24},{9,... | collective-permute-start | bytes 786440 | tf_op jit(solution)/shard_map/ppermute | solution.py:195
  53.6 5.5 %collective-permute-done.13 = bf16[256,512]{1,0:T(8,128)(2,1)S(1)} collective-permute-done((bf16[256,512]{1,0:T(8,128)(2,1)S(1)}, bf16[256,512]{1,0:T(8,128)(2,1)S(1)}, u32[]{:S(2)}, u32[]{:S(2)}) %collective-permute-start.13) | collective-permute-done | bytes 262176 | tf_op jit(solution)/shard_map/ppermute | solution.py:195
  65.3 3.1 %fusion.5 = (bf16[1024,64]{1,0:T(8,128)(2,1)}, bf16[1024,64]{1,0:T(8,128)(2,1)}) fusion(f32[1024,1,128]{2,0,1:T(8,128)S(1)} %bitcast.97, f32[64]{0:T(128)S(1)} %multiply_power_fusion, f32[1024]{0:T(1024)S(1)} %fusion.24), kind=kLoop, calls=%fused_computation.19 | loop fusion | flops 589824 | bytes 790784 | tf_op jit(solution)/shard_map/concatenate | solution.py:52
  72.5 6.6 %fusion.29.refs_0_ = f32[1024,512]{1,0:T(8,128)} fusion(bf16[1024,2048]{1,0:T(8,128)(2,1)} %copy-done.1, bf16[2048,512]{1,0:T(8,128)(2,1)} %param.14), kind=kOutput, calls=%fused_computation.163 | convolution fusion | flops 2147483648 | bytes 8388608 | tf_op jit(solution)/shard_map/dot_general | solution.py:233
  81.1 12.3 %shard_map.113 = bf16[1024,512]{1,0:T(8,128)(2,1)} custom-call(f32[1024,512]{1,0:T(8,128)} %fusion.29.refs_0_, f32[1024,128]{1,0:T(8,128)} %get-tuple-element.77.refs_1_, f32[1024,128]{1,0:T(8,128)} %get-tuple-element.78.refs_2_, bf16[1024,128]{1,0:T(8,128)(2,1)} %get-tuple-element.17.refs_3_, bf16[1024,128]{1,0:T(8,128)(2,1)} %get-tuple-element.16.refs_4_, ...), custom_call_target="tpu_custom_call" | custom-call | flops 1610612736 | bytes 4718592 | tf_op jit(solution)/shard_map/pallas_call | solution.py:159
  93.4 3.6 %convolution_convert_fusion = bf16[1024,2048]{1,0:T(8,128)(2,1)S(1)} fusion(bf16[1024,512]{1,0:T(8,128)(2,1)} %shard_map.113, bf16[512,2048]{1,0:T(8,128)(2,1)S(1)} %copy-done), kind=kOutput, calls=%fused_computation.1 | convolution fusion | flops 2149580800 | bytes 7340032 | tf_op jit(solution)/shard_map/dot_general | solution.py:243
  100.5 1.5 %collective-permute-start.27 = (bf16[256,512]{1,0:T(8,128)(2,1)S(1)}, bf16[256,512]{1,0:T(8,128)(2,1)S(1)}, u32[]{:S(2)}, u32[]{:S(2)}) collective-permute-start(bf16[256,512]{1,0:T(8,128)(2,1)S(1)} %constant_dynamic-slice_fusion.13), channel_id=1, source_target_pairs={{0,4},{1,5},{2,6},{3,7},{4,0},{5,1},{6,2},{7,3},{8,12},{9,13},{10,... | collective-permute-start | bytes 786440 | tf_op jit(solution)/shard_map/ppermute | solution.py:100
  102.5 2.1 %collective-permute-start.37 = (bf16[256,512]{1,0:T(8,128)(2,1)S(1)}, bf16[256,512]{1,0:T(8,128)(2,1)S(1)}, u32[]{:S(2)}, u32[]{:S(2)}) collective-permute-start(bf16[256,512]{1,0:T(8,128)(2,1)S(1)} %constant_dynamic-slice_fusion.3), channel_id=1, source_target_pairs={{0,16},{1,17},{2,18},{3,19},{4,20},{5,21},{6,22},{7,23},{8,24},{9,... | collective-permute-start | bytes 786440 | tf_op jit(solution)/shard_map/ppermute | solution.py:100
  104.6 3.7 %collective-permute-done.22 = bf16[256,512]{1,0:T(8,128)(2,1)S(1)} collective-permute-done((bf16[256,512]{1,0:T(8,128)(2,1)S(1)}, bf16[256,512]{1,0:T(8,128)(2,1)S(1)}, u32[]{:S(2)}, u32[]{:S(2)}) %collective-permute-start.22) | collective-permute-done | bytes 262176 | tf_op jit(solution)/shard_map/ppermute | solution.py:100
  108.4 1.6 %collective-permute-start.23 = (bf16[128,512]{1,0:T(8,128)(2,1)S(1)}, bf16[128,512]{1,0:T(8,128)(2,1)S(1)}, u32[]{:S(2)}, u32[]{:S(2)}) collective-permute-start(bf16[128,512]{1,0:T(8,128)(2,1)S(1)} %constant_dynamic-slice_fusion.17), channel_id=1, source_target_pairs={{0,4},{1,5},{2,6},{3,7},{4,0},{5,1},{6,2},{7,3},{8,12},{9,13},{10,... | collective-permute-start | bytes 393224 | tf_op jit(solution)/shard_map/ppermute | solution.py:100
  110.2 6.2 %collective-permute-done.32 = bf16[256,512]{1,0:T(8,128)(2,1)S(1)} collective-permute-done((bf16[256,512]{1,0:T(8,128)(2,1)S(1)}, bf16[256,512]{1,0:T(8,128)(2,1)S(1)}, u32[]{:S(2)}, u32[]{:S(2)}) %collective-permute-start.32) | collective-permute-done | bytes 262176 | tf_op jit(solution)/shard_map/ppermute | solution.py:100
  119.0 2.1 %collective-permute-start.24 = (bf16[64,512]{1,0:T(8,128)(2,1)S(1)}, bf16[64,512]{1,0:T(8,128)(2,1)S(1)}, u32[]{:S(2)}, u32[]{:S(2)}) collective-permute-start(bf16[64,512]{1,0:T(8,128)(2,1)S(1)} %constant_dynamic-slice_fusion.16), channel_id=1, source_target_pairs={{0,8},{1,9},{2,10},{3,11},{4,12},{5,13},{6,14},{7,15},{8,0},{9,1},... | collective-permute-start | bytes 196616 | tf_op jit(solution)/shard_map/ppermute | solution.py:100
  121.8 2.8 %collective-permute-done.33 = bf16[128,512]{1,0:T(8,128)(2,1)S(1)} collective-permute-done((bf16[128,512]{1,0:T(8,128)(2,1)S(1)}, bf16[128,512]{1,0:T(8,128)(2,1)S(1)}, u32[]{:S(2)}, u32[]{:S(2)}) %collective-permute-start.33) | collective-permute-done | bytes 131104 | tf_op jit(solution)/shard_map/ppermute | solution.py:100
  124.7 2.8 %collective-permute-start.34 = (bf16[64,512]{1,0:T(8,128)(2,1)S(1)}, bf16[64,512]{1,0:T(8,128)(2,1)S(1)}, u32[]{:S(2)}, u32[]{:S(2)}) collective-permute-start(bf16[64,512]{1,0:T(8,128)(2,1)S(1)} %constant_dynamic-slice_fusion.6), channel_id=1, source_target_pairs={{0,2},{1,3},{2,0},{3,1},{4,6},{5,7},{6,4},{7,5},{8,10},{9,11},{10,... | collective-permute-start | bytes 196616 | tf_op jit(solution)/shard_map/ppermute | solution.py:100
  130.2 1.6 %collective-permute-done.39 = bf16[64,512]{1,0:T(8,128)(2,1)S(1)} collective-permute-done((bf16[64,512]{1,0:T(8,128)(2,1)S(1)}, bf16[64,512]{1,0:T(8,128)(2,1)S(1)}, u32[]{:S(2)}, u32[]{:S(2)}) %collective-permute-start.39) | collective-permute-done | bytes 65568 | tf_op jit(solution)/shard_map/ppermute | solution.py:100
  133.7 2.1 %collective-permute-done.40 = bf16[32,512]{1,0:T(8,128)(2,1)S(1)} collective-permute-done((bf16[32,512]{1,0:T(8,128)(2,1)S(1)}, bf16[32,512]{1,0:T(8,128)(2,1)S(1)}, u32[]{:S(2)}, u32[]{:S(2)}) %collective-permute-start.40) | collective-permute-done | bytes 32800 | tf_op jit(solution)/shard_map/ppermute | solution.py:100
  (212 shorter events, 42.8 us)
Async XLA Ops:
  3.6 30.2 %collective-permute-start = (bf16[32,512]{1,0:T(8,128)(2,1)S(1)}, bf16[32,512]{1,0:T(8,128)(2,1)S(1)}, u32[]{:S(2)}, u32[]{:S(2)}) collective-permute-start(bf16[32,512]{1,0:T(8,128)(2,1)S(1)} %get-tuple-element.50), channel_id=1, source_target_pairs={{0,16},{1,17},{2,18},{3,19},{4,20},{5,21},{6,22},{7,23},{8,24},{9,... | collective-permute-start | bytes 98312 | tf_op jit(solution)/shard_map/ppermute | solution.py:195
  7.7 26.1 %collective-permute-start.10 = (bf16[32,512]{1,0:T(8,128)(2,1)S(1)}, bf16[32,512]{1,0:T(8,128)(2,1)S(1)}, u32[]{:S(2)}, u32[]{:S(2)}) collective-permute-start(bf16[32,512]{1,0:T(8,128)(2,1)S(1)} %get-tuple-element.52), channel_id=1, source_target_pairs={{0,4},{1,5},{2,6},{3,7},{4,0},{5,1},{6,2},{7,3},{8,12},{9,13},{10,... | collective-permute-start | bytes 98312 | tf_op jit(solution)/shard_map/ppermute | solution.py:195
  9.2 24.6 %collective-permute-start.15 = (bf16[32,512]{1,0:T(8,128)(2,1)S(1)}, bf16[32,512]{1,0:T(8,128)(2,1)S(1)}, u32[]{:S(2)}, u32[]{:S(2)}) collective-permute-start(bf16[32,512]{1,0:T(8,128)(2,1)S(1)} %get-tuple-element.51), channel_id=1, source_target_pairs={{0,8},{1,9},{2,10},{3,11},{4,12},{5,13},{6,14},{7,15},{8,0},{9,1},... | collective-permute-start | bytes 98312 | tf_op jit(solution)/shard_map/ppermute | solution.py:195
  10.8 23.0 %collective-permute-start.5 = (bf16[32,512]{1,0:T(8,128)(2,1)S(1)}, bf16[32,512]{1,0:T(8,128)(2,1)S(1)}, u32[]{:S(2)}, u32[]{:S(2)}) collective-permute-start(bf16[32,512]{1,0:T(8,128)(2,1)S(1)} %get-tuple-element.53), channel_id=1, source_target_pairs={{0,2},{1,3},{2,0},{3,1},{4,6},{5,7},{6,4},{7,5},{8,10},{9,11},{10,... | collective-permute-start | bytes 98312 | tf_op jit(solution)/shard_map/ppermute | solution.py:195
  34.7 7.1 %collective-permute-start.11 = (bf16[64,512]{1,0:T(8,128)(2,1)S(1)}, bf16[64,512]{1,0:T(8,128)(2,1)S(1)}, u32[]{:S(2)}, u32[]{:S(2)}) collective-permute-start(bf16[64,512]{1,0:T(8,128)(2,1)S(1)} %pad_maximum_fusion.21), channel_id=1, source_target_pairs={{0,2},{1,3},{2,0},{3,1},{4,6},{5,7},{6,4},{7,5},{8,10},{9,11},{10,... | collective-permute-start | bytes 196616 | tf_op jit(solution)/shard_map/ppermute | solution.py:195
  35.3 6.6 %collective-permute-start.16 = (bf16[64,512]{1,0:T(8,128)(2,1)S(1)}, bf16[64,512]{1,0:T(8,128)(2,1)S(1)}, u32[]{:S(2)}, u32[]{:S(2)}) collective-permute-start(bf16[64,512]{1,0:T(8,128)(2,1)S(1)} %pad_maximum_fusion.22), channel_id=1, source_target_pairs={{0,4},{1,5},{2,6},{3,7},{4,0},{5,1},{6,2},{7,3},{8,12},{9,13},{10,... | collective-permute-start | bytes 196616 | tf_op jit(solution)/shard_map/ppermute | solution.py:195
  41.9 7.3 %collective-permute-start.12 = (bf16[128,512]{1,0:T(8,128)(2,1)S(1)}, bf16[128,512]{1,0:T(8,128)(2,1)S(1)}, u32[]{:S(2)}, u32[]{:S(2)}) collective-permute-start(bf16[128,512]{1,0:T(8,128)(2,1)S(1)} %pad_maximum_fusion.17), channel_id=1, source_target_pairs={{0,16},{1,17},{2,18},{3,19},{4,20},{5,21},{6,22},{7,23},{8,24},{9,... | collective-permute-start | bytes 393224 | tf_op jit(solution)/shard_map/ppermute | solution.py:195
  44.8 7.9 %collective-permute-start.3 = (bf16[256,512]{1,0:T(8,128)(2,1)S(1)}, bf16[256,512]{1,0:T(8,128)(2,1)S(1)}, u32[]{:S(2)}, u32[]{:S(2)}) collective-permute-start(bf16[256,512]{1,0:T(8,128)(2,1)S(1)} %pad_maximum_fusion.11), channel_id=1, source_target_pairs={{0,2},{1,3},{2,0},{3,1},{4,6},{5,7},{6,4},{7,5},{8,10},{9,11},{10,... | collective-permute-start | bytes 786440 | tf_op jit(solution)/shard_map/ppermute | solution.py:195
  46.6 6.4 %collective-permute-start.8 = (bf16[256,512]{1,0:T(8,128)(2,1)S(1)}, bf16[256,512]{1,0:T(8,128)(2,1)S(1)}, u32[]{:S(2)}, u32[]{:S(2)}) collective-permute-start(bf16[256,512]{1,0:T(8,128)(2,1)S(1)} %pad_maximum_fusion.12), channel_id=1, source_target_pairs={{0,4},{1,5},{2,6},{3,7},{4,0},{5,1},{6,2},{7,3},{8,12},{9,13},{10,... | collective-permute-start | bytes 786440 | tf_op jit(solution)/shard_map/ppermute | solution.py:195
  49.3 9.8 %collective-permute-start.13 = (bf16[256,512]{1,0:T(8,128)(2,1)S(1)}, bf16[256,512]{1,0:T(8,128)(2,1)S(1)}, u32[]{:S(2)}, u32[]{:S(2)}) collective-permute-start(bf16[256,512]{1,0:T(8,128)(2,1)S(1)} %pad_maximum_fusion.13), channel_id=1, source_target_pairs={{0,8},{1,9},{2,10},{3,11},{4,12},{5,13},{6,14},{7,15},{8,0},{9,1},... | collective-permute-start | bytes 786440 | tf_op jit(solution)/shard_map/ppermute | solution.py:195
  49.5 11.0 %collective-permute-start.18 = (bf16[256,512]{1,0:T(8,128)(2,1)S(1)}, bf16[256,512]{1,0:T(8,128)(2,1)S(1)}, u32[]{:S(2)}, u32[]{:S(2)}) collective-permute-start(bf16[256,512]{1,0:T(8,128)(2,1)S(1)} %pad_maximum_fusion.14), channel_id=1, source_target_pairs={{0,16},{1,17},{2,18},{3,19},{4,20},{5,21},{6,22},{7,23},{8,24},{9,... | collective-permute-start | bytes 786440 | tf_op jit(solution)/shard_map/ppermute | solution.py:195
  52.8 7.9 %collective-permute-start.4 = (bf16[512,512]{1,0:T(8,128)(2,1)S(1)}, bf16[512,512]{1,0:T(8,128)(2,1)S(1)}, u32[]{:S(2)}, u32[]{:S(2)}) collective-permute-start(bf16[512,512]{1,0:T(8,128)(2,1)S(1)} %pad_maximum_fusion.5), channel_id=1, source_target_pairs={{0,1},{1,0},{2,3},{3,2},{4,5},{5,4},{6,7},{7,6},{8,9},{9,8},{10,11... | collective-permute-start | bytes 1572872 | tf_op jit(solution)/shard_map/ppermute | solution.py:195
  53.2 7.8 %collective-permute-start.9 = (bf16[512,512]{1,0:T(8,128)(2,1)S(1)}, bf16[512,512]{1,0:T(8,128)(2,1)S(1)}, u32[]{:S(2)}, u32[]{:S(2)}) collective-permute-start(bf16[512,512]{1,0:T(8,128)(2,1)S(1)} %pad_maximum_fusion.6), channel_id=1, source_target_pairs={{0,1},{1,0},{2,3},{3,2},{4,5},{5,4},{6,7},{7,6},{8,9},{9,8},{10,11... | collective-permute-start | bytes 1572872 | tf_op jit(solution)/shard_map/ppermute | solution.py:195
  72.3 7.9 %collective-permute-start.20 = (bf16[1024,128]{1,0:T(8,128)(2,1)S(1)}, bf16[1024,128]{1,0:T(8,128)(2,1)S(1)}, u32[]{:S(2)}, u32[]{:S(2)}) collective-permute-start(bf16[1024,128]{1,0:T(8,128)(2,1)S(1)} %fusion.8), channel_id=1, source_target_pairs={{0,1},{1,0},{2,3},{3,2},{4,5},{5,4},{6,7},{7,6},{8,9},{9,8},{10,11... | collective-permute-start | bytes 786440 | tf_op jit(solution)/shard_map/ppermute | solution.py:18
  99.7 8.6 %collective-permute-start.22 = (bf16[256,512]{1,0:T(8,128)(2,1)S(1)}, bf16[256,512]{1,0:T(8,128)(2,1)S(1)}, u32[]{:S(2)}, u32[]{:S(2)}) collective-permute-start(bf16[256,512]{1,0:T(8,128)(2,1)S(1)} %constant_dynamic-slice_fusion.18), channel_id=1, source_target_pairs={{0,2},{1,3},{2,0},{3,1},{4,6},{5,7},{6,4},{7,5},{8,10},{9,11},{10,... | collective-permute-start | bytes 786440 | tf_op jit(solution)/shard_map/ppermute | solution.py:100
  100.5 9.4 %collective-permute-start.27 = (bf16[256,512]{1,0:T(8,128)(2,1)S(1)}, bf16[256,512]{1,0:T(8,128)(2,1)S(1)}, u32[]{:S(2)}, u32[]{:S(2)}) collective-permute-start(bf16[256,512]{1,0:T(8,128)(2,1)S(1)} %constant_dynamic-slice_fusion.13), channel_id=1, source_target_pairs={{0,4},{1,5},{2,6},{3,7},{4,0},{5,1},{6,2},{7,3},{8,12},{9,13},{10,... | collective-permute-start | bytes 786440 | tf_op jit(solution)/shard_map/ppermute | solution.py:100
  102.3 14.1 %collective-permute-start.32 = (bf16[256,512]{1,0:T(8,128)(2,1)S(1)}, bf16[256,512]{1,0:T(8,128)(2,1)S(1)}, u32[]{:S(2)}, u32[]{:S(2)}) collective-permute-start(bf16[256,512]{1,0:T(8,128)(2,1)S(1)} %constant_dynamic-slice_fusion.8), channel_id=1, source_target_pairs={{0,8},{1,9},{2,10},{3,11},{4,12},{5,13},{6,14},{7,15},{8,0},{9,1},... | collective-permute-start | bytes 786440 | tf_op jit(solution)/shard_map/ppermute | solution.py:100
  102.5 14.9 %collective-permute-start.37 = (bf16[256,512]{1,0:T(8,128)(2,1)S(1)}, bf16[256,512]{1,0:T(8,128)(2,1)S(1)}, u32[]{:S(2)}, u32[]{:S(2)}) collective-permute-start(bf16[256,512]{1,0:T(8,128)(2,1)S(1)} %constant_dynamic-slice_fusion.3), channel_id=1, source_target_pairs={{0,16},{1,17},{2,18},{3,19},{4,20},{5,21},{6,22},{7,23},{8,24},{9,... | collective-permute-start | bytes 786440 | tf_op jit(solution)/shard_map/ppermute | solution.py:100
  108.4 10.6 %collective-permute-start.23 = (bf16[128,512]{1,0:T(8,128)(2,1)S(1)}, bf16[128,512]{1,0:T(8,128)(2,1)S(1)}, u32[]{:S(2)}, u32[]{:S(2)}) collective-permute-start(bf16[128,512]{1,0:T(8,128)(2,1)S(1)} %constant_dynamic-slice_fusion.17), channel_id=1, source_target_pairs={{0,4},{1,5},{2,6},{3,7},{4,0},{5,1},{6,2},{7,3},{8,12},{9,13},{10,... | collective-permute-start | bytes 393224 | tf_op jit(solution)/shard_map/ppermute | solution.py:100
  110.1 11.0 %collective-permute-start.28 = (bf16[128,512]{1,0:T(8,128)(2,1)S(1)}, bf16[128,512]{1,0:T(8,128)(2,1)S(1)}, u32[]{:S(2)}, u32[]{:S(2)}) collective-permute-start(bf16[128,512]{1,0:T(8,128)(2,1)S(1)} %constant_dynamic-slice_fusion.12), channel_id=1, source_target_pairs={{0,8},{1,9},{2,10},{3,11},{4,12},{5,13},{6,14},{7,15},{8,0},{9,1},... | collective-permute-start | bytes 393224 | tf_op jit(solution)/shard_map/ppermute | solution.py:100
  116.4 8.2 %collective-permute-start.33 = (bf16[128,512]{1,0:T(8,128)(2,1)S(1)}, bf16[128,512]{1,0:T(8,128)(2,1)S(1)}, u32[]{:S(2)}, u32[]{:S(2)}) collective-permute-start(bf16[128,512]{1,0:T(8,128)(2,1)S(1)} %constant_dynamic-slice_fusion.7), channel_id=1, source_target_pairs={{0,16},{1,17},{2,18},{3,19},{4,20},{5,21},{6,22},{7,23},{8,24},{9,... | collective-permute-start | bytes 393224 | tf_op jit(solution)/shard_map/ppermute | solution.py:100
  117.6 9.9 %collective-permute-start.38 = (bf16[128,512]{1,0:T(8,128)(2,1)S(1)}, bf16[128,512]{1,0:T(8,128)(2,1)S(1)}, u32[]{:S(2)}, u32[]{:S(2)}) collective-permute-start(bf16[128,512]{1,0:T(8,128)(2,1)S(1)} %constant_dynamic-slice_fusion.2), channel_id=1, source_target_pairs={{0,2},{1,3},{2,0},{3,1},{4,6},{5,7},{6,4},{7,5},{8,10},{9,11},{10,... | collective-permute-start | bytes 393224 | tf_op jit(solution)/shard_map/ppermute | solution.py:100
  119.0 8.6 %collective-permute-start.24 = (bf16[64,512]{1,0:T(8,128)(2,1)S(1)}, bf16[64,512]{1,0:T(8,128)(2,1)S(1)}, u32[]{:S(2)}, u32[]{:S(2)}) collective-permute-start(bf16[64,512]{1,0:T(8,128)(2,1)S(1)} %constant_dynamic-slice_fusion.16), channel_id=1, source_target_pairs={{0,8},{1,9},{2,10},{3,11},{4,12},{5,13},{6,14},{7,15},{8,0},{9,1},... | collective-permute-start | bytes 196616 | tf_op jit(solution)/shard_map/ppermute | solution.py:100
  121.2 6.6 %collective-permute-start.29 = (bf16[64,512]{1,0:T(8,128)(2,1)S(1)}, bf16[64,512]{1,0:T(8,128)(2,1)S(1)}, u32[]{:S(2)}, u32[]{:S(2)}) collective-permute-start(bf16[64,512]{1,0:T(8,128)(2,1)S(1)} %constant_dynamic-slice_fusion.11), channel_id=1, source_target_pairs={{0,16},{1,17},{2,18},{3,19},{4,20},{5,21},{6,22},{7,23},{8,24},{9,... | collective-permute-start | bytes 196616 | tf_op jit(solution)/shard_map/ppermute | solution.py:100
  (30 other events, 271.6 us)
